TPU v7x, 512 devices: a whole 4x4x16 slice. The times are simulated.
512 devices in a mesh: row: 32 (over x, z_hi, core), col: 16 (over z_lo, y).
Axes of the slice: x: 4, y: 4, z: 16 (z_hi: 4, z_lo: 4; z = z_hi * 4 + z_lo), core: 2. Of those that a mesh axis runs over, the one named last changes fastest.
Arguments:
- images: bfloat16 [32, 128, 128, 256], P('row', 'col'), may hold values from -6 to 6
- weight: bfloat16 [3, 3, 256, 256], P(None, None, None, 'col'), may hold values from -0.125 to 0.125
- norm_gain: float32 [256], replicated, may hold values from 0.5 to 1.5
- cotangent: bfloat16 [32, 128, 128, 256], P('row', 'col'), may hold values from -6 to 6
Outputs:
- features: bfloat16 [32, 128, 128, 256], P('row', 'col')
- input_grad: bfloat16 [32, 128, 128, 256], P('row', 'col')
- weight_grad: float32 [3, 3, 256, 256], P(None, None, None, 'col')
All inputs are finite; a program needn't handle non-finite values.
Results may differ from a plain program's by a relative error of at most 0.013.
Values may be sent and summed in bfloat16 or wider, within the bound.
No kernel may reach another device: no remote copies, remote signals or barrier semaphores. Data moves between devices by JAX's collectives and lax.ppermute only.
A program may use at most 64 MiB of HBM per device.

v0:
```python
import math

import jax
import jax.numpy as jnp
from jax import lax
from jax.sharding import PartitionSpec as P

epsilon = 1e-06
root_half = 0.7071067811865476
norm_const = 0.3989422804014327


def padded_2(value, sides, width):
    for axis, dim in sides:
        peers, length = (lax.axis_size(axis), value.shape[dim])
        up = [(i, (i + 1) % peers) for i in range(peers - 1)]
        down = [(j, i) for i, j in up]
        last = lax.slice_in_dim(value, length - width, length, axis=dim)
        initial = lax.slice_in_dim(value, 0, width, axis=dim)
        before = lax.ppermute(last, axis, up)
        after = lax.ppermute(initial, axis, down)
        value = jnp.concatenate([before, value, after], axis=dim)
    return value


def norm_act(conv_out, upper, norm_gain):
    mean_val = jnp.mean(conv_out, axis=-1, keepdims=True)
    centred = conv_out - mean_val
    variance = jnp.mean(centred * centred, axis=-1, keepdims=True)
    inv_std = lax.rsqrt(variance + epsilon)
    unit = centred * inv_std
    normed = unit * norm_gain
    cdf_val = 0.5 * (1.0 + lax.erf(normed * root_half))
    density = jnp.exp(-0.5 * normed * normed) * norm_const
    outputs = (normed * cdf_val).astype(jnp.bfloat16)
    upstream = upper.astype(jnp.float32) * (cdf_val + normed * density) * norm_gain
    mean_up = jnp.mean(upstream, axis=-1, keepdims=True)
    mean_cross = jnp.mean(upstream * unit, axis=-1, keepdims=True)
    grad_pre = inv_std * (upstream - mean_up - unit * mean_cross)
    return (outputs, grad_pre.astype(jnp.bfloat16))


def window(padded, tap_row, tap_col, tile_rows, tile_cols):
    return padded[:, tap_row : tap_row + tile_rows, tap_col : tap_col + tile_cols, :].reshape(
        -1, padded.shape[-1]
    )


def on_device(images, weight, norm_gain, cotangent):
    img_count, tile_rows, tile_cols, in_chan = images.shape
    whole_kernel = lax.all_gather(weight, "col", axis=3, tiled=True)
    out_chan = whole_kernel.shape[3]
    rimmed = padded_2(images, (("col", 1),), 1)
    padded = jnp.pad(rimmed, ((0, 0), (0, 0), (1, 1), (0, 0)))
    conv_out = jnp.zeros((img_count * tile_rows * tile_cols, out_chan), jnp.float32)
    for tap_row in range(3):
        for tap_col in range(3):
            conv_out = conv_out + jnp.dot(
                window(padded, tap_row, tap_col, tile_rows, tile_cols),
                whole_kernel[tap_row, tap_col],
                preferred_element_type=jnp.float32,
            )
    outputs, grad_pre = norm_act(conv_out, cotangent.reshape(-1, out_chan), norm_gain)
    grad_grid = grad_pre.reshape(img_count, tile_rows, tile_cols, out_chan)
    grad_rimmed = padded_2(grad_grid, (("col", 1),), 1)
    grad_pad = jnp.pad(grad_rimmed, ((0, 0), (0, 0), (1, 1), (0, 0)))
    grad_input = jnp.zeros((img_count * tile_rows * tile_cols, in_chan), jnp.float32)
    pieces = []
    for tap_row in range(3):
        for tap_col in range(3):
            grad_input = grad_input + lax.dot_general(
                window(grad_pad, 2 - tap_row, 2 - tap_col, tile_rows, tile_cols),
                whole_kernel[tap_row, tap_col],
                (((1,), (1,)), ((), ())),
                preferred_element_type=jnp.float32,
            )
            pieces.append(
                lax.dot_general(
                    window(padded, tap_row, tap_col, tile_rows, tile_cols),
                    grad_pre,
                    (((0,), (0,)), ((), ())),
                    preferred_element_type=jnp.float32,
                )
            )
    partial_value = jnp.stack(pieces).reshape(3, 3, in_chan, out_chan)
    totals = lax.psum(partial_value, ("row", "col"))
    col_share = out_chan // lax.axis_size("col")
    own_share = lax.dynamic_slice_in_dim(totals, lax.axis_index("col") * col_share, col_share, 3)
    pixels = img_count * lax.axis_size("row") * tile_rows * lax.axis_size("col") * tile_cols
    weight_grad = own_share * (1.0 / math.sqrt(pixels))
    features = outputs.reshape(img_count, tile_rows, tile_cols, out_chan)
    input_grad = grad_input.astype(jnp.bfloat16).reshape(img_count, tile_rows, tile_cols, in_chan)
    return (features, input_grad, weight_grad)


def solution(mesh):
    placed = (
        P("row", "col", None, None),
        P(None, None, None, "col"),
        P(),
        P("row", "col", None, None),
    )
    return jax.shard_map(
        on_device,
        mesh=mesh,
        in_specs=placed,
        out_specs=(
            P("row", "col", None, None),
            P("row", "col", None, None),
            P(None, None, None, "col"),
        ),
        check_vma=False,
    )
```

profile of v0, /device:TPU:4, one launch (start us, length us, event | category | flops | bytes accessed | tf_op | source)
XLA Modules:
  0.0 616.7 jit_solution(12036107945683514388)
XLA Ops:
  7.2 0.0 copy-start
  7.2 0.0 all-gather.2.cloned.1.call-start
  7.2 0.7 all-gather.2.cloned.1.call-update
  7.9 0.0 all-reduce.4.cloned.1.call-start
  8.0 0.9 fusion.29
  8.8 3.5 collective-permute-start
  12.3 1.3 collective-permute-start.1
  13.6 0.6 collective-permute-done
  14.2 4.3 collective-permute-done.1
  18.5 1.2 select_maximum_fusion.2
  19.7 1.0 pad_maximum_fusion.2
  20.8 1.4 fusion.27
  22.1 79.1 %all-gather.2.cloned.1.call-done = bf16[3,3,256,256]{2,3,1,0:T(8,128)(2,1)} async-done(((bf16[3,3,256,16]{2,3,1,0:T(8,128)(2,1)}), bf16[3,3,256,256]{2,3,1,0:T(8,128)(2,1)}) %all-gather.2.cloned.1.call-update) | async-done | bytes 1179664 | tf_op jit(solution)/shard_map/all_gather | solution.py:51
  101.3 1.4 fusion.21
  102.6 0.3 fusion.23
  103.0 0.3 convolution_add_fusion.13
  103.3 0.0 copy-start.5
  103.3 0.7 copy-done.6
  104.0 0.3 convolution_add_fusion.12
  104.3 0.1 copy-done.5
  104.4 0.3 convolution_add_fusion.11
  104.8 0.0 copy-start.4
  104.8 0.3 convolution_add_fusion.10
  105.1 0.7 copy-done.4
  105.8 0.3 convolution_add_fusion.9
  106.1 0.0 copy-start.7
  106.2 0.0 copy-done.2
  106.2 0.3 convolution_add_fusion.8
  106.5 0.7 copy-done.7
  107.2 0.4 fusion.30
  107.6 0.0 copy-start.9
  107.6 0.4 multiply_reduce_fusion.1
  108.0 0.6 copy-done.9
  108.7 1.9 fusion.24
  110.6 0.8 multiply_convert_fusion
  111.4 1.0 fusion.12
  112.5 1.1 fusion.11
  113.5 1.1 fusion.10
  114.6 1.1 fusion.9
  115.6 1.0 fusion.8
  116.7 1.0 fusion.7
  117.7 1.0 fusion.6
  118.8 1.0 fusion.5
  119.8 3.0 collective-permute-start.2
  122.8 1.3 collective-permute-start.3
  124.1 1.0 fusion.4
  125.2 3.1 copy.8
  128.3 0.0 all-reduce.4.cloned.1.call-update
  128.3 0.0 collective-permute-done.2
  128.4 0.6 collective-permute-done.3
  129.0 0.2 select_maximum_fusion
  129.2 0.4 fusion.26
  129.6 0.1 pad_maximum_fusion
  129.7 0.3 fusion.20
  130.0 0.3 fusion.22
  130.3 0.3 convolution_add_fusion.6
  130.6 0.3 convolution_add_fusion.5
  130.9 0.3 convolution_add_fusion.4
  131.2 0.3 convolution_add_fusion.3
  131.5 0.3 convolution_add_fusion.2
  131.8 0.3 convolution_add_fusion.1
  132.1 1.1 fusion.3
  133.2 475.1 %all-reduce.4.cloned.1.call-done = f32[3,3,256,256]{2,3,1,0:T(8,128)} async-done(((f32[3,3,256,256]{2,3,1,0:T(8,128)}), f32[3,3,256,256]{2,3,1,0:T(8,128)}) %all-reduce.4.cloned.1.call-update) | async-done | bytes 2359312 | tf_op jit(solution)/shard_map/psum | solution.py:86
  608.2 1.6 dynamic-slice_multiply_fusion
  (15 shorter events, 0.0 us)
Async XLA Ops:
  7.2 12.6 %copy-start = (bf16[1,8,128,256]{3,2,1,0:T(8,128)(2,1)S(1)}, bf16[1,8,128,256]{3,2,1,0:T(8,128)(2,1)}, u32[]{:S(2)}) copy-start(bf16[1,8,128,256]{3,2,1,0:T(8,128)(2,1)} %param.4) | copy-start | bytes 1572868
  7.2 94.1 %all-gather.2.cloned.1.call-start = ((), (), s32[]{:S(2)}) async-start(), calls=%async_computation | async-start | bytes 1253376 | tf_op jit(solution)/shard_map/all_gather | solution.py:51
  7.9 600.3 %all-reduce.4.cloned.1.call-start = ((), (), s32[]{:S(2)}) async-start(), calls=%async_computation.1 | async-start | bytes 4718592 | tf_op jit(solution)/shard_map/psum | solution.py:86
  8.8 5.4 collective-permute-start
  12.3 6.2 collective-permute-start.1
  22.1 84.0 %copy-start.2 = (bf16[1,8,128,256]{3,2,1,0:T(8,128)(2,1)}, bf16[1,8,128,256]{3,2,1,0:T(8,128)(2,1)S(1)}, u32[]{:S(2)}) copy-start(bf16[1,8,128,256]{3,2,1,0:T(8,128)(2,1)S(1)} %get-tuple-element.13) | copy-start | bytes 1572868
  101.3 1.4 copy-start.1
  101.3 1.7 copy-start.8
  103.0 1.0 copy-start.6
  103.3 1.1 copy-start.5
  104.8 1.0 copy-start.4
  106.1 1.0 copy-start.7
  107.2 0.8 copy-start.10
  107.6 1.0 copy-start.9
  115.6 2.1 copy-start.3
  119.8 8.5 %collective-permute-start.2 = (bf16[1,1,128,256]{3,2,1,0:T(8,128)(2,1)S(1)}, bf16[1,1,128,256]{3,2,1,0:T(8,128)(2,1)S(1)}, u32[]{:S(2)}, u32[]{:S(2)}) collective-permute-start(bf16[1,1,128,256]{3,2,1,0:T(8,128)(2,1)S(1)} %get-tuple-element.21), channel_id=1, source_target_pairs={{0,1},{1,2},{2,3},{3,4},{4,5},{5,6},{6,7},{7,8},{8,9},{9,10},{10,1... | collective-permute-start | bytes 196616 | tf_op jit(solution)/shard_map/ppermute | solution.py:20
  122.8 6.2 collective-permute-start.3
Sparse Core Ops, SparseCore 0:
  10.1 91.1 all-gather.1
  128.5 479.7 all-reduce.3
where the time goes:
time: 617 us
  waiting for transfers between devices  560 us (91%)
  matrix products  17 us (3%)
  between operations  14.3 us (2%)
  starting transfers between devices  9.16 us (1%)
  local copies, waits for them, and re-layouts  8.58 us (1%)
  other arithmetic  7.21 us (1%)
    psum x1, waiting for transfers between devices, on_device(): totals = lax.psum(partial_value, ('row', 'col'))  475 us
    all_gather x1, waiting for transfers between devices, on_device(): whole_kernel = lax.all_gather(weight, 'col', axis=3, tiled=True)  79.1 us
  transfers between devices with their start and end apart: 6, of which 5 were waited for; matrix products, arithmetic and copies ran while one was open for 2% of the time, Pallas kernels for 0%

commit v1 on v0

--- a/solution.py
+++ b/solution.py
@@ -83,9 +83,8 @@
                 )
             )
     partial_value = jnp.stack(pieces).reshape(3, 3, in_chan, out_chan)
-    totals = lax.psum(partial_value, ("row", "col"))
-    col_share = out_chan // lax.axis_size("col")
-    own_share = lax.dynamic_slice_in_dim(totals, lax.axis_index("col") * col_share, col_share, 3)
+    col_sum = lax.psum_scatter(partial_value, "col", scatter_dimension=3, tiled=True)
+    own_share = lax.psum(col_sum, "row")
     pixels = img_count * lax.axis_size("row") * tile_rows * lax.axis_size("col") * tile_cols
     weight_grad = own_share * (1.0 / math.sqrt(pixels))
     features = outputs.reshape(img_count, tile_rows, tile_cols, out_chan)

time: 617 us -> 547 us (0.89)
  the two profiles are of different devices: /device:TPU:4 before, /device:TPU:1 now
where the time goes in v1:
time: 547 us
  waiting for transfers between devices  488 us (89%)
  matrix products  18 us (3%)
  between operations  14 us (3%)
  starting transfers between devices  9.47 us (2%)
  local copies, waits for them, and re-layouts  8.58 us (2%)
  other arithmetic  8.02 us (1%)
    psum x1, waiting for transfers between devices, on_device(): own_share = lax.psum(col_sum, 'row')  330 us
    reduce_scatter x1, waiting for transfers between devices, on_device(): lax.psum_scatter(partial_value, 'col', scatter_dimension=3, tiled=True)  79.9 us
    all_gather x1, waiting for transfers between devices, on_device(): whole_kernel = lax.all_gather(weight, 'col', axis=3, tiled=True)  70.6 us
  transfers between devices with their start and end apart: 7, of which 5 were waited for; matrix products, arithmetic and copies ran while one was open for 2% of the time, Pallas kernels for 0%

profile of v1, /device:TPU:1, one launch (start us, length us, event | category | flops | bytes accessed | tf_op | source)
XLA Modules:
  0.0 546.5 jit_solution(15703114254889258676)
XLA Ops:
  7.2 0.0 copy-start
  7.2 0.0 all-gather.2.cloned.1.call-start
  7.2 0.7 all-gather.2.cloned.1.call-update
  7.9 0.0 reduce-scatter.2.cloned.1.call-start
  8.0 0.9 fusion.29
  8.8 4.0 collective-permute-start
  12.9 1.3 collective-permute-start.1
  14.2 0.0 collective-permute-done
  14.2 3.7 collective-permute-done.1
  17.9 1.2 select_maximum_fusion.2
  19.1 1.0 pad_maximum_fusion.2
  20.2 1.4 fusion.27
  21.5 70.6 %all-gather.2.cloned.1.call-done = bf16[3,3,256,256]{2,3,1,0:T(8,128)(2,1)} async-done(((bf16[3,3,256,16]{2,3,1,0:T(8,128)(2,1)}), bf16[3,3,256,256]{2,3,1,0:T(8,128)(2,1)}) %all-gather.2.cloned.1.call-update) | async-done | bytes 1179664 | tf_op jit(solution)/shard_map/all_gather | solution.py:51
  92.2 1.4 fusion.21
  93.5 0.3 fusion.23
  93.9 0.3 convolution_add_fusion.13
  94.2 0.0 copy-start.5
  94.3 0.7 copy-done.6
  94.9 0.3 convolution_add_fusion.12
  95.3 0.1 copy-done.5
  95.3 0.3 convolution_add_fusion.11
  95.7 0.0 copy-start.4
  95.7 0.3 convolution_add_fusion.10
  96.0 0.7 copy-done.4
  96.7 0.3 convolution_add_fusion.9
  97.1 0.3 convolution_add_fusion.8
  97.4 0.7 copy-done.7
  98.1 0.4 fusion.30
  98.5 0.4 multiply_reduce_fusion.1
  98.9 0.6 copy-done.9
  99.6 1.9 fusion.24
  101.5 0.8 multiply_convert_fusion
  102.3 1.0 fusion.12
  103.4 1.1 fusion.11
  104.4 1.1 fusion.10
  105.5 1.0 fusion.9
  106.5 1.0 fusion.8
  107.6 1.1 fusion.7
  108.6 1.0 fusion.6
  109.6 1.0 fusion.5
  110.7 1.0 fusion.4
  111.7 3.1 copy.8
  114.9 0.0 reduce-scatter.2.cloned.1.call-update
  114.9 0.0 all-reduce.4.cloned.1.call-start
  115.0 2.7 collective-permute-start.2
  117.7 1.3 collective-permute-start.3
  119.0 0.0 collective-permute-done.2
  119.0 3.7 collective-permute-done.3
  122.7 0.2 select_maximum_fusion
  122.9 0.9 pad_maximum_fusion
  123.8 0.4 fusion.26
  124.2 0.3 fusion.20
  124.5 0.3 fusion.22
  124.8 0.3 convolution_add_fusion.6
  125.1 0.3 convolution_add_fusion.5
  125.4 0.3 convolution_add_fusion.4
  125.7 0.3 convolution_add_fusion.3
  126.0 0.3 convolution_add_fusion.2
  126.3 0.3 convolution_add_fusion.1
  126.6 79.9 %reduce-scatter.2.cloned.1.call-done = f32[3,3,256,16]{2,3,1,0:T(8,128)} async-done(((f32[3,3,256,256]{2,3,1,0:T(8,128)}), f32[3,3,256,16]{2,3,1,0:T(8,128)}) %reduce-scatter.2.cloned.1.call-update) | async-done | bytes 147472 | tf_op jit(solution)/shard_map/reduce_scatter | solution.py:86
  206.5 0.0 all-reduce.4.cloned.1.call-update
  206.6 2.1 fusion.3
  208.7 329.7 %all-reduce.4.cloned.1.call-done = f32[3,3,256,16]{2,3,1,0:T(8,128)} async-done(((f32[3,3,256,16]{2,3,1,0:T(8,128)}), f32[3,3,256,16]{2,3,1,0:T(8,128)}) %all-reduce.4.cloned.1.call-update) | async-done | bytes 147472 | tf_op jit(solution)/shard_map/psum | solution.py:87
  538.4 1.6 broadcast_multiply_fusion
  (18 shorter events, 0.1 us)
Async XLA Ops:
  7.2 12.0 %copy-start = (bf16[1,8,128,256]{3,2,1,0:T(8,128)(2,1)S(1)}, bf16[1,8,128,256]{3,2,1,0:T(8,128)(2,1)}, u32[]{:S(2)}) copy-start(bf16[1,8,128,256]{3,2,1,0:T(8,128)(2,1)} %param.4) | copy-start | bytes 1572868
  7.2 85.0 %all-gather.2.cloned.1.call-start = ((), (), s32[]{:S(2)}) async-start(), calls=%async_computation.1 | async-start | bytes 1253376 | tf_op jit(solution)/shard_map/all_gather | solution.py:51
  7.9 198.6 %reduce-scatter.2.cloned.1.call-start = ((), (), s32[]{:S(2)}) async-start(), calls=%async_computation.2 | async-start | bytes 2506752 | tf_op jit(solution)/shard_map/reduce_scatter | solution.py:86
  8.8 5.4 collective-permute-start
  12.9 5.0 collective-permute-start.1
  21.5 75.5 %copy-start.2 = (bf16[1,8,128,256]{3,2,1,0:T(8,128)(2,1)}, bf16[1,8,128,256]{3,2,1,0:T(8,128)(2,1)S(1)}, u32[]{:S(2)}) copy-start(bf16[1,8,128,256]{3,2,1,0:T(8,128)(2,1)S(1)} %get-tuple-element.13) | copy-start | bytes 1572868
  92.2 1.4 copy-start.1
  92.2 1.7 copy-start.8
  93.9 1.0 copy-start.6
  94.2 1.1 copy-start.5
  95.7 1.0 copy-start.4
  97.0 1.0 copy-start.7
  98.1 0.8 copy-start.10
  98.5 1.0 copy-start.9
  106.5 2.1 copy-start.3
  114.9 423.5 %all-reduce.4.cloned.1.call-start = ((), (), s32[]{:S(2)}) async-start(), calls=%async_computation.3 | async-start | bytes 294912 | tf_op jit(solution)/shard_map/psum | solution.py:87
  115.0 4.1 collective-permute-start.2
  117.7 5.0 collective-permute-start.3
Sparse Core Ops, SparseCore 0:
  10.1 82.0 all-gather.1
  115.0 91.4 reduce-scatter.1
  209.5 328.8 all-reduce.3

commit v2 on v1

--- a/solution.py
+++ b/solution.py
@@ -20,6 +20,42 @@
         before = lax.ppermute(last, axis, up)
         after = lax.ppermute(initial, axis, down)
         value = jnp.concatenate([before, value, after], axis=dim)
+    return value
+
+
+def exchange(value, axis, bit):
+    peers = lax.axis_size(axis)
+    pairs = [(i, i ^ (1 << bit)) for i in range(peers)]
+    return lax.ppermute(value, axis, pairs)
+
+
+def gather_chunks(value, axis):
+    peers, me = lax.axis_size(axis), lax.axis_index(axis)
+    held = value[None]
+    for bit in range(peers.bit_length() - 1):
+        other = exchange(held, axis, bit)
+        upper = (me >> bit) & 1
+        held = jnp.where(upper == 0, jnp.concatenate([held, other]), jnp.concatenate([other, held]))
+    return held
+
+
+def scatter_sum(value, axis):
+    peers, me = lax.axis_size(axis), lax.axis_index(axis)
+    held = value
+    for bit in reversed(range(peers.bit_length() - 1)):
+        half = held.shape[0] // 2
+        low, high = held[:half], held[half:]
+        upper = ((me >> bit) & 1) == 1
+        keep = jnp.where(upper, high, low)
+        send = jnp.where(upper, low, high)
+        held = keep + exchange(send, axis, bit)
+    return held
+
+
+def total_sum(value, axis):
+    peers = lax.axis_size(axis)
+    for bit in range(peers.bit_length() - 1):
+        value = value + exchange(value, axis, bit)
     return value
 
 
@@ -48,8 +84,11 @@
 
 def on_device(images, weight, norm_gain, cotangent):
     img_count, tile_rows, tile_cols, in_chan = images.shape
-    whole_kernel = lax.all_gather(weight, "col", axis=3, tiled=True)
-    out_chan = whole_kernel.shape[3]
+    taps, share = 9 * in_chan, weight.shape[3]
+    local_t = weight.reshape(taps, share).T
+    kernel_t = gather_chunks(local_t, "col").reshape(-1, taps)
+    out_chan = kernel_t.shape[0]
+    whole_kernel = kernel_t.T.reshape(3, 3, in_chan, out_chan)
     rimmed = padded_2(images, (("col", 1),), 1)
     padded = jnp.pad(rimmed, ((0, 0), (0, 0), (1, 1), (0, 0)))
     conv_out = jnp.zeros((img_count * tile_rows * tile_cols, out_chan), jnp.float32)
@@ -76,17 +115,17 @@
             )
             pieces.append(
                 lax.dot_general(
+                    grad_pre,
                     window(padded, tap_row, tap_col, tile_rows, tile_cols),
-                    grad_pre,
                     (((0,), (0,)), ((), ())),
                     preferred_element_type=jnp.float32,
                 )
             )
-    partial_value = jnp.stack(pieces).reshape(3, 3, in_chan, out_chan)
-    col_sum = lax.psum_scatter(partial_value, "col", scatter_dimension=3, tiled=True)
-    own_share = lax.psum(col_sum, "row")
+    partial_value = jnp.stack(pieces, axis=1).reshape(out_chan, taps)
+    col_sum = scatter_sum(partial_value, "col")
+    own_share = total_sum(col_sum, "row")
     pixels = img_count * lax.axis_size("row") * tile_rows * lax.axis_size("col") * tile_cols
-    weight_grad = own_share * (1.0 / math.sqrt(pixels))
+    weight_grad = (own_share * (1.0 / math.sqrt(pixels))).T.reshape(3, 3, in_chan, share)
     features = outputs.reshape(img_count, tile_rows, tile_cols, out_chan)
     input_grad = grad_input.astype(jnp.bfloat16).reshape(img_count, tile_rows, tile_cols, in_chan)
     return (features, input_grad, weight_grad)

time: 547 us -> 240 us (0.44)
  the two profiles are of different devices: /device:TPU:1 before, /device:TPU:4 now
where the time goes in v2:
time: 240 us; the launch traced here: 239 us
  waiting for transfers between devices  140 us (58%)
  starting transfers between devices  64.2 us (27%)
  local copies, waits for them, and re-layouts  13.1 us (5%)
  matrix products  10.7 us (4%)
  other arithmetic  9.67 us (4%)
    ppermute x13, waiting for transfers between devices, exchange(): return lax.ppermute(value, axis, pairs)  137 us
    ppermute x13, starting transfers between devices, exchange(): return lax.ppermute(value, axis, pairs)  56.8 us
    unnamed x26, local copies, waits for them, and re-layouts  6.23 us
  transfers between devices with their start and end apart: 17, of which 13 were waited for; matrix products, arithmetic and copies ran while one was open for 4% of the time, Pallas kernels for 0%

profile of v2, /device:TPU:4, one launch (start us, length us, event | category | flops | bytes accessed | tf_op | source)
XLA Modules:
  0.0 238.9 jit_solution(14682853859440728412)
XLA Ops:
  0.6 1.0 copy.8
  1.7 3.5 %collective-permute-start.2 = (bf16[1,16,2304]{2,1,0:T(8,128)(2,1)S(1)}, bf16[1,16,2304]{2,1,0:T(8,128)(2,1)S(1)}, u32[]{:S(2)}, u32[]{:S(2)}) collective-permute-start(bf16[1,16,2304]{2,1,0:T(8,128)(2,1)S(1)} %bitcast.209), channel_id=1, source_target_pairs={{0,1},{1,0},{2,3},{3,2},{4,5},{5,4},{6,7},{7,6},{8,9},{9,8},{10,11... | collective-permute-start | bytes 221192 | tf_op jit(solution)/shard_map/ppermute | solution.py:29
  5.2 2.7 %collective-permute-done.2 = bf16[1,16,2304]{2,1,0:T(8,128)(2,1)S(1)} collective-permute-done((bf16[1,16,2304]{2,1,0:T(8,128)(2,1)S(1)}, bf16[1,16,2304]{2,1,0:T(8,128)(2,1)S(1)}, u32[]{:S(2)}, u32[]{:S(2)}) %collective-permute-start.2) | collective-permute-done | bytes 73760 | tf_op jit(solution)/shard_map/ppermute | solution.py:29
  8.0 5.1 %collective-permute-start.3 = (bf16[2,16,2304]{2,1,0:T(8,128)(2,1)S(1)}, bf16[2,16,2304]{2,1,0:T(8,128)(2,1)S(1)}, u32[]{:S(2)}, u32[]{:S(2)}) collective-permute-start(bf16[2,16,2304]{2,1,0:T(8,128)(2,1)S(1)} %maximum_select_fusion.3), channel_id=1, source_target_pairs={{0,2},{1,3},{2,0},{3,1},{4,6},{5,7},{6,4},{7,5},{8,10},{9,11},{10,... | collective-permute-start | bytes 442376 | tf_op jit(solution)/shard_map/ppermute | solution.py:29
  13.1 3.4 %collective-permute-done.3 = bf16[2,16,2304]{2,1,0:T(8,128)(2,1)S(1)} collective-permute-done((bf16[2,16,2304]{2,1,0:T(8,128)(2,1)S(1)}, bf16[2,16,2304]{2,1,0:T(8,128)(2,1)S(1)}, u32[]{:S(2)}, u32[]{:S(2)}) %collective-permute-start.3) | collective-permute-done | bytes 147488 | tf_op jit(solution)/shard_map/ppermute | solution.py:29
  16.6 3.8 %collective-permute-start.4 = (bf16[4,16,2304]{2,1,0:T(8,128)(2,1)S(1)}, bf16[4,16,2304]{2,1,0:T(8,128)(2,1)S(1)}, u32[]{:S(2)}, u32[]{:S(2)}) collective-permute-start(bf16[4,16,2304]{2,1,0:T(8,128)(2,1)S(1)} %maximum_select_fusion.2), channel_id=1, source_target_pairs={{0,4},{1,5},{2,6},{3,7},{4,0},{5,1},{6,2},{7,3},{8,12},{9,13},{10,... | collective-permute-start | bytes 884744 | tf_op jit(solution)/shard_map/ppermute | solution.py:29
  20.4 3.5 %collective-permute-start = (bf16[1,1,128,256]{3,2,1,0:T(8,128)(2,1)S(1)}, bf16[1,1,128,256]{3,2,1,0:T(8,128)(2,1)S(1)}, u32[]{:S(2)}, u32[]{:S(2)}) collective-permute-start(bf16[1,1,128,256]{3,2,1,0:T(8,128)(2,1)S(1)} %get-tuple-element.30), channel_id=1, source_target_pairs={{0,1},{1,2},{2,3},{3,4},{4,5},{5,6},{6,7},{7,8},{8,9},{9,10},{10,1... | collective-permute-start | bytes 196616 | tf_op jit(solution)/shard_map/ppermute | solution.py:20
  23.9 1.3 collective-permute-start.1
  25.4 8.4 %collective-permute-start.5 = (bf16[8,16,2304]{2,1,0:T(8,128)(2,1)S(1)}, bf16[8,16,2304]{2,1,0:T(8,128)(2,1)}, u32[]{:S(2)}, u32[]{:S(2)}) collective-permute-start(bf16[8,16,2304]{2,1,0:T(8,128)(2,1)S(1)} %maximum_select_fusion.1), channel_id=1, source_target_pairs={{0,8},{1,9},{2,10},{3,11},{4,12},{5,13},{6,14},{7,15},{8,0},{9,1},... | collective-permute-start | bytes 1769480 | tf_op jit(solution)/shard_map/ppermute | solution.py:29
  33.9 1.0 pad_maximum_fusion.2
  35.0 1.6 fusion.32
  36.5 20.8 %collective-permute-done.5 = bf16[8,16,2304]{2,1,0:T(8,128)(2,1)} collective-permute-done((bf16[8,16,2304]{2,1,0:T(8,128)(2,1)S(1)}, bf16[8,16,2304]{2,1,0:T(8,128)(2,1)}, u32[]{:S(2)}, u32[]{:S(2)}) %collective-permute-start.5) | collective-permute-done | bytes 589856 | tf_op jit(solution)/shard_map/ppermute | solution.py:29
  57.3 1.8 maximum_select_fusion
  59.2 0.6 copy.9
  59.8 1.4 fusion.24
  61.5 0.7 copy-done.2
  62.9 0.7 copy-done.8
  63.9 0.7 copy-done.6
  64.9 0.7 copy-done.5
  66.3 0.7 copy-done.7
  67.0 0.4 fusion.35
  67.5 0.4 multiply_reduce_fusion.1
  67.8 0.6 copy-done.10
  68.5 1.9 fusion.29
  70.4 0.8 multiply_convert_fusion
  71.4 0.3 fusion.15
  71.8 0.3 fusion.14
  72.2 0.3 fusion.13
  72.5 0.3 fusion.12
  72.9 0.3 fusion.11
  73.2 0.3 fusion.10
  73.6 0.3 fusion.9
  73.9 0.3 fusion.8
  74.3 0.3 fusion.7
  74.6 1.3 slice_select_fusion
  75.9 2.7 %copy.11 = f32[128,2304]{1,0:T(8,128)} copy(f32[128,2304]{0,1:T(8,128)} %bitcast.181) | data formatting | bytes 2359296 | tf_op jit(solution)/shard_map/jit(_where)/select_n | solution.py:50
  78.6 1.9 collective-permute-start.8
  80.5 1.3 collective-permute-start.6
  81.8 1.3 collective-permute-start.7
  83.1 1.4 copy.12
  84.5 3.5 %collective-permute-done.7 = bf16[1,1,128,256]{3,2,1,0:T(8,128)(2,1)S(1)} collective-permute-done((bf16[1,1,128,256]{3,2,1,0:T(8,128)(2,1)S(1)}, bf16[1,1,128,256]{3,2,1,0:T(8,128)(2,1)S(1)}, u32[]{:S(2)}, u32[]{:S(2)}) %collective-permute-start.7) | collective-permute-done | bytes 65568 | tf_op jit(solution)/shard_map/ppermute | solution.py:21
  88.1 45.4 %collective-permute-done.8 = f32[128,2304]{1,0:T(8,128)} collective-permute-done((f32[128,2304]{1,0:T(8,128)}, f32[128,2304]{1,0:T(8,128)}, u32[]{:S(2)}, u32[]{:S(2)}) %collective-permute-start.8) | collective-permute-done | bytes 1179680 | tf_op jit(solution)/shard_map/ppermute | solution.py:29
  133.4 1.4 add.120
  134.9 1.9 collective-permute-start.9
  137.0 0.4 fusion.31
  137.8 14.2 %collective-permute-done.9 = f32[64,2304]{1,0:T(8,128)S(1)} collective-permute-done((f32[64,2304]{1,0:T(8,128)S(1)}, f32[64,2304]{1,0:T(8,128)S(1)}, u32[]{:S(2)}, u32[]{:S(2)}) %collective-permute-start.9) | collective-permute-done | bytes 589856 | tf_op jit(solution)/shard_map/ppermute | solution.py:29
  152.1 2.7 %collective-permute-start.10 = (f32[32,2304]{1,0:T(8,128)S(1)}, f32[32,2304]{1,0:T(8,128)S(1)}, u32[]{:S(2)}, u32[]{:S(2)}) collective-permute-start(f32[32,2304]{1,0:T(8,128)S(1)} %slice_select_fusion.3), channel_id=1, source_target_pairs={{0,2},{1,3},{2,0},{3,1},{4,6},{5,7},{6,4},{7,5},{8,10},{9,11},{10,... | collective-permute-start | bytes 884744 | tf_op jit(solution)/shard_map/ppermute | solution.py:29
  154.8 0.3 convolution_add_fusion.6
  155.5 8.0 %collective-permute-done.10 = f32[32,2304]{1,0:T(8,128)S(1)} collective-permute-done((f32[32,2304]{1,0:T(8,128)S(1)}, f32[32,2304]{1,0:T(8,128)S(1)}, u32[]{:S(2)}, u32[]{:S(2)}) %collective-permute-start.10) | collective-permute-done | bytes 294944 | tf_op jit(solution)/shard_map/ppermute | solution.py:29
  163.6 2.9 %collective-permute-start.11 = (f32[16,2304]{1,0:T(8,128)S(1)}, f32[16,2304]{1,0:T(8,128)S(1)}, u32[]{:S(2)}, u32[]{:S(2)}) collective-permute-start(f32[16,2304]{1,0:T(8,128)S(1)} %slice_select_fusion.4), channel_id=1, source_target_pairs={{0,1},{1,0},{2,3},{3,2},{4,5},{5,4},{6,7},{7,6},{8,9},{9,8},{10,11... | collective-permute-start | bytes 442376 | tf_op jit(solution)/shard_map/ppermute | solution.py:29
  166.8 3.8 %collective-permute-done.11 = f32[16,2304]{1,0:T(8,128)S(1)} collective-permute-done((f32[16,2304]{1,0:T(8,128)S(1)}, f32[16,2304]{1,0:T(8,128)S(1)}, u32[]{:S(2)}, u32[]{:S(2)}) %collective-permute-start.11) | collective-permute-done | bytes 147488 | tf_op jit(solution)/shard_map/ppermute | solution.py:29
  170.6 1.9 collective-permute-start.12
  172.9 1.0 collective-permute-done.12
  173.9 9.1 %collective-permute-start.13 = (f32[16,2304]{1,0:T(8,128)S(1)}, f32[16,2304]{1,0:T(8,128)S(1)}, u32[]{:S(2)}, u32[]{:S(2)}) collective-permute-start(f32[16,2304]{1,0:T(8,128)S(1)} %add.124), channel_id=1, source_target_pairs={{0,32},{16,48},{32,0},{48,16},{64,96},{80,112},{96,64},{112,80},{1... | collective-permute-start | bytes 442376 | tf_op jit(solution)/shard_map/ppermute | solution.py:29
  183.4 13.3 %collective-permute-done.13 = f32[16,2304]{1,0:T(8,128)S(1)} collective-permute-done((f32[16,2304]{1,0:T(8,128)S(1)}, f32[16,2304]{1,0:T(8,128)S(1)}, u32[]{:S(2)}, u32[]{:S(2)}) %collective-permute-start.13) | collective-permute-done | bytes 147488 | tf_op jit(solution)/shard_map/ppermute | solution.py:29
  196.7 10.2 %collective-permute-start.14 = (f32[16,2304]{1,0:T(8,128)S(1)}, f32[16,2304]{1,0:T(8,128)S(1)}, u32[]{:S(2)}, u32[]{:S(2)}) collective-permute-start(f32[16,2304]{1,0:T(8,128)S(1)} %add.125), channel_id=1, source_target_pairs={{0,64},{16,80},{32,96},{48,112},{64,0},{80,16},{96,32},{112,48},{1... | collective-permute-start | bytes 442376 | tf_op jit(solution)/shard_map/ppermute | solution.py:29
  206.9 0.3 convolution_add_fusion.1
  207.2 15.3 %collective-permute-done.14 = f32[16,2304]{1,0:T(8,128)S(1)} collective-permute-done((f32[16,2304]{1,0:T(8,128)S(1)}, f32[16,2304]{1,0:T(8,128)S(1)}, u32[]{:S(2)}, u32[]{:S(2)}) %collective-permute-start.14) | collective-permute-done | bytes 147488 | tf_op jit(solution)/shard_map/ppermute | solution.py:29
  222.5 3.1 %collective-permute-start.15 = (f32[16,2304]{1,0:T(8,128)S(1)}, f32[16,2304]{1,0:T(8,128)S(1)}, u32[]{:S(2)}, u32[]{:S(2)}) collective-permute-start(f32[16,2304]{1,0:T(8,128)S(1)} %add.126), channel_id=1, source_target_pairs={{0,128},{16,144},{32,160},{48,176},{64,192},{80,208},{96,224},{112... | collective-permute-start | bytes 442376 | tf_op jit(solution)/shard_map/ppermute | solution.py:29
  226.0 3.6 %collective-permute-done.15 = f32[16,2304]{1,0:T(8,128)S(1)} collective-permute-done((f32[16,2304]{1,0:T(8,128)S(1)}, f32[16,2304]{1,0:T(8,128)S(1)}, u32[]{:S(2)}, u32[]{:S(2)}) %collective-permute-start.15) | collective-permute-done | bytes 147488 | tf_op jit(solution)/shard_map/ppermute | solution.py:29
  229.6 2.4 %collective-permute-start.16 = (f32[16,2304]{1,0:T(8,128)S(1)}, f32[16,2304]{1,0:T(8,128)S(1)}, u32[]{:S(2)}, u32[]{:S(2)}) collective-permute-start(f32[16,2304]{1,0:T(8,128)S(1)} %add.127), channel_id=1, source_target_pairs={{0,256},{16,272},{32,288},{48,304},{64,320},{80,336},{96,352},{112... | collective-permute-start | bytes 442376 | tf_op jit(solution)/shard_map/ppermute | solution.py:29
  232.0 1.1 fusion.6
  233.1 5.0 %collective-permute-done.16 = f32[16,2304]{1,0:T(8,128)S(1)} collective-permute-done((f32[16,2304]{1,0:T(8,128)S(1)}, f32[16,2304]{1,0:T(8,128)S(1)}, u32[]{:S(2)}, u32[]{:S(2)}) %collective-permute-start.16) | collective-permute-done | bytes 147488 | tf_op jit(solution)/shard_map/ppermute | solution.py:29
  238.2 0.7 copy.13
  (59 shorter events, 5.4 us)
Async XLA Ops:
  0.6 19.8 %copy-start = (bf16[1,8,128,256]{3,2,1,0:T(8,128)(2,1)S(1)}, bf16[1,8,128,256]{3,2,1,0:T(8,128)(2,1)}, u32[]{:S(2)}) copy-start(bf16[1,8,128,256]{3,2,1,0:T(8,128)(2,1)} %param.4) | copy-start | bytes 1572868
  1.7 6.2 %collective-permute-start.2 = (bf16[1,16,2304]{2,1,0:T(8,128)(2,1)S(1)}, bf16[1,16,2304]{2,1,0:T(8,128)(2,1)S(1)}, u32[]{:S(2)}, u32[]{:S(2)}) collective-permute-start(bf16[1,16,2304]{2,1,0:T(8,128)(2,1)S(1)} %bitcast.209), channel_id=1, source_target_pairs={{0,1},{1,0},{2,3},{3,2},{4,5},{5,4},{6,7},{7,6},{8,9},{9,8},{10,11... | collective-permute-start | bytes 221192 | tf_op jit(solution)/shard_map/ppermute | solution.py:29
  8.0 8.5 %collective-permute-start.3 = (bf16[2,16,2304]{2,1,0:T(8,128)(2,1)S(1)}, bf16[2,16,2304]{2,1,0:T(8,128)(2,1)S(1)}, u32[]{:S(2)}, u32[]{:S(2)}) collective-permute-start(bf16[2,16,2304]{2,1,0:T(8,128)(2,1)S(1)} %maximum_select_fusion.3), channel_id=1, source_target_pairs={{0,2},{1,3},{2,0},{3,1},{4,6},{5,7},{6,4},{7,5},{8,10},{9,11},{10,... | collective-permute-start | bytes 442376 | tf_op jit(solution)/shard_map/ppermute | solution.py:29
  16.6 8.7 %collective-permute-start.4 = (bf16[4,16,2304]{2,1,0:T(8,128)(2,1)S(1)}, bf16[4,16,2304]{2,1,0:T(8,128)(2,1)S(1)}, u32[]{:S(2)}, u32[]{:S(2)}) collective-permute-start(bf16[4,16,2304]{2,1,0:T(8,128)(2,1)S(1)} %maximum_select_fusion.2), channel_id=1, source_target_pairs={{0,4},{1,5},{2,6},{3,7},{4,0},{5,1},{6,2},{7,3},{8,12},{9,13},{10,... | collective-permute-start | bytes 884744 | tf_op jit(solution)/shard_map/ppermute | solution.py:29
  20.4 13.3 %collective-permute-start = (bf16[1,1,128,256]{3,2,1,0:T(8,128)(2,1)S(1)}, bf16[1,1,128,256]{3,2,1,0:T(8,128)(2,1)S(1)}, u32[]{:S(2)}, u32[]{:S(2)}) collective-permute-start(bf16[1,1,128,256]{3,2,1,0:T(8,128)(2,1)S(1)} %get-tuple-element.30), channel_id=1, source_target_pairs={{0,1},{1,2},{2,3},{3,4},{4,5},{5,6},{6,7},{7,8},{8,9},{9,10},{10,1... | collective-permute-start | bytes 196616 | tf_op jit(solution)/shard_map/ppermute | solution.py:20
  23.9 9.8 %collective-permute-start.1 = (bf16[1,1,128,256]{3,2,1,0:T(8,128)(2,1)S(1)}, bf16[1,1,128,256]{3,2,1,0:T(8,128)(2,1)S(1)}, u32[]{:S(2)}, u32[]{:S(2)}) collective-permute-start(bf16[1,1,128,256]{3,2,1,0:T(8,128)(2,1)S(1)} %get-tuple-element.31), channel_id=1, source_target_pairs={{1,0},{2,1},{3,2},{4,3},{5,4},{6,5},{7,6},{8,7},{9,8},{10,9},{11,1... | collective-permute-start | bytes 196616 | tf_op jit(solution)/shard_map/ppermute | solution.py:21
  25.3 11.2 %copy-start.9 = (bf16[8,16,2304]{2,1,0:T(8,128)(2,1)}, bf16[8,16,2304]{2,1,0:T(8,128)(2,1)S(1)}, u32[]{:S(2)}) copy-start(bf16[8,16,2304]{2,1,0:T(8,128)(2,1)S(1)} %maximum_select_fusion.1) | copy-start | bytes 1769476
  25.4 32.0 %collective-permute-start.5 = (bf16[8,16,2304]{2,1,0:T(8,128)(2,1)S(1)}, bf16[8,16,2304]{2,1,0:T(8,128)(2,1)}, u32[]{:S(2)}, u32[]{:S(2)}) collective-permute-start(bf16[8,16,2304]{2,1,0:T(8,128)(2,1)S(1)} %maximum_select_fusion.1), channel_id=1, source_target_pairs={{0,8},{1,9},{2,10},{3,11},{4,12},{5,13},{6,14},{7,15},{8,0},{9,1},... | collective-permute-start | bytes 1769480 | tf_op jit(solution)/shard_map/ppermute | solution.py:29
  59.8 1.4 copy-start.3
  61.2 1.0 copy-start.2
  62.6 1.0 copy-start.8
  63.6 1.0 copy-start.6
  64.6 1.0 copy-start.5
  66.0 1.0 copy-start.7
  67.0 0.8 copy-start.11
  67.4 1.0 copy-start.10
  70.4 1.0 copy-start.4
  78.6 54.8 %collective-permute-start.8 = (f32[128,2304]{1,0:T(8,128)}, f32[128,2304]{1,0:T(8,128)}, u32[]{:S(2)}, u32[]{:S(2)}) collective-permute-start(f32[128,2304]{1,0:T(8,128)} %copy.11), channel_id=1, source_target_pairs={{0,8},{1,9},{2,10},{3,11},{4,12},{5,13},{6,14},{7,15},{8,0},{9,1},... | collective-permute-start | bytes 3538952 | tf_op jit(solution)/shard_map/ppermute | solution.py:29
  80.5 4.0 %collective-permute-start.6 = (bf16[1,1,128,256]{3,2,1,0:T(8,128)(2,1)S(1)}, bf16[1,1,128,256]{3,2,1,0:T(8,128)(2,1)S(1)}, u32[]{:S(2)}, u32[]{:S(2)}) collective-permute-start(bf16[1,1,128,256]{3,2,1,0:T(8,128)(2,1)S(1)} %get-tuple-element.26), channel_id=1, source_target_pairs={{0,1},{1,2},{2,3},{3,4},{4,5},{5,6},{6,7},{7,8},{8,9},{9,10},{10,1... | collective-permute-start | bytes 196616 | tf_op jit(solution)/shard_map/ppermute | solution.py:20
  81.8 6.2 %collective-permute-start.7 = (bf16[1,1,128,256]{3,2,1,0:T(8,128)(2,1)S(1)}, bf16[1,1,128,256]{3,2,1,0:T(8,128)(2,1)S(1)}, u32[]{:S(2)}, u32[]{:S(2)}) collective-permute-start(bf16[1,1,128,256]{3,2,1,0:T(8,128)(2,1)S(1)} %get-tuple-element.27), channel_id=1, source_target_pairs={{1,0},{2,1},{3,2},{4,3},{5,4},{6,5},{7,6},{8,7},{9,8},{10,9},{11,1... | collective-permute-start | bytes 196616 | tf_op jit(solution)/shard_map/ppermute | solution.py:21
  84.5 48.9 %copy-start.1 = (f32[128,2304]{1,0:T(8,128)S(1)}, f32[128,2304]{1,0:T(8,128)}, u32[]{:S(2)}) copy-start(f32[128,2304]{1,0:T(8,128)} %copy.12) | copy-start | bytes 3538948
  134.9 17.1 %collective-permute-start.9 = (f32[64,2304]{1,0:T(8,128)S(1)}, f32[64,2304]{1,0:T(8,128)S(1)}, u32[]{:S(2)}, u32[]{:S(2)}) collective-permute-start(f32[64,2304]{1,0:T(8,128)S(1)} %slice_select_fusion.2), channel_id=1, source_target_pairs={{0,4},{1,5},{2,6},{3,7},{4,0},{5,1},{6,2},{7,3},{8,12},{9,13},{10,... | collective-permute-start | bytes 1769480 | tf_op jit(solution)/shard_map/ppermute | solution.py:29
  152.1 11.4 %collective-permute-start.10 = (f32[32,2304]{1,0:T(8,128)S(1)}, f32[32,2304]{1,0:T(8,128)S(1)}, u32[]{:S(2)}, u32[]{:S(2)}) collective-permute-start(f32[32,2304]{1,0:T(8,128)S(1)} %slice_select_fusion.3), channel_id=1, source_target_pairs={{0,2},{1,3},{2,0},{3,1},{4,6},{5,7},{6,4},{7,5},{8,10},{9,11},{10,... | collective-permute-start | bytes 884744 | tf_op jit(solution)/shard_map/ppermute | solution.py:29
  163.6 7.0 %collective-permute-start.11 = (f32[16,2304]{1,0:T(8,128)S(1)}, f32[16,2304]{1,0:T(8,128)S(1)}, u32[]{:S(2)}, u32[]{:S(2)}) collective-permute-start(f32[16,2304]{1,0:T(8,128)S(1)} %slice_select_fusion.4), channel_id=1, source_target_pairs={{0,1},{1,0},{2,3},{3,2},{4,5},{5,4},{6,7},{7,6},{8,9},{9,8},{10,11... | collective-permute-start | bytes 442376 | tf_op jit(solution)/shard_map/ppermute | solution.py:29
  170.6 3.3 %collective-permute-start.12 = (f32[16,2304]{1,0:T(8,128)S(1)}, f32[16,2304]{1,0:T(8,128)S(1)}, u32[]{:S(2)}, u32[]{:S(2)}) collective-permute-start(f32[16,2304]{1,0:T(8,128)S(1)} %select_add_fusion.2), channel_id=1, source_target_pairs={{0,16},{16,0},{32,48},{48,32},{64,80},{80,64},{96,112},{112,96},{1... | collective-permute-start | bytes 442376 | tf_op jit(solution)/shard_map/ppermute | solution.py:29
  173.9 22.7 %collective-permute-start.13 = (f32[16,2304]{1,0:T(8,128)S(1)}, f32[16,2304]{1,0:T(8,128)S(1)}, u32[]{:S(2)}, u32[]{:S(2)}) collective-permute-start(f32[16,2304]{1,0:T(8,128)S(1)} %add.124), channel_id=1, source_target_pairs={{0,32},{16,48},{32,0},{48,16},{64,96},{80,112},{96,64},{112,80},{1... | collective-permute-start | bytes 442376 | tf_op jit(solution)/shard_map/ppermute | solution.py:29
  196.7 25.8 %collective-permute-start.14 = (f32[16,2304]{1,0:T(8,128)S(1)}, f32[16,2304]{1,0:T(8,128)S(1)}, u32[]{:S(2)}, u32[]{:S(2)}) collective-permute-start(f32[16,2304]{1,0:T(8,128)S(1)} %add.125), channel_id=1, source_target_pairs={{0,64},{16,80},{32,96},{48,112},{64,0},{80,16},{96,32},{112,48},{1... | collective-permute-start | bytes 442376 | tf_op jit(solution)/shard_map/ppermute | solution.py:29
  222.5 7.0 %collective-permute-start.15 = (f32[16,2304]{1,0:T(8,128)S(1)}, f32[16,2304]{1,0:T(8,128)S(1)}, u32[]{:S(2)}, u32[]{:S(2)}) collective-permute-start(f32[16,2304]{1,0:T(8,128)S(1)} %add.126), channel_id=1, source_target_pairs={{0,128},{16,144},{32,160},{48,176},{64,192},{80,208},{96,224},{112... | collective-permute-start | bytes 442376 | tf_op jit(solution)/shard_map/ppermute | solution.py:29
  229.6 8.5 %collective-permute-start.16 = (f32[16,2304]{1,0:T(8,128)S(1)}, f32[16,2304]{1,0:T(8,128)S(1)}, u32[]{:S(2)}, u32[]{:S(2)}) collective-permute-start(f32[16,2304]{1,0:T(8,128)S(1)} %add.127), channel_id=1, source_target_pairs={{0,256},{16,272},{32,288},{48,304},{64,320},{80,336},{96,352},{112... | collective-permute-start | bytes 442376 | tf_op jit(solution)/shard_map/ppermute | solution.py:29

commit v3 on v1

--- a/solution.py
+++ b/solution.py
@@ -20,6 +20,54 @@
         before = lax.ppermute(last, axis, up)
         after = lax.ppermute(initial, axis, down)
         value = jnp.concatenate([before, value, after], axis=dim)
+    return value
+
+
+def exchange(value, axis, bit):
+    peers = lax.axis_size(axis)
+    pairs = [(i, i ^ (1 << bit)) for i in range(peers)]
+    return lax.ppermute(value, axis, pairs)
+
+
+def gather_chunks(value, axis):
+    peers = lax.axis_size(axis)
+    copies = jnp.broadcast_to(value[None], (peers,) + value.shape)
+    return lax.all_to_all(copies, axis, 0, 0, tiled=False)
+
+
+def scatter_sum(value, axis):
+    peers = lax.axis_size(axis)
+    blocks = value.reshape((peers, value.shape[0] // peers) + value.shape[1:])
+    return lax.all_to_all(blocks, axis, 0, 0, tiled=False).sum(0)
+
+
+def split_pair(value, upper, dim):
+    low, high = jnp.split(value, 2, axis=dim)
+    return jnp.where(upper, high, low), jnp.where(upper, low, high)
+
+
+def join_pair(value, other, upper, dim):
+    return jnp.where(upper, jnp.concatenate([other, value], dim), jnp.concatenate([value, other], dim))
+
+
+def halve_sum(value, axis, bits, dim):
+    me = lax.axis_index(axis)
+    for bit in bits:
+        keep, send = split_pair(value, ((me >> bit) & 1) == 1, dim)
+        value = keep + exchange(send, axis, bit)
+    return value
+
+
+def double_sum(value, axis, bits):
+    for bit in bits:
+        value = value + exchange(value, axis, bit)
+    return value
+
+
+def double_join(value, axis, bits, dim):
+    me = lax.axis_index(axis)
+    for bit in bits:
+        value = join_pair(value, exchange(value, axis, bit), ((me >> bit) & 1) == 1, dim)
     return value
 
 
@@ -48,8 +96,13 @@
 
 def on_device(images, weight, norm_gain, cotangent):
     img_count, tile_rows, tile_cols, in_chan = images.shape
-    whole_kernel = lax.all_gather(weight, "col", axis=3, tiled=True)
-    out_chan = whole_kernel.shape[3]
+    taps, share = 9 * in_chan, weight.shape[3]
+    local_t = weight.reshape(taps, share).T
+    core_bit = [0]
+    half_t, _ = split_pair(local_t, (lax.axis_index("row") & 1) == 1, 1)
+    kernel_t = double_join(gather_chunks(half_t, "col"), "row", core_bit, 2).reshape(-1, taps)
+    out_chan = kernel_t.shape[0]
+    whole_kernel = kernel_t.T.reshape(3, 3, in_chan, out_chan)
     rimmed = padded_2(images, (("col", 1),), 1)
     padded = jnp.pad(rimmed, ((0, 0), (0, 0), (1, 1), (0, 0)))
     conv_out = jnp.zeros((img_count * tile_rows * tile_cols, out_chan), jnp.float32)
@@ -76,17 +129,20 @@
             )
             pieces.append(
                 lax.dot_general(
+                    grad_pre,
                     window(padded, tap_row, tap_col, tile_rows, tile_cols),
-                    grad_pre,
                     (((0,), (0,)), ((), ())),
                     preferred_element_type=jnp.float32,
                 )
             )
-    partial_value = jnp.stack(pieces).reshape(3, 3, in_chan, out_chan)
-    col_sum = lax.psum_scatter(partial_value, "col", scatter_dimension=3, tiled=True)
-    own_share = lax.psum(col_sum, "row")
+    partial_value = jnp.stack(pieces, axis=1).reshape(out_chan, taps)
+    core_sum = halve_sum(partial_value, "row", core_bit, 1)
+    col_sum = scatter_sum(core_sum, "col")
+    x_piece = halve_sum(col_sum, "row", [3, 4], 1)
+    row_piece = double_sum(x_piece, "row", [1, 2])
+    own_share = double_join(row_piece, "row", [4, 3, 0], 1)
     pixels = img_count * lax.axis_size("row") * tile_rows * lax.axis_size("col") * tile_cols
-    weight_grad = own_share * (1.0 / math.sqrt(pixels))
+    weight_grad = (own_share * (1.0 / math.sqrt(pixels))).T.reshape(3, 3, in_chan, share)
     features = outputs.reshape(img_count, tile_rows, tile_cols, out_chan)
     input_grad = grad_input.astype(jnp.bfloat16).reshape(img_count, tile_rows, tile_cols, in_chan)
     return (features, input_grad, weight_grad)

time: 547 us -> 155 us (0.28)
  the two profiles are of different devices: /device:TPU:1 before, /device:TPU:65 now
where the time goes in v3:
time: 155 us; the launch traced here: 154 us
  starting transfers between devices  77.3 us (50%)
  waiting for transfers between devices  40.1 us (26%)
  local copies, waits for them, and re-layouts  14.7 us (9%)
  matrix products  13.5 us (9%)
  other arithmetic  6.76 us (4%)
    ppermute x9, starting transfers between devices, exchange(): return lax.ppermute(value, axis, pairs)  50.1 us
    ppermute x2, waiting for transfers between devices, padded_2(): before = lax.ppermute(last, axis, up)  22.2 us
    ppermute x9, waiting for transfers between devices, exchange(): return lax.ppermute(value, axis, pairs)  9.35 us
    unnamed x36, local copies, waits for them, and re-layouts  8.67 us
    ppermute x2, starting transfers between devices, padded_2(): after = lax.ppermute(initial, axis, down)  8.6 us
    all_to_all x1, waiting for transfers between devices, gather_chunks(): return lax.all_to_all(copies, axis, 0, 0, tiled=False)  8.48 us
    all_to_all x1, starting transfers between devices, gather_chunks(): return lax.all_to_all(copies, axis, 0, 0, tiled=False)  7.64 us
    dot_general x9, matrix products, on_device(): lax.dot_general(window(grad_pad, 2 - tap_row, 2 - tap_col, tile_rows, til...  6.19 us
  transfers between devices with their start and end apart: 15, of which 8 were waited for; matrix products, arithmetic and copies ran while one was open for 7% of the time, Pallas kernels for 0%

profile of v3, /device:TPU:65, one launch (start us, length us, event | category | flops | bytes accessed | tf_op | source)
XLA Modules:
  0.0 153.5 jit_solution(12101492735140006240)
XLA Ops:
  0.6 1.0 copy.14
  1.8 0.9 broadcast_in_dim.2
  2.6 7.6 %all-to-all-start = ((bf16[16,16,1152]{2,1,0:T(8,128)(2,1)}), bf16[16,16,1152]{2,1,0:T(8,128)(2,1)S(1)}, u32[]{:S(2)}, u32[]{:S(2)}) async-start(bf16[16,16,1152]{2,1,0:T(8,128)(2,1)} %broadcast_in_dim.2), calls=%async_computation | async-start | bytes 1179648 | tf_op jit(solution)/shard_map/all_to_all | solution.py:35
  10.3 3.1 %collective-permute-start = (bf16[1,1,128,256]{3,2,1,0:T(8,128)(2,1)S(1)}, bf16[1,1,128,256]{3,2,1,0:T(8,128)(2,1)S(1)}, u32[]{:S(2)}, u32[]{:S(2)}) collective-permute-start(bf16[1,1,128,256]{3,2,1,0:T(8,128)(2,1)S(1)} %get-tuple-element.33), channel_id=1, source_target_pairs={{0,1},{1,2},{2,3},{3,4},{4,5},{5,6},{6,7},{7,8},{8,9},{9,10},{10,1... | collective-permute-start | bytes 196616 | tf_op jit(solution)/shard_map/ppermute | solution.py:20
  13.4 4.3 %collective-permute-start.1 = (bf16[1,1,128,256]{3,2,1,0:T(8,128)(2,1)S(1)}, bf16[1,1,128,256]{3,2,1,0:T(8,128)(2,1)S(1)}, u32[]{:S(2)}, u32[]{:S(2)}) collective-permute-start(bf16[1,1,128,256]{3,2,1,0:T(8,128)(2,1)S(1)} %get-tuple-element.34), channel_id=1, source_target_pairs={{1,0},{2,1},{3,2},{4,3},{5,4},{6,5},{7,6},{8,7},{9,8},{10,9},{11,1... | collective-permute-start | bytes 196616 | tf_op jit(solution)/shard_map/ppermute | solution.py:21
  17.7 8.5 %all-to-all-done = bf16[16,16,1152]{2,1,0:T(8,128)(2,1)S(1)} async-done(((bf16[16,16,1152]{2,1,0:T(8,128)(2,1)}), bf16[16,16,1152]{2,1,0:T(8,128)(2,1)S(1)}, u32[]{:S(2)}, u32[]{:S(2)}) %all-to-all-start) | async-done | bytes 589856 | tf_op jit(solution)/shard_map/all_to_all | solution.py:35
  26.2 3.3 %collective-permute-start.2 = (bf16[16,16,1152]{2,1,0:T(8,128)(2,1)S(1)}, bf16[16,16,1152]{2,1,0:T(8,128)(2,1)S(1)}, u32[]{:S(2)}, u32[]{:S(2)}) collective-permute-start(bf16[16,16,1152]{2,1,0:T(8,128)(2,1)S(1)} %all-to-all-done), channel_id=1, source_target_pairs={{0,16},{16,0},{32,48},{48,32},{64,80},{80,64},{96,112},{112,96},{1... | collective-permute-start | bytes 1769480 | tf_op jit(solution)/shard_map/ppermute | solution.py:29
  29.8 1.0 pad_maximum_fusion.2
  30.8 1.6 %fusion.36 = (bf16[1,8,128,256]{3,2,1,0:T(8,128)(2,1)}, bf16[1,8,128,256]{3,2,1,0:T(8,128)(2,1)}, bf16[1,8,128,256]{3,2,1,0:T(8,128)(2,1)}, bf16[1,8,128,256]{3,...) fusion(bf16[1,10,130,256]{3,2,1,0:T(8,128)(2,1)S(1)} %select_maximum_fusion.2), kind=kLoop, calls=%fused_computation.97 | loop fusion | bytes 6291456 | tf_op jit(solution)/shard_map/slice | solution.py:92
  32.7 0.6 copy.15
  33.3 1.8 %fusion.27 = f32[1024,256]{1,0:T(8,128)S(1)} fusion(bf16[1024,256]{1,0:T(8,128)(2,1)} %bitcast.186, bf16[3,3,256,256]{3,2,1,0:T(8,128)(2,1)S(1)} %bitcast.159), kind=kOutput, calls=%fused_computation.78 | convolution fusion | flops 134217728 | bytes 1703936 | tf_op jit(solution)/shard_map/dot_general | solution.py:111
  35.4 0.7 copy-done.3
  36.7 0.7 copy-done.9
  37.8 0.7 copy-done.7
  38.8 0.7 copy-done.6
  40.2 0.7 copy-done.8
  40.9 0.4 fusion.39
  41.3 0.4 multiply_reduce_fusion.1
  41.7 0.6 copy-done.14
  42.3 1.9 %fusion.32 = (f32[1024]{0:T(1024)S(1)}, f32[1024]{0:T(1024)S(1)}, f32[1024,256]{1,0:T(8,128)S(1)}, bf16[1024,256]{1,0:T(8,128)(2,1)}) fusion(f32[1024]{0:T(1024)S(1)} %add_rsqrt_fusion, f32[1024,256]{1,0:T(8,128)S(1)} %get-tuple-element.36, f32[1024]{0:T(1024)S(1)} %broadcast_multiply_fusion.2, f32[256]{0:T(256)S(1)} %copy-done.15, ...), kind=kLoop, calls=%fused_computation.94 | loop fusion | flops 4978688 | bytes 3163136 | tf_op jit(solution)/shard_map/reduce_sum | solution.py:85
  44.2 0.8 multiply_convert_fusion
  45.3 0.3 fusion.16
  45.6 0.3 fusion.15
  46.0 0.3 fusion.14
  46.4 0.3 fusion.13
  46.7 0.3 fusion.12
  47.1 0.3 fusion.11
  47.4 0.3 fusion.10
  47.8 0.3 fusion.9
  48.1 0.3 fusion.8
  48.5 1.2 fusion.34
  49.6 0.4 copy.21
  50.0 1.6 %copy.22 = f32[256,1152]{1,0:T(8,128)S(1)} copy(f32[256,1152]{0,1:T(8,128)} %get-tuple-element.13) | data formatting | bytes 2359296
  51.8 2.0 %collective-permute-start.5 = (f32[256,1152]{1,0:T(8,128)S(1)}, f32[256,1152]{1,0:T(8,128)S(1)}, u32[]{:S(2)}, u32[]{:S(2)}) collective-permute-start(f32[256,1152]{1,0:T(8,128)S(1)} %broadcast_select_fusion), channel_id=1, source_target_pairs={{0,16},{16,0},{32,48},{48,32},{64,80},{80,64},{96,112},{112,96},{1... | collective-permute-start | bytes 3538952 | tf_op jit(solution)/shard_map/ppermute | solution.py:29
  53.8 2.8 %collective-permute-done.5 = f32[256,1152]{1,0:T(8,128)S(1)} collective-permute-done((f32[256,1152]{1,0:T(8,128)S(1)}, f32[256,1152]{1,0:T(8,128)S(1)}, u32[]{:S(2)}, u32[]{:S(2)}) %collective-permute-start.5) | collective-permute-done | bytes 1179680 | tf_op jit(solution)/shard_map/ppermute | solution.py:29
  56.5 1.2 select_add_fusion
  57.7 4.7 %all-to-all-start.1 = ((f32[16,16,1152]{2,1,0:T(8,128)}), f32[16,16,1152]{2,1,0:T(8,128)S(1)}, u32[]{:S(2)}, u32[]{:S(2)}) async-start(f32[16,16,1152]{2,1,0:T(8,128)} %bitcast.179), calls=%async_computation.1 | async-start | bytes 2359296 | tf_op jit(solution)/shard_map/all_to_all | solution.py:41
  62.5 3.1 %collective-permute-start.3 = (bf16[1,1,128,256]{3,2,1,0:T(8,128)(2,1)S(1)}, bf16[1,1,128,256]{3,2,1,0:T(8,128)(2,1)S(1)}, u32[]{:S(2)}, u32[]{:S(2)}) collective-permute-start(bf16[1,1,128,256]{3,2,1,0:T(8,128)(2,1)S(1)} %get-tuple-element.29), channel_id=1, source_target_pairs={{0,1},{1,2},{2,3},{3,4},{4,5},{5,6},{6,7},{7,8},{8,9},{9,10},{10,1... | collective-permute-start | bytes 196616 | tf_op jit(solution)/shard_map/ppermute | solution.py:20
  65.6 4.3 %collective-permute-start.4 = (bf16[1,1,128,256]{3,2,1,0:T(8,128)(2,1)S(1)}, bf16[1,1,128,256]{3,2,1,0:T(8,128)(2,1)S(1)}, u32[]{:S(2)}, u32[]{:S(2)}) collective-permute-start(bf16[1,1,128,256]{3,2,1,0:T(8,128)(2,1)S(1)} %get-tuple-element.30), channel_id=1, source_target_pairs={{1,0},{2,1},{3,2},{4,3},{5,4},{6,5},{7,6},{8,7},{9,8},{10,9},{11,1... | collective-permute-start | bytes 196616 | tf_op jit(solution)/shard_map/ppermute | solution.py:21
  69.9 22.2 %collective-permute-done.3 = bf16[1,1,128,256]{3,2,1,0:T(8,128)(2,1)S(1)} collective-permute-done((bf16[1,1,128,256]{3,2,1,0:T(8,128)(2,1)S(1)}, bf16[1,1,128,256]{3,2,1,0:T(8,128)(2,1)S(1)}, u32[]{:S(2)}, u32[]{:S(2)}) %collective-permute-start.3) | collective-permute-done | bytes 65568 | tf_op jit(solution)/shard_map/ppermute | solution.py:20
  92.4 1.5 %fusion.35 = (bf16[1,8,128,256]{3,2,1,0:T(8,128)(2,1)}, bf16[1,8,128,256]{3,2,1,0:T(8,128)(2,1)}, bf16[1,8,128,256]{3,2,1,0:T(8,128)(2,1)}, bf16[1,8,128,256]{3,...) fusion(bf16[1,10,130,256]{3,2,1,0:T(8,128)(2,1)S(1)} %select_maximum_fusion), kind=kLoop, calls=%fused_computation.96 | loop fusion | bytes 6291456 | tf_op jit(solution)/shard_map/slice | solution.py:92
  94.0 0.5 copy-done.1
  94.4 0.3 fusion.26
  94.7 1.3 convolution_add_fusion.6
  96.2 3.1 %collective-permute-start.6 = (f32[16,576]{1,0:T(8,128)S(1)}, f32[16,576]{1,0:T(8,128)S(1)}, u32[]{:S(2)}, u32[]{:S(2)}) collective-permute-start(f32[16,576]{1,0:T(8,128)S(1)} %slice_select_fusion), channel_id=1, source_target_pairs={{0,128},{16,144},{32,160},{48,176},{64,192},{80,208},{96,224},{112... | collective-permute-start | bytes 110600 | tf_op jit(solution)/shard_map/ppermute | solution.py:29
  99.4 1.8 %convolution_add_fusion.5 = f32[1024,256]{1,0:T(8,128)S(1)} fusion(f32[1024,256]{1,0:T(8,128)} %convolution_add_fusion.6, bf16[1024,256]{1,0:T(8,128)(2,1)} %bitcast.204, bf16[3,3,256,256]{3,2,1,0:T(8,128)(2,1)S(1)} %bitcast.170), kind=kOutput, calls=%fused_computation.14 | convolution fusion | flops 134479872 | bytes 2752512 | tf_op jit(solution)/shard_map/dot_general | solution.py:124
  101.3 4.5 %collective-permute-start.7 = (f32[16,288]{1,0:T(8,128)S(1)}, f32[16,288]{1,0:T(8,128)S(1)}, u32[]{:S(2)}, u32[]{:S(2)}) collective-permute-start(f32[16,288]{1,0:T(8,128)S(1)} %slice_select_fusion.2), channel_id=1, source_target_pairs={{0,256},{16,272},{32,288},{48,304},{64,320},{80,336},{96,352},{112... | collective-permute-start | bytes 55304 | tf_op jit(solution)/shard_map/ppermute | solution.py:29
  105.8 0.3 convolution_add_fusion.4
  106.1 1.3 collective-permute-done.7
  107.5 8.9 %collective-permute-start.8 = (f32[16,288]{1,0:T(8,128)S(1)}, f32[16,288]{1,0:T(8,128)S(1)}, u32[]{:S(2)}, u32[]{:S(2)}) collective-permute-start(f32[16,288]{1,0:T(8,128)S(1)} %select_add_fusion.2), channel_id=1, source_target_pairs={{0,32},{16,48},{32,0},{48,16},{64,96},{80,112},{96,64},{112,80},{1... | collective-permute-start | bytes 55304 | tf_op jit(solution)/shard_map/ppermute | solution.py:29
  116.4 0.3 convolution_add_fusion.3
  116.8 0.9 collective-permute-done.8
  117.6 11.2 %collective-permute-start.9 = (f32[16,288]{1,0:T(8,128)S(1)}, f32[16,288]{1,0:T(8,128)S(1)}, u32[]{:S(2)}, u32[]{:S(2)}) collective-permute-start(f32[16,288]{1,0:T(8,128)S(1)} %add.111), channel_id=1, source_target_pairs={{0,64},{16,80},{32,96},{48,112},{64,0},{80,16},{96,32},{112,48},{1... | collective-permute-start | bytes 55304 | tf_op jit(solution)/shard_map/ppermute | solution.py:29
  128.8 0.3 convolution_add_fusion.2
  129.2 1.7 %collective-permute-done.9 = f32[16,288]{1,0:T(8,128)S(1)} collective-permute-done((f32[16,288]{1,0:T(8,128)S(1)}, f32[16,288]{1,0:T(8,128)S(1)}, u32[]{:S(2)}, u32[]{:S(2)}) %collective-permute-start.9) | collective-permute-done | bytes 18464 | tf_op jit(solution)/shard_map/ppermute | solution.py:29
  130.9 4.5 %collective-permute-start.10 = (f32[16,288]{1,0:T(8,128)S(1)}, f32[16,288]{1,0:T(8,128)S(1)}, u32[]{:S(2)}, u32[]{:S(2)}) collective-permute-start(f32[16,288]{1,0:T(8,128)S(1)} %add.112), channel_id=1, source_target_pairs={{0,256},{16,272},{32,288},{48,304},{64,320},{80,336},{96,352},{112... | collective-permute-start | bytes 55304 | tf_op jit(solution)/shard_map/ppermute | solution.py:29
  135.4 0.3 convolution_add_fusion.1
  135.7 1.2 collective-permute-done.10
  137.0 2.9 %collective-permute-start.11 = (f32[16,576]{1,0:T(8,128)S(1)}, f32[16,576]{1,0:T(8,128)S(1)}, u32[]{:S(2)}, u32[]{:S(2)}) collective-permute-start(f32[16,576]{1,0:T(8,128)S(1)} %maximum_select_fusion.3), channel_id=1, source_target_pairs={{0,128},{16,144},{32,160},{48,176},{64,192},{80,208},{96,224},{112... | collective-permute-start | bytes 110600 | tf_op jit(solution)/shard_map/ppermute | solution.py:29
  140.0 0.3 fusion.30
  140.3 1.5 collective-permute-done.11
  141.9 9.7 %collective-permute-start.12 = (f32[16,1152]{1,0:T(8,128)S(1)}, f32[16,1152]{1,0:T(8,128)S(1)}, u32[]{:S(2)}, u32[]{:S(2)}) collective-permute-start(f32[16,1152]{1,0:T(8,128)S(1)} %maximum_select_fusion.2), channel_id=1, source_target_pairs={{0,16},{16,0},{32,48},{48,32},{64,80},{80,64},{96,112},{112,96},{1... | collective-permute-start | bytes 221192 | tf_op jit(solution)/shard_map/ppermute | solution.py:29
  151.6 1.1 fusion.6
  152.8 0.7 copy.19
  (62 shorter events, 3.9 us)
Async XLA Ops:
  0.6 9.7 %copy-start.2 = (bf16[1,8,128,256]{3,2,1,0:T(8,128)(2,1)S(1)}, bf16[1,8,128,256]{3,2,1,0:T(8,128)(2,1)}, u32[]{:S(2)}) copy-start(bf16[1,8,128,256]{3,2,1,0:T(8,128)(2,1)} %param.4) | copy-start | bytes 1572868
  2.6 23.6 %all-to-all-start = ((bf16[16,16,1152]{2,1,0:T(8,128)(2,1)}), bf16[16,16,1152]{2,1,0:T(8,128)(2,1)S(1)}, u32[]{:S(2)}, u32[]{:S(2)}) async-start(bf16[16,16,1152]{2,1,0:T(8,128)(2,1)} %broadcast_in_dim.2), calls=%async_computation | async-start | bytes 1179648 | tf_op jit(solution)/shard_map/all_to_all | solution.py:35
  10.3 19.2 %collective-permute-start = (bf16[1,1,128,256]{3,2,1,0:T(8,128)(2,1)S(1)}, bf16[1,1,128,256]{3,2,1,0:T(8,128)(2,1)S(1)}, u32[]{:S(2)}, u32[]{:S(2)}) collective-permute-start(bf16[1,1,128,256]{3,2,1,0:T(8,128)(2,1)S(1)} %get-tuple-element.33), channel_id=1, source_target_pairs={{0,1},{1,2},{2,3},{3,4},{4,5},{5,6},{6,7},{7,8},{8,9},{9,10},{10,1... | collective-permute-start | bytes 196616 | tf_op jit(solution)/shard_map/ppermute | solution.py:20
  13.4 16.2 %collective-permute-start.1 = (bf16[1,1,128,256]{3,2,1,0:T(8,128)(2,1)S(1)}, bf16[1,1,128,256]{3,2,1,0:T(8,128)(2,1)S(1)}, u32[]{:S(2)}, u32[]{:S(2)}) collective-permute-start(bf16[1,1,128,256]{3,2,1,0:T(8,128)(2,1)S(1)} %get-tuple-element.34), channel_id=1, source_target_pairs={{1,0},{2,1},{3,2},{4,3},{5,4},{6,5},{7,6},{8,7},{9,8},{10,9},{11,1... | collective-permute-start | bytes 196616 | tf_op jit(solution)/shard_map/ppermute | solution.py:21
  26.2 6.2 %collective-permute-start.2 = (bf16[16,16,1152]{2,1,0:T(8,128)(2,1)S(1)}, bf16[16,16,1152]{2,1,0:T(8,128)(2,1)S(1)}, u32[]{:S(2)}, u32[]{:S(2)}) collective-permute-start(bf16[16,16,1152]{2,1,0:T(8,128)(2,1)S(1)} %all-to-all-done), channel_id=1, source_target_pairs={{0,16},{16,0},{32,48},{48,32},{64,80},{80,64},{96,112},{112,96},{1... | collective-permute-start | bytes 1769480 | tf_op jit(solution)/shard_map/ppermute | solution.py:29
  33.3 6.9 %copy-start = (bf16[2304,256]{1,0:T(8,128)(2,1)}, bf16[2304,256]{1,0:T(8,128)(2,1)S(1)}, u32[]{:S(2)}) copy-start(bf16[2304,256]{1,0:T(8,128)(2,1)S(1)} %copy.15) | copy-start | bytes 3538948
  33.3 1.8 %copy-start.4 = (bf16[1,8,128,256]{3,2,1,0:T(8,128)(2,1)S(1)}, bf16[1,8,128,256]{3,2,1,0:T(8,128)(2,1)}, u32[]{:S(2)}) copy-start(bf16[1,8,128,256]{3,2,1,0:T(8,128)(2,1)} %get-tuple-element.23) | copy-start | bytes 1572868
  35.1 1.0 copy-start.3
  36.4 1.0 copy-start.9
  37.4 1.0 copy-start.7
  38.5 1.0 copy-start.6
  39.8 1.0 copy-start.8
  40.9 0.8 copy-start.15
  41.3 1.0 copy-start.14
  44.2 1.0 copy-start.5
  51.8 4.7 %collective-permute-start.5 = (f32[256,1152]{1,0:T(8,128)S(1)}, f32[256,1152]{1,0:T(8,128)S(1)}, u32[]{:S(2)}, u32[]{:S(2)}) collective-permute-start(f32[256,1152]{1,0:T(8,128)S(1)} %broadcast_select_fusion), channel_id=1, source_target_pairs={{0,16},{16,0},{32,48},{48,32},{64,80},{80,64},{96,112},{112,96},{1... | collective-permute-start | bytes 3538952 | tf_op jit(solution)/shard_map/ppermute | solution.py:29
  57.7 38.4 %all-to-all-start.1 = ((f32[16,16,1152]{2,1,0:T(8,128)}), f32[16,16,1152]{2,1,0:T(8,128)S(1)}, u32[]{:S(2)}, u32[]{:S(2)}) async-start(f32[16,16,1152]{2,1,0:T(8,128)} %bitcast.179), calls=%async_computation.1 | async-start | bytes 2359296 | tf_op jit(solution)/shard_map/all_to_all | solution.py:41
  62.5 29.7 %collective-permute-start.3 = (bf16[1,1,128,256]{3,2,1,0:T(8,128)(2,1)S(1)}, bf16[1,1,128,256]{3,2,1,0:T(8,128)(2,1)S(1)}, u32[]{:S(2)}, u32[]{:S(2)}) collective-permute-start(bf16[1,1,128,256]{3,2,1,0:T(8,128)(2,1)S(1)} %get-tuple-element.29), channel_id=1, source_target_pairs={{0,1},{1,2},{2,3},{3,4},{4,5},{5,6},{6,7},{7,8},{8,9},{9,10},{10,1... | collective-permute-start | bytes 196616 | tf_op jit(solution)/shard_map/ppermute | solution.py:20
  65.6 26.6 %collective-permute-start.4 = (bf16[1,1,128,256]{3,2,1,0:T(8,128)(2,1)S(1)}, bf16[1,1,128,256]{3,2,1,0:T(8,128)(2,1)S(1)}, u32[]{:S(2)}, u32[]{:S(2)}) collective-permute-start(bf16[1,1,128,256]{3,2,1,0:T(8,128)(2,1)S(1)} %get-tuple-element.30), channel_id=1, source_target_pairs={{1,0},{2,1},{3,2},{4,3},{5,4},{6,5},{7,6},{8,7},{9,8},{10,9},{11,1... | collective-permute-start | bytes 196616 | tf_op jit(solution)/shard_map/ppermute | solution.py:21
  92.4 2.0 %copy-start.1 = (bf16[2304,256]{1,0:T(8,128)(2,1)S(1)}, bf16[2304,256]{1,0:T(8,128)(2,1)}, u32[]{:S(2)}) copy-start(bf16[2304,256]{1,0:T(8,128)(2,1)} %copy-done) | copy-start | bytes 3538948
  96.2 4.9 %collective-permute-start.6 = (f32[16,576]{1,0:T(8,128)S(1)}, f32[16,576]{1,0:T(8,128)S(1)}, u32[]{:S(2)}, u32[]{:S(2)}) collective-permute-start(f32[16,576]{1,0:T(8,128)S(1)} %slice_select_fusion), channel_id=1, source_target_pairs={{0,128},{16,144},{32,160},{48,176},{64,192},{80,208},{96,224},{112... | collective-permute-start | bytes 110600 | tf_op jit(solution)/shard_map/ppermute | solution.py:29
  99.4 6.4 %copy-start.13 = (bf16[1,8,128,256]{3,2,1,0:T(8,128)(2,1)S(1)}, bf16[1,8,128,256]{3,2,1,0:T(8,128)(2,1)}, u32[]{:S(2)}) copy-start(bf16[1,8,128,256]{3,2,1,0:T(8,128)(2,1)} %get-tuple-element.17) | copy-start | bytes 1572868
  101.3 6.1 %collective-permute-start.7 = (f32[16,288]{1,0:T(8,128)S(1)}, f32[16,288]{1,0:T(8,128)S(1)}, u32[]{:S(2)}, u32[]{:S(2)}) collective-permute-start(f32[16,288]{1,0:T(8,128)S(1)} %slice_select_fusion.2), channel_id=1, source_target_pairs={{0,256},{16,272},{32,288},{48,304},{64,320},{80,336},{96,352},{112... | collective-permute-start | bytes 55304 | tf_op jit(solution)/shard_map/ppermute | solution.py:29
  107.5 21.3 %copy-start.12 = (bf16[1,8,128,256]{3,2,1,0:T(8,128)(2,1)S(1)}, bf16[1,8,128,256]{3,2,1,0:T(8,128)(2,1)}, u32[]{:S(2)}) copy-start(bf16[1,8,128,256]{3,2,1,0:T(8,128)(2,1)} %get-tuple-element.16) | copy-start | bytes 1572868
  107.5 10.1 %collective-permute-start.8 = (f32[16,288]{1,0:T(8,128)S(1)}, f32[16,288]{1,0:T(8,128)S(1)}, u32[]{:S(2)}, u32[]{:S(2)}) collective-permute-start(f32[16,288]{1,0:T(8,128)S(1)} %select_add_fusion.2), channel_id=1, source_target_pairs={{0,32},{16,48},{32,0},{48,16},{64,96},{80,112},{96,64},{112,80},{1... | collective-permute-start | bytes 55304 | tf_op jit(solution)/shard_map/ppermute | solution.py:29
  117.6 13.3 %collective-permute-start.9 = (f32[16,288]{1,0:T(8,128)S(1)}, f32[16,288]{1,0:T(8,128)S(1)}, u32[]{:S(2)}, u32[]{:S(2)}) collective-permute-start(f32[16,288]{1,0:T(8,128)S(1)} %add.111), channel_id=1, source_target_pairs={{0,64},{16,80},{32,96},{48,112},{64,0},{80,16},{96,32},{112,48},{1... | collective-permute-start | bytes 55304 | tf_op jit(solution)/shard_map/ppermute | solution.py:29
  128.8 6.5 %copy-start.11 = (bf16[1,8,128,256]{3,2,1,0:T(8,128)(2,1)S(1)}, bf16[1,8,128,256]{3,2,1,0:T(8,128)(2,1)}, u32[]{:S(2)}) copy-start(bf16[1,8,128,256]{3,2,1,0:T(8,128)(2,1)} %get-tuple-element.15) | copy-start | bytes 1572868
  130.9 6.1 %collective-permute-start.10 = (f32[16,288]{1,0:T(8,128)S(1)}, f32[16,288]{1,0:T(8,128)S(1)}, u32[]{:S(2)}, u32[]{:S(2)}) collective-permute-start(f32[16,288]{1,0:T(8,128)S(1)} %add.112), channel_id=1, source_target_pairs={{0,256},{16,272},{32,288},{48,304},{64,320},{80,336},{96,352},{112... | collective-permute-start | bytes 55304 | tf_op jit(solution)/shard_map/ppermute | solution.py:29
  135.4 4.6 %copy-start.10 = (bf16[1,8,128,256]{3,2,1,0:T(8,128)(2,1)S(1)}, bf16[1,8,128,256]{3,2,1,0:T(8,128)(2,1)}, u32[]{:S(2)}) copy-start(bf16[1,8,128,256]{3,2,1,0:T(8,128)(2,1)} %get-tuple-element.20) | copy-start | bytes 1572868
  137.0 4.7 %collective-permute-start.11 = (f32[16,576]{1,0:T(8,128)S(1)}, f32[16,576]{1,0:T(8,128)S(1)}, u32[]{:S(2)}, u32[]{:S(2)}) collective-permute-start(f32[16,576]{1,0:T(8,128)S(1)} %maximum_select_fusion.3), channel_id=1, source_target_pairs={{0,128},{16,144},{32,160},{48,176},{64,192},{80,208},{96,224},{112... | collective-permute-start | bytes 110600 | tf_op jit(solution)/shard_map/ppermute | solution.py:29
  141.9 10.9 %collective-permute-start.12 = (f32[16,1152]{1,0:T(8,128)S(1)}, f32[16,1152]{1,0:T(8,128)S(1)}, u32[]{:S(2)}, u32[]{:S(2)}) collective-permute-start(f32[16,1152]{1,0:T(8,128)S(1)} %maximum_select_fusion.2), channel_id=1, source_target_pairs={{0,16},{16,0},{32,48},{48,32},{64,80},{80,64},{96,112},{112,96},{1... | collective-permute-start | bytes 221192 | tf_op jit(solution)/shard_map/ppermute | solution.py:29

commit v4 on v3

--- a/solution.py
+++ b/solution.py
@@ -1,3 +1,4 @@
+import itertools
 import math
 
 import jax
@@ -46,10 +47,6 @@
     return jnp.where(upper, high, low), jnp.where(upper, low, high)
 
 
-def join_pair(value, other, upper, dim):
-    return jnp.where(upper, jnp.concatenate([other, value], dim), jnp.concatenate([value, other], dim))
-
-
 def halve_sum(value, axis, bits, dim):
     me = lax.axis_index(axis)
     for bit in bits:
@@ -58,17 +55,46 @@
     return value
 
 
-def double_sum(value, axis, bits):
-    for bit in bits:
-        value = value + exchange(value, axis, bit)
-    return value
+def field_shift(peers, low, size, step):
+    mask = (size - 1) << low
+    return [(i, (i & ~mask) | (((((i >> low) % size) + step) % size) << low)) for i in range(peers)]
 
 
-def double_join(value, axis, bits, dim):
-    me = lax.axis_index(axis)
-    for bit in bits:
-        value = join_pair(value, exchange(value, axis, bit), ((me >> bit) & 1) == 1, dim)
-    return value
+def field_of(axis, low, size):
+    return (lax.axis_index(axis) >> low) % size
+
+
+def scatter_field(value, axis, low, size, dim):
+    peers, me = lax.axis_size(axis), field_of(axis, low, size)
+    pieces = jnp.stack(jnp.split(value, size, axis=dim))
+    got = [jnp.take(pieces, me, axis=0)]
+    for step in range(1, size):
+        sent = jnp.take(pieces, (me + step) % size, axis=0)
+        got.append(lax.ppermute(sent, axis, field_shift(peers, low, size, step)))
+    got = jnp.stack(got)
+    return jnp.take(got, (me - jnp.arange(size)) % size, axis=0).sum(0)
+
+
+def sum_field(value, axis, low, size):
+    peers, me = lax.axis_size(axis), field_of(axis, low, size)
+    got = [value] + [lax.ppermute(value, axis, field_shift(peers, low, size, step)) for step in range(1, size)]
+    got = jnp.stack(got)
+    return jnp.take(got, (me - jnp.arange(size)) % size, axis=0).sum(0)
+
+
+def gather_fields(value, axis, fields):
+    peers = lax.axis_size(axis)
+    shape = tuple(size for _, size in fields)
+    held = jnp.zeros(shape + value.shape, value.dtype)
+    for offsets in itertools.product(*[range(size) for _, size in fields]):
+        target = list(range(peers))
+        for (low, size), step in zip(fields, offsets):
+            moved = dict(field_shift(peers, low, size, step))
+            target = [moved[j] for j in target]
+        source = tuple((field_of(axis, low, size) - step) % size for (low, size), step in zip(fields, offsets))
+        piece = lax.ppermute(value, axis, list(enumerate(target))) if any(offsets) else value
+        held = held.at[source].set(piece)
+    return held
 
 
 def norm_act(conv_out, upper, norm_gain):
@@ -100,7 +126,8 @@
     local_t = weight.reshape(taps, share).T
     core_bit = [0]
     half_t, _ = split_pair(local_t, (lax.axis_index("row") & 1) == 1, 1)
-    kernel_t = double_join(gather_chunks(half_t, "col"), "row", core_bit, 2).reshape(-1, taps)
+    halves = gather_fields(gather_chunks(half_t, "col"), "row", [(0, 2)])
+    kernel_t = jnp.concatenate([halves[0], halves[1]], 2).reshape(-1, taps)
     out_chan = kernel_t.shape[0]
     whole_kernel = kernel_t.T.reshape(3, 3, in_chan, out_chan)
     rimmed = padded_2(images, (("col", 1),), 1)
@@ -138,9 +165,10 @@
     partial_value = jnp.stack(pieces, axis=1).reshape(out_chan, taps)
     core_sum = halve_sum(partial_value, "row", core_bit, 1)
     col_sum = scatter_sum(core_sum, "col")
-    x_piece = halve_sum(col_sum, "row", [3, 4], 1)
-    row_piece = double_sum(x_piece, "row", [1, 2])
-    own_share = double_join(row_piece, "row", [4, 3, 0], 1)
+    x_piece = scatter_field(col_sum, "row", 3, 4, 1)
+    row_piece = sum_field(x_piece, "row", 1, 4)
+    pieces = gather_fields(row_piece, "row", [(0, 2), (3, 4)])
+    own_share = pieces.transpose(2, 0, 1, 3).reshape(row_piece.shape[0], -1)
     pixels = img_count * lax.axis_size("row") * tile_rows * lax.axis_size("col") * tile_cols
     weight_grad = (own_share * (1.0 / math.sqrt(pixels))).T.reshape(3, 3, in_chan, share)
     features = outputs.reshape(img_count, tile_rows, tile_cols, out_chan)

time: 155 us -> 173 us (1.12)
  starting transfers between devices: 77.3 us -> 89.6 us
  other arithmetic: 6.76 us -> 17.7 us
  waiting for transfers between devices: 40.1 us -> 31.7 us
  matrix products: 13.5 us -> 15.3 us
    ppermute x0 -> x14, starting transfers between devices: none -> 61.2 us  [the longest x8 28.6 us: gather_fields(): lax.ppermute(value, axis, list(enumerate(target)))]
    ppermute x9 -> x1, starting transfers between devices: 50.1 us -> 1.98 us  [exchange(): return lax.ppermute(value, axis, pairs)]
    all_to_all x1, waiting for transfers between devices: 8.48 us -> 0.01 us  [gather_chunks(): return lax.all_to_all(copies, axis, 0, 0, tiled=False)]
    ppermute x9 -> x1, waiting for transfers between devices: 9.35 us -> 2.75 us  [exchange(): return lax.ppermute(value, axis, pairs)]
    scatter x0 -> x10, other arithmetic: none -> 6.55 us  [gather_fields(): held = held.at[source].set(piece)]
    ppermute x2, waiting for transfers between devices: 22.2 us -> 27.9 us  [padded_2(): before = lax.ppermute(last, axis, up)]
    another operation x0 -> x8, other arithmetic: none -> 3.82 us
    dot_general x9, matrix products: 6.19 us -> 8.04 us  [on_device(): lax.dot_general(window(grad_pad, 2 - tap_row, 2 - tap_col, tile_rows, til...]
  transfers between devices with their start and end apart: 15 -> 21, of which waited for: 8 -> 4; matrix products, arithmetic and copies ran while one was open for 7% -> 12% of each run, Pallas kernels for 0% -> 0%
where the time goes in v4:
time: 173 us; the launch traced here: 172 us
  starting transfers between devices  89.6 us (52%)
  waiting for transfers between devices  31.7 us (18%)
  other arithmetic  17.7 us (10%)
  local copies, waits for them, and re-layouts  15.9 us (9%)
  matrix products  15.3 us (9%)
    ppermute x8, starting transfers between devices, gather_fields(): lax.ppermute(value, axis, list(enumerate(target)))  28.6 us
    ppermute x2, waiting for transfers between devices, padded_2(): before = lax.ppermute(last, axis, up)  27.9 us
    ppermute x3, starting transfers between devices, sum_field(): lax.ppermute(value, axis, field_shift(peers, low, size, step))  21.9 us
    ppermute x3, starting transfers between devices, scatter_field(): got.append(lax.ppermute(sent, axis, field_shift(peers, low, size, step)))  10.7 us
    ppermute x2, starting transfers between devices, padded_2(): after = lax.ppermute(initial, axis, down)  8.93 us
    dot_general x9, matrix products, on_device(): lax.dot_general(window(grad_pad, 2 - tap_row, 2 - tap_col, tile_rows, til...  8.04 us
    unnamed x34, local copies, waits for them, and re-layouts  7.91 us
    all_to_all x1, starting transfers between devices, gather_chunks(): return lax.all_to_all(copies, axis, 0, 0, tiled=False)  7.64 us
  transfers between devices with their start and end apart: 21, of which 4 were waited for; matrix products, arithmetic and copies ran while one was open for 12% of the time, Pallas kernels for 0%

profile of v4, /device:TPU:65, one launch (start us, length us, event | category | flops | bytes accessed | tf_op | source)
XLA Modules:
  0.0 171.9 jit_solution(65971668157665195)
XLA Ops:
  0.6 1.0 copy.34
  1.8 0.9 broadcast_in_dim.33
  2.6 7.6 %all-to-all-start = ((bf16[16,16,1152]{2,1,0:T(8,128)(2,1)}), bf16[16,16,1152]{2,1,0:T(8,128)(2,1)S(1)}, u32[]{:S(2)}, u32[]{:S(2)}) async-start(bf16[16,16,1152]{2,1,0:T(8,128)(2,1)} %broadcast_in_dim.33), calls=%async_computation | async-start | bytes 1179648 | tf_op jit(solution)/shard_map/all_to_all | solution.py:36
  10.3 3.1 %collective-permute-start = (bf16[1,1,128,256]{3,2,1,0:T(8,128)(2,1)S(1)}, bf16[1,1,128,256]{3,2,1,0:T(8,128)(2,1)S(1)}, u32[]{:S(2)}, u32[]{:S(2)}) collective-permute-start(bf16[1,1,128,256]{3,2,1,0:T(8,128)(2,1)S(1)} %get-tuple-element.181), channel_id=1, source_target_pairs={{0,1},{1,2},{2,3},{3,4},{4,5},{5,6},{6,7},{7,8},{8,9},{9,10},{10,1... | collective-permute-start | bytes 196616 | tf_op jit(solution)/shard_map/ppermute | solution.py:21
  13.4 4.3 %collective-permute-start.1 = (bf16[1,1,128,256]{3,2,1,0:T(8,128)(2,1)S(1)}, bf16[1,1,128,256]{3,2,1,0:T(8,128)(2,1)S(1)}, u32[]{:S(2)}, u32[]{:S(2)}) collective-permute-start(bf16[1,1,128,256]{3,2,1,0:T(8,128)(2,1)S(1)} %get-tuple-element.182), channel_id=1, source_target_pairs={{1,0},{2,1},{3,2},{4,3},{5,4},{6,5},{7,6},{8,7},{9,8},{10,9},{11,1... | collective-permute-start | bytes 196616 | tf_op jit(solution)/shard_map/ppermute | solution.py:22
  17.8 0.7 and_reduce_fusion.8
  18.5 9.1 %collective-permute-done = bf16[1,1,128,256]{3,2,1,0:T(8,128)(2,1)S(1)} collective-permute-done((bf16[1,1,128,256]{3,2,1,0:T(8,128)(2,1)S(1)}, bf16[1,1,128,256]{3,2,1,0:T(8,128)(2,1)S(1)}, u32[]{:S(2)}, u32[]{:S(2)}) %collective-permute-start) | collective-permute-done | bytes 65568 | tf_op jit(solution)/shard_map/ppermute | solution.py:21
  27.8 1.4 fusion.44
  29.2 2.9 %collective-permute-start.2 = (bf16[16,16,1152]{2,1,0:T(8,128)(2,1)S(1)}, bf16[16,16,1152]{2,1,0:T(8,128)(2,1)S(1)}, u32[]{:S(2)}, u32[]{:S(2)}) collective-permute-start(bf16[16,16,1152]{2,1,0:T(8,128)(2,1)S(1)} %all-to-all-done), channel_id=1, source_target_pairs={{0,16},{16,0},{32,48},{48,32},{64,80},{80,64},{96,112},{112,96},{1... | collective-permute-start | bytes 1769480 | tf_op jit(solution)/shard_map/ppermute | solution.py:95
  32.2 1.0 pad_maximum_fusion.2
  33.3 0.8 bitcast_dynamic-update-slice_fusion
  34.1 0.8 fusion.23
  34.9 1.1 maximum_bitcast_fusion
  36.1 1.6 copy.35
  37.6 1.7 fusion.25
  40.3 0.7 copy-done.9
  41.3 0.7 copy-done.7
  42.3 0.7 copy-done.6
  43.7 0.7 copy-done.8
  45.2 0.6 copy-done.11
  45.9 1.9 %fusion.39 = (f32[1024]{0:T(1024)S(1)}, f32[1024]{0:T(1024)S(1)}, f32[1024,256]{1,0:T(8,128)S(1)}, bf16[1024,256]{1,0:T(8,128)(2,1)}) fusion(f32[1024]{0:T(1024)S(1)} %add_rsqrt_fusion, f32[1024,256]{1,0:T(8,128)S(1)} %get-tuple-element.192, f32[1024]{0:T(1024)S(1)} %broadcast_multiply_fusion.2, f32[256]{0:T(256)S(1)} %copy-done.13, ...), kind=kLoop, calls=%fused_computation.164 | loop fusion | flops 4978688 | bytes 3163136 | tf_op jit(solution)/shard_map/reduce_sum | solution.py:111
  47.8 0.8 multiply_convert_fusion
  52.4 1.2 fusion.41
  53.9 1.6 copy.43
  55.7 2.0 %collective-permute-start.5 = (f32[256,1152]{1,0:T(8,128)S(1)}, f32[256,1152]{1,0:T(8,128)S(1)}, u32[]{:S(2)}, u32[]{:S(2)}) collective-permute-start(f32[256,1152]{1,0:T(8,128)S(1)} %broadcast_select_fusion), channel_id=1, source_target_pairs={{0,16},{16,0},{32,48},{48,32},{64,80},{80,64},{96,112},{112,96},{1... | collective-permute-start | bytes 3538952 | tf_op jit(solution)/shard_map/ppermute | solution.py:30
  57.7 2.7 %collective-permute-done.5 = f32[256,1152]{1,0:T(8,128)S(1)} collective-permute-done((f32[256,1152]{1,0:T(8,128)S(1)}, f32[256,1152]{1,0:T(8,128)S(1)}, u32[]{:S(2)}, u32[]{:S(2)}) %collective-permute-start.5) | collective-permute-done | bytes 1179680 | tf_op jit(solution)/shard_map/ppermute | solution.py:30
  60.4 1.2 select_add_fusion
  61.6 3.8 %all-to-all-start.1 = ((f32[16,16,1152]{2,1,0:T(8,128)}), f32[16,16,1152]{2,1,0:T(8,128)S(1)}, u32[]{:S(2)}, u32[]{:S(2)}) async-start(f32[16,16,1152]{2,1,0:T(8,128)} %bitcast.244), calls=%async_computation.1 | async-start | bytes 2359296 | tf_op jit(solution)/shard_map/all_to_all | solution.py:42
  65.6 0.8 and_reduce_fusion.6
  66.4 0.7 and_reduce_fusion.2
  67.2 0.8 and_reduce_fusion.4
  67.9 0.7 and_reduce_fusion
  68.7 2.9 %collective-permute-start.3 = (bf16[1,1,128,256]{3,2,1,0:T(8,128)(2,1)S(1)}, bf16[1,1,128,256]{3,2,1,0:T(8,128)(2,1)S(1)}, u32[]{:S(2)}, u32[]{:S(2)}) collective-permute-start(bf16[1,1,128,256]{3,2,1,0:T(8,128)(2,1)S(1)} %get-tuple-element.177), channel_id=1, source_target_pairs={{0,1},{1,2},{2,3},{3,4},{4,5},{5,6},{6,7},{7,8},{8,9},{9,10},{10,1... | collective-permute-start | bytes 196616 | tf_op jit(solution)/shard_map/ppermute | solution.py:21
  71.6 4.6 %collective-permute-start.4 = (bf16[1,1,128,256]{3,2,1,0:T(8,128)(2,1)S(1)}, bf16[1,1,128,256]{3,2,1,0:T(8,128)(2,1)S(1)}, u32[]{:S(2)}, u32[]{:S(2)}) collective-permute-start(bf16[1,1,128,256]{3,2,1,0:T(8,128)(2,1)S(1)} %get-tuple-element.178), channel_id=1, source_target_pairs={{1,0},{2,1},{3,2},{4,3},{5,4},{6,5},{7,6},{8,7},{9,8},{10,9},{11,1... | collective-permute-start | bytes 196616 | tf_op jit(solution)/shard_map/ppermute | solution.py:22
  76.3 18.8 %collective-permute-done.3 = bf16[1,1,128,256]{3,2,1,0:T(8,128)(2,1)S(1)} collective-permute-done((bf16[1,1,128,256]{3,2,1,0:T(8,128)(2,1)S(1)}, bf16[1,1,128,256]{3,2,1,0:T(8,128)(2,1)S(1)}, u32[]{:S(2)}, u32[]{:S(2)}) %collective-permute-start.3) | collective-permute-done | bytes 65568 | tf_op jit(solution)/shard_map/ppermute | solution.py:21
  95.4 1.2 fusion.43
  98.6 1.3 convolution_add_fusion.1
  100.2 3.3 %collective-permute-start.6 = (f32[16,288]{1,0:T(8,128)S(1)}, f32[16,288]{1,0:T(8,128)S(1)}, u32[]{:S(2)}, u32[]{:S(2)}) collective-permute-start(f32[16,288]{1,0:T(8,128)S(1)} %get-tuple-element.186), channel_id=1, source_target_pairs={{0,128},{16,144},{32,160},{48,176},{64,192},{80,208},{96,224},{112... | collective-permute-start | bytes 55304 | tf_op jit(solution)/shard_map/ppermute | solution.py:73
  103.4 4.4 %collective-permute-start.7 = (f32[16,288]{1,0:T(8,128)S(1)}, f32[16,288]{1,0:T(8,128)S(1)}, u32[]{:S(2)}, u32[]{:S(2)}) collective-permute-start(f32[16,288]{1,0:T(8,128)S(1)} %get-tuple-element.185), channel_id=1, source_target_pairs={{0,256},{16,272},{32,288},{48,304},{64,320},{80,336},{96,352},{112... | collective-permute-start | bytes 55304 | tf_op jit(solution)/shard_map/ppermute | solution.py:73
  107.8 3.1 %collective-permute-start.8 = (f32[16,288]{1,0:T(8,128)S(1)}, f32[16,288]{1,0:T(8,128)S(1)}, u32[]{:S(2)}, u32[]{:S(2)}) collective-permute-start(f32[16,288]{1,0:T(8,128)S(1)} %get-tuple-element.184), channel_id=1, source_target_pairs={{0,384},{16,400},{32,416},{48,432},{64,448},{80,464},{96,480},{112... | collective-permute-start | bytes 55304 | tf_op jit(solution)/shard_map/ppermute | solution.py:73
  110.9 2.4 %fusion.28 = f32[1024,256]{1,0:T(8,128)} fusion(bf16[1024,256]{1,0:T(8,128)(2,1)} %bitcast.265, bf16[3,3,256,256]{3,2,1,0:T(8,128)(2,1)S(1)} %bitcast.240), kind=kOutput, calls=%fused_computation.83 | convolution fusion | flops 134217728 | bytes 1703936 | tf_op jit(solution)/shard_map/dot_general | solution.py:151
  113.3 0.6 gather_fusion
  114.0 8.8 %collective-permute-start.9 = (f32[16,288]{1,0:T(8,128)S(1)}, f32[16,288]{1,0:T(8,128)S(1)}, u32[]{:S(2)}, u32[]{:S(2)}) collective-permute-start(f32[16,288]{1,0:T(8,128)S(1)} %select_reduce_fusion.1), channel_id=1, source_target_pairs={{0,32},{16,48},{32,64},{48,80},{64,96},{80,112},{96,0},{112,16},{1... | collective-permute-start | bytes 55304 | tf_op jit(solution)/shard_map/ppermute | solution.py:80
  122.8 8.0 %collective-permute-start.10 = (f32[16,288]{1,0:T(8,128)S(1)}, f32[16,288]{1,0:T(8,128)S(1)}, u32[]{:S(2)}, u32[]{:S(2)}) collective-permute-start(f32[16,288]{1,0:T(8,128)S(1)} %select_reduce_fusion.1), channel_id=1, source_target_pairs={{0,64},{16,80},{32,96},{48,112},{64,0},{80,16},{96,32},{112,48},{1... | collective-permute-start | bytes 55304 | tf_op jit(solution)/shard_map/ppermute | solution.py:80
  130.7 5.2 %collective-permute-start.11 = (f32[16,288]{1,0:T(8,128)S(1)}, f32[16,288]{1,0:T(8,128)S(1)}, u32[]{:S(2)}, u32[]{:S(2)}) collective-permute-start(f32[16,288]{1,0:T(8,128)S(1)} %select_reduce_fusion.1), channel_id=1, source_target_pairs={{0,96},{16,112},{32,0},{48,16},{64,32},{80,48},{96,64},{112,80},{1... | collective-permute-start | bytes 55304 | tf_op jit(solution)/shard_map/ppermute | solution.py:80
  135.9 2.3 %fusion.6 = bf16[1024,256]{1,0:T(8,128)(2,1)} fusion(f32[1024,256]{1,0:T(8,128)} %fusion.28, f32[1024,256]{1,0:T(8,128)S(1)} %copy-done.10, bf16[1024,256]{1,0:T(8,128)(2,1)S(1)} %bitcast.264, bf16[3,3,256,256]{3,2,1,0:T(8,128)(2,1)S(1)} %bitcast.241), kind=kOutput, calls=%fused_computation.23 | convolution fusion | flops 135004160 | bytes 3276800 | tf_op jit(solution)/shard_map/dot_general | solution.py:151
  138.3 1.0 collective-permute-done.11
  139.3 0.6 gather_fusion.1
  140.0 2.2 %collective-permute-start.12 = (f32[16,288]{1,0:T(8,128)S(1)}, f32[16,288]{1,0:T(8,128)S(1)}, u32[]{:S(2)}, u32[]{:S(2)}) collective-permute-start(f32[16,288]{1,0:T(8,128)S(1)} %select_reduce_fusion), channel_id=1, source_target_pairs={{0,128},{16,144},{32,160},{48,176},{64,192},{80,208},{96,224},{112... | collective-permute-start | bytes 55304 | tf_op jit(solution)/shard_map/ppermute | solution.py:95
  142.2 4.4 %collective-permute-start.13 = (f32[16,288]{1,0:T(8,128)S(1)}, f32[16,288]{1,0:T(8,128)S(1)}, u32[]{:S(2)}, u32[]{:S(2)}) collective-permute-start(f32[16,288]{1,0:T(8,128)S(1)} %select_reduce_fusion), channel_id=1, source_target_pairs={{0,256},{16,272},{32,288},{48,304},{64,320},{80,336},{96,352},{112... | collective-permute-start | bytes 55304 | tf_op jit(solution)/shard_map/ppermute | solution.py:95
  146.6 1.9 %collective-permute-start.14 = (f32[16,288]{1,0:T(8,128)S(1)}, f32[16,288]{1,0:T(8,128)S(1)}, u32[]{:S(2)}, u32[]{:S(2)}) collective-permute-start(f32[16,288]{1,0:T(8,128)S(1)} %select_reduce_fusion), channel_id=1, source_target_pairs={{0,384},{16,400},{32,416},{48,432},{64,448},{80,464},{96,480},{112... | collective-permute-start | bytes 55304 | tf_op jit(solution)/shard_map/ppermute | solution.py:95
  148.5 7.0 %collective-permute-start.15 = (f32[16,288]{1,0:T(8,128)S(1)}, f32[16,288]{1,0:T(8,128)S(1)}, u32[]{:S(2)}, u32[]{:S(2)}) collective-permute-start(f32[16,288]{1,0:T(8,128)S(1)} %select_reduce_fusion), channel_id=1, source_target_pairs={{0,16},{16,0},{32,48},{48,32},{64,80},{80,64},{96,112},{112,96},{1... | collective-permute-start | bytes 55304 | tf_op jit(solution)/shard_map/ppermute | solution.py:95
  155.5 3.5 %collective-permute-start.16 = (f32[16,288]{1,0:T(8,128)S(1)}, f32[16,288]{1,0:T(8,128)S(1)}, u32[]{:S(2)}, u32[]{:S(2)}) collective-permute-start(f32[16,288]{1,0:T(8,128)S(1)} %select_reduce_fusion), channel_id=1, source_target_pairs={{0,144},{16,128},{32,176},{48,160},{64,208},{80,192},{96,240},{112... | collective-permute-start | bytes 55304 | tf_op jit(solution)/shard_map/ppermute | solution.py:95
  159.1 0.6 bitcast_dynamic-update-slice_fusion.1
  159.7 2.1 %collective-permute-start.17 = (f32[16,288]{1,0:T(8,128)S(1)}, f32[16,288]{1,0:T(8,128)S(1)}, u32[]{:S(2)}, u32[]{:S(2)}) collective-permute-start(f32[16,288]{1,0:T(8,128)S(1)} %select_reduce_fusion), channel_id=1, source_target_pairs={{0,272},{16,256},{32,304},{48,288},{64,336},{80,320},{96,368},{112... | collective-permute-start | bytes 55304 | tf_op jit(solution)/shard_map/ppermute | solution.py:95
  161.8 0.7 fusion.36
  162.5 4.5 %collective-permute-start.18 = (f32[16,288]{1,0:T(8,128)S(1)}, f32[16,288]{1,0:T(8,128)S(1)}, u32[]{:S(2)}, u32[]{:S(2)}) collective-permute-start(f32[16,288]{1,0:T(8,128)S(1)} %select_reduce_fusion), channel_id=1, source_target_pairs={{0,400},{16,384},{32,432},{48,416},{64,464},{80,448},{96,496},{112... | collective-permute-start | bytes 55304 | tf_op jit(solution)/shard_map/ppermute | solution.py:95
  167.1 0.6 fusion.35
  167.7 0.6 fusion.34
  168.3 0.6 fusion.33
  169.0 0.6 fusion.32
  169.6 0.6 fusion.31
  170.2 0.6 fusion.30
  171.2 0.7 copy.40
  (98 shorter events, 10.6 us)
Async XLA Ops:
  0.6 9.6 %copy-start.2 = (bf16[1,8,128,256]{3,2,1,0:T(8,128)(2,1)S(1)}, bf16[1,8,128,256]{3,2,1,0:T(8,128)(2,1)}, u32[]{:S(2)}) copy-start(bf16[1,8,128,256]{3,2,1,0:T(8,128)(2,1)} %param.28) | copy-start | bytes 1572868
  1.7 16.0 %copy-start.14 = (s32[4]{0:T(128)S(1)}, s32[4]{0:T(128)}, u32[]{:S(2)}) copy-start(s32[4]{0:T(128)} %constant.390.clone.1) | copy-start | bytes 52
  2.6 26.6 %all-to-all-start = ((bf16[16,16,1152]{2,1,0:T(8,128)(2,1)}), bf16[16,16,1152]{2,1,0:T(8,128)(2,1)S(1)}, u32[]{:S(2)}, u32[]{:S(2)}) async-start(bf16[16,16,1152]{2,1,0:T(8,128)(2,1)} %broadcast_in_dim.33), calls=%async_computation | async-start | bytes 1179648 | tf_op jit(solution)/shard_map/all_to_all | solution.py:36
  10.3 17.3 %collective-permute-start = (bf16[1,1,128,256]{3,2,1,0:T(8,128)(2,1)S(1)}, bf16[1,1,128,256]{3,2,1,0:T(8,128)(2,1)S(1)}, u32[]{:S(2)}, u32[]{:S(2)}) collective-permute-start(bf16[1,1,128,256]{3,2,1,0:T(8,128)(2,1)S(1)} %get-tuple-element.181), channel_id=1, source_target_pairs={{0,1},{1,2},{2,3},{3,4},{4,5},{5,6},{6,7},{7,8},{8,9},{9,10},{10,1... | collective-permute-start | bytes 196616 | tf_op jit(solution)/shard_map/ppermute | solution.py:21
  13.4 14.2 %collective-permute-start.1 = (bf16[1,1,128,256]{3,2,1,0:T(8,128)(2,1)S(1)}, bf16[1,1,128,256]{3,2,1,0:T(8,128)(2,1)S(1)}, u32[]{:S(2)}, u32[]{:S(2)}) collective-permute-start(bf16[1,1,128,256]{3,2,1,0:T(8,128)(2,1)S(1)} %get-tuple-element.182), channel_id=1, source_target_pairs={{1,0},{2,1},{3,2},{4,3},{5,4},{6,5},{7,6},{8,7},{9,8},{10,9},{11,1... | collective-permute-start | bytes 196616 | tf_op jit(solution)/shard_map/ppermute | solution.py:22
  29.2 10.1 %copy-start.3 = (bf16[1,8,128,256]{3,2,1,0:T(8,128)(2,1)}, bf16[1,8,128,256]{3,2,1,0:T(8,128)(2,1)S(1)}, u32[]{:S(2)}) copy-start(bf16[1,8,128,256]{3,2,1,0:T(8,128)(2,1)S(1)} %get-tuple-element.171) | copy-start | bytes 1572868
  29.2 4.8 %collective-permute-start.2 = (bf16[16,16,1152]{2,1,0:T(8,128)(2,1)S(1)}, bf16[16,16,1152]{2,1,0:T(8,128)(2,1)S(1)}, u32[]{:S(2)}, u32[]{:S(2)}) collective-permute-start(bf16[16,16,1152]{2,1,0:T(8,128)(2,1)S(1)} %all-to-all-done), channel_id=1, source_target_pairs={{0,16},{16,0},{32,48},{48,32},{64,80},{80,64},{96,112},{112,96},{1... | collective-permute-start | bytes 1769480 | tf_op jit(solution)/shard_map/ppermute | solution.py:95
  37.6 6.1 %copy-start = (bf16[2304,256]{1,0:T(8,128)(2,1)}, bf16[2304,256]{1,0:T(8,128)(2,1)S(1)}, u32[]{:S(2)}) copy-start(bf16[2304,256]{1,0:T(8,128)(2,1)S(1)} %copy.35) | copy-start | bytes 3538948
  40.0 1.0 copy-start.9
  41.0 1.0 copy-start.7
  42.0 1.0 copy-start.6
  43.4 1.0 copy-start.8
  44.4 0.8 copy-start.13
  44.8 1.0 copy-start.11
  47.8 1.0 copy-start.5
  49.9 1.0 copy-start.4
  55.7 4.7 %collective-permute-start.5 = (f32[256,1152]{1,0:T(8,128)S(1)}, f32[256,1152]{1,0:T(8,128)S(1)}, u32[]{:S(2)}, u32[]{:S(2)}) collective-permute-start(f32[256,1152]{1,0:T(8,128)S(1)} %broadcast_select_fusion), channel_id=1, source_target_pairs={{0,16},{16,0},{32,48},{48,32},{64,80},{80,64},{96,112},{112,96},{1... | collective-permute-start | bytes 3538952 | tf_op jit(solution)/shard_map/ppermute | solution.py:30
  61.6 4.0 %copy-start.12 = (s32[4]{0:T(128)S(1)}, s32[4]{0:T(128)}, u32[]{:S(2)}) copy-start(s32[4]{0:T(128)} %constant.403.clone.1) | copy-start | bytes 52
  61.6 38.3 %all-to-all-start.1 = ((f32[16,16,1152]{2,1,0:T(8,128)}), f32[16,16,1152]{2,1,0:T(8,128)S(1)}, u32[]{:S(2)}, u32[]{:S(2)}) async-start(f32[16,16,1152]{2,1,0:T(8,128)} %bitcast.244), calls=%async_computation.1 | async-start | bytes 2359296 | tf_op jit(solution)/shard_map/all_to_all | solution.py:42
  68.7 26.4 %collective-permute-start.3 = (bf16[1,1,128,256]{3,2,1,0:T(8,128)(2,1)S(1)}, bf16[1,1,128,256]{3,2,1,0:T(8,128)(2,1)S(1)}, u32[]{:S(2)}, u32[]{:S(2)}) collective-permute-start(bf16[1,1,128,256]{3,2,1,0:T(8,128)(2,1)S(1)} %get-tuple-element.177), channel_id=1, source_target_pairs={{0,1},{1,2},{2,3},{3,4},{4,5},{5,6},{6,7},{7,8},{8,9},{9,10},{10,1... | collective-permute-start | bytes 196616 | tf_op jit(solution)/shard_map/ppermute | solution.py:21
  71.6 23.5 %collective-permute-start.4 = (bf16[1,1,128,256]{3,2,1,0:T(8,128)(2,1)S(1)}, bf16[1,1,128,256]{3,2,1,0:T(8,128)(2,1)S(1)}, u32[]{:S(2)}, u32[]{:S(2)}) collective-permute-start(bf16[1,1,128,256]{3,2,1,0:T(8,128)(2,1)S(1)} %get-tuple-element.178), channel_id=1, source_target_pairs={{1,0},{2,1},{3,2},{4,3},{5,4},{6,5},{7,6},{8,7},{9,8},{10,9},{11,1... | collective-permute-start | bytes 196616 | tf_op jit(solution)/shard_map/ppermute | solution.py:22
  95.4 1.3 copy-start.1
  100.1 35.8 %copy-start.10 = (f32[1024,256]{1,0:T(8,128)S(1)}, f32[1024,256]{1,0:T(8,128)}, u32[]{:S(2)}) copy-start(f32[1024,256]{1,0:T(8,128)} %convolution_add_fusion.1) | copy-start | bytes 3145732
  100.2 13.1 %collective-permute-start.6 = (f32[16,288]{1,0:T(8,128)S(1)}, f32[16,288]{1,0:T(8,128)S(1)}, u32[]{:S(2)}, u32[]{:S(2)}) collective-permute-start(f32[16,288]{1,0:T(8,128)S(1)} %get-tuple-element.186), channel_id=1, source_target_pairs={{0,128},{16,144},{32,160},{48,176},{64,192},{80,208},{96,224},{112... | collective-permute-start | bytes 55304 | tf_op jit(solution)/shard_map/ppermute | solution.py:73
  103.4 9.9 %collective-permute-start.7 = (f32[16,288]{1,0:T(8,128)S(1)}, f32[16,288]{1,0:T(8,128)S(1)}, u32[]{:S(2)}, u32[]{:S(2)}) collective-permute-start(f32[16,288]{1,0:T(8,128)S(1)} %get-tuple-element.185), channel_id=1, source_target_pairs={{0,256},{16,272},{32,288},{48,304},{64,320},{80,336},{96,352},{112... | collective-permute-start | bytes 55304 | tf_op jit(solution)/shard_map/ppermute | solution.py:73
  107.8 5.5 %collective-permute-start.8 = (f32[16,288]{1,0:T(8,128)S(1)}, f32[16,288]{1,0:T(8,128)S(1)}, u32[]{:S(2)}, u32[]{:S(2)}) collective-permute-start(f32[16,288]{1,0:T(8,128)S(1)} %get-tuple-element.184), channel_id=1, source_target_pairs={{0,384},{16,400},{32,416},{48,432},{64,448},{80,464},{96,480},{112... | collective-permute-start | bytes 55304 | tf_op jit(solution)/shard_map/ppermute | solution.py:73
  114.0 24.3 %collective-permute-start.9 = (f32[16,288]{1,0:T(8,128)S(1)}, f32[16,288]{1,0:T(8,128)S(1)}, u32[]{:S(2)}, u32[]{:S(2)}) collective-permute-start(f32[16,288]{1,0:T(8,128)S(1)} %select_reduce_fusion.1), channel_id=1, source_target_pairs={{0,32},{16,48},{32,64},{48,80},{64,96},{80,112},{96,0},{112,16},{1... | collective-permute-start | bytes 55304 | tf_op jit(solution)/shard_map/ppermute | solution.py:80
  122.8 15.5 %collective-permute-start.10 = (f32[16,288]{1,0:T(8,128)S(1)}, f32[16,288]{1,0:T(8,128)S(1)}, u32[]{:S(2)}, u32[]{:S(2)}) collective-permute-start(f32[16,288]{1,0:T(8,128)S(1)} %select_reduce_fusion.1), channel_id=1, source_target_pairs={{0,64},{16,80},{32,96},{48,112},{64,0},{80,16},{96,32},{112,48},{1... | collective-permute-start | bytes 55304 | tf_op jit(solution)/shard_map/ppermute | solution.py:80
  130.7 8.6 %collective-permute-start.11 = (f32[16,288]{1,0:T(8,128)S(1)}, f32[16,288]{1,0:T(8,128)S(1)}, u32[]{:S(2)}, u32[]{:S(2)}) collective-permute-start(f32[16,288]{1,0:T(8,128)S(1)} %select_reduce_fusion.1), channel_id=1, source_target_pairs={{0,96},{16,112},{32,0},{48,16},{64,32},{80,48},{96,64},{112,80},{1... | collective-permute-start | bytes 55304 | tf_op jit(solution)/shard_map/ppermute | solution.py:80
  140.0 19.7 %collective-permute-start.12 = (f32[16,288]{1,0:T(8,128)S(1)}, f32[16,288]{1,0:T(8,128)S(1)}, u32[]{:S(2)}, u32[]{:S(2)}) collective-permute-start(f32[16,288]{1,0:T(8,128)S(1)} %select_reduce_fusion), channel_id=1, source_target_pairs={{0,128},{16,144},{32,160},{48,176},{64,192},{80,208},{96,224},{112... | collective-permute-start | bytes 55304 | tf_op jit(solution)/shard_map/ppermute | solution.py:95
  142.2 20.3 %collective-permute-start.13 = (f32[16,288]{1,0:T(8,128)S(1)}, f32[16,288]{1,0:T(8,128)S(1)}, u32[]{:S(2)}, u32[]{:S(2)}) collective-permute-start(f32[16,288]{1,0:T(8,128)S(1)} %select_reduce_fusion), channel_id=1, source_target_pairs={{0,256},{16,272},{32,288},{48,304},{64,320},{80,336},{96,352},{112... | collective-permute-start | bytes 55304 | tf_op jit(solution)/shard_map/ppermute | solution.py:95
  146.6 21.0 %collective-permute-start.14 = (f32[16,288]{1,0:T(8,128)S(1)}, f32[16,288]{1,0:T(8,128)S(1)}, u32[]{:S(2)}, u32[]{:S(2)}) collective-permute-start(f32[16,288]{1,0:T(8,128)S(1)} %select_reduce_fusion), channel_id=1, source_target_pairs={{0,384},{16,400},{32,416},{48,432},{64,448},{80,464},{96,480},{112... | collective-permute-start | bytes 55304 | tf_op jit(solution)/shard_map/ppermute | solution.py:95
  148.5 19.8 %collective-permute-start.15 = (f32[16,288]{1,0:T(8,128)S(1)}, f32[16,288]{1,0:T(8,128)S(1)}, u32[]{:S(2)}, u32[]{:S(2)}) collective-permute-start(f32[16,288]{1,0:T(8,128)S(1)} %select_reduce_fusion), channel_id=1, source_target_pairs={{0,16},{16,0},{32,48},{48,32},{64,80},{80,64},{96,112},{112,96},{1... | collective-permute-start | bytes 55304 | tf_op jit(solution)/shard_map/ppermute | solution.py:95
  155.5 13.4 %collective-permute-start.16 = (f32[16,288]{1,0:T(8,128)S(1)}, f32[16,288]{1,0:T(8,128)S(1)}, u32[]{:S(2)}, u32[]{:S(2)}) collective-permute-start(f32[16,288]{1,0:T(8,128)S(1)} %select_reduce_fusion), channel_id=1, source_target_pairs={{0,144},{16,128},{32,176},{48,160},{64,208},{80,192},{96,240},{112... | collective-permute-start | bytes 55304 | tf_op jit(solution)/shard_map/ppermute | solution.py:95
  159.7 9.9 %collective-permute-start.17 = (f32[16,288]{1,0:T(8,128)S(1)}, f32[16,288]{1,0:T(8,128)S(1)}, u32[]{:S(2)}, u32[]{:S(2)}) collective-permute-start(f32[16,288]{1,0:T(8,128)S(1)} %select_reduce_fusion), channel_id=1, source_target_pairs={{0,272},{16,256},{32,304},{48,288},{64,336},{80,320},{96,368},{112... | collective-permute-start | bytes 55304 | tf_op jit(solution)/shard_map/ppermute | solution.py:95
  162.5 7.7 %collective-permute-start.18 = (f32[16,288]{1,0:T(8,128)S(1)}, f32[16,288]{1,0:T(8,128)S(1)}, u32[]{:S(2)}, u32[]{:S(2)}) collective-permute-start(f32[16,288]{1,0:T(8,128)S(1)} %select_reduce_fusion), channel_id=1, source_target_pairs={{0,400},{16,384},{32,432},{48,416},{64,464},{80,448},{96,496},{112... | collective-permute-start | bytes 55304 | tf_op jit(solution)/shard_map/ppermute | solution.py:95

commit v5 on v3

--- a/solution.py
+++ b/solution.py
@@ -138,9 +138,8 @@
     partial_value = jnp.stack(pieces, axis=1).reshape(out_chan, taps)
     core_sum = halve_sum(partial_value, "row", core_bit, 1)
     col_sum = scatter_sum(core_sum, "col")
-    x_piece = halve_sum(col_sum, "row", [3, 4], 1)
-    row_piece = double_sum(x_piece, "row", [1, 2])
-    own_share = double_join(row_piece, "row", [4, 3, 0], 1)
+    row_piece = double_sum(col_sum, "row", [3, 4, 1, 2])
+    own_share = double_join(row_piece, "row", core_bit, 1)
     pixels = img_count * lax.axis_size("row") * tile_rows * lax.axis_size("col") * tile_cols
     weight_grad = (own_share * (1.0 / math.sqrt(pixels))).T.reshape(3, 3, in_chan, share)
     features = outputs.reshape(img_count, tile_rows, tile_cols, out_chan)

time: 155 us -> 144 us (0.929)
  the two profiles are of different devices: /device:TPU:65 before, /device:TPU:59 now
where the time goes in v5:
time: 144 us; the launch traced here: 143 us
  starting transfers between devices  64.2 us (45%)
  waiting for transfers between devices  43.5 us (30%)
  local copies, waits for them, and re-layouts  14.5 us (10%)
  matrix products  13.3 us (9%)
  other arithmetic  6.32 us (4%)
    ppermute x7, starting transfers between devices, exchange(): return lax.ppermute(value, axis, pairs)  40.1 us
    ppermute x2, waiting for transfers between devices, padded_2(): before = lax.ppermute(last, axis, up)  21.3 us
    ppermute x7, waiting for transfers between devices, exchange(): return lax.ppermute(value, axis, pairs)  11.4 us
    all_to_all x1, waiting for transfers between devices, gather_chunks(): return lax.all_to_all(copies, axis, 0, 0, tiled=False)  8.89 us
    unnamed x34, local copies, waits for them, and re-layouts  8.78 us
    all_to_all x1, starting transfers between devices, gather_chunks(): return lax.all_to_all(copies, axis, 0, 0, tiled=False)  7.75 us
    ppermute x2, starting transfers between devices, padded_2(): before = lax.ppermute(last, axis, up)  6.18 us
    dot_general x9, matrix products, on_device(): lax.dot_general(window(grad_pad, 2 - tap_row, 2 - tap_col, tile_rows, til...  5.98 us
  transfers between devices with their start and end apart: 13, of which 8 were waited for; matrix products, arithmetic and copies ran while one was open for 7% of the time, Pallas kernels for 0%

profile of v5, /device:TPU:59, one launch (start us, length us, event | category | flops | bytes accessed | tf_op | source)
XLA Modules:
  0.0 143.0 jit_solution(18398854664753360883)
XLA Ops:
  0.6 1.0 copy.14
  1.8 0.9 broadcast_in_dim.2
  2.6 7.8 %all-to-all-start = ((bf16[16,16,1152]{2,1,0:T(8,128)(2,1)}), bf16[16,16,1152]{2,1,0:T(8,128)(2,1)S(1)}, u32[]{:S(2)}, u32[]{:S(2)}) async-start(bf16[16,16,1152]{2,1,0:T(8,128)(2,1)} %broadcast_in_dim.2), calls=%async_computation | async-start | bytes 1179648 | tf_op jit(solution)/shard_map/all_to_all | solution.py:35
  10.4 3.1 %collective-permute-start = (bf16[1,1,128,256]{3,2,1,0:T(8,128)(2,1)S(1)}, bf16[1,1,128,256]{3,2,1,0:T(8,128)(2,1)S(1)}, u32[]{:S(2)}, u32[]{:S(2)}) collective-permute-start(bf16[1,1,128,256]{3,2,1,0:T(8,128)(2,1)S(1)} %get-tuple-element.33), channel_id=1, source_target_pairs={{0,1},{1,2},{2,3},{3,4},{4,5},{5,6},{6,7},{7,8},{8,9},{9,10},{10,1... | collective-permute-start | bytes 196616 | tf_op jit(solution)/shard_map/ppermute | solution.py:20
  13.5 2.2 %collective-permute-start.1 = (bf16[1,1,128,256]{3,2,1,0:T(8,128)(2,1)S(1)}, bf16[1,1,128,256]{3,2,1,0:T(8,128)(2,1)S(1)}, u32[]{:S(2)}, u32[]{:S(2)}) collective-permute-start(bf16[1,1,128,256]{3,2,1,0:T(8,128)(2,1)S(1)} %get-tuple-element.34), channel_id=1, source_target_pairs={{1,0},{2,1},{3,2},{4,3},{5,4},{6,5},{7,6},{8,7},{9,8},{10,9},{11,1... | collective-permute-start | bytes 196616 | tf_op jit(solution)/shard_map/ppermute | solution.py:21
  15.7 8.9 %all-to-all-done = bf16[16,16,1152]{2,1,0:T(8,128)(2,1)S(1)} async-done(((bf16[16,16,1152]{2,1,0:T(8,128)(2,1)}), bf16[16,16,1152]{2,1,0:T(8,128)(2,1)S(1)}, u32[]{:S(2)}, u32[]{:S(2)}) %all-to-all-start) | async-done | bytes 589856 | tf_op jit(solution)/shard_map/all_to_all | solution.py:35
  24.6 4.1 %collective-permute-start.2 = (bf16[16,16,1152]{2,1,0:T(8,128)(2,1)S(1)}, bf16[16,16,1152]{2,1,0:T(8,128)(2,1)S(1)}, u32[]{:S(2)}, u32[]{:S(2)}) collective-permute-start(bf16[16,16,1152]{2,1,0:T(8,128)(2,1)S(1)} %all-to-all-done), channel_id=1, source_target_pairs={{0,16},{16,0},{32,48},{48,32},{64,80},{80,64},{96,112},{112,96},{1... | collective-permute-start | bytes 1769480 | tf_op jit(solution)/shard_map/ppermute | solution.py:29
  28.9 1.1 pad_maximum_fusion.2
  29.9 1.6 %fusion.36 = (bf16[1,8,128,256]{3,2,1,0:T(8,128)(2,1)}, bf16[1,8,128,256]{3,2,1,0:T(8,128)(2,1)}, bf16[1,8,128,256]{3,2,1,0:T(8,128)(2,1)}, bf16[1,8,128,256]{3,...) fusion(bf16[1,10,130,256]{3,2,1,0:T(8,128)(2,1)S(1)} %select_maximum_fusion.2), kind=kLoop, calls=%fused_computation.91 | loop fusion | bytes 6291456 | tf_op jit(solution)/shard_map/slice | solution.py:92
  31.8 0.6 copy.15
  32.4 1.8 %fusion.27 = f32[1024,256]{1,0:T(8,128)S(1)} fusion(bf16[1024,256]{1,0:T(8,128)(2,1)} %bitcast.186, bf16[3,3,256,256]{3,2,1,0:T(8,128)(2,1)S(1)} %bitcast.159), kind=kOutput, calls=%fused_computation.78 | convolution fusion | flops 134217728 | bytes 1703936 | tf_op jit(solution)/shard_map/dot_general | solution.py:111
  34.5 0.7 copy-done.3
  35.8 0.7 copy-done.9
  36.9 0.7 copy-done.7
  37.6 0.3 convolution_add_fusion.9
  37.9 0.7 copy-done.6
  39.0 0.3 fusion.3
  39.3 0.7 copy-done.8
  40.0 0.4 fusion.39
  40.4 0.4 multiply_reduce_fusion.1
  40.8 0.6 copy-done.13
  41.5 1.9 %fusion.32 = (f32[1024]{0:T(1024)S(1)}, f32[1024]{0:T(1024)S(1)}, f32[1024,256]{1,0:T(8,128)S(1)}, bf16[1024,256]{1,0:T(8,128)(2,1)}) fusion(f32[1024]{0:T(1024)S(1)} %add_rsqrt_fusion, f32[1024,256]{1,0:T(8,128)S(1)} %get-tuple-element.36, f32[1024]{0:T(1024)S(1)} %broadcast_multiply_fusion.2, f32[256]{0:T(256)S(1)} %copy-done.14, ...), kind=kLoop, calls=%fused_computation.88 | loop fusion | flops 4978688 | bytes 3163136 | tf_op jit(solution)/shard_map/reduce_sum | solution.py:85
  43.4 0.8 multiply_convert_fusion
  44.4 0.3 fusion.16
  44.8 0.3 fusion.15
  45.1 0.3 fusion.14
  45.5 0.3 fusion.13
  45.8 0.3 fusion.12
  46.2 0.3 fusion.11
  46.5 0.3 fusion.10
  46.9 0.3 fusion.9
  47.3 0.3 fusion.8
  47.6 1.2 fusion.34
  48.8 0.4 copy.21
  49.1 1.6 %copy.22 = f32[256,1152]{1,0:T(8,128)S(1)} copy(f32[256,1152]{0,1:T(8,128)} %get-tuple-element.13) | data formatting | bytes 2359296
  50.9 1.9 %collective-permute-start.5 = (f32[256,1152]{1,0:T(8,128)S(1)}, f32[256,1152]{1,0:T(8,128)S(1)}, u32[]{:S(2)}, u32[]{:S(2)}) collective-permute-start(f32[256,1152]{1,0:T(8,128)S(1)} %broadcast_select_fusion), channel_id=1, source_target_pairs={{0,16},{16,0},{32,48},{48,32},{64,80},{80,64},{96,112},{112,96},{1... | collective-permute-start | bytes 3538952 | tf_op jit(solution)/shard_map/ppermute | solution.py:29
  52.8 2.8 %collective-permute-done.5 = f32[256,1152]{1,0:T(8,128)S(1)} collective-permute-done((f32[256,1152]{1,0:T(8,128)S(1)}, f32[256,1152]{1,0:T(8,128)S(1)}, u32[]{:S(2)}, u32[]{:S(2)}) %collective-permute-start.5) | collective-permute-done | bytes 1179680 | tf_op jit(solution)/shard_map/ppermute | solution.py:29
  55.7 1.2 select_add_fusion
  56.8 5.7 %all-to-all-start.1 = ((f32[16,16,1152]{2,1,0:T(8,128)}), f32[16,16,1152]{2,1,0:T(8,128)S(1)}, u32[]{:S(2)}, u32[]{:S(2)}) async-start(f32[16,16,1152]{2,1,0:T(8,128)} %bitcast.179), calls=%async_computation.1 | async-start | bytes 2359296 | tf_op jit(solution)/shard_map/all_to_all | solution.py:41
  62.6 3.1 %collective-permute-start.3 = (bf16[1,1,128,256]{3,2,1,0:T(8,128)(2,1)S(1)}, bf16[1,1,128,256]{3,2,1,0:T(8,128)(2,1)S(1)}, u32[]{:S(2)}, u32[]{:S(2)}) collective-permute-start(bf16[1,1,128,256]{3,2,1,0:T(8,128)(2,1)S(1)} %get-tuple-element.29), channel_id=1, source_target_pairs={{0,1},{1,2},{2,3},{3,4},{4,5},{5,6},{6,7},{7,8},{8,9},{9,10},{10,1... | collective-permute-start | bytes 196616 | tf_op jit(solution)/shard_map/ppermute | solution.py:20
  65.7 2.2 %collective-permute-start.4 = (bf16[1,1,128,256]{3,2,1,0:T(8,128)(2,1)S(1)}, bf16[1,1,128,256]{3,2,1,0:T(8,128)(2,1)S(1)}, u32[]{:S(2)}, u32[]{:S(2)}) collective-permute-start(bf16[1,1,128,256]{3,2,1,0:T(8,128)(2,1)S(1)} %get-tuple-element.30), channel_id=1, source_target_pairs={{1,0},{2,1},{3,2},{4,3},{5,4},{6,5},{7,6},{8,7},{9,8},{10,9},{11,1... | collective-permute-start | bytes 196616 | tf_op jit(solution)/shard_map/ppermute | solution.py:21
  67.9 21.3 %collective-permute-done.3 = bf16[1,1,128,256]{3,2,1,0:T(8,128)(2,1)S(1)} collective-permute-done((bf16[1,1,128,256]{3,2,1,0:T(8,128)(2,1)S(1)}, bf16[1,1,128,256]{3,2,1,0:T(8,128)(2,1)S(1)}, u32[]{:S(2)}, u32[]{:S(2)}) %collective-permute-start.3) | collective-permute-done | bytes 65568 | tf_op jit(solution)/shard_map/ppermute | solution.py:20
  89.1 1.9 %collective-permute-done.4 = bf16[1,1,128,256]{3,2,1,0:T(8,128)(2,1)S(1)} collective-permute-done((bf16[1,1,128,256]{3,2,1,0:T(8,128)(2,1)S(1)}, bf16[1,1,128,256]{3,2,1,0:T(8,128)(2,1)S(1)}, u32[]{:S(2)}, u32[]{:S(2)}) %collective-permute-start.4) | collective-permute-done | bytes 65568 | tf_op jit(solution)/shard_map/ppermute | solution.py:21
  91.3 1.3 fusion.35
  92.6 0.6 copy-done.1
  93.1 0.3 fusion.26
  93.5 0.3 convolution_add_fusion.6
  93.8 0.3 convolution_add_fusion.5
  94.1 1.3 convolution_add_fusion.4
  95.6 2.3 %collective-permute-start.6 = (f32[16,1152]{1,0:T(8,128)S(1)}, f32[16,1152]{1,0:T(8,128)S(1)}, u32[]{:S(2)}, u32[]{:S(2)}) collective-permute-start(f32[16,1152]{1,0:T(8,128)S(1)} %reduce_sum.49), channel_id=1, source_target_pairs={{0,128},{16,144},{32,160},{48,176},{64,192},{80,208},{96,224},{112... | collective-permute-start | bytes 221192 | tf_op jit(solution)/shard_map/ppermute | solution.py:29
  97.9 1.6 %convolution_add_fusion.3 = f32[1024,256]{1,0:T(8,128)S(1)} fusion(f32[1024,256]{1,0:T(8,128)} %convolution_add_fusion.4, bf16[1024,256]{1,0:T(8,128)(2,1)S(1)} %multiply_convert_fusion, bf16[3,3,256,256]{3,2,1,0:T(8,128)(2,1)S(1)} %bitcast.172), kind=kOutput, calls=%fused_computation.12 | convolution fusion | flops 134479872 | bytes 2752512 | tf_op jit(solution)/shard_map/dot_general | solution.py:124
  99.5 1.3 collective-permute-done.6
  100.8 3.8 %collective-permute-start.7 = (f32[16,1152]{1,0:T(8,128)S(1)}, f32[16,1152]{1,0:T(8,128)S(1)}, u32[]{:S(2)}, u32[]{:S(2)}) collective-permute-start(f32[16,1152]{1,0:T(8,128)S(1)} %add.109), channel_id=1, source_target_pairs={{0,256},{16,272},{32,288},{48,304},{64,320},{80,336},{96,352},{112... | collective-permute-start | bytes 221192 | tf_op jit(solution)/shard_map/ppermute | solution.py:29
  104.6 0.3 convolution_add_fusion.2
  104.9 2.5 %collective-permute-done.7 = f32[16,1152]{1,0:T(8,128)S(1)} collective-permute-done((f32[16,1152]{1,0:T(8,128)S(1)}, f32[16,1152]{1,0:T(8,128)S(1)}, u32[]{:S(2)}, u32[]{:S(2)}) %collective-permute-start.7) | collective-permute-done | bytes 73760 | tf_op jit(solution)/shard_map/ppermute | solution.py:29
  107.4 8.8 %collective-permute-start.8 = (f32[16,1152]{1,0:T(8,128)S(1)}, f32[16,1152]{1,0:T(8,128)S(1)}, u32[]{:S(2)}, u32[]{:S(2)}) collective-permute-start(f32[16,1152]{1,0:T(8,128)S(1)} %add.110), channel_id=1, source_target_pairs={{0,32},{16,48},{32,0},{48,16},{64,96},{80,112},{96,64},{112,80},{1... | collective-permute-start | bytes 221192 | tf_op jit(solution)/shard_map/ppermute | solution.py:29
  116.3 0.3 convolution_add_fusion.1
  116.6 1.7 %collective-permute-done.8 = f32[16,1152]{1,0:T(8,128)S(1)} collective-permute-done((f32[16,1152]{1,0:T(8,128)S(1)}, f32[16,1152]{1,0:T(8,128)S(1)}, u32[]{:S(2)}, u32[]{:S(2)}) %collective-permute-start.8) | collective-permute-done | bytes 73760 | tf_op jit(solution)/shard_map/ppermute | solution.py:29
  118.3 11.6 %collective-permute-start.9 = (f32[16,1152]{1,0:T(8,128)S(1)}, f32[16,1152]{1,0:T(8,128)S(1)}, u32[]{:S(2)}, u32[]{:S(2)}) collective-permute-start(f32[16,1152]{1,0:T(8,128)S(1)} %add.111), channel_id=1, source_target_pairs={{0,64},{16,80},{32,96},{48,112},{64,0},{80,16},{96,32},{112,48},{1... | collective-permute-start | bytes 221192 | tf_op jit(solution)/shard_map/ppermute | solution.py:29
  130.0 0.3 fusion.30
  130.3 3.1 %collective-permute-done.9 = f32[16,1152]{1,0:T(8,128)S(1)} collective-permute-done((f32[16,1152]{1,0:T(8,128)S(1)}, f32[16,1152]{1,0:T(8,128)S(1)}, u32[]{:S(2)}, u32[]{:S(2)}) %collective-permute-start.9) | collective-permute-done | bytes 73760 | tf_op jit(solution)/shard_map/ppermute | solution.py:29
  133.4 7.6 %collective-permute-start.10 = (f32[16,1152]{1,0:T(8,128)S(1)}, f32[16,1152]{1,0:T(8,128)S(1)}, u32[]{:S(2)}, u32[]{:S(2)}) collective-permute-start(f32[16,1152]{1,0:T(8,128)S(1)} %add.112), channel_id=1, source_target_pairs={{0,16},{16,0},{32,48},{48,32},{64,80},{80,64},{96,112},{112,96},{1... | collective-permute-start | bytes 221192 | tf_op jit(solution)/shard_map/ppermute | solution.py:29
  141.0 1.1 fusion.6
  142.3 0.7 copy.19
  (52 shorter events, 2.9 us)
Async XLA Ops:
  0.6 9.8 %copy-start.2 = (bf16[1,8,128,256]{3,2,1,0:T(8,128)(2,1)S(1)}, bf16[1,8,128,256]{3,2,1,0:T(8,128)(2,1)}, u32[]{:S(2)}) copy-start(bf16[1,8,128,256]{3,2,1,0:T(8,128)(2,1)} %param.4) | copy-start | bytes 1572868
  2.6 22.0 %all-to-all-start = ((bf16[16,16,1152]{2,1,0:T(8,128)(2,1)}), bf16[16,16,1152]{2,1,0:T(8,128)(2,1)S(1)}, u32[]{:S(2)}, u32[]{:S(2)}) async-start(bf16[16,16,1152]{2,1,0:T(8,128)(2,1)} %broadcast_in_dim.2), calls=%async_computation | async-start | bytes 1179648 | tf_op jit(solution)/shard_map/all_to_all | solution.py:35
  10.4 18.3 %collective-permute-start = (bf16[1,1,128,256]{3,2,1,0:T(8,128)(2,1)S(1)}, bf16[1,1,128,256]{3,2,1,0:T(8,128)(2,1)S(1)}, u32[]{:S(2)}, u32[]{:S(2)}) collective-permute-start(bf16[1,1,128,256]{3,2,1,0:T(8,128)(2,1)S(1)} %get-tuple-element.33), channel_id=1, source_target_pairs={{0,1},{1,2},{2,3},{3,4},{4,5},{5,6},{6,7},{7,8},{8,9},{9,10},{10,1... | collective-permute-start | bytes 196616 | tf_op jit(solution)/shard_map/ppermute | solution.py:20
  13.5 15.2 %collective-permute-start.1 = (bf16[1,1,128,256]{3,2,1,0:T(8,128)(2,1)S(1)}, bf16[1,1,128,256]{3,2,1,0:T(8,128)(2,1)S(1)}, u32[]{:S(2)}, u32[]{:S(2)}) collective-permute-start(bf16[1,1,128,256]{3,2,1,0:T(8,128)(2,1)S(1)} %get-tuple-element.34), channel_id=1, source_target_pairs={{1,0},{2,1},{3,2},{4,3},{5,4},{6,5},{7,6},{8,7},{9,8},{10,9},{11,1... | collective-permute-start | bytes 196616 | tf_op jit(solution)/shard_map/ppermute | solution.py:21
  24.6 6.9 %collective-permute-start.2 = (bf16[16,16,1152]{2,1,0:T(8,128)(2,1)S(1)}, bf16[16,16,1152]{2,1,0:T(8,128)(2,1)S(1)}, u32[]{:S(2)}, u32[]{:S(2)}) collective-permute-start(bf16[16,16,1152]{2,1,0:T(8,128)(2,1)S(1)} %all-to-all-done), channel_id=1, source_target_pairs={{0,16},{16,0},{32,48},{48,32},{64,80},{80,64},{96,112},{112,96},{1... | collective-permute-start | bytes 1769480 | tf_op jit(solution)/shard_map/ppermute | solution.py:29
  32.4 6.9 %copy-start = (bf16[2304,256]{1,0:T(8,128)(2,1)}, bf16[2304,256]{1,0:T(8,128)(2,1)S(1)}, u32[]{:S(2)}) copy-start(bf16[2304,256]{1,0:T(8,128)(2,1)S(1)} %copy.15) | copy-start | bytes 3538948
  32.4 1.8 %copy-start.4 = (bf16[1,8,128,256]{3,2,1,0:T(8,128)(2,1)S(1)}, bf16[1,8,128,256]{3,2,1,0:T(8,128)(2,1)}, u32[]{:S(2)}) copy-start(bf16[1,8,128,256]{3,2,1,0:T(8,128)(2,1)} %get-tuple-element.23) | copy-start | bytes 1572868
  34.2 1.0 copy-start.3
  35.5 1.0 copy-start.9
  36.6 1.0 copy-start.7
  37.6 1.0 copy-start.6
  39.0 1.0 copy-start.8
  40.0 0.8 copy-start.14
  40.4 1.0 copy-start.13
  43.4 1.0 copy-start.5
  50.9 4.7 %collective-permute-start.5 = (f32[256,1152]{1,0:T(8,128)S(1)}, f32[256,1152]{1,0:T(8,128)S(1)}, u32[]{:S(2)}, u32[]{:S(2)}) collective-permute-start(f32[256,1152]{1,0:T(8,128)S(1)} %broadcast_select_fusion), channel_id=1, source_target_pairs={{0,16},{16,0},{32,48},{48,32},{64,80},{80,64},{96,112},{112,96},{1... | collective-permute-start | bytes 3538952 | tf_op jit(solution)/shard_map/ppermute | solution.py:29
  56.8 38.6 %all-to-all-start.1 = ((f32[16,16,1152]{2,1,0:T(8,128)}), f32[16,16,1152]{2,1,0:T(8,128)S(1)}, u32[]{:S(2)}, u32[]{:S(2)}) async-start(f32[16,16,1152]{2,1,0:T(8,128)} %bitcast.179), calls=%async_computation.1 | async-start | bytes 2359296 | tf_op jit(solution)/shard_map/all_to_all | solution.py:41
  62.6 26.6 %collective-permute-start.3 = (bf16[1,1,128,256]{3,2,1,0:T(8,128)(2,1)S(1)}, bf16[1,1,128,256]{3,2,1,0:T(8,128)(2,1)S(1)}, u32[]{:S(2)}, u32[]{:S(2)}) collective-permute-start(bf16[1,1,128,256]{3,2,1,0:T(8,128)(2,1)S(1)} %get-tuple-element.29), channel_id=1, source_target_pairs={{0,1},{1,2},{2,3},{3,4},{4,5},{5,6},{6,7},{7,8},{8,9},{9,10},{10,1... | collective-permute-start | bytes 196616 | tf_op jit(solution)/shard_map/ppermute | solution.py:20
  65.7 25.4 %collective-permute-start.4 = (bf16[1,1,128,256]{3,2,1,0:T(8,128)(2,1)S(1)}, bf16[1,1,128,256]{3,2,1,0:T(8,128)(2,1)S(1)}, u32[]{:S(2)}, u32[]{:S(2)}) collective-permute-start(bf16[1,1,128,256]{3,2,1,0:T(8,128)(2,1)S(1)} %get-tuple-element.30), channel_id=1, source_target_pairs={{1,0},{2,1},{3,2},{4,3},{5,4},{6,5},{7,6},{8,7},{9,8},{10,9},{11,1... | collective-permute-start | bytes 196616 | tf_op jit(solution)/shard_map/ppermute | solution.py:21
  91.3 1.8 %copy-start.1 = (bf16[2304,256]{1,0:T(8,128)(2,1)S(1)}, bf16[2304,256]{1,0:T(8,128)(2,1)}, u32[]{:S(2)}) copy-start(bf16[2304,256]{1,0:T(8,128)(2,1)} %copy-done) | copy-start | bytes 3538948
  95.5 9.0 %copy-start.12 = (bf16[1,8,128,256]{3,2,1,0:T(8,128)(2,1)S(1)}, bf16[1,8,128,256]{3,2,1,0:T(8,128)(2,1)}, u32[]{:S(2)}) copy-start(bf16[1,8,128,256]{3,2,1,0:T(8,128)(2,1)} %get-tuple-element.16) | copy-start | bytes 1572868
  95.6 5.2 %collective-permute-start.6 = (f32[16,1152]{1,0:T(8,128)S(1)}, f32[16,1152]{1,0:T(8,128)S(1)}, u32[]{:S(2)}, u32[]{:S(2)}) collective-permute-start(f32[16,1152]{1,0:T(8,128)S(1)} %reduce_sum.49), channel_id=1, source_target_pairs={{0,128},{16,144},{32,160},{48,176},{64,192},{80,208},{96,224},{112... | collective-permute-start | bytes 221192 | tf_op jit(solution)/shard_map/ppermute | solution.py:29
  100.8 6.6 %collective-permute-start.7 = (f32[16,1152]{1,0:T(8,128)S(1)}, f32[16,1152]{1,0:T(8,128)S(1)}, u32[]{:S(2)}, u32[]{:S(2)}) collective-permute-start(f32[16,1152]{1,0:T(8,128)S(1)} %add.109), channel_id=1, source_target_pairs={{0,256},{16,272},{32,288},{48,304},{64,320},{80,336},{96,352},{112... | collective-permute-start | bytes 221192 | tf_op jit(solution)/shard_map/ppermute | solution.py:29
  104.6 11.6 %copy-start.11 = (bf16[1,8,128,256]{3,2,1,0:T(8,128)(2,1)S(1)}, bf16[1,8,128,256]{3,2,1,0:T(8,128)(2,1)}, u32[]{:S(2)}) copy-start(bf16[1,8,128,256]{3,2,1,0:T(8,128)(2,1)} %get-tuple-element.15) | copy-start | bytes 1572868
  107.4 10.9 %collective-permute-start.8 = (f32[16,1152]{1,0:T(8,128)S(1)}, f32[16,1152]{1,0:T(8,128)S(1)}, u32[]{:S(2)}, u32[]{:S(2)}) collective-permute-start(f32[16,1152]{1,0:T(8,128)S(1)} %add.110), channel_id=1, source_target_pairs={{0,32},{16,48},{32,0},{48,16},{64,96},{80,112},{96,64},{112,80},{1... | collective-permute-start | bytes 221192 | tf_op jit(solution)/shard_map/ppermute | solution.py:29
  116.2 13.7 %copy-start.10 = (bf16[1,8,128,256]{3,2,1,0:T(8,128)(2,1)S(1)}, bf16[1,8,128,256]{3,2,1,0:T(8,128)(2,1)}, u32[]{:S(2)}) copy-start(bf16[1,8,128,256]{3,2,1,0:T(8,128)(2,1)} %get-tuple-element.20) | copy-start | bytes 1572868
  118.3 15.0 %collective-permute-start.9 = (f32[16,1152]{1,0:T(8,128)S(1)}, f32[16,1152]{1,0:T(8,128)S(1)}, u32[]{:S(2)}, u32[]{:S(2)}) collective-permute-start(f32[16,1152]{1,0:T(8,128)S(1)} %add.111), channel_id=1, source_target_pairs={{0,64},{16,80},{32,96},{48,112},{64,0},{80,16},{96,32},{112,48},{1... | collective-permute-start | bytes 221192 | tf_op jit(solution)/shard_map/ppermute | solution.py:29
  133.4 8.8 %collective-permute-start.10 = (f32[16,1152]{1,0:T(8,128)S(1)}, f32[16,1152]{1,0:T(8,128)S(1)}, u32[]{:S(2)}, u32[]{:S(2)}) collective-permute-start(f32[16,1152]{1,0:T(8,128)S(1)} %add.112), channel_id=1, source_target_pairs={{0,16},{16,0},{32,48},{48,32},{64,80},{80,64},{96,112},{112,96},{1... | collective-permute-start | bytes 221192 | tf_op jit(solution)/shard_map/ppermute | solution.py:29

commit v6 on v5

--- a/solution.py
+++ b/solution.py
@@ -23,9 +23,10 @@
     return value
 
 
-def exchange(value, axis, bit):
+def exchange(value, axis, bit, mask=None):
     peers = lax.axis_size(axis)
-    pairs = [(i, i ^ (1 << bit)) for i in range(peers)]
+    mask = 1 << bit if mask is None else mask
+    pairs = [(i, i ^ mask) for i in range(peers)]
     return lax.ppermute(value, axis, pairs)
 
 
@@ -58,9 +59,9 @@
     return value
 
 
-def double_sum(value, axis, bits):
-    for bit in bits:
-        value = value + exchange(value, axis, bit)
+def double_sum(value, axis, masks):
+    for mask in masks:
+        value = value + exchange(value, axis, 0, mask)
     return value
 
 
@@ -138,7 +139,7 @@
     partial_value = jnp.stack(pieces, axis=1).reshape(out_chan, taps)
     core_sum = halve_sum(partial_value, "row", core_bit, 1)
     col_sum = scatter_sum(core_sum, "col")
-    row_piece = double_sum(col_sum, "row", [3, 4, 1, 2])
+    row_piece = double_sum(col_sum, "row", [1 << 3, 3 << 3, 1 << 1, 3 << 1])
     own_share = double_join(row_piece, "row", core_bit, 1)
     pixels = img_count * lax.axis_size("row") * tile_rows * lax.axis_size("col") * tile_cols
     weight_grad = (own_share * (1.0 / math.sqrt(pixels))).T.reshape(3, 3, in_chan, share)

time: 144 us -> 140 us (0.972)
  the two profiles are of different devices: /device:TPU:59 before, /device:TPU:65 now
where the time goes in v6:
time: 140 us; the launch traced here: 139 us
  starting transfers between devices  65.1 us (46%)
  waiting for transfers between devices  38.3 us (27%)
  local copies, waits for them, and re-layouts  14.5 us (10%)
  matrix products  13.3 us (10%)
  other arithmetic  6.32 us (5%)
    ppermute x7, starting transfers between devices, exchange(): return lax.ppermute(value, axis, pairs)  37.9 us
    ppermute x2, waiting for transfers between devices, padded_2(): before = lax.ppermute(last, axis, up)  22.3 us
    unnamed x34, local copies, waits for them, and re-layouts  8.78 us
    ppermute x2, starting transfers between devices, padded_2(): after = lax.ppermute(initial, axis, down)  8.6 us
    all_to_all x1, waiting for transfers between devices, gather_chunks(): return lax.all_to_all(copies, axis, 0, 0, tiled=False)  8.48 us
    all_to_all x1, starting transfers between devices, gather_chunks(): return lax.all_to_all(copies, axis, 0, 0, tiled=False)  7.64 us
    ppermute x7, waiting for transfers between devices, exchange(): return lax.ppermute(value, axis, pairs)  7.58 us
    ppermute x2, starting transfers between devices, padded_2(): before = lax.ppermute(last, axis, up)  6.18 us
  transfers between devices with their start and end apart: 13, of which 7 were waited for; matrix products, arithmetic and copies ran while one was open for 7% of the time, Pallas kernels for 0%

profile of v6, /device:TPU:65, one launch (start us, length us, event | category | flops | bytes accessed | tf_op | source)
XLA Modules:
  0.0 138.7 jit_solution(10021950739429073203)
XLA Ops:
  0.6 1.0 copy.14
  1.8 0.9 broadcast_in_dim.2
  2.6 7.6 %all-to-all-start = ((bf16[16,16,1152]{2,1,0:T(8,128)(2,1)}), bf16[16,16,1152]{2,1,0:T(8,128)(2,1)S(1)}, u32[]{:S(2)}, u32[]{:S(2)}) async-start(bf16[16,16,1152]{2,1,0:T(8,128)(2,1)} %broadcast_in_dim.2), calls=%async_computation | async-start | bytes 1179648 | tf_op jit(solution)/shard_map/all_to_all | solution.py:36
  10.3 3.1 %collective-permute-start = (bf16[1,1,128,256]{3,2,1,0:T(8,128)(2,1)S(1)}, bf16[1,1,128,256]{3,2,1,0:T(8,128)(2,1)S(1)}, u32[]{:S(2)}, u32[]{:S(2)}) collective-permute-start(bf16[1,1,128,256]{3,2,1,0:T(8,128)(2,1)S(1)} %get-tuple-element.33), channel_id=1, source_target_pairs={{0,1},{1,2},{2,3},{3,4},{4,5},{5,6},{6,7},{7,8},{8,9},{9,10},{10,1... | collective-permute-start | bytes 196616 | tf_op jit(solution)/shard_map/ppermute | solution.py:20
  13.4 4.3 %collective-permute-start.1 = (bf16[1,1,128,256]{3,2,1,0:T(8,128)(2,1)S(1)}, bf16[1,1,128,256]{3,2,1,0:T(8,128)(2,1)S(1)}, u32[]{:S(2)}, u32[]{:S(2)}) collective-permute-start(bf16[1,1,128,256]{3,2,1,0:T(8,128)(2,1)S(1)} %get-tuple-element.34), channel_id=1, source_target_pairs={{1,0},{2,1},{3,2},{4,3},{5,4},{6,5},{7,6},{8,7},{9,8},{10,9},{11,1... | collective-permute-start | bytes 196616 | tf_op jit(solution)/shard_map/ppermute | solution.py:21
  17.7 8.5 %all-to-all-done = bf16[16,16,1152]{2,1,0:T(8,128)(2,1)S(1)} async-done(((bf16[16,16,1152]{2,1,0:T(8,128)(2,1)}), bf16[16,16,1152]{2,1,0:T(8,128)(2,1)S(1)}, u32[]{:S(2)}, u32[]{:S(2)}) %all-to-all-start) | async-done | bytes 589856 | tf_op jit(solution)/shard_map/all_to_all | solution.py:36
  26.2 3.3 %collective-permute-start.2 = (bf16[16,16,1152]{2,1,0:T(8,128)(2,1)S(1)}, bf16[16,16,1152]{2,1,0:T(8,128)(2,1)S(1)}, u32[]{:S(2)}, u32[]{:S(2)}) collective-permute-start(bf16[16,16,1152]{2,1,0:T(8,128)(2,1)S(1)} %all-to-all-done), channel_id=1, source_target_pairs={{0,16},{16,0},{32,48},{48,32},{64,80},{80,64},{96,112},{112,96},{1... | collective-permute-start | bytes 1769480 | tf_op jit(solution)/shard_map/ppermute | solution.py:30
  29.8 1.1 pad_maximum_fusion.2
  30.8 1.6 %fusion.36 = (bf16[1,8,128,256]{3,2,1,0:T(8,128)(2,1)}, bf16[1,8,128,256]{3,2,1,0:T(8,128)(2,1)}, bf16[1,8,128,256]{3,2,1,0:T(8,128)(2,1)}, bf16[1,8,128,256]{3,...) fusion(bf16[1,10,130,256]{3,2,1,0:T(8,128)(2,1)S(1)} %select_maximum_fusion.2), kind=kLoop, calls=%fused_computation.91 | loop fusion | bytes 6291456 | tf_op jit(solution)/shard_map/slice | solution.py:93
  32.7 0.6 copy.15
  33.3 1.8 %fusion.27 = f32[1024,256]{1,0:T(8,128)S(1)} fusion(bf16[1024,256]{1,0:T(8,128)(2,1)} %bitcast.186, bf16[3,3,256,256]{3,2,1,0:T(8,128)(2,1)S(1)} %bitcast.159), kind=kOutput, calls=%fused_computation.78 | convolution fusion | flops 134217728 | bytes 1703936 | tf_op jit(solution)/shard_map/dot_general | solution.py:112
  35.4 0.7 copy-done.3
  36.7 0.7 copy-done.9
  37.5 0.3 convolution_add_fusion.10
  37.8 0.7 copy-done.7
  38.5 0.3 convolution_add_fusion.9
  38.8 0.7 copy-done.6
  39.9 0.3 fusion.3
  40.2 0.7 copy-done.8
  40.9 0.4 fusion.39
  41.3 0.4 multiply_reduce_fusion.1
  41.7 0.6 copy-done.13
  42.3 1.9 %fusion.32 = (f32[1024]{0:T(1024)S(1)}, f32[1024]{0:T(1024)S(1)}, f32[1024,256]{1,0:T(8,128)S(1)}, bf16[1024,256]{1,0:T(8,128)(2,1)}) fusion(f32[1024]{0:T(1024)S(1)} %add_rsqrt_fusion, f32[1024,256]{1,0:T(8,128)S(1)} %get-tuple-element.36, f32[1024]{0:T(1024)S(1)} %broadcast_multiply_fusion.2, f32[256]{0:T(256)S(1)} %copy-done.14, ...), kind=kLoop, calls=%fused_computation.88 | loop fusion | flops 4978688 | bytes 3163136 | tf_op jit(solution)/shard_map/reduce_sum | solution.py:86
  44.3 0.8 multiply_convert_fusion
  45.3 0.3 fusion.16
  45.7 0.3 fusion.15
  46.0 0.3 fusion.14
  46.4 0.3 fusion.13
  46.7 0.3 fusion.12
  47.1 0.3 fusion.11
  47.4 0.3 fusion.10
  47.8 0.3 fusion.9
  48.1 0.3 fusion.8
  48.5 1.2 fusion.34
  49.6 0.4 copy.21
  50.0 1.6 %copy.22 = f32[256,1152]{1,0:T(8,128)S(1)} copy(f32[256,1152]{0,1:T(8,128)} %get-tuple-element.13) | data formatting | bytes 2359296
  51.8 1.9 %collective-permute-start.5 = (f32[256,1152]{1,0:T(8,128)S(1)}, f32[256,1152]{1,0:T(8,128)S(1)}, u32[]{:S(2)}, u32[]{:S(2)}) collective-permute-start(f32[256,1152]{1,0:T(8,128)S(1)} %broadcast_select_fusion), channel_id=1, source_target_pairs={{0,16},{16,0},{32,48},{48,32},{64,80},{80,64},{96,112},{112,96},{1... | collective-permute-start | bytes 3538952 | tf_op jit(solution)/shard_map/ppermute | solution.py:30
  53.7 2.8 %collective-permute-done.5 = f32[256,1152]{1,0:T(8,128)S(1)} collective-permute-done((f32[256,1152]{1,0:T(8,128)S(1)}, f32[256,1152]{1,0:T(8,128)S(1)}, u32[]{:S(2)}, u32[]{:S(2)}) %collective-permute-start.5) | collective-permute-done | bytes 1179680 | tf_op jit(solution)/shard_map/ppermute | solution.py:30
  56.5 1.2 select_add_fusion
  57.7 4.8 %all-to-all-start.1 = ((f32[16,16,1152]{2,1,0:T(8,128)}), f32[16,16,1152]{2,1,0:T(8,128)S(1)}, u32[]{:S(2)}, u32[]{:S(2)}) async-start(f32[16,16,1152]{2,1,0:T(8,128)} %bitcast.179), calls=%async_computation.1 | async-start | bytes 2359296 | tf_op jit(solution)/shard_map/all_to_all | solution.py:42
  62.5 3.1 %collective-permute-start.3 = (bf16[1,1,128,256]{3,2,1,0:T(8,128)(2,1)S(1)}, bf16[1,1,128,256]{3,2,1,0:T(8,128)(2,1)S(1)}, u32[]{:S(2)}, u32[]{:S(2)}) collective-permute-start(bf16[1,1,128,256]{3,2,1,0:T(8,128)(2,1)S(1)} %get-tuple-element.29), channel_id=1, source_target_pairs={{0,1},{1,2},{2,3},{3,4},{4,5},{5,6},{6,7},{7,8},{8,9},{9,10},{10,1... | collective-permute-start | bytes 196616 | tf_op jit(solution)/shard_map/ppermute | solution.py:20
  65.6 4.3 %collective-permute-start.4 = (bf16[1,1,128,256]{3,2,1,0:T(8,128)(2,1)S(1)}, bf16[1,1,128,256]{3,2,1,0:T(8,128)(2,1)S(1)}, u32[]{:S(2)}, u32[]{:S(2)}) collective-permute-start(bf16[1,1,128,256]{3,2,1,0:T(8,128)(2,1)S(1)} %get-tuple-element.30), channel_id=1, source_target_pairs={{1,0},{2,1},{3,2},{4,3},{5,4},{6,5},{7,6},{8,7},{9,8},{10,9},{11,1... | collective-permute-start | bytes 196616 | tf_op jit(solution)/shard_map/ppermute | solution.py:21
  69.9 22.3 %collective-permute-done.3 = bf16[1,1,128,256]{3,2,1,0:T(8,128)(2,1)S(1)} collective-permute-done((bf16[1,1,128,256]{3,2,1,0:T(8,128)(2,1)S(1)}, bf16[1,1,128,256]{3,2,1,0:T(8,128)(2,1)S(1)}, u32[]{:S(2)}, u32[]{:S(2)}) %collective-permute-start.3) | collective-permute-done | bytes 65568 | tf_op jit(solution)/shard_map/ppermute | solution.py:20
  92.4 1.3 fusion.35
  93.7 0.6 copy-done.1
  94.3 0.3 fusion.26
  94.6 0.3 convolution_add_fusion.6
  94.9 0.3 convolution_add_fusion.5
  95.2 1.3 convolution_add_fusion.4
  96.7 3.2 %collective-permute-start.6 = (f32[16,1152]{1,0:T(8,128)S(1)}, f32[16,1152]{1,0:T(8,128)S(1)}, u32[]{:S(2)}, u32[]{:S(2)}) collective-permute-start(f32[16,1152]{1,0:T(8,128)S(1)} %reduce_sum.49), channel_id=1, source_target_pairs={{0,128},{16,144},{32,160},{48,176},{64,192},{80,208},{96,224},{112... | collective-permute-start | bytes 221192 | tf_op jit(solution)/shard_map/ppermute | solution.py:30
  99.9 1.6 %convolution_add_fusion.3 = f32[1024,256]{1,0:T(8,128)S(1)} fusion(f32[1024,256]{1,0:T(8,128)} %convolution_add_fusion.4, bf16[1024,256]{1,0:T(8,128)(2,1)S(1)} %multiply_convert_fusion, bf16[3,3,256,256]{3,2,1,0:T(8,128)(2,1)S(1)} %bitcast.172), kind=kOutput, calls=%fused_computation.12 | convolution fusion | flops 134479872 | bytes 2752512 | tf_op jit(solution)/shard_map/dot_general | solution.py:125
  101.5 0.4 collective-permute-done.6
  101.9 4.4 %collective-permute-start.7 = (f32[16,1152]{1,0:T(8,128)S(1)}, f32[16,1152]{1,0:T(8,128)S(1)}, u32[]{:S(2)}, u32[]{:S(2)}) collective-permute-start(f32[16,1152]{1,0:T(8,128)S(1)} %add.109), channel_id=1, source_target_pairs={{0,384},{16,400},{32,416},{48,432},{64,448},{80,464},{96,480},{112... | collective-permute-start | bytes 221192 | tf_op jit(solution)/shard_map/ppermute | solution.py:30
  106.3 0.3 convolution_add_fusion.2
  106.6 1.6 %collective-permute-done.7 = f32[16,1152]{1,0:T(8,128)S(1)} collective-permute-done((f32[16,1152]{1,0:T(8,128)S(1)}, f32[16,1152]{1,0:T(8,128)S(1)}, u32[]{:S(2)}, u32[]{:S(2)}) %collective-permute-start.7) | collective-permute-done | bytes 73760 | tf_op jit(solution)/shard_map/ppermute | solution.py:30
  108.2 8.8 %collective-permute-start.8 = (f32[16,1152]{1,0:T(8,128)S(1)}, f32[16,1152]{1,0:T(8,128)S(1)}, u32[]{:S(2)}, u32[]{:S(2)}) collective-permute-start(f32[16,1152]{1,0:T(8,128)S(1)} %add.110), channel_id=1, source_target_pairs={{0,32},{16,48},{32,0},{48,16},{64,96},{80,112},{96,64},{112,80},{1... | collective-permute-start | bytes 221192 | tf_op jit(solution)/shard_map/ppermute | solution.py:30
  117.1 0.3 convolution_add_fusion.1
  117.4 1.4 collective-permute-done.8
  118.8 8.2 %collective-permute-start.9 = (f32[16,1152]{1,0:T(8,128)S(1)}, f32[16,1152]{1,0:T(8,128)S(1)}, u32[]{:S(2)}, u32[]{:S(2)}) collective-permute-start(f32[16,1152]{1,0:T(8,128)S(1)} %add.111), channel_id=1, source_target_pairs={{0,96},{16,112},{32,64},{48,80},{64,32},{80,48},{96,0},{112,16},{1... | collective-permute-start | bytes 221192 | tf_op jit(solution)/shard_map/ppermute | solution.py:30
  127.0 0.3 fusion.30
  127.3 1.4 collective-permute-done.9
  128.7 8.0 %collective-permute-start.10 = (f32[16,1152]{1,0:T(8,128)S(1)}, f32[16,1152]{1,0:T(8,128)S(1)}, u32[]{:S(2)}, u32[]{:S(2)}) collective-permute-start(f32[16,1152]{1,0:T(8,128)S(1)} %add.112), channel_id=1, source_target_pairs={{0,16},{16,0},{32,48},{48,32},{64,80},{80,64},{96,112},{112,96},{1... | collective-permute-start | bytes 221192 | tf_op jit(solution)/shard_map/ppermute | solution.py:30
  136.8 1.1 fusion.6
  138.0 0.7 copy.19
  (52 shorter events, 2.6 us)
Async XLA Ops:
  0.6 9.7 %copy-start.2 = (bf16[1,8,128,256]{3,2,1,0:T(8,128)(2,1)S(1)}, bf16[1,8,128,256]{3,2,1,0:T(8,128)(2,1)}, u32[]{:S(2)}) copy-start(bf16[1,8,128,256]{3,2,1,0:T(8,128)(2,1)} %param.4) | copy-start | bytes 1572868
  2.6 23.6 %all-to-all-start = ((bf16[16,16,1152]{2,1,0:T(8,128)(2,1)}), bf16[16,16,1152]{2,1,0:T(8,128)(2,1)S(1)}, u32[]{:S(2)}, u32[]{:S(2)}) async-start(bf16[16,16,1152]{2,1,0:T(8,128)(2,1)} %broadcast_in_dim.2), calls=%async_computation | async-start | bytes 1179648 | tf_op jit(solution)/shard_map/all_to_all | solution.py:36
  10.3 19.2 %collective-permute-start = (bf16[1,1,128,256]{3,2,1,0:T(8,128)(2,1)S(1)}, bf16[1,1,128,256]{3,2,1,0:T(8,128)(2,1)S(1)}, u32[]{:S(2)}, u32[]{:S(2)}) collective-permute-start(bf16[1,1,128,256]{3,2,1,0:T(8,128)(2,1)S(1)} %get-tuple-element.33), channel_id=1, source_target_pairs={{0,1},{1,2},{2,3},{3,4},{4,5},{5,6},{6,7},{7,8},{8,9},{9,10},{10,1... | collective-permute-start | bytes 196616 | tf_op jit(solution)/shard_map/ppermute | solution.py:20
  13.4 16.2 %collective-permute-start.1 = (bf16[1,1,128,256]{3,2,1,0:T(8,128)(2,1)S(1)}, bf16[1,1,128,256]{3,2,1,0:T(8,128)(2,1)S(1)}, u32[]{:S(2)}, u32[]{:S(2)}) collective-permute-start(bf16[1,1,128,256]{3,2,1,0:T(8,128)(2,1)S(1)} %get-tuple-element.34), channel_id=1, source_target_pairs={{1,0},{2,1},{3,2},{4,3},{5,4},{6,5},{7,6},{8,7},{9,8},{10,9},{11,1... | collective-permute-start | bytes 196616 | tf_op jit(solution)/shard_map/ppermute | solution.py:21
  26.2 6.2 %collective-permute-start.2 = (bf16[16,16,1152]{2,1,0:T(8,128)(2,1)S(1)}, bf16[16,16,1152]{2,1,0:T(8,128)(2,1)S(1)}, u32[]{:S(2)}, u32[]{:S(2)}) collective-permute-start(bf16[16,16,1152]{2,1,0:T(8,128)(2,1)S(1)} %all-to-all-done), channel_id=1, source_target_pairs={{0,16},{16,0},{32,48},{48,32},{64,80},{80,64},{96,112},{112,96},{1... | collective-permute-start | bytes 1769480 | tf_op jit(solution)/shard_map/ppermute | solution.py:30
  33.3 6.9 %copy-start = (bf16[2304,256]{1,0:T(8,128)(2,1)}, bf16[2304,256]{1,0:T(8,128)(2,1)S(1)}, u32[]{:S(2)}) copy-start(bf16[2304,256]{1,0:T(8,128)(2,1)S(1)} %copy.15) | copy-start | bytes 3538948
  33.3 1.8 %copy-start.4 = (bf16[1,8,128,256]{3,2,1,0:T(8,128)(2,1)S(1)}, bf16[1,8,128,256]{3,2,1,0:T(8,128)(2,1)}, u32[]{:S(2)}) copy-start(bf16[1,8,128,256]{3,2,1,0:T(8,128)(2,1)} %get-tuple-element.23) | copy-start | bytes 1572868
  35.1 1.0 copy-start.3
  36.4 1.0 copy-start.9
  37.5 1.0 copy-start.7
  38.5 1.0 copy-start.6
  39.9 1.0 copy-start.8
  40.9 0.8 copy-start.14
  41.3 1.0 copy-start.13
  44.3 1.0 copy-start.5
  51.8 4.7 %collective-permute-start.5 = (f32[256,1152]{1,0:T(8,128)S(1)}, f32[256,1152]{1,0:T(8,128)S(1)}, u32[]{:S(2)}, u32[]{:S(2)}) collective-permute-start(f32[256,1152]{1,0:T(8,128)S(1)} %broadcast_select_fusion), channel_id=1, source_target_pairs={{0,16},{16,0},{32,48},{48,32},{64,80},{80,64},{96,112},{112,96},{1... | collective-permute-start | bytes 3538952 | tf_op jit(solution)/shard_map/ppermute | solution.py:30
  57.7 38.9 %all-to-all-start.1 = ((f32[16,16,1152]{2,1,0:T(8,128)}), f32[16,16,1152]{2,1,0:T(8,128)S(1)}, u32[]{:S(2)}, u32[]{:S(2)}) async-start(f32[16,16,1152]{2,1,0:T(8,128)} %bitcast.179), calls=%async_computation.1 | async-start | bytes 2359296 | tf_op jit(solution)/shard_map/all_to_all | solution.py:42
  62.5 29.7 %collective-permute-start.3 = (bf16[1,1,128,256]{3,2,1,0:T(8,128)(2,1)S(1)}, bf16[1,1,128,256]{3,2,1,0:T(8,128)(2,1)S(1)}, u32[]{:S(2)}, u32[]{:S(2)}) collective-permute-start(bf16[1,1,128,256]{3,2,1,0:T(8,128)(2,1)S(1)} %get-tuple-element.29), channel_id=1, source_target_pairs={{0,1},{1,2},{2,3},{3,4},{4,5},{5,6},{6,7},{7,8},{8,9},{9,10},{10,1... | collective-permute-start | bytes 196616 | tf_op jit(solution)/shard_map/ppermute | solution.py:20
  65.6 26.6 %collective-permute-start.4 = (bf16[1,1,128,256]{3,2,1,0:T(8,128)(2,1)S(1)}, bf16[1,1,128,256]{3,2,1,0:T(8,128)(2,1)S(1)}, u32[]{:S(2)}, u32[]{:S(2)}) collective-permute-start(bf16[1,1,128,256]{3,2,1,0:T(8,128)(2,1)S(1)} %get-tuple-element.30), channel_id=1, source_target_pairs={{1,0},{2,1},{3,2},{4,3},{5,4},{6,5},{7,6},{8,7},{9,8},{10,9},{11,1... | collective-permute-start | bytes 196616 | tf_op jit(solution)/shard_map/ppermute | solution.py:21
  92.4 1.8 %copy-start.1 = (bf16[2304,256]{1,0:T(8,128)(2,1)S(1)}, bf16[2304,256]{1,0:T(8,128)(2,1)}, u32[]{:S(2)}) copy-start(bf16[2304,256]{1,0:T(8,128)(2,1)} %copy-done) | copy-start | bytes 3538948
  96.7 9.6 %copy-start.12 = (bf16[1,8,128,256]{3,2,1,0:T(8,128)(2,1)S(1)}, bf16[1,8,128,256]{3,2,1,0:T(8,128)(2,1)}, u32[]{:S(2)}) copy-start(bf16[1,8,128,256]{3,2,1,0:T(8,128)(2,1)} %get-tuple-element.16) | copy-start | bytes 1572868
  96.7 5.2 %collective-permute-start.6 = (f32[16,1152]{1,0:T(8,128)S(1)}, f32[16,1152]{1,0:T(8,128)S(1)}, u32[]{:S(2)}, u32[]{:S(2)}) collective-permute-start(f32[16,1152]{1,0:T(8,128)S(1)} %reduce_sum.49), channel_id=1, source_target_pairs={{0,128},{16,144},{32,160},{48,176},{64,192},{80,208},{96,224},{112... | collective-permute-start | bytes 221192 | tf_op jit(solution)/shard_map/ppermute | solution.py:30
  101.9 6.3 %collective-permute-start.7 = (f32[16,1152]{1,0:T(8,128)S(1)}, f32[16,1152]{1,0:T(8,128)S(1)}, u32[]{:S(2)}, u32[]{:S(2)}) collective-permute-start(f32[16,1152]{1,0:T(8,128)S(1)} %add.109), channel_id=1, source_target_pairs={{0,384},{16,400},{32,416},{48,432},{64,448},{80,464},{96,480},{112... | collective-permute-start | bytes 221192 | tf_op jit(solution)/shard_map/ppermute | solution.py:30
  106.3 10.7 %copy-start.11 = (bf16[1,8,128,256]{3,2,1,0:T(8,128)(2,1)S(1)}, bf16[1,8,128,256]{3,2,1,0:T(8,128)(2,1)}, u32[]{:S(2)}) copy-start(bf16[1,8,128,256]{3,2,1,0:T(8,128)(2,1)} %get-tuple-element.15) | copy-start | bytes 1572868
  108.2 10.5 %collective-permute-start.8 = (f32[16,1152]{1,0:T(8,128)S(1)}, f32[16,1152]{1,0:T(8,128)S(1)}, u32[]{:S(2)}, u32[]{:S(2)}) collective-permute-start(f32[16,1152]{1,0:T(8,128)S(1)} %add.110), channel_id=1, source_target_pairs={{0,32},{16,48},{32,0},{48,16},{64,96},{80,112},{96,64},{112,80},{1... | collective-permute-start | bytes 221192 | tf_op jit(solution)/shard_map/ppermute | solution.py:30
  117.1 9.9 %copy-start.10 = (bf16[1,8,128,256]{3,2,1,0:T(8,128)(2,1)S(1)}, bf16[1,8,128,256]{3,2,1,0:T(8,128)(2,1)}, u32[]{:S(2)}) copy-start(bf16[1,8,128,256]{3,2,1,0:T(8,128)(2,1)} %get-tuple-element.20) | copy-start | bytes 1572868
  118.8 9.9 %collective-permute-start.9 = (f32[16,1152]{1,0:T(8,128)S(1)}, f32[16,1152]{1,0:T(8,128)S(1)}, u32[]{:S(2)}, u32[]{:S(2)}) collective-permute-start(f32[16,1152]{1,0:T(8,128)S(1)} %add.111), channel_id=1, source_target_pairs={{0,96},{16,112},{32,64},{48,80},{64,32},{80,48},{96,0},{112,16},{1... | collective-permute-start | bytes 221192 | tf_op jit(solution)/shard_map/ppermute | solution.py:30
  128.7 9.2 %collective-permute-start.10 = (f32[16,1152]{1,0:T(8,128)S(1)}, f32[16,1152]{1,0:T(8,128)S(1)}, u32[]{:S(2)}, u32[]{:S(2)}) collective-permute-start(f32[16,1152]{1,0:T(8,128)S(1)} %add.112), channel_id=1, source_target_pairs={{0,16},{16,0},{32,48},{48,32},{64,80},{80,64},{96,112},{112,96},{1... | collective-permute-start | bytes 221192 | tf_op jit(solution)/shard_map/ppermute | solution.py:30

commit v7 on v6

--- a/solution.py
+++ b/solution.py
@@ -117,6 +117,7 @@
     outputs, grad_pre = norm_act(conv_out, cotangent.reshape(-1, out_chan), norm_gain)
     grad_grid = grad_pre.reshape(img_count, tile_rows, tile_cols, out_chan)
     grad_rimmed = padded_2(grad_grid, (("col", 1),), 1)
+    grad_rimmed, grad_pre = lax.optimization_barrier((grad_rimmed, grad_pre))
     grad_pad = jnp.pad(grad_rimmed, ((0, 0), (0, 0), (1, 1), (0, 0)))
     grad_input = jnp.zeros((img_count * tile_rows * tile_cols, in_chan), jnp.float32)
     pieces = []

time: 140 us -> 146 us (1.043)
  starting transfers between devices: 65.1 us -> 68.5 us
  waiting for transfers between devices: 38.3 us -> 41.3 us
    all_to_all x1, waiting for transfers between devices: 0.01 us -> 24.2 us  [scatter_sum(): return lax.all_to_all(blocks, axis, 0, 0, tiled=False).sum(0)]
    ppermute x2, waiting for transfers between devices: 22.3 us -> 0.29 us  [padded_2(): before = lax.ppermute(last, axis, up)]
    all_to_all x1, starting transfers between devices: 4.75 us -> 6.67 us  [scatter_sum(): return lax.all_to_all(blocks, axis, 0, 0, tiled=False).sum(0)]
  transfers between devices with their start and end apart: 13 -> 13, of which waited for: 7 -> 9; matrix products, arithmetic and copies ran while one was open for 7% -> 7% of each run, Pallas kernels for 0% -> 0%
where the time goes in v7:
time: 146 us; the launch traced here: 145 us
  starting transfers between devices  68.5 us (47%)
  waiting for transfers between devices  41.3 us (28%)
  local copies, waits for them, and re-layouts  14.4 us (10%)
  matrix products  13.6 us (9%)
  other arithmetic  6.16 us (4%)
    ppermute x7, starting transfers between devices, exchange(): return lax.ppermute(value, axis, pairs)  39.4 us
    all_to_all x1, waiting for transfers between devices, scatter_sum(): return lax.all_to_all(blocks, axis, 0, 0, tiled=False).sum(0)  24.2 us
    ppermute x2, starting transfers between devices, padded_2(): after = lax.ppermute(initial, axis, down)  9.12 us
    all_to_all x1, waiting for transfers between devices, gather_chunks(): return lax.all_to_all(copies, axis, 0, 0, tiled=False)  8.48 us
    unnamed x34, local copies, waits for them, and re-layouts  8.34 us
    all_to_all x1, starting transfers between devices, gather_chunks(): return lax.all_to_all(copies, axis, 0, 0, tiled=False)  7.64 us
    ppermute x7, waiting for transfers between devices, exchange(): return lax.ppermute(value, axis, pairs)  7.31 us
    all_to_all x1, starting transfers between devices, scatter_sum(): return lax.all_to_all(blocks, axis, 0, 0, tiled=False).sum(0)  6.67 us
  transfers between devices with their start and end apart: 13, of which 9 were waited for; matrix products, arithmetic and copies ran while one was open for 7% of the time, Pallas kernels for 0%

profile of v7, /device:TPU:65, one launch (start us, length us, event | category | flops | bytes accessed | tf_op | source)
XLA Modules:
  0.0 145.1 jit_solution(12182967605817386130)
XLA Ops:
  0.6 1.0 copy.14
  1.8 0.9 broadcast_in_dim.2
  2.6 7.6 %all-to-all-start = ((bf16[16,16,1152]{2,1,0:T(8,128)(2,1)}), bf16[16,16,1152]{2,1,0:T(8,128)(2,1)S(1)}, u32[]{:S(2)}, u32[]{:S(2)}) async-start(bf16[16,16,1152]{2,1,0:T(8,128)(2,1)} %broadcast_in_dim.2), calls=%async_computation | async-start | bytes 1179648 | tf_op jit(solution)/shard_map/all_to_all | solution.py:36
  10.3 3.1 %collective-permute-start = (bf16[1,1,128,256]{3,2,1,0:T(8,128)(2,1)S(1)}, bf16[1,1,128,256]{3,2,1,0:T(8,128)(2,1)S(1)}, u32[]{:S(2)}, u32[]{:S(2)}) collective-permute-start(bf16[1,1,128,256]{3,2,1,0:T(8,128)(2,1)S(1)} %get-tuple-element.38), channel_id=1, source_target_pairs={{0,1},{1,2},{2,3},{3,4},{4,5},{5,6},{6,7},{7,8},{8,9},{9,10},{10,1... | collective-permute-start | bytes 196616 | tf_op jit(solution)/shard_map/ppermute | solution.py:20
  13.4 4.3 %collective-permute-start.1 = (bf16[1,1,128,256]{3,2,1,0:T(8,128)(2,1)S(1)}, bf16[1,1,128,256]{3,2,1,0:T(8,128)(2,1)S(1)}, u32[]{:S(2)}, u32[]{:S(2)}) collective-permute-start(bf16[1,1,128,256]{3,2,1,0:T(8,128)(2,1)S(1)} %get-tuple-element.39), channel_id=1, source_target_pairs={{1,0},{2,1},{3,2},{4,3},{5,4},{6,5},{7,6},{8,7},{9,8},{10,9},{11,1... | collective-permute-start | bytes 196616 | tf_op jit(solution)/shard_map/ppermute | solution.py:21
  17.7 8.5 %all-to-all-done = bf16[16,16,1152]{2,1,0:T(8,128)(2,1)S(1)} async-done(((bf16[16,16,1152]{2,1,0:T(8,128)(2,1)}), bf16[16,16,1152]{2,1,0:T(8,128)(2,1)S(1)}, u32[]{:S(2)}, u32[]{:S(2)}) %all-to-all-start) | async-done | bytes 589856 | tf_op jit(solution)/shard_map/all_to_all | solution.py:36
  26.2 3.3 %collective-permute-start.2 = (bf16[16,16,1152]{2,1,0:T(8,128)(2,1)S(1)}, bf16[16,16,1152]{2,1,0:T(8,128)(2,1)S(1)}, u32[]{:S(2)}, u32[]{:S(2)}) collective-permute-start(bf16[16,16,1152]{2,1,0:T(8,128)(2,1)S(1)} %all-to-all-done), channel_id=1, source_target_pairs={{0,16},{16,0},{32,48},{48,32},{64,80},{80,64},{96,112},{112,96},{1... | collective-permute-start | bytes 1769480 | tf_op jit(solution)/shard_map/ppermute | solution.py:30
  29.7 1.1 pad_maximum_fusion.1
  30.8 1.6 %fusion.37 = (bf16[1,8,128,256]{3,2,1,0:T(8,128)(2,1)}, bf16[1,8,128,256]{3,2,1,0:T(8,128)(2,1)}, bf16[1,8,128,256]{3,2,1,0:T(8,128)(2,1)}, bf16[1,8,128,256]{3,...) fusion(bf16[1,10,130,256]{3,2,1,0:T(8,128)(2,1)S(1)} %fusion.26), kind=kLoop, calls=%fused_computation.94 | loop fusion | bytes 6291456 | tf_op jit(solution)/shard_map/slice | solution.py:93
  32.7 0.6 copy.15
  33.3 1.8 %fusion.32 = f32[1024,256]{1,0:T(8,128)S(1)} fusion(bf16[1024,256]{1,0:T(8,128)(2,1)} %bitcast.182, bf16[3,3,256,256]{3,2,1,0:T(8,128)(2,1)S(1)} %bitcast.159), kind=kOutput, calls=%fused_computation.85 | convolution fusion | flops 134217728 | bytes 1703936 | tf_op jit(solution)/shard_map/dot_general | solution.py:112
  35.1 0.3 fusion.31
  35.4 0.7 copy-done.5
  36.7 0.7 copy-done.9
  37.8 0.7 copy-done.7
  38.5 0.3 convolution_add_fusion.10
  38.8 0.7 copy-done.6
  39.8 0.3 fusion.3
  40.2 0.7 copy-done.8
  40.9 0.4 fusion.40
  41.3 0.4 multiply_reduce_fusion.1
  41.7 0.6 copy-done.13
  42.3 1.9 %fusion.34 = (f32[1024]{0:T(1024)S(1)}, f32[1024]{0:T(1024)S(1)}, f32[1024,256]{1,0:T(8,128)S(1)}, bf16[1024,256]{1,0:T(8,128)(2,1)}) fusion(f32[1024]{0:T(1024)S(1)} %add_rsqrt_fusion, f32[1024,256]{1,0:T(8,128)S(1)} %get-tuple-element.41, f32[1024]{0:T(1024)S(1)} %broadcast_multiply_fusion.2, f32[256]{0:T(256)S(1)} %copy-done.14, ...), kind=kLoop, calls=%fused_computation.92 | loop fusion | flops 4978688 | bytes 3163136 | tf_op jit(solution)/shard_map/reduce_sum | solution.py:86
  44.2 0.8 multiply_convert_fusion
  45.1 2.6 %collective-permute-start.3 = (bf16[1,1,128,256]{3,2,1,0:T(8,128)(2,1)S(1)}, bf16[1,1,128,256]{3,2,1,0:T(8,128)(2,1)S(1)}, u32[]{:S(2)}, u32[]{:S(2)}) collective-permute-start(bf16[1,1,128,256]{3,2,1,0:T(8,128)(2,1)S(1)} %get-tuple-element.34), channel_id=1, source_target_pairs={{0,1},{1,2},{2,3},{3,4},{4,5},{5,6},{6,7},{7,8},{8,9},{9,10},{10,1... | collective-permute-start | bytes 196616 | tf_op jit(solution)/shard_map/ppermute | solution.py:20
  47.7 4.8 %collective-permute-start.4 = (bf16[1,1,128,256]{3,2,1,0:T(8,128)(2,1)S(1)}, bf16[1,1,128,256]{3,2,1,0:T(8,128)(2,1)S(1)}, u32[]{:S(2)}, u32[]{:S(2)}) collective-permute-start(bf16[1,1,128,256]{3,2,1,0:T(8,128)(2,1)S(1)} %get-tuple-element.35), channel_id=1, source_target_pairs={{1,0},{2,1},{3,2},{4,3},{5,4},{6,5},{7,6},{8,7},{9,8},{10,9},{11,1... | collective-permute-start | bytes 196616 | tf_op jit(solution)/shard_map/ppermute | solution.py:21
  52.8 1.0 collective-permute-done.4
  53.9 0.3 fusion.15
  54.3 0.3 fusion.14
  54.6 0.3 fusion.13
  55.0 0.3 fusion.12
  55.3 0.3 fusion.11
  55.7 0.3 fusion.10
  56.0 0.3 copy-done.3
  56.4 0.3 fusion.9
  56.7 0.3 fusion.8
  57.1 0.3 fusion.7
  57.4 1.2 fusion.36
  58.6 0.4 copy.21
  59.0 1.6 %copy.22 = f32[256,1152]{1,0:T(8,128)S(1)} copy(f32[256,1152]{0,1:T(8,128)} %get-tuple-element.17) | data formatting | bytes 2359296
  60.7 3.1 %collective-permute-start.5 = (f32[256,1152]{1,0:T(8,128)S(1)}, f32[256,1152]{1,0:T(8,128)S(1)}, u32[]{:S(2)}, u32[]{:S(2)}) collective-permute-start(f32[256,1152]{1,0:T(8,128)S(1)} %broadcast_select_fusion), channel_id=1, source_target_pairs={{0,16},{16,0},{32,48},{48,32},{64,80},{80,64},{96,112},{112,96},{1... | collective-permute-start | bytes 3538952 | tf_op jit(solution)/shard_map/ppermute | solution.py:30
  63.8 2.5 %collective-permute-done.5 = f32[256,1152]{1,0:T(8,128)S(1)} collective-permute-done((f32[256,1152]{1,0:T(8,128)S(1)}, f32[256,1152]{1,0:T(8,128)S(1)}, u32[]{:S(2)}, u32[]{:S(2)}) %collective-permute-start.5) | collective-permute-done | bytes 1179680 | tf_op jit(solution)/shard_map/ppermute | solution.py:30
  66.3 1.2 select_add_fusion
  67.5 6.7 %all-to-all-start.1 = ((f32[16,16,1152]{2,1,0:T(8,128)}), f32[16,16,1152]{2,1,0:T(8,128)S(1)}, u32[]{:S(2)}, u32[]{:S(2)}) async-start(f32[16,16,1152]{2,1,0:T(8,128)} %bitcast.179), calls=%async_computation.1 | async-start | bytes 2359296 | tf_op jit(solution)/shard_map/all_to_all | solution.py:42
  74.1 1.7 %pad_slice_fusion = (bf16[1,8,128,256]{3,2,1,0:T(8,128)(2,1)S(1)}, bf16[1,8,128,256]{3,2,1,0:T(8,128)(2,1)S(1)}, bf16[1,8,128,256]{3,2,1,0:T(8,128)(2,1)S(1)}, b...) fusion(bf16[1,10,128,256]{3,2,1,0:T(8,128)(2,1)S(1)} %pad_maxim, ...), kind=kLoop, calls=%fused_computation.64 | loop fusion | bytes 6946816 | tf_op jit(solution)/shard_map/slice | solution.py:93
  75.8 0.3 fusion.29
  76.2 0.3 convolution_add_fusion.7
  76.5 0.3 convolution_add_fusion.6
  76.8 1.3 convolution_add_fusion.5
  78.2 24.2 %all-to-all-done.1 = f32[16,16,1152]{2,1,0:T(8,128)S(1)} async-done(((f32[16,16,1152]{2,1,0:T(8,128)}), f32[16,16,1152]{2,1,0:T(8,128)S(1)}, u32[]{:S(2)}, u32[]{:S(2)}) %all-to-all-start.1) | async-done | bytes 1179680 | tf_op jit(solution)/shard_map/all_to_all | solution.py:42
  102.4 3.1 %collective-permute-start.6 = (f32[16,1152]{1,0:T(8,128)S(1)}, f32[16,1152]{1,0:T(8,128)S(1)}, u32[]{:S(2)}, u32[]{:S(2)}) collective-permute-start(f32[16,1152]{1,0:T(8,128)S(1)} %reduce_sum.49), channel_id=1, source_target_pairs={{0,128},{16,144},{32,160},{48,176},{64,192},{80,208},{96,224},{112... | collective-permute-start | bytes 221192 | tf_op jit(solution)/shard_map/ppermute | solution.py:30
  105.6 1.8 %convolution_add_fusion.4 = f32[1024,256]{1,0:T(8,128)S(1)} fusion(f32[1024,256]{1,0:T(8,128)} %convolution_add_fusion.5, bf16[1024,256]{1,0:T(8,128)(2,1)} %bitcast.203, bf16[3,3,256,256]{3,2,1,0:T(8,128)(2,1)S(1)} %bitcast.172), kind=kOutput, calls=%fused_computation.12 | convolution fusion | flops 134479872 | bytes 2752512 | tf_op jit(solution)/shard_map/dot_general | solution.py:126
  107.6 4.4 %collective-permute-start.7 = (f32[16,1152]{1,0:T(8,128)S(1)}, f32[16,1152]{1,0:T(8,128)S(1)}, u32[]{:S(2)}, u32[]{:S(2)}) collective-permute-start(f32[16,1152]{1,0:T(8,128)S(1)} %add.109), channel_id=1, source_target_pairs={{0,384},{16,400},{32,416},{48,432},{64,448},{80,464},{96,480},{112... | collective-permute-start | bytes 221192 | tf_op jit(solution)/shard_map/ppermute | solution.py:30
  112.0 0.3 convolution_add_fusion.3
  112.3 1.6 %collective-permute-done.7 = f32[16,1152]{1,0:T(8,128)S(1)} collective-permute-done((f32[16,1152]{1,0:T(8,128)S(1)}, f32[16,1152]{1,0:T(8,128)S(1)}, u32[]{:S(2)}, u32[]{:S(2)}) %collective-permute-start.7) | collective-permute-done | bytes 73760 | tf_op jit(solution)/shard_map/ppermute | solution.py:30
  113.9 8.8 %collective-permute-start.8 = (f32[16,1152]{1,0:T(8,128)S(1)}, f32[16,1152]{1,0:T(8,128)S(1)}, u32[]{:S(2)}, u32[]{:S(2)}) collective-permute-start(f32[16,1152]{1,0:T(8,128)S(1)} %add.110), channel_id=1, source_target_pairs={{0,32},{16,48},{32,0},{48,16},{64,96},{80,112},{96,64},{112,80},{1... | collective-permute-start | bytes 221192 | tf_op jit(solution)/shard_map/ppermute | solution.py:30
  122.7 0.3 convolution_add_fusion.2
  123.1 1.4 collective-permute-done.8
  124.5 8.2 %collective-permute-start.9 = (f32[16,1152]{1,0:T(8,128)S(1)}, f32[16,1152]{1,0:T(8,128)S(1)}, u32[]{:S(2)}, u32[]{:S(2)}) collective-permute-start(f32[16,1152]{1,0:T(8,128)S(1)} %add.111), channel_id=1, source_target_pairs={{0,96},{16,112},{32,64},{48,80},{64,32},{80,48},{96,0},{112,16},{1... | collective-permute-start | bytes 221192 | tf_op jit(solution)/shard_map/ppermute | solution.py:30
  132.7 0.3 convolution_add_fusion.1
  133.0 1.7 %collective-permute-done.9 = f32[16,1152]{1,0:T(8,128)S(1)} collective-permute-done((f32[16,1152]{1,0:T(8,128)S(1)}, f32[16,1152]{1,0:T(8,128)S(1)}, u32[]{:S(2)}, u32[]{:S(2)}) %collective-permute-start.9) | collective-permute-done | bytes 73760 | tf_op jit(solution)/shard_map/ppermute | solution.py:30
  134.7 8.4 %collective-permute-start.10 = (f32[16,1152]{1,0:T(8,128)S(1)}, f32[16,1152]{1,0:T(8,128)S(1)}, u32[]{:S(2)}, u32[]{:S(2)}) collective-permute-start(f32[16,1152]{1,0:T(8,128)S(1)} %add.112), channel_id=1, source_target_pairs={{0,16},{16,0},{32,48},{48,32},{64,80},{80,64},{96,112},{112,96},{1... | collective-permute-start | bytes 221192 | tf_op jit(solution)/shard_map/ppermute | solution.py:30
  143.2 1.1 fusion.5
  144.4 0.7 copy.19
  (51 shorter events, 2.7 us)
Async XLA Ops:
  0.6 9.6 %copy-start.2 = (bf16[1,8,128,256]{3,2,1,0:T(8,128)(2,1)S(1)}, bf16[1,8,128,256]{3,2,1,0:T(8,128)(2,1)}, u32[]{:S(2)}) copy-start(bf16[1,8,128,256]{3,2,1,0:T(8,128)(2,1)} %param.4) | copy-start | bytes 1572868
  2.6 23.6 %all-to-all-start = ((bf16[16,16,1152]{2,1,0:T(8,128)(2,1)}), bf16[16,16,1152]{2,1,0:T(8,128)(2,1)S(1)}, u32[]{:S(2)}, u32[]{:S(2)}) async-start(bf16[16,16,1152]{2,1,0:T(8,128)(2,1)} %broadcast_in_dim.2), calls=%async_computation | async-start | bytes 1179648 | tf_op jit(solution)/shard_map/all_to_all | solution.py:36
  10.3 19.2 %collective-permute-start = (bf16[1,1,128,256]{3,2,1,0:T(8,128)(2,1)S(1)}, bf16[1,1,128,256]{3,2,1,0:T(8,128)(2,1)S(1)}, u32[]{:S(2)}, u32[]{:S(2)}) collective-permute-start(bf16[1,1,128,256]{3,2,1,0:T(8,128)(2,1)S(1)} %get-tuple-element.38), channel_id=1, source_target_pairs={{0,1},{1,2},{2,3},{3,4},{4,5},{5,6},{6,7},{7,8},{8,9},{9,10},{10,1... | collective-permute-start | bytes 196616 | tf_op jit(solution)/shard_map/ppermute | solution.py:20
  13.4 16.2 %collective-permute-start.1 = (bf16[1,1,128,256]{3,2,1,0:T(8,128)(2,1)S(1)}, bf16[1,1,128,256]{3,2,1,0:T(8,128)(2,1)S(1)}, u32[]{:S(2)}, u32[]{:S(2)}) collective-permute-start(bf16[1,1,128,256]{3,2,1,0:T(8,128)(2,1)S(1)} %get-tuple-element.39), channel_id=1, source_target_pairs={{1,0},{2,1},{3,2},{4,3},{5,4},{6,5},{7,6},{8,7},{9,8},{10,9},{11,1... | collective-permute-start | bytes 196616 | tf_op jit(solution)/shard_map/ppermute | solution.py:21
  26.2 6.2 %collective-permute-start.2 = (bf16[16,16,1152]{2,1,0:T(8,128)(2,1)S(1)}, bf16[16,16,1152]{2,1,0:T(8,128)(2,1)S(1)}, u32[]{:S(2)}, u32[]{:S(2)}) collective-permute-start(bf16[16,16,1152]{2,1,0:T(8,128)(2,1)S(1)} %all-to-all-done), channel_id=1, source_target_pairs={{0,16},{16,0},{32,48},{48,32},{64,80},{80,64},{96,112},{112,96},{1... | collective-permute-start | bytes 1769480 | tf_op jit(solution)/shard_map/ppermute | solution.py:30
  33.3 6.9 %copy-start = (bf16[2304,256]{1,0:T(8,128)(2,1)}, bf16[2304,256]{1,0:T(8,128)(2,1)S(1)}, u32[]{:S(2)}) copy-start(bf16[2304,256]{1,0:T(8,128)(2,1)S(1)} %copy.15) | copy-start | bytes 3538948
  33.3 1.8 %copy-start.4 = (bf16[1,8,128,256]{3,2,1,0:T(8,128)(2,1)S(1)}, bf16[1,8,128,256]{3,2,1,0:T(8,128)(2,1)}, u32[]{:S(2)}) copy-start(bf16[1,8,128,256]{3,2,1,0:T(8,128)(2,1)} %get-tuple-element.21) | copy-start | bytes 1572868
  35.1 1.0 copy-start.5
  36.4 1.0 copy-start.9
  37.5 1.0 copy-start.7
  38.5 1.0 copy-start.6
  39.8 1.0 copy-start.8
  40.9 0.8 copy-start.14
  41.3 1.0 copy-start.13
  45.1 7.7 %collective-permute-start.3 = (bf16[1,1,128,256]{3,2,1,0:T(8,128)(2,1)S(1)}, bf16[1,1,128,256]{3,2,1,0:T(8,128)(2,1)S(1)}, u32[]{:S(2)}, u32[]{:S(2)}) collective-permute-start(bf16[1,1,128,256]{3,2,1,0:T(8,128)(2,1)S(1)} %get-tuple-element.34), channel_id=1, source_target_pairs={{0,1},{1,2},{2,3},{3,4},{4,5},{5,6},{6,7},{7,8},{8,9},{9,10},{10,1... | collective-permute-start | bytes 196616 | tf_op jit(solution)/shard_map/ppermute | solution.py:20
  47.7 6.1 %collective-permute-start.4 = (bf16[1,1,128,256]{3,2,1,0:T(8,128)(2,1)S(1)}, bf16[1,1,128,256]{3,2,1,0:T(8,128)(2,1)S(1)}, u32[]{:S(2)}, u32[]{:S(2)}) collective-permute-start(bf16[1,1,128,256]{3,2,1,0:T(8,128)(2,1)S(1)} %get-tuple-element.35), channel_id=1, source_target_pairs={{1,0},{2,1},{3,2},{4,3},{5,4},{6,5},{7,6},{8,7},{9,8},{10,9},{11,1... | collective-permute-start | bytes 196616 | tf_op jit(solution)/shard_map/ppermute | solution.py:21
  55.3 1.0 copy-start.3
  60.7 5.5 %collective-permute-start.5 = (f32[256,1152]{1,0:T(8,128)S(1)}, f32[256,1152]{1,0:T(8,128)S(1)}, u32[]{:S(2)}, u32[]{:S(2)}) collective-permute-start(f32[256,1152]{1,0:T(8,128)S(1)} %broadcast_select_fusion), channel_id=1, source_target_pairs={{0,16},{16,0},{32,48},{48,32},{64,80},{80,64},{96,112},{112,96},{1... | collective-permute-start | bytes 3538952 | tf_op jit(solution)/shard_map/ppermute | solution.py:30
  67.5 34.9 %all-to-all-start.1 = ((f32[16,16,1152]{2,1,0:T(8,128)}), f32[16,16,1152]{2,1,0:T(8,128)S(1)}, u32[]{:S(2)}, u32[]{:S(2)}) async-start(f32[16,16,1152]{2,1,0:T(8,128)} %bitcast.179), calls=%async_computation.1 | async-start | bytes 2359296 | tf_op jit(solution)/shard_map/all_to_all | solution.py:42
  74.1 1.7 %copy-start.1 = (bf16[2304,256]{1,0:T(8,128)(2,1)S(1)}, bf16[2304,256]{1,0:T(8,128)(2,1)}, u32[]{:S(2)}) copy-start(bf16[2304,256]{1,0:T(8,128)(2,1)} %copy-done) | copy-start | bytes 3538948
  102.4 5.1 %collective-permute-start.6 = (f32[16,1152]{1,0:T(8,128)S(1)}, f32[16,1152]{1,0:T(8,128)S(1)}, u32[]{:S(2)}, u32[]{:S(2)}) collective-permute-start(f32[16,1152]{1,0:T(8,128)S(1)} %reduce_sum.49), channel_id=1, source_target_pairs={{0,128},{16,144},{32,160},{48,176},{64,192},{80,208},{96,224},{112... | collective-permute-start | bytes 221192 | tf_op jit(solution)/shard_map/ppermute | solution.py:30
  105.6 6.4 %copy-start.12 = (bf16[1,8,128,256]{3,2,1,0:T(8,128)(2,1)S(1)}, bf16[1,8,128,256]{3,2,1,0:T(8,128)(2,1)}, u32[]{:S(2)}) copy-start(bf16[1,8,128,256]{3,2,1,0:T(8,128)(2,1)} %get-tuple-element.28) | copy-start | bytes 1572868
  107.6 6.3 %collective-permute-start.7 = (f32[16,1152]{1,0:T(8,128)S(1)}, f32[16,1152]{1,0:T(8,128)S(1)}, u32[]{:S(2)}, u32[]{:S(2)}) collective-permute-start(f32[16,1152]{1,0:T(8,128)S(1)} %add.109), channel_id=1, source_target_pairs={{0,384},{16,400},{32,416},{48,432},{64,448},{80,464},{96,480},{112... | collective-permute-start | bytes 221192 | tf_op jit(solution)/shard_map/ppermute | solution.py:30
  112.0 10.7 %copy-start.11 = (bf16[1,8,128,256]{3,2,1,0:T(8,128)(2,1)S(1)}, bf16[1,8,128,256]{3,2,1,0:T(8,128)(2,1)}, u32[]{:S(2)}) copy-start(bf16[1,8,128,256]{3,2,1,0:T(8,128)(2,1)} %get-tuple-element.29) | copy-start | bytes 1572868
  113.9 10.6 %collective-permute-start.8 = (f32[16,1152]{1,0:T(8,128)S(1)}, f32[16,1152]{1,0:T(8,128)S(1)}, u32[]{:S(2)}, u32[]{:S(2)}) collective-permute-start(f32[16,1152]{1,0:T(8,128)S(1)} %add.110), channel_id=1, source_target_pairs={{0,32},{16,48},{32,0},{48,16},{64,96},{80,112},{96,64},{112,80},{1... | collective-permute-start | bytes 221192 | tf_op jit(solution)/shard_map/ppermute | solution.py:30
  122.7 10.0 %copy-start.10 = (bf16[1,8,128,256]{3,2,1,0:T(8,128)(2,1)S(1)}, bf16[1,8,128,256]{3,2,1,0:T(8,128)(2,1)}, u32[]{:S(2)}) copy-start(bf16[1,8,128,256]{3,2,1,0:T(8,128)(2,1)} %get-tuple-element.30) | copy-start | bytes 1572868
  124.5 10.2 %collective-permute-start.9 = (f32[16,1152]{1,0:T(8,128)S(1)}, f32[16,1152]{1,0:T(8,128)S(1)}, u32[]{:S(2)}, u32[]{:S(2)}) collective-permute-start(f32[16,1152]{1,0:T(8,128)S(1)} %add.111), channel_id=1, source_target_pairs={{0,96},{16,112},{32,64},{48,80},{64,32},{80,48},{96,0},{112,16},{1... | collective-permute-start | bytes 221192 | tf_op jit(solution)/shard_map/ppermute | solution.py:30
  134.7 9.6 %collective-permute-start.10 = (f32[16,1152]{1,0:T(8,128)S(1)}, f32[16,1152]{1,0:T(8,128)S(1)}, u32[]{:S(2)}, u32[]{:S(2)}) collective-permute-start(f32[16,1152]{1,0:T(8,128)S(1)} %add.112), channel_id=1, source_target_pairs={{0,16},{16,0},{32,48},{48,32},{64,80},{80,64},{96,112},{112,96},{1... | collective-permute-start | bytes 221192 | tf_op jit(solution)/shard_map/ppermute | solution.py:30

commit v8 on v6

--- a/solution.py
+++ b/solution.py
@@ -138,9 +138,14 @@
             )
     partial_value = jnp.stack(pieces, axis=1).reshape(out_chan, taps)
     core_sum = halve_sum(partial_value, "row", core_bit, 1)
-    col_sum = scatter_sum(core_sum, "col")
-    row_piece = double_sum(col_sum, "row", [1 << 3, 3 << 3, 1 << 1, 3 << 1])
-    own_share = double_join(row_piece, "row", core_bit, 1)
+    ring_x = lax.axis_index("row") >> 3
+    x_upper = ((ring_x ^ (ring_x >> 1)) & 1) == 1
+    keep, send = split_pair(core_sum, x_upper, 1)
+    x_sum = keep + exchange(send, "row", 0, 1 << 3)
+    col_sum = scatter_sum(x_sum, "col")
+    row_piece = double_sum(col_sum, "row", [3 << 3, 1 << 1, 3 << 1])
+    x_joined = join_pair(row_piece, exchange(row_piece, "row", 0, 1 << 3), x_upper, 1)
+    own_share = double_join(x_joined, "row", core_bit, 1)
     pixels = img_count * lax.axis_size("row") * tile_rows * lax.axis_size("col") * tile_cols
     weight_grad = (own_share * (1.0 / math.sqrt(pixels))).T.reshape(3, 3, in_chan, share)
     features = outputs.reshape(img_count, tile_rows, tile_cols, out_chan)

time: 140 us -> 148 us (1.057)
  waiting for transfers between devices: 38.3 us -> 42.4 us
  other arithmetic: 6.32 us -> 9.91 us
  matrix products: 13.3 us -> 11.1 us
  local copies, waits for them, and re-layouts: 14.5 us -> 16.1 us
    ppermute x7 -> x8, waiting for transfers between devices: 7.58 us -> 22.5 us  [exchange(): return lax.ppermute(value, axis, pairs)]
    ppermute x2, waiting for transfers between devices: 22.3 us -> 11.3 us  [padded_2(): before = lax.ppermute(last, axis, up)]
    dot_general x9, matrix products: 5.98 us -> 3.77 us  [on_device(): lax.dot_general(window(grad_pad, 2 - tap_row, 2 - tap_col, tile_rows, til...]
    ppermute x7 -> x8, starting transfers between devices: 37.9 us -> 38.7 us  [exchange(): return lax.ppermute(value, axis, pairs)]
    unnamed x34 -> x38, local copies, waits for them, and re-layouts: 8.78 us -> 8.87 us
  transfers between devices with their start and end apart: 13 -> 14, of which waited for: 7 -> 8; matrix products, arithmetic and copies ran while one was open for 7% -> 6% of each run, Pallas kernels for 0% -> 0%
where the time goes in v8:
time: 148 us; the launch traced here: 147 us
  starting transfers between devices  65.8 us (44%)
  waiting for transfers between devices  42.4 us (29%)
  local copies, waits for them, and re-layouts  16.1 us (11%)
  matrix products  11.1 us (8%)
  other arithmetic  9.91 us (7%)
    ppermute x8, starting transfers between devices, exchange(): return lax.ppermute(value, axis, pairs)  38.7 us
    ppermute x8, waiting for transfers between devices, exchange(): return lax.ppermute(value, axis, pairs)  22.5 us
    ppermute x2, waiting for transfers between devices, padded_2(): before = lax.ppermute(last, axis, up)  11.3 us
    unnamed x38, local copies, waits for them, and re-layouts  8.87 us
    ppermute x2, starting transfers between devices, padded_2(): after = lax.ppermute(initial, axis, down)  8.6 us
    all_to_all x1, waiting for transfers between devices, gather_chunks(): return lax.all_to_all(copies, axis, 0, 0, tiled=False)  8.48 us
    all_to_all x1, starting transfers between devices, gather_chunks(): return lax.all_to_all(copies, axis, 0, 0, tiled=False)  7.64 us
    ppermute x2, starting transfers between devices, padded_2(): before = lax.ppermute(last, axis, up)  6.18 us
  transfers between devices with their start and end apart: 14, of which 8 were waited for; matrix products, arithmetic and copies ran while one was open for 6% of the time, Pallas kernels for 0%

profile of v8, /device:TPU:65, one launch (start us, length us, event | category | flops | bytes accessed | tf_op | source)
XLA Modules:
  0.0 146.6 jit_solution(1671387854012633523)
XLA Ops:
  0.6 1.0 copy.20
  1.8 0.9 broadcast_in_dim.2
  2.6 7.6 %all-to-all-start = ((bf16[16,16,1152]{2,1,0:T(8,128)(2,1)}), bf16[16,16,1152]{2,1,0:T(8,128)(2,1)S(1)}, u32[]{:S(2)}, u32[]{:S(2)}) async-start(bf16[16,16,1152]{2,1,0:T(8,128)(2,1)} %broadcast_in_dim.2), calls=%async_computation | async-start | bytes 1179648 | tf_op jit(solution)/shard_map/all_to_all | solution.py:36
  10.3 3.1 %collective-permute-start = (bf16[1,1,128,256]{3,2,1,0:T(8,128)(2,1)S(1)}, bf16[1,1,128,256]{3,2,1,0:T(8,128)(2,1)S(1)}, u32[]{:S(2)}, u32[]{:S(2)}) collective-permute-start(bf16[1,1,128,256]{3,2,1,0:T(8,128)(2,1)S(1)} %get-tuple-element.36), channel_id=1, source_target_pairs={{0,1},{1,2},{2,3},{3,4},{4,5},{5,6},{6,7},{7,8},{8,9},{9,10},{10,1... | collective-permute-start | bytes 196616 | tf_op jit(solution)/shard_map/ppermute | solution.py:20
  13.4 4.3 %collective-permute-start.1 = (bf16[1,1,128,256]{3,2,1,0:T(8,128)(2,1)S(1)}, bf16[1,1,128,256]{3,2,1,0:T(8,128)(2,1)S(1)}, u32[]{:S(2)}, u32[]{:S(2)}) collective-permute-start(bf16[1,1,128,256]{3,2,1,0:T(8,128)(2,1)S(1)} %get-tuple-element.37), channel_id=1, source_target_pairs={{1,0},{2,1},{3,2},{4,3},{5,4},{6,5},{7,6},{8,7},{9,8},{10,9},{11,1... | collective-permute-start | bytes 196616 | tf_op jit(solution)/shard_map/ppermute | solution.py:21
  17.7 8.5 %all-to-all-done = bf16[16,16,1152]{2,1,0:T(8,128)(2,1)S(1)} async-done(((bf16[16,16,1152]{2,1,0:T(8,128)(2,1)}), bf16[16,16,1152]{2,1,0:T(8,128)(2,1)S(1)}, u32[]{:S(2)}, u32[]{:S(2)}) %all-to-all-start) | async-done | bytes 589856 | tf_op jit(solution)/shard_map/all_to_all | solution.py:36
  26.2 3.3 %collective-permute-start.2 = (bf16[16,16,1152]{2,1,0:T(8,128)(2,1)S(1)}, bf16[16,16,1152]{2,1,0:T(8,128)(2,1)S(1)}, u32[]{:S(2)}, u32[]{:S(2)}) collective-permute-start(bf16[16,16,1152]{2,1,0:T(8,128)(2,1)S(1)} %all-to-all-done), channel_id=1, source_target_pairs={{0,16},{16,0},{32,48},{48,32},{64,80},{80,64},{96,112},{112,96},{1... | collective-permute-start | bytes 1769480 | tf_op jit(solution)/shard_map/ppermute | solution.py:30
  29.8 1.0 pad_maximum_fusion.2
  30.8 1.6 %fusion.36 = (bf16[1,8,128,256]{3,2,1,0:T(8,128)(2,1)}, bf16[1,8,128,256]{3,2,1,0:T(8,128)(2,1)}, bf16[1,8,128,256]{3,2,1,0:T(8,128)(2,1)}, bf16[1,8,128,256]{3,...) fusion(bf16[1,10,130,256]{3,2,1,0:T(8,128)(2,1)S(1)} %select_maximum_fusion.2), kind=kLoop, calls=%fused_computation.94 | loop fusion | bytes 6291456 | tf_op jit(solution)/shard_map/slice | solution.py:93
  32.7 0.6 copy.21
  33.3 1.8 %fusion.27 = f32[1024,256]{1,0:T(8,128)S(1)} fusion(bf16[1024,256]{1,0:T(8,128)(2,1)} %bitcast.185, bf16[3,3,256,256]{3,2,1,0:T(8,128)(2,1)S(1)} %bitcast.159), kind=kOutput, calls=%fused_computation.80 | convolution fusion | flops 134217728 | bytes 1703936 | tf_op jit(solution)/shard_map/dot_general | solution.py:112
  35.4 0.7 copy-done.4
  36.7 0.7 copy-done.10
  37.8 0.7 copy-done.8
  38.8 0.7 copy-done.7
  40.2 0.7 copy-done.9
  40.9 0.4 fusion.39
  41.3 0.4 multiply_reduce_fusion.1
  41.7 0.6 copy-done.15
  42.3 1.9 %fusion.32 = (f32[1024]{0:T(1024)S(1)}, f32[1024]{0:T(1024)S(1)}, f32[1024,256]{1,0:T(8,128)S(1)}, bf16[1024,256]{1,0:T(8,128)(2,1)}) fusion(f32[1024]{0:T(1024)S(1)} %add_rsqrt_fusion, f32[1024,256]{1,0:T(8,128)S(1)} %get-tuple-element.39, f32[1024]{0:T(1024)S(1)} %broadcast_multiply_fusion.2, f32[256]{0:T(256)S(1)} %copy-done.16, ...), kind=kLoop, calls=%fused_computation.91 | loop fusion | flops 4978688 | bytes 3163136 | tf_op jit(solution)/shard_map/reduce_sum | solution.py:86
  44.2 0.8 multiply_convert_fusion
  45.3 0.3 fusion.16
  45.6 0.3 fusion.15
  46.0 0.3 fusion.14
  46.4 0.3 fusion.13
  46.7 0.3 fusion.12
  47.1 0.3 fusion.11
  47.4 0.3 fusion.10
  47.8 0.3 fusion.9
  48.1 0.3 fusion.8
  48.5 1.2 fusion.34
  49.6 0.4 copy.29
  50.0 1.6 %copy.30 = f32[256,1152]{1,0:T(8,128)S(1)} copy(f32[256,1152]{0,1:T(8,128)} %get-tuple-element.16) | data formatting | bytes 2359296
  51.7 1.3 broadcast_select_fusion
  53.1 1.9 %collective-permute-start.5 = (f32[256,1152]{1,0:T(8,128)}, f32[256,1152]{1,0:T(8,128)}, u32[]{:S(2)}, u32[]{:S(2)}) collective-permute-start(f32[256,1152]{1,0:T(8,128)} %broadcast_select_fusion), channel_id=1, source_target_pairs={{0,16},{16,0},{32,48},{48,32},{64,80},{80,64},{96,112},{112,96},{1... | collective-permute-start | bytes 3538952 | tf_op jit(solution)/shard_map/ppermute | solution.py:30
  55.1 3.1 %collective-permute-done.5 = f32[256,1152]{1,0:T(8,128)} collective-permute-done((f32[256,1152]{1,0:T(8,128)}, f32[256,1152]{1,0:T(8,128)}, u32[]{:S(2)}, u32[]{:S(2)}) %collective-permute-start.5) | collective-permute-done | bytes 1179680 | tf_op jit(solution)/shard_map/ppermute | solution.py:30
  58.2 1.4 select_add_fusion
  60.1 3.1 %collective-permute-start.6 = (f32[256,576]{0,1:T(8,128)S(1)}, f32[256,576]{0,1:T(8,128)}, u32[]{:S(2)}, u32[]{:S(2)}) collective-permute-start(f32[256,576]{0,1:T(8,128)S(1)} %copy.25), channel_id=1, source_target_pairs={{0,128},{16,144},{32,160},{48,176},{64,192},{80,208},{96,224},{112... | collective-permute-start | bytes 1769480 | tf_op jit(solution)/shard_map/ppermute | solution.py:30
  63.2 13.3 %collective-permute-done.6 = f32[256,576]{0,1:T(8,128)} collective-permute-done((f32[256,576]{0,1:T(8,128)S(1)}, f32[256,576]{0,1:T(8,128)}, u32[]{:S(2)}, u32[]{:S(2)}) %collective-permute-start.6) | collective-permute-done | bytes 589856 | tf_op jit(solution)/shard_map/ppermute | solution.py:30
  76.5 1.3 copy.26
  77.8 1.1 select_add_fusion.1
  78.9 4.7 %all-to-all-start.1 = ((f32[16,16,576]{2,1,0:T(8,128)}), f32[16,16,576]{2,1,0:T(8,128)S(1)}, u32[]{:S(2)}, u32[]{:S(2)}) async-start(f32[16,16,576]{2,1,0:T(8,128)} %bitcast.46), calls=%async_computation.1 | async-start | bytes 1310720 | tf_op jit(solution)/shard_map/all_to_all | solution.py:42
  83.6 3.1 %collective-permute-start.3 = (bf16[1,1,128,256]{3,2,1,0:T(8,128)(2,1)S(1)}, bf16[1,1,128,256]{3,2,1,0:T(8,128)(2,1)S(1)}, u32[]{:S(2)}, u32[]{:S(2)}) collective-permute-start(bf16[1,1,128,256]{3,2,1,0:T(8,128)(2,1)S(1)} %get-tuple-element.32), channel_id=1, source_target_pairs={{0,1},{1,2},{2,3},{3,4},{4,5},{5,6},{6,7},{7,8},{8,9},{9,10},{10,1... | collective-permute-start | bytes 196616 | tf_op jit(solution)/shard_map/ppermute | solution.py:20
  86.7 4.3 %collective-permute-start.4 = (bf16[1,1,128,256]{3,2,1,0:T(8,128)(2,1)S(1)}, bf16[1,1,128,256]{3,2,1,0:T(8,128)(2,1)S(1)}, u32[]{:S(2)}, u32[]{:S(2)}) collective-permute-start(bf16[1,1,128,256]{3,2,1,0:T(8,128)(2,1)S(1)} %get-tuple-element.33), channel_id=1, source_target_pairs={{1,0},{2,1},{3,2},{4,3},{5,4},{6,5},{7,6},{8,7},{9,8},{10,9},{11,1... | collective-permute-start | bytes 196616 | tf_op jit(solution)/shard_map/ppermute | solution.py:21
  91.0 11.3 %collective-permute-done.3 = bf16[1,1,128,256]{3,2,1,0:T(8,128)(2,1)S(1)} collective-permute-done((bf16[1,1,128,256]{3,2,1,0:T(8,128)(2,1)S(1)}, bf16[1,1,128,256]{3,2,1,0:T(8,128)(2,1)S(1)}, u32[]{:S(2)}, u32[]{:S(2)}) %collective-permute-start.3) | collective-permute-done | bytes 65568 | tf_op jit(solution)/shard_map/ppermute | solution.py:20
  102.5 0.9 pad_maximum_fusion
  103.4 1.3 fusion.35
  104.8 0.5 copy-done.2
  105.3 0.3 fusion.26
  105.6 0.3 convolution_add_fusion.6
  106.3 0.3 convolution_add_fusion.4
  106.7 4.5 %collective-permute-start.7 = (f32[16,576]{1,0:T(8,128)S(1)}, f32[16,576]{1,0:T(8,128)S(1)}, u32[]{:S(2)}, u32[]{:S(2)}) collective-permute-start(f32[16,576]{1,0:T(8,128)S(1)} %reduce_sum.49), channel_id=1, source_target_pairs={{0,384},{16,400},{32,416},{48,432},{64,448},{80,464},{96,480},{112... | collective-permute-start | bytes 110600 | tf_op jit(solution)/shard_map/ppermute | solution.py:30
  111.5 1.2 collective-permute-done.7
  112.8 8.8 %collective-permute-start.8 = (f32[16,576]{1,0:T(8,128)S(1)}, f32[16,576]{1,0:T(8,128)S(1)}, u32[]{:S(2)}, u32[]{:S(2)}) collective-permute-start(f32[16,576]{1,0:T(8,128)S(1)} %add.110), channel_id=1, source_target_pairs={{0,32},{16,48},{32,0},{48,16},{64,96},{80,112},{96,64},{112,80},{1... | collective-permute-start | bytes 110600 | tf_op jit(solution)/shard_map/ppermute | solution.py:30
  121.6 0.3 convolution_add_fusion.2
  122.0 1.0 collective-permute-done.8
  123.0 8.2 %collective-permute-start.9 = (f32[16,576]{1,0:T(8,128)S(1)}, f32[16,576]{1,0:T(8,128)S(1)}, u32[]{:S(2)}, u32[]{:S(2)}) collective-permute-start(f32[16,576]{1,0:T(8,128)S(1)} %add.111), channel_id=1, source_target_pairs={{0,96},{16,112},{32,64},{48,80},{64,32},{80,48},{96,0},{112,16},{1... | collective-permute-start | bytes 110600 | tf_op jit(solution)/shard_map/ppermute | solution.py:30
  131.2 0.3 convolution_add_fusion.1
  131.6 1.4 collective-permute-done.9
  133.0 1.9 %collective-permute-start.10 = (f32[16,576]{1,0:T(8,128)S(1)}, f32[16,576]{1,0:T(8,128)S(1)}, u32[]{:S(2)}, u32[]{:S(2)}) collective-permute-start(f32[16,576]{1,0:T(8,128)S(1)} %add.112), channel_id=1, source_target_pairs={{0,128},{16,144},{32,160},{48,176},{64,192},{80,208},{96,224},{112... | collective-permute-start | bytes 110600 | tf_op jit(solution)/shard_map/ppermute | solution.py:30
  135.3 2.5 %collective-permute-done.10 = f32[16,576]{1,0:T(8,128)S(1)} collective-permute-done((f32[16,576]{1,0:T(8,128)S(1)}, f32[16,576]{1,0:T(8,128)S(1)}, u32[]{:S(2)}, u32[]{:S(2)}) %collective-permute-start.10) | collective-permute-done | bytes 36896 | tf_op jit(solution)/shard_map/ppermute | solution.py:30
  137.9 6.8 %collective-permute-start.11 = (f32[16,1152]{1,0:T(8,128)S(1)}, f32[16,1152]{1,0:T(8,128)S(1)}, u32[]{:S(2)}, u32[]{:S(2)}) collective-permute-start(f32[16,1152]{1,0:T(8,128)S(1)} %maximum_select_fusion.2), channel_id=1, source_target_pairs={{0,16},{16,0},{32,48},{48,32},{64,80},{80,64},{96,112},{112,96},{1... | collective-permute-start | bytes 221192 | tf_op jit(solution)/shard_map/ppermute | solution.py:30
  144.7 1.1 fusion.6
  145.9 0.7 copy.27
  (62 shorter events, 4.9 us)
Async XLA Ops:
  0.6 9.7 %copy-start.3 = (bf16[1,8,128,256]{3,2,1,0:T(8,128)(2,1)S(1)}, bf16[1,8,128,256]{3,2,1,0:T(8,128)(2,1)}, u32[]{:S(2)}) copy-start(bf16[1,8,128,256]{3,2,1,0:T(8,128)(2,1)} %param.4) | copy-start | bytes 1572868
  2.6 23.6 %all-to-all-start = ((bf16[16,16,1152]{2,1,0:T(8,128)(2,1)}), bf16[16,16,1152]{2,1,0:T(8,128)(2,1)S(1)}, u32[]{:S(2)}, u32[]{:S(2)}) async-start(bf16[16,16,1152]{2,1,0:T(8,128)(2,1)} %broadcast_in_dim.2), calls=%async_computation | async-start | bytes 1179648 | tf_op jit(solution)/shard_map/all_to_all | solution.py:36
  10.3 19.2 %collective-permute-start = (bf16[1,1,128,256]{3,2,1,0:T(8,128)(2,1)S(1)}, bf16[1,1,128,256]{3,2,1,0:T(8,128)(2,1)S(1)}, u32[]{:S(2)}, u32[]{:S(2)}) collective-permute-start(bf16[1,1,128,256]{3,2,1,0:T(8,128)(2,1)S(1)} %get-tuple-element.36), channel_id=1, source_target_pairs={{0,1},{1,2},{2,3},{3,4},{4,5},{5,6},{6,7},{7,8},{8,9},{9,10},{10,1... | collective-permute-start | bytes 196616 | tf_op jit(solution)/shard_map/ppermute | solution.py:20
  13.4 16.2 %collective-permute-start.1 = (bf16[1,1,128,256]{3,2,1,0:T(8,128)(2,1)S(1)}, bf16[1,1,128,256]{3,2,1,0:T(8,128)(2,1)S(1)}, u32[]{:S(2)}, u32[]{:S(2)}) collective-permute-start(bf16[1,1,128,256]{3,2,1,0:T(8,128)(2,1)S(1)} %get-tuple-element.37), channel_id=1, source_target_pairs={{1,0},{2,1},{3,2},{4,3},{5,4},{6,5},{7,6},{8,7},{9,8},{10,9},{11,1... | collective-permute-start | bytes 196616 | tf_op jit(solution)/shard_map/ppermute | solution.py:21
  26.2 6.2 %collective-permute-start.2 = (bf16[16,16,1152]{2,1,0:T(8,128)(2,1)S(1)}, bf16[16,16,1152]{2,1,0:T(8,128)(2,1)S(1)}, u32[]{:S(2)}, u32[]{:S(2)}) collective-permute-start(bf16[16,16,1152]{2,1,0:T(8,128)(2,1)S(1)} %all-to-all-done), channel_id=1, source_target_pairs={{0,16},{16,0},{32,48},{48,32},{64,80},{80,64},{96,112},{112,96},{1... | collective-permute-start | bytes 1769480 | tf_op jit(solution)/shard_map/ppermute | solution.py:30
  33.3 6.9 %copy-start.1 = (bf16[2304,256]{1,0:T(8,128)(2,1)}, bf16[2304,256]{1,0:T(8,128)(2,1)S(1)}, u32[]{:S(2)}) copy-start(bf16[2304,256]{1,0:T(8,128)(2,1)S(1)} %copy.21) | copy-start | bytes 3538948
  33.3 1.8 %copy-start.5 = (bf16[1,8,128,256]{3,2,1,0:T(8,128)(2,1)S(1)}, bf16[1,8,128,256]{3,2,1,0:T(8,128)(2,1)}, u32[]{:S(2)}) copy-start(bf16[1,8,128,256]{3,2,1,0:T(8,128)(2,1)} %get-tuple-element.26) | copy-start | bytes 1572868
  35.1 1.0 copy-start.4
  36.4 1.0 copy-start.10
  37.4 1.0 copy-start.8
  38.5 1.0 copy-start.7
  39.8 1.0 copy-start.9
  40.9 0.8 copy-start.16
  41.3 1.0 copy-start.15
  44.2 1.0 copy-start.6
  51.7 1.4 copy-start
  53.1 5.1 %collective-permute-start.5 = (f32[256,1152]{1,0:T(8,128)}, f32[256,1152]{1,0:T(8,128)}, u32[]{:S(2)}, u32[]{:S(2)}) collective-permute-start(f32[256,1152]{1,0:T(8,128)} %broadcast_select_fusion), channel_id=1, source_target_pairs={{0,16},{16,0},{32,48},{48,32},{64,80},{80,64},{96,112},{112,96},{1... | collective-permute-start | bytes 3538952 | tf_op jit(solution)/shard_map/ppermute | solution.py:30
  60.1 16.4 %collective-permute-start.6 = (f32[256,576]{0,1:T(8,128)S(1)}, f32[256,576]{0,1:T(8,128)}, u32[]{:S(2)}, u32[]{:S(2)}) collective-permute-start(f32[256,576]{0,1:T(8,128)S(1)} %copy.25), channel_id=1, source_target_pairs={{0,128},{16,144},{32,160},{48,176},{64,192},{80,208},{96,224},{112... | collective-permute-start | bytes 1769480 | tf_op jit(solution)/shard_map/ppermute | solution.py:30
  78.9 27.7 %all-to-all-start.1 = ((f32[16,16,576]{2,1,0:T(8,128)}), f32[16,16,576]{2,1,0:T(8,128)S(1)}, u32[]{:S(2)}, u32[]{:S(2)}) async-start(f32[16,16,576]{2,1,0:T(8,128)} %bitcast.46), calls=%async_computation.1 | async-start | bytes 1310720 | tf_op jit(solution)/shard_map/all_to_all | solution.py:42
  83.6 18.7 %collective-permute-start.3 = (bf16[1,1,128,256]{3,2,1,0:T(8,128)(2,1)S(1)}, bf16[1,1,128,256]{3,2,1,0:T(8,128)(2,1)S(1)}, u32[]{:S(2)}, u32[]{:S(2)}) collective-permute-start(bf16[1,1,128,256]{3,2,1,0:T(8,128)(2,1)S(1)} %get-tuple-element.32), channel_id=1, source_target_pairs={{0,1},{1,2},{2,3},{3,4},{4,5},{5,6},{6,7},{7,8},{8,9},{9,10},{10,1... | collective-permute-start | bytes 196616 | tf_op jit(solution)/shard_map/ppermute | solution.py:20
  86.7 15.6 %collective-permute-start.4 = (bf16[1,1,128,256]{3,2,1,0:T(8,128)(2,1)S(1)}, bf16[1,1,128,256]{3,2,1,0:T(8,128)(2,1)S(1)}, u32[]{:S(2)}, u32[]{:S(2)}) collective-permute-start(bf16[1,1,128,256]{3,2,1,0:T(8,128)(2,1)S(1)} %get-tuple-element.33), channel_id=1, source_target_pairs={{1,0},{2,1},{3,2},{4,3},{5,4},{6,5},{7,6},{8,7},{9,8},{10,9},{11,1... | collective-permute-start | bytes 196616 | tf_op jit(solution)/shard_map/ppermute | solution.py:21
  103.4 1.8 %copy-start.2 = (bf16[2304,256]{1,0:T(8,128)(2,1)S(1)}, bf16[2304,256]{1,0:T(8,128)(2,1)}, u32[]{:S(2)}) copy-start(bf16[2304,256]{1,0:T(8,128)(2,1)} %copy-done.1) | copy-start | bytes 3538948
  106.7 14.9 %copy-start.14 = (bf16[1,8,128,256]{3,2,1,0:T(8,128)(2,1)S(1)}, bf16[1,8,128,256]{3,2,1,0:T(8,128)(2,1)}, u32[]{:S(2)}) copy-start(bf16[1,8,128,256]{3,2,1,0:T(8,128)(2,1)} %get-tuple-element.19) | copy-start | bytes 1572868
  106.7 6.1 %collective-permute-start.7 = (f32[16,576]{1,0:T(8,128)S(1)}, f32[16,576]{1,0:T(8,128)S(1)}, u32[]{:S(2)}, u32[]{:S(2)}) collective-permute-start(f32[16,576]{1,0:T(8,128)S(1)} %reduce_sum.49), channel_id=1, source_target_pairs={{0,384},{16,400},{32,416},{48,432},{64,448},{80,464},{96,480},{112... | collective-permute-start | bytes 110600 | tf_op jit(solution)/shard_map/ppermute | solution.py:30
  112.8 10.2 %collective-permute-start.8 = (f32[16,576]{1,0:T(8,128)S(1)}, f32[16,576]{1,0:T(8,128)S(1)}, u32[]{:S(2)}, u32[]{:S(2)}) collective-permute-start(f32[16,576]{1,0:T(8,128)S(1)} %add.110), channel_id=1, source_target_pairs={{0,32},{16,48},{32,0},{48,16},{64,96},{80,112},{96,64},{112,80},{1... | collective-permute-start | bytes 110600 | tf_op jit(solution)/shard_map/ppermute | solution.py:30
  121.6 9.6 %copy-start.13 = (bf16[1,8,128,256]{3,2,1,0:T(8,128)(2,1)S(1)}, bf16[1,8,128,256]{3,2,1,0:T(8,128)(2,1)}, u32[]{:S(2)}) copy-start(bf16[1,8,128,256]{3,2,1,0:T(8,128)(2,1)} %get-tuple-element.18) | copy-start | bytes 1572868
  123.0 10.0 %collective-permute-start.9 = (f32[16,576]{1,0:T(8,128)S(1)}, f32[16,576]{1,0:T(8,128)S(1)}, u32[]{:S(2)}, u32[]{:S(2)}) collective-permute-start(f32[16,576]{1,0:T(8,128)S(1)} %add.111), channel_id=1, source_target_pairs={{0,96},{16,112},{32,64},{48,80},{64,32},{80,48},{96,0},{112,16},{1... | collective-permute-start | bytes 110600 | tf_op jit(solution)/shard_map/ppermute | solution.py:30
  131.2 3.7 %copy-start.12 = (bf16[1,8,128,256]{3,2,1,0:T(8,128)(2,1)S(1)}, bf16[1,8,128,256]{3,2,1,0:T(8,128)(2,1)}, u32[]{:S(2)}) copy-start(bf16[1,8,128,256]{3,2,1,0:T(8,128)(2,1)} %get-tuple-element.23) | copy-start | bytes 1572868
  131.6 13.1 %copy-start.11 = (bf16[1,8,128,256]{3,2,1,0:T(8,128)(2,1)S(1)}, bf16[1,8,128,256]{3,2,1,0:T(8,128)(2,1)}, u32[]{:S(2)}) copy-start(bf16[1,8,128,256]{3,2,1,0:T(8,128)(2,1)} %get-tuple-element.30) | copy-start | bytes 1572868
  133.0 4.7 %collective-permute-start.10 = (f32[16,576]{1,0:T(8,128)S(1)}, f32[16,576]{1,0:T(8,128)S(1)}, u32[]{:S(2)}, u32[]{:S(2)}) collective-permute-start(f32[16,576]{1,0:T(8,128)S(1)} %add.112), channel_id=1, source_target_pairs={{0,128},{16,144},{32,160},{48,176},{64,192},{80,208},{96,224},{112... | collective-permute-start | bytes 110600 | tf_op jit(solution)/shard_map/ppermute | solution.py:30
  137.9 8.0 %collective-permute-start.11 = (f32[16,1152]{1,0:T(8,128)S(1)}, f32[16,1152]{1,0:T(8,128)S(1)}, u32[]{:S(2)}, u32[]{:S(2)}) collective-permute-start(f32[16,1152]{1,0:T(8,128)S(1)} %maximum_select_fusion.2), channel_id=1, source_target_pairs={{0,16},{16,0},{32,48},{48,32},{64,80},{80,64},{96,112},{112,96},{1... | collective-permute-start | bytes 221192 | tf_op jit(solution)/shard_map/ppermute | solution.py:30

commit v9 on v6

--- a/solution.py
+++ b/solution.py
@@ -106,37 +106,23 @@
     whole_kernel = kernel_t.T.reshape(3, 3, in_chan, out_chan)
     rimmed = padded_2(images, (("col", 1),), 1)
     padded = jnp.pad(rimmed, ((0, 0), (0, 0), (1, 1), (0, 0)))
-    conv_out = jnp.zeros((img_count * tile_rows * tile_cols, out_chan), jnp.float32)
-    for tap_row in range(3):
-        for tap_col in range(3):
-            conv_out = conv_out + jnp.dot(
-                window(padded, tap_row, tap_col, tile_rows, tile_cols),
-                whole_kernel[tap_row, tap_col],
-                preferred_element_type=jnp.float32,
-            )
+    spec = ("NHWC", "HWIO", "NHWC")
+    conv_out = lax.conv_general_dilated(
+        padded, whole_kernel, (1, 1), "VALID", dimension_numbers=spec, preferred_element_type=jnp.float32
+    ).reshape(-1, out_chan)
     outputs, grad_pre = norm_act(conv_out, cotangent.reshape(-1, out_chan), norm_gain)
     grad_grid = grad_pre.reshape(img_count, tile_rows, tile_cols, out_chan)
     grad_rimmed = padded_2(grad_grid, (("col", 1),), 1)
     grad_pad = jnp.pad(grad_rimmed, ((0, 0), (0, 0), (1, 1), (0, 0)))
-    grad_input = jnp.zeros((img_count * tile_rows * tile_cols, in_chan), jnp.float32)
-    pieces = []
-    for tap_row in range(3):
-        for tap_col in range(3):
-            grad_input = grad_input + lax.dot_general(
-                window(grad_pad, 2 - tap_row, 2 - tap_col, tile_rows, tile_cols),
-                whole_kernel[tap_row, tap_col],
-                (((1,), (1,)), ((), ())),
-                preferred_element_type=jnp.float32,
-            )
-            pieces.append(
-                lax.dot_general(
-                    grad_pre,
-                    window(padded, tap_row, tap_col, tile_rows, tile_cols),
-                    (((0,), (0,)), ((), ())),
-                    preferred_element_type=jnp.float32,
-                )
-            )
-    partial_value = jnp.stack(pieces, axis=1).reshape(out_chan, taps)
+    flipped = kernel_t.reshape(out_chan, 3, 3, in_chan)[:, ::-1, ::-1, :]
+    grad_input = lax.conv_general_dilated(
+        grad_pad, flipped, (1, 1), "VALID", dimension_numbers=("NHWC", "IHWO", "NHWC"),
+        preferred_element_type=jnp.float32,
+    ).reshape(-1, in_chan)
+    partial_value = lax.conv_general_dilated(
+        padded, grad_grid, (1, 1), "VALID", dimension_numbers=("CHWN", "IHWO", "CHWN"),
+        preferred_element_type=jnp.float32,
+    ).reshape(out_chan, taps)
     core_sum = halve_sum(partial_value, "row", core_bit, 1)
     col_sum = scatter_sum(core_sum, "col")
     row_piece = double_sum(col_sum, "row", [1 << 3, 3 << 3, 1 << 1, 3 << 1])

time: 140 us -> 146 us (1.043)
  the two profiles are of different devices: /device:TPU:65 before, /device:TPU:97 now
where the time goes in v9:
time: 146 us; the launch traced here: 145 us
  starting transfers between devices  58.4 us (40%)
  blocking collectives  34.9 us (24%)
  waiting for transfers between devices  19.4 us (13%)
  local copies, waits for them, and re-layouts  14.6 us (10%)
  matrix products  11.6 us (8%)
  other arithmetic  5.43 us (4%)
    ppermute x7, starting transfers between devices, exchange(): return lax.ppermute(value, axis, pairs)  38.3 us
    all_to_all x1, blocking collectives, scatter_sum(): return lax.all_to_all(blocks, axis, 0, 0, tiled=False).sum(0)  34.9 us
    all_to_all x1, waiting for transfers between devices, gather_chunks(): return lax.all_to_all(copies, axis, 0, 0, tiled=False)  10.8 us
    unnamed x45, local copies, waits for them, and re-layouts  8.38 us
    ppermute x2, starting transfers between devices, padded_2(): after = lax.ppermute(initial, axis, down)  7.81 us
    conv_general_dilated x1, matrix products, on_device(): lax.conv_general_dilated(padded, grad_grid, (1, 1), 'VALID', dimension_nu...  7.52 us
    all_to_all x1, starting transfers between devices, gather_chunks(): return lax.all_to_all(copies, axis, 0, 0, tiled=False)  7.19 us
    ppermute x2, starting transfers between devices, padded_2(): before = lax.ppermute(last, axis, up)  5.09 us
  transfers between devices with their start and end apart: 12, of which 5 were waited for; matrix products, arithmetic and copies ran while one was open for 7% of the time, Pallas kernels for 0%

profile of v9, /device:TPU:97, one launch (start us, length us, event | category | flops | bytes accessed | tf_op | source)
XLA Modules:
  0.0 145.4 jit_solution(11140102501013864136)
XLA Ops:
  0.6 1.0 copy.36
  1.6 0.1 reshape.183
  1.8 0.9 broadcast_in_dim.2
  2.6 7.2 %all-to-all-start = ((bf16[16,16,1152]{2,1,0:T(8,128)(2,1)}), bf16[16,16,1152]{2,1,0:T(8,128)(2,1)S(1)}, u32[]{:S(2)}, u32[]{:S(2)}) async-start(bf16[16,16,1152]{2,1,0:T(8,128)(2,1)} %broadcast_in_dim.2), calls=%async_computation | async-start | bytes 1179648 | tf_op jit(solution)/shard_map/all_to_all | solution.py:36
  9.8 0.1 copy.63
  10.0 3.1 %collective-permute-start = (bf16[1,1,128,256]{3,0,2,1:T(2,128)(2,1)S(1)}, bf16[1,1,128,256]{3,0,2,1:T(2,128)(2,1)S(1)}, u32[]{:S(2)}, u32[]{:S(2)}) collective-permute-start(bf16[1,1,128,256]{3,0,2,1:T(2,128)(2,1)S(1)} %copy.63), channel_id=1, source_target_pairs={{0,1},{1,2},{2,3},{3,4},{4,5},{5,6},{6,7},{7,8},{8,9},{9,10},{10,1... | collective-permute-start | bytes 196616 | tf_op jit(solution)/shard_map/ppermute | solution.py:20
  13.1 10.8 %all-to-all-done = bf16[16,16,1152]{2,1,0:T(8,128)(2,1)S(1)} async-done(((bf16[16,16,1152]{2,1,0:T(8,128)(2,1)}), bf16[16,16,1152]{2,1,0:T(8,128)(2,1)S(1)}, u32[]{:S(2)}, u32[]{:S(2)}) %all-to-all-start) | async-done | bytes 589856 | tf_op jit(solution)/shard_map/all_to_all | solution.py:36
  23.9 3.7 %collective-permute-start.2 = (bf16[16,16,1152]{2,1,0:T(8,128)(2,1)S(1)}, bf16[16,16,1152]{2,1,0:T(8,128)(2,1)S(1)}, u32[]{:S(2)}, u32[]{:S(2)}) collective-permute-start(bf16[16,16,1152]{2,1,0:T(8,128)(2,1)S(1)} %all-to-all-done), channel_id=1, source_target_pairs={{0,16},{16,0},{32,48},{48,32},{64,80},{80,64},{96,112},{112,96},{1... | collective-permute-start | bytes 1769480 | tf_op jit(solution)/shard_map/ppermute | solution.py:30
  27.6 0.1 copy.64
  27.7 2.4 %collective-permute-start.1 = (bf16[1,1,128,256]{3,0,2,1:T(2,128)(2,1)S(1)}, bf16[1,1,128,256]{3,0,2,1:T(2,128)(2,1)S(1)}, u32[]{:S(2)}, u32[]{:S(2)}) collective-permute-start(bf16[1,1,128,256]{3,0,2,1:T(2,128)(2,1)S(1)} %copy.64), channel_id=1, source_target_pairs={{1,0},{2,1},{3,2},{4,3},{5,4},{6,5},{7,6},{8,7},{9,8},{10,9},{11,1... | collective-permute-start | bytes 196616 | tf_op jit(solution)/shard_map/ppermute | solution.py:21
  30.1 0.1 constant_dynamic-update-slice_fusion.2
  30.3 0.9 constant_dynamic-update-slice_fusion.1
  31.1 3.5 %collective-permute-done.1 = bf16[1,1,128,256]{3,0,2,1:T(2,128)(2,1)S(1)} collective-permute-done((bf16[1,1,128,256]{3,0,2,1:T(2,128)(2,1)S(1)}, bf16[1,1,128,256]{3,0,2,1:T(2,128)(2,1)S(1)}, u32[]{:S(2)}, u32[]{:S(2)}) %collective-permute-start.1) | collective-permute-done | bytes 65568 | tf_op jit(solution)/shard_map/ppermute | solution.py:21
  34.7 0.1 constant_dynamic-update-slice_fusion
  34.9 0.1 copy.66
  35.0 1.0 copy-done.7
  36.0 0.2 pad.3
  36.1 0.2 reshape.190
  36.4 0.1 copy.35
  36.5 0.7 slice.22
  37.3 0.1 copy-done.10
  37.4 0.3 fusion.3
  37.7 0.4 copy-done.4
  38.1 0.6 copy.37
  38.7 0.3 copy-done.13
  39.0 2.6 %convolution_select_fusion.1 = f32[8,8,17,256]{3,1,2,0:T(8,128)S(1)} fusion(bf16[3,3,256,256]{3,2,1,0:T(8,128)(2,1)S(1)} %bitcast.68, bf16[10,1,7,2,256]{4,2,3,0,1:T(8,128)(2,1)S(1)} %copy-done.13, bf16[10,1,8,17,256]{4,2,3,0,1:T(8,128)(2,1)} %copy-done.10, pred[8,17]{0,1:T(8,128)(4,1)S(1)} %copy-done.15), kind=kOutput, calls=%fused_computation.5 | convolution fusion | flops 1286070272 | bytes 3061896 | tf_op jit(solution)/shard_map/conv_general_dilated | solution.py:110
  41.6 0.4 copy.38
  41.9 0.2 slice_reduce_fusion
  42.2 0.4 multiply_reduce_fusion.1
  42.6 0.4 copy-done.12
  43.0 2.4 %fusion.36 = (f32[8,128]{0,1:T(8,128)S(1)}, f32[8,128]{0,1:T(8,128)S(1)}, f32[1,8,128,256]{3,1,2,0:T(8,128)S(1)}, bf16[1,8,128,256]{3,1,2,0:T(8,128)(2,1)}) fusion(f32[8,128]{0,1:T(8,128)S(1)} %add_rsqrt_fusion, f32[8,128]{0,1:T(8,128)S(1)} %broadcast_multiply_fusion.2, f32[8,1,136,256]{3,0,2,1:T(8,128)S(1)} %bitcast.59, f32[256]{0:T(256)S(1)} %copy-done.14, ...), kind=kLoop, calls=%fused_computation.61 | loop fusion | flops 4978688 | bytes 3163136 | tf_op jit(solution)/shard_map/reduce_sum | solution.py:86
  45.4 0.7 multiply_convert_fusion
  46.2 0.6 copy-done.8
  46.8 7.5 %fusion.11 = f32[256,3,3,256]{0,3,2,1:T(8,128)S(1)} fusion(bf16[1,10,128,256]{3,0,2,1:T(2,128)(2,1)S(1)} %copy-done.8, bf16[1,8,128,256]{3,1,2,0:T(8,128)(2,1)S(1)} %multiply_convert_fusion), kind=kOutput, calls=%fused_computation.25 | convolution fusion | flops 1201668096 | bytes 3538944 | tf_op jit(solution)/shard_map/conv_general_dilated | solution.py:122
  54.3 0.2 fusion.38
  54.5 0.4 copy.54
  54.8 0.4 copy.55
  55.2 0.1 broadcast_select_fusion
  55.3 2.7 %collective-permute-start.5 = (f32[256,1152]{1,0:T(8,128)S(1)}, f32[256,1152]{1,0:T(8,128)S(1)}, u32[]{:S(2)}, u32[]{:S(2)}) collective-permute-start(f32[256,1152]{1,0:T(8,128)S(1)} %broadcast_select_fusion), channel_id=1, source_target_pairs={{0,16},{16,0},{32,48},{48,32},{64,80},{80,64},{96,112},{112,96},{1... | collective-permute-start | bytes 3538952 | tf_op jit(solution)/shard_map/ppermute | solution.py:30
  58.0 2.5 %collective-permute-done.5 = f32[256,1152]{1,0:T(8,128)S(1)} collective-permute-done((f32[256,1152]{1,0:T(8,128)S(1)}, f32[256,1152]{1,0:T(8,128)S(1)}, u32[]{:S(2)}, u32[]{:S(2)}) %collective-permute-start.5) | collective-permute-done | bytes 1179680 | tf_op jit(solution)/shard_map/ppermute | solution.py:30
  60.5 0.2 select_add_fusion
  60.7 34.9 %all_to_all.10 = f32[16,16,1152]{2,1,0:T(8,128)S(1)} all-to-all(f32[16,16,1152]{2,1,0:T(8,128)S(1)} %bitcast.62), channel_id=1, replica_groups=mesh['row'=32,'col'=16] {'col'}, dimensions={0} | all-to-all | bytes 2359296 | tf_op jit(solution)/shard_map/all_to_all | solution.py:42
  95.6 0.1 reduce_sum.49
  95.6 3.5 %collective-permute-start.6 = (f32[16,1152]{1,0:T(8,128)S(1)}, f32[16,1152]{1,0:T(8,128)S(1)}, u32[]{:S(2)}, u32[]{:S(2)}) collective-permute-start(f32[16,1152]{1,0:T(8,128)S(1)} %reduce_sum.49), channel_id=1, source_target_pairs={{0,128},{16,144},{32,160},{48,176},{64,192},{80,208},{96,224},{112... | collective-permute-start | bytes 221192 | tf_op jit(solution)/shard_map/ppermute | solution.py:30
  99.1 0.2 fusion.39
  99.3 2.0 %collective-permute-start.3 = (bf16[1,1,128,256]{3,1,2,0:T(2,128)(2,1)S(1)}, bf16[1,1,128,256]{3,1,2,0:T(2,128)(2,1)S(1)}, u32[]{:S(2)}, u32[]{:S(2)}) collective-permute-start(bf16[1,1,128,256]{3,1,2,0:T(2,128)(2,1)S(1)} %get-tuple-element.15), channel_id=1, source_target_pairs={{0,1},{1,2},{2,3},{3,4},{4,5},{5,6},{6,7},{7,8},{8,9},{9,10},{10,1... | collective-permute-start | bytes 196616 | tf_op jit(solution)/shard_map/ppermute | solution.py:20
  101.3 5.4 %collective-permute-start.4 = (bf16[1,1,128,256]{3,1,2,0:T(2,128)(2,1)S(1)}, bf16[1,1,128,256]{3,1,2,0:T(2,128)(2,1)S(1)}, u32[]{:S(2)}, u32[]{:S(2)}) collective-permute-start(bf16[1,1,128,256]{3,1,2,0:T(2,128)(2,1)S(1)} %get-tuple-element.16), channel_id=1, source_target_pairs={{1,0},{2,1},{3,2},{4,3},{5,4},{6,5},{7,6},{8,7},{9,8},{10,9},{11,1... | collective-permute-start | bytes 196616 | tf_op jit(solution)/shard_map/ppermute | solution.py:21
  106.7 3.7 %collective-permute-start.7 = (f32[16,1152]{1,0:T(8,128)S(1)}, f32[16,1152]{1,0:T(8,128)S(1)}, u32[]{:S(2)}, u32[]{:S(2)}) collective-permute-start(f32[16,1152]{1,0:T(8,128)S(1)} %add.48), channel_id=1, source_target_pairs={{0,384},{16,400},{32,416},{48,432},{64,448},{80,464},{96,480},{112... | collective-permute-start | bytes 221192 | tf_op jit(solution)/shard_map/ppermute | solution.py:30
  110.5 0.3 maximum_select_fusion.1
  110.8 1.9 %select_n.51 = bf16[256,3,3,256]{3,2,1,0:T(4,128)(2,1)} reshape(bf16[16,16,2304]{2,1,0:T(8,128)(2,1)S(1)} %maximum_select_fusion.1) | data formatting | bytes 2359296 | tf_op jit(solution)/shard_map/jit(_where)/select_n | solution.py:51
  112.7 0.9 copy.48
  113.6 8.8 %collective-permute-start.8 = (f32[16,1152]{1,0:T(8,128)S(1)}, f32[16,1152]{1,0:T(8,128)S(1)}, u32[]{:S(2)}, u32[]{:S(2)}) collective-permute-start(f32[16,1152]{1,0:T(8,128)S(1)} %add.49), channel_id=1, source_target_pairs={{0,32},{16,48},{32,0},{48,16},{64,96},{80,112},{96,64},{112,80},{1... | collective-permute-start | bytes 221192 | tf_op jit(solution)/shard_map/ppermute | solution.py:30
  122.5 0.7 maximum_bitcast_fusion
  123.2 0.1 pad.5
  123.3 0.2 copy.42
  123.6 0.8 collective-permute-done.8
  124.4 10.4 %collective-permute-start.9 = (f32[16,1152]{1,0:T(8,128)S(1)}, f32[16,1152]{1,0:T(8,128)S(1)}, u32[]{:S(2)}, u32[]{:S(2)}) collective-permute-start(f32[16,1152]{1,0:T(8,128)S(1)} %add.50), channel_id=1, source_target_pairs={{0,96},{16,112},{32,64},{48,80},{64,32},{80,48},{96,0},{112,16},{1... | collective-permute-start | bytes 221192 | tf_op jit(solution)/shard_map/ppermute | solution.py:30
  134.8 1.5 %fusion.2 = bf16[8,8,17,256]{3,1,2,0:T(8,128)(2,1)S(1)} fusion(bf16[256,3,3,256]{3,2,1,0:T(4,128)(2,1)S(1)} %copy-done.9, bf16[10,1,7,2,256]{4,2,3,0,1:T(8,128)(2,1)S(1)} %slice.26, bf16[10,1,8,17,256]{4,2,3,0,1:T(8,128)(2,1)S(1)} %copy.42, pred[8,17]{0,1:T(8,128)(4,1)S(1)} %copy-done.16), kind=kOutput, calls=%fused_computation.6 | convolution fusion | flops 1286348800 | bytes 2504840 | tf_op jit(solution)/shard_map/conv_general_dilated | solution.py:118
  136.3 0.1 copy.44
  136.4 1.8 %collective-permute-done.9 = f32[16,1152]{1,0:T(8,128)S(1)} collective-permute-done((f32[16,1152]{1,0:T(8,128)S(1)}, f32[16,1152]{1,0:T(8,128)S(1)}, u32[]{:S(2)}, u32[]{:S(2)}) %collective-permute-start.9) | collective-permute-done | bytes 73760 | tf_op jit(solution)/shard_map/ppermute | solution.py:30
  138.2 5.5 %collective-permute-start.10 = (f32[16,1152]{1,0:T(8,128)S(1)}, f32[16,1152]{1,0:T(8,128)S(1)}, u32[]{:S(2)}, u32[]{:S(2)}) collective-permute-start(f32[16,1152]{1,0:T(8,128)S(1)} %add.51), channel_id=1, source_target_pairs={{0,16},{16,0},{32,48},{48,32},{64,80},{80,64},{96,112},{112,96},{1... | collective-permute-start | bytes 221192 | tf_op jit(solution)/shard_map/ppermute | solution.py:30
  143.7 0.9 copy.49
  144.6 0.1 reshape.187
  144.7 0.7 copy.50
  (47 shorter events, 0.3 us)
Async XLA Ops:
  0.6 9.2 %copy-start.11 = (bf16[1,8,128,256]{3,2,1,0:T(8,128)(2,1)S(1)}, bf16[1,8,128,256]{3,2,1,0:T(8,128)(2,1)}, u32[]{:S(2)}) copy-start(bf16[1,8,128,256]{3,2,1,0:T(8,128)(2,1)} %param.4) | copy-start | bytes 1572868
  2.6 21.2 %all-to-all-start = ((bf16[16,16,1152]{2,1,0:T(8,128)(2,1)}), bf16[16,16,1152]{2,1,0:T(8,128)(2,1)S(1)}, u32[]{:S(2)}, u32[]{:S(2)}) async-start(bf16[16,16,1152]{2,1,0:T(8,128)(2,1)} %broadcast_in_dim.2), calls=%async_computation | async-start | bytes 1179648 | tf_op jit(solution)/shard_map/all_to_all | solution.py:36
  10.0 20.2 %collective-permute-start = (bf16[1,1,128,256]{3,0,2,1:T(2,128)(2,1)S(1)}, bf16[1,1,128,256]{3,0,2,1:T(2,128)(2,1)S(1)}, u32[]{:S(2)}, u32[]{:S(2)}) collective-permute-start(bf16[1,1,128,256]{3,0,2,1:T(2,128)(2,1)S(1)} %copy.63), channel_id=1, source_target_pairs={{0,1},{1,2},{2,3},{3,4},{4,5},{5,6},{6,7},{7,8},{8,9},{9,10},{10,1... | collective-permute-start | bytes 196616 | tf_op jit(solution)/shard_map/ppermute | solution.py:20
  23.9 13.6 %copy-start = (bf16[16,16,1152]{2,1,0:T(8,128)(2,1)}, bf16[16,16,1152]{2,1,0:T(8,128)(2,1)S(1)}, u32[]{:S(2)}) copy-start(bf16[16,16,1152]{2,1,0:T(8,128)(2,1)S(1)} %all-to-all-done) | copy-start | bytes 1769476
  23.9 13.4 %collective-permute-start.2 = (bf16[16,16,1152]{2,1,0:T(8,128)(2,1)S(1)}, bf16[16,16,1152]{2,1,0:T(8,128)(2,1)S(1)}, u32[]{:S(2)}, u32[]{:S(2)}) collective-permute-start(bf16[16,16,1152]{2,1,0:T(8,128)(2,1)S(1)} %all-to-all-done), channel_id=1, source_target_pairs={{0,16},{16,0},{32,48},{48,32},{64,80},{80,64},{96,112},{112,96},{1... | collective-permute-start | bytes 1769480 | tf_op jit(solution)/shard_map/ppermute | solution.py:30
  27.7 7.0 %collective-permute-start.1 = (bf16[1,1,128,256]{3,0,2,1:T(2,128)(2,1)S(1)}, bf16[1,1,128,256]{3,0,2,1:T(2,128)(2,1)S(1)}, u32[]{:S(2)}, u32[]{:S(2)}) collective-permute-start(bf16[1,1,128,256]{3,0,2,1:T(2,128)(2,1)S(1)} %copy.64), channel_id=1, source_target_pairs={{1,0},{2,1},{3,2},{4,3},{5,4},{6,5},{7,6},{8,7},{9,8},{10,9},{11,1... | collective-permute-start | bytes 196616 | tf_op jit(solution)/shard_map/ppermute | solution.py:21
  34.8 1.1 copy-start.7
  36.5 0.9 copy-start.10
  37.3 0.8 copy-start.4
  38.1 0.9 copy-start.13
  38.1 0.9 copy-start.15
  41.9 1.0 copy-start.12
  41.9 1.0 copy-start.14
  45.4 1.3 copy-start.8
  46.8 7.5 %copy-start.2 = (bf16[1,8,128,256]{3,1,2,0:T(8,128)(2,1)}, bf16[1,8,128,256]{3,1,2,0:T(8,128)(2,1)S(1)}, u32[]{:S(2)}) copy-start(bf16[1,8,128,256]{3,1,2,0:T(8,128)(2,1)S(1)} %multiply_convert_fusion) | copy-start | bytes 1572868
  55.3 5.2 %collective-permute-start.5 = (f32[256,1152]{1,0:T(8,128)S(1)}, f32[256,1152]{1,0:T(8,128)S(1)}, u32[]{:S(2)}, u32[]{:S(2)}) collective-permute-start(f32[256,1152]{1,0:T(8,128)S(1)} %broadcast_select_fusion), channel_id=1, source_target_pairs={{0,16},{16,0},{32,48},{48,32},{64,80},{80,64},{96,112},{112,96},{1... | collective-permute-start | bytes 3538952 | tf_op jit(solution)/shard_map/ppermute | solution.py:30
  95.6 3.6 %copy-start.3 = (bf16[1,8,128,256]{3,1,2,0:T(8,128)(2,1)S(1)}, bf16[1,8,128,256]{3,1,2,0:T(8,128)(2,1)}, u32[]{:S(2)}) copy-start(bf16[1,8,128,256]{3,1,2,0:T(8,128)(2,1)} %copy-done.2) | copy-start | bytes 1572868
  95.6 14.9 %copy-start.1 = (bf16[16,16,1152]{2,1,0:T(8,128)(2,1)S(1)}, bf16[16,16,1152]{2,1,0:T(8,128)(2,1)}, u32[]{:S(2)}) copy-start(bf16[16,16,1152]{2,1,0:T(8,128)(2,1)} %copy-done) | copy-start | bytes 1769476
  95.6 14.9 %copy-start.5 = (bf16[16,16,1152]{2,1,0:T(8,128)(2,1)S(1)}, bf16[16,16,1152]{2,1,0:T(8,128)(2,1)}, u32[]{:S(2)}) copy-start(bf16[16,16,1152]{2,1,0:T(8,128)(2,1)} %copy-done.4) | copy-start | bytes 1769476
  95.6 11.1 %collective-permute-start.6 = (f32[16,1152]{1,0:T(8,128)S(1)}, f32[16,1152]{1,0:T(8,128)S(1)}, u32[]{:S(2)}, u32[]{:S(2)}) collective-permute-start(f32[16,1152]{1,0:T(8,128)S(1)} %reduce_sum.49), channel_id=1, source_target_pairs={{0,128},{16,144},{32,160},{48,176},{64,192},{80,208},{96,224},{112... | collective-permute-start | bytes 221192 | tf_op jit(solution)/shard_map/ppermute | solution.py:30
  99.3 23.2 %collective-permute-start.3 = (bf16[1,1,128,256]{3,1,2,0:T(2,128)(2,1)S(1)}, bf16[1,1,128,256]{3,1,2,0:T(2,128)(2,1)S(1)}, u32[]{:S(2)}, u32[]{:S(2)}) collective-permute-start(bf16[1,1,128,256]{3,1,2,0:T(2,128)(2,1)S(1)} %get-tuple-element.15), channel_id=1, source_target_pairs={{0,1},{1,2},{2,3},{3,4},{4,5},{5,6},{6,7},{7,8},{8,9},{9,10},{10,1... | collective-permute-start | bytes 196616 | tf_op jit(solution)/shard_map/ppermute | solution.py:20
  101.3 21.2 %collective-permute-start.4 = (bf16[1,1,128,256]{3,1,2,0:T(2,128)(2,1)S(1)}, bf16[1,1,128,256]{3,1,2,0:T(2,128)(2,1)S(1)}, u32[]{:S(2)}, u32[]{:S(2)}) collective-permute-start(bf16[1,1,128,256]{3,1,2,0:T(2,128)(2,1)S(1)} %get-tuple-element.16), channel_id=1, source_target_pairs={{1,0},{2,1},{3,2},{4,3},{5,4},{6,5},{7,6},{8,7},{9,8},{10,9},{11,1... | collective-permute-start | bytes 196616 | tf_op jit(solution)/shard_map/ppermute | solution.py:21
  106.7 6.9 %collective-permute-start.7 = (f32[16,1152]{1,0:T(8,128)S(1)}, f32[16,1152]{1,0:T(8,128)S(1)}, u32[]{:S(2)}, u32[]{:S(2)}) collective-permute-start(f32[16,1152]{1,0:T(8,128)S(1)} %add.48), channel_id=1, source_target_pairs={{0,384},{16,400},{32,416},{48,432},{64,448},{80,464},{96,480},{112... | collective-permute-start | bytes 221192 | tf_op jit(solution)/shard_map/ppermute | solution.py:30
  110.8 1.9 %copy-start.6 = (bf16[1,8,128,256]{3,1,2,0:T(8,128)(2,1)S(1)}, bf16[1,8,128,256]{3,1,2,0:T(8,128)(2,1)}, u32[]{:S(2)}) copy-start(bf16[1,8,128,256]{3,1,2,0:T(8,128)(2,1)} %get-tuple-element.14) | copy-start | bytes 1572868
  113.6 10.7 %collective-permute-start.8 = (f32[16,1152]{1,0:T(8,128)S(1)}, f32[16,1152]{1,0:T(8,128)S(1)}, u32[]{:S(2)}, u32[]{:S(2)}) collective-permute-start(f32[16,1152]{1,0:T(8,128)S(1)} %add.49), channel_id=1, source_target_pairs={{0,32},{16,48},{32,0},{48,16},{64,96},{80,112},{96,64},{112,80},{1... | collective-permute-start | bytes 221192 | tf_op jit(solution)/shard_map/ppermute | solution.py:30
  123.3 11.5 %copy-start.9 = (bf16[256,3,3,256]{3,2,1,0:T(4,128)(2,1)S(1)}, bf16[256,3,3,256]{3,2,1,0:T(4,128)(2,1)}, u32[]{:S(2)}) copy-start(bf16[256,3,3,256]{3,2,1,0:T(4,128)(2,1)} %select_n.51) | copy-start | bytes 3538948
  123.3 11.5 %copy-start.16 = (pred[8,17]{0,1:T(8,128)(4,1)S(1)}, pred[8,17]{0,1:T(8,128)(4,1)}, u32[]{:S(2)}) copy-start(pred[8,17]{0,1:T(8,128)(4,1)} %constant.43) | copy-start | bytes 412
  124.4 13.8 %collective-permute-start.9 = (f32[16,1152]{1,0:T(8,128)S(1)}, f32[16,1152]{1,0:T(8,128)S(1)}, u32[]{:S(2)}, u32[]{:S(2)}) collective-permute-start(f32[16,1152]{1,0:T(8,128)S(1)} %add.50), channel_id=1, source_target_pairs={{0,96},{16,112},{32,64},{48,80},{64,32},{80,48},{96,0},{112,16},{1... | collective-permute-start | bytes 221192 | tf_op jit(solution)/shard_map/ppermute | solution.py:30
  138.2 6.4 %collective-permute-start.10 = (f32[16,1152]{1,0:T(8,128)S(1)}, f32[16,1152]{1,0:T(8,128)S(1)}, u32[]{:S(2)}, u32[]{:S(2)}) collective-permute-start(f32[16,1152]{1,0:T(8,128)S(1)} %add.51), channel_id=1, source_target_pairs={{0,16},{16,0},{32,48},{48,32},{64,80},{80,64},{96,112},{112,96},{1... | collective-permute-start | bytes 221192 | tf_op jit(solution)/shard_map/ppermute | solution.py:30

commit v10 on v9

--- a/solution.py
+++ b/solution.py
@@ -119,10 +119,17 @@
         grad_pad, flipped, (1, 1), "VALID", dimension_numbers=("NHWC", "IHWO", "NHWC"),
         preferred_element_type=jnp.float32,
     ).reshape(-1, in_chan)
-    partial_value = lax.conv_general_dilated(
-        padded, grad_grid, (1, 1), "VALID", dimension_numbers=("CHWN", "IHWO", "CHWN"),
-        preferred_element_type=jnp.float32,
-    ).reshape(out_chan, taps)
+    pieces = [
+        lax.dot_general(
+            grad_pre,
+            window(padded, tap_row, tap_col, tile_rows, tile_cols),
+            (((0,), (0,)), ((), ())),
+            preferred_element_type=jnp.float32,
+        )
+        for tap_row in range(3)
+        for tap_col in range(3)
+    ]
+    partial_value = jnp.stack(pieces, axis=1).reshape(out_chan, taps)
     core_sum = halve_sum(partial_value, "row", core_bit, 1)
     col_sum = scatter_sum(core_sum, "col")
     row_piece = double_sum(col_sum, "row", [1 << 3, 3 << 3, 1 << 1, 3 << 1])

time: 146 us -> 151 us (1.034)
  the two profiles are of different devices: /device:TPU:97 before, /device:TPU:65 now
where the time goes in v10:
time: 151 us; the launch traced here: 150 us
  blocking collectives  59.6 us (39%)
  starting transfers between devices  50.8 us (34%)
  local copies, waits for them, and re-layouts  14.5 us (10%)
  matrix products  8.24 us (5%)
  waiting for transfers between devices  7.97 us (5%)
  other arithmetic  7.38 us (5%)
    all_to_all x1, blocking collectives, scatter_sum(): return lax.all_to_all(blocks, axis, 0, 0, tiled=False).sum(0)  35.9 us
    ppermute x7, starting transfers between devices, exchange(): return lax.ppermute(value, axis, pairs)  35.8 us
    all_to_all x1, blocking collectives, gather_chunks(): return lax.all_to_all(copies, axis, 0, 0, tiled=False)  23.7 us
    ppermute x2, starting transfers between devices, padded_2(): after = lax.ppermute(initial, axis, down)  10.4 us
    unnamed x37, local copies, waits for them, and re-layouts  8.15 us
    ppermute x7, waiting for transfers between devices, exchange(): return lax.ppermute(value, axis, pairs)  5.39 us
    ppermute x2, starting transfers between devices, padded_2(): before = lax.ppermute(last, axis, up)  4.57 us
    dot_general x9, matrix products, on_device(): lax.dot_general(grad_pre, window(padded, tap_row, tap_col, tile_rows, til...  3.81 us
  transfers between devices with their start and end apart: 11, of which 5 were waited for; matrix products, arithmetic and copies ran while one was open for 6% of the time, Pallas kernels for 0%

profile of v10, /device:TPU:65, one launch (start us, length us, event | category | flops | bytes accessed | tf_op | source)
XLA Modules:
  0.0 149.7 jit_solution(14286047789201784957)
XLA Ops:
  0.6 1.0 copy.51
  1.6 0.1 reshape.626
  1.8 23.7 %all_to_all.10 = bf16[16,16,1152]{2,1,0:T(8,128)(2,1)S(1)} all-to-all(bf16[16,16,1152]{2,1,0:T(8,128)(2,1)S(1)} %broadcast_in_dim.2), channel_id=1, replica_groups=mesh['row'=32,'col'=16] {'col'}, dimensions={0} | all-to-all | bytes 1179648 | tf_op jit(solution)/shard_map/all_to_all | solution.py:36
  25.5 2.8 %collective-permute-start.2 = (bf16[16,16,1152]{2,1,0:T(8,128)(2,1)S(1)}, bf16[16,16,1152]{2,1,0:T(8,128)(2,1)S(1)}, u32[]{:S(2)}, u32[]{:S(2)}) collective-permute-start(bf16[16,16,1152]{2,1,0:T(8,128)(2,1)S(1)} %all_to_all.10), channel_id=1, source_target_pairs={{0,16},{16,0},{32,48},{48,32},{64,80},{80,64},{96,112},{112,96},{1... | collective-permute-start | bytes 1769480 | tf_op jit(solution)/shard_map/ppermute | solution.py:30
  28.3 0.3 copy.45
  28.6 0.2 fusion.90
  28.8 2.2 %collective-permute-start = (bf16[1,1,128,256]{3,1,2,0:T(2,128)(2,1)S(1)}, bf16[1,1,128,256]{3,1,2,0:T(2,128)(2,1)S(1)}, u32[]{:S(2)}, u32[]{:S(2)}) collective-permute-start(bf16[1,1,128,256]{3,1,2,0:T(2,128)(2,1)S(1)} %get-tuple-element.19), channel_id=1, source_target_pairs={{0,1},{1,2},{2,3},{3,4},{4,5},{5,6},{6,7},{7,8},{8,9},{9,10},{10,1... | collective-permute-start | bytes 196616 | tf_op jit(solution)/shard_map/ppermute | solution.py:20
  31.0 5.2 %collective-permute-start.1 = (bf16[1,1,128,256]{3,1,2,0:T(2,128)(2,1)S(1)}, bf16[1,1,128,256]{3,1,2,0:T(2,128)(2,1)S(1)}, u32[]{:S(2)}, u32[]{:S(2)}) collective-permute-start(bf16[1,1,128,256]{3,1,2,0:T(2,128)(2,1)S(1)} %get-tuple-element.20), channel_id=1, source_target_pairs={{1,0},{2,1},{3,2},{4,3},{5,4},{6,5},{7,6},{8,7},{9,8},{10,9},{11,1... | collective-permute-start | bytes 196616 | tf_op jit(solution)/shard_map/ppermute | solution.py:21
  36.2 1.7 %collective-permute-done = bf16[1,1,128,256]{3,1,2,0:T(2,128)(2,1)S(1)} collective-permute-done((bf16[1,1,128,256]{3,1,2,0:T(2,128)(2,1)S(1)}, bf16[1,1,128,256]{3,1,2,0:T(2,128)(2,1)S(1)}, u32[]{:S(2)}, u32[]{:S(2)}) %collective-permute-start) | collective-permute-done | bytes 65568 | tf_op jit(solution)/shard_map/ppermute | solution.py:20
  37.9 0.9 collective-permute-done.1
  38.8 0.7 pad_maximum_fusion
  39.5 0.1 pad.6
  39.7 0.2 copy.50
  39.9 0.8 copy-done.8
  40.7 0.2 copy-done.2
  40.9 1.5 %fusion.3 = bf16[2304,256]{0,1:T(8,128)(2,1)S(1)} fusion(bf16[256,1152]{1,0:T(8,128)(2,1)S(1)} %bitcast.145, bf16[256,1152]{1,0:T(8,128)(2,1)} %bitcast.150, pred[]{:T(512)S(6)} %eq.8), kind=kLoop, calls=%fused_computation.8 | loop fusion | flops 5308416 | bytes 2359297 | tf_op jit(solution)/shard_map/transpose | solution.py:106
  42.5 1.4 copy.52
  43.9 3.0 %convolution_select_fusion.1 = f32[8,8,17,256]{3,1,2,0:T(8,128)S(1)} fusion(bf16[3,3,256,256]{3,2,1,0:T(8,128)(2,1)} %bitcast.153, bf16[10,1,7,2,256]{4,2,3,0,1:T(8,128)(2,1)S(1)} %slice.60, bf16[10,1,8,17,256]{4,2,3,0,1:T(8,128)(2,1)} %copy-done.8, pred[8,17]{0,1:T(8,128)(4,1)S(1)} %copy-done.13), kind=kOutput, calls=%fused_computation.5 | convolution fusion | flops 1286070272 | bytes 3061896 | tf_op jit(solution)/shard_map/conv_general_dilated | solution.py:110
  46.9 0.4 copy.53
  47.3 0.2 slice_reduce_fusion
  47.5 0.4 multiply_reduce_fusion.1
  47.9 0.4 copy-done.9
  48.3 2.4 %fusion.86 = (f32[8,128]{0,1:T(8,128)S(1)}, f32[8,128]{0,1:T(8,128)S(1)}, f32[1,8,128,256]{3,1,2,0:T(8,128)S(1)}, bf16[1,8,128,256]{3,1,2,0:T(8,128)(2,1)}) fusion(f32[8,128]{0,1:T(8,128)S(1)} %add_rsqrt_fusion, f32[8,128]{0,1:T(8,128)S(1)} %broadcast_multiply_fusion.2, f32[8,1,136,256]{3,0,2,1:T(8,128)S(1)} %bitcast.143, f32[256]{0:T(256)S(1)} %copy-done.12, ...), kind=kLoop, calls=%fused_computation.117 | loop fusion | flops 4978688 | bytes 3163136 | tf_op jit(solution)/shard_map/reduce_sum | solution.py:86
  50.7 0.7 multiply_convert_fusion
  51.5 0.4 fusion.13
  51.8 0.7 copy-done.1
  52.5 0.4 fusion.12
  53.0 0.4 fusion.11
  53.4 0.4 fusion.10
  53.8 0.2 copy-done.6
  54.0 0.5 fusion.9
  54.5 0.4 fusion.8
  55.0 0.4 fusion.7
  55.4 0.5 fusion.6
  55.9 0.4 fusion.5
  56.3 1.2 fusion.88
  57.5 0.4 copy.74
  57.9 1.6 %copy.75 = f32[256,1152]{1,0:T(8,128)S(1)} copy(f32[256,1152]{0,1:T(8,128)} %get-tuple-element.13) | data formatting | bytes 2359296
  59.5 0.1 broadcast_select_fusion
  59.6 3.0 %collective-permute-start.5 = (f32[256,1152]{1,0:T(8,128)S(1)}, f32[256,1152]{1,0:T(8,128)S(1)}, u32[]{:S(2)}, u32[]{:S(2)}) collective-permute-start(f32[256,1152]{1,0:T(8,128)S(1)} %broadcast_select_fusion), channel_id=1, source_target_pairs={{0,16},{16,0},{32,48},{48,32},{64,80},{80,64},{96,112},{112,96},{1... | collective-permute-start | bytes 3538952 | tf_op jit(solution)/shard_map/ppermute | solution.py:30
  62.7 2.5 %collective-permute-done.5 = f32[256,1152]{1,0:T(8,128)S(1)} collective-permute-done((f32[256,1152]{1,0:T(8,128)S(1)}, f32[256,1152]{1,0:T(8,128)S(1)}, u32[]{:S(2)}, u32[]{:S(2)}) %collective-permute-start.5) | collective-permute-done | bytes 1179680 | tf_op jit(solution)/shard_map/ppermute | solution.py:30
  65.1 0.2 select_add_fusion
  65.3 35.9 %all_to_all.11 = f32[16,16,1152]{2,1,0:T(8,128)S(1)} all-to-all(f32[16,16,1152]{2,1,0:T(8,128)S(1)} %bitcast.146), channel_id=1, replica_groups=mesh['row'=32,'col'=16] {'col'}, dimensions={0} | all-to-all | bytes 2359296 | tf_op jit(solution)/shard_map/all_to_all | solution.py:42
  101.2 3.3 %collective-permute-start.6 = (f32[16,1152]{1,0:T(8,128)S(1)}, f32[16,1152]{1,0:T(8,128)S(1)}, u32[]{:S(2)}, u32[]{:S(2)}) collective-permute-start(f32[16,1152]{1,0:T(8,128)S(1)} %reduce_sum.49), channel_id=1, source_target_pairs={{0,128},{16,144},{32,160},{48,176},{64,192},{80,208},{96,224},{112... | collective-permute-start | bytes 221192 | tf_op jit(solution)/shard_map/ppermute | solution.py:30
  104.5 0.2 fusion.89
  104.7 2.4 %collective-permute-start.3 = (bf16[1,1,128,256]{3,1,2,0:T(2,128)(2,1)S(1)}, bf16[1,1,128,256]{3,1,2,0:T(2,128)(2,1)S(1)}, u32[]{:S(2)}, u32[]{:S(2)}) collective-permute-start(bf16[1,1,128,256]{3,1,2,0:T(2,128)(2,1)S(1)} %get-tuple-element.17), channel_id=1, source_target_pairs={{0,1},{1,2},{2,3},{3,4},{4,5},{5,6},{6,7},{7,8},{8,9},{9,10},{10,1... | collective-permute-start | bytes 196616 | tf_op jit(solution)/shard_map/ppermute | solution.py:20
  107.1 5.2 %collective-permute-start.4 = (bf16[1,1,128,256]{3,1,2,0:T(2,128)(2,1)S(1)}, bf16[1,1,128,256]{3,1,2,0:T(2,128)(2,1)S(1)}, u32[]{:S(2)}, u32[]{:S(2)}) collective-permute-start(bf16[1,1,128,256]{3,1,2,0:T(2,128)(2,1)S(1)} %get-tuple-element.18), channel_id=1, source_target_pairs={{1,0},{2,1},{3,2},{4,3},{5,4},{6,5},{7,6},{8,7},{9,8},{10,9},{11,1... | collective-permute-start | bytes 196616 | tf_op jit(solution)/shard_map/ppermute | solution.py:21
  112.3 3.7 %collective-permute-start.7 = (f32[16,1152]{1,0:T(8,128)S(1)}, f32[16,1152]{1,0:T(8,128)S(1)}, u32[]{:S(2)}, u32[]{:S(2)}) collective-permute-start(f32[16,1152]{1,0:T(8,128)S(1)} %add.68), channel_id=1, source_target_pairs={{0,384},{16,400},{32,416},{48,432},{64,448},{80,464},{96,480},{112... | collective-permute-start | bytes 221192 | tf_op jit(solution)/shard_map/ppermute | solution.py:30
  116.0 0.3 maximum_select_fusion.1
  116.3 1.9 %select_n.51 = bf16[256,3,3,256]{3,2,1,0:T(4,128)(2,1)} reshape(bf16[16,16,2304]{2,1,0:T(8,128)(2,1)S(1)} %maximum_select_fusion.1) | data formatting | bytes 2359296 | tf_op jit(solution)/shard_map/jit(_where)/select_n | solution.py:51
  118.3 0.9 copy.65
  119.2 8.8 %collective-permute-start.8 = (f32[16,1152]{1,0:T(8,128)S(1)}, f32[16,1152]{1,0:T(8,128)S(1)}, u32[]{:S(2)}, u32[]{:S(2)}) collective-permute-start(f32[16,1152]{1,0:T(8,128)S(1)} %add.69), channel_id=1, source_target_pairs={{0,32},{16,48},{32,0},{48,16},{64,96},{80,112},{96,64},{112,80},{1... | collective-permute-start | bytes 221192 | tf_op jit(solution)/shard_map/ppermute | solution.py:30
  128.0 0.7 maximum_bitcast_fusion
  128.7 0.1 pad.8
  128.9 0.2 copy.57
  129.1 1.8 %collective-permute-done.8 = f32[16,1152]{1,0:T(8,128)S(1)} collective-permute-done((f32[16,1152]{1,0:T(8,128)S(1)}, f32[16,1152]{1,0:T(8,128)S(1)}, u32[]{:S(2)}, u32[]{:S(2)}) %collective-permute-start.8) | collective-permute-done | bytes 73760 | tf_op jit(solution)/shard_map/ppermute | solution.py:30
  130.9 8.7 %collective-permute-start.9 = (f32[16,1152]{1,0:T(8,128)S(1)}, f32[16,1152]{1,0:T(8,128)S(1)}, u32[]{:S(2)}, u32[]{:S(2)}) collective-permute-start(f32[16,1152]{1,0:T(8,128)S(1)} %add.70), channel_id=1, source_target_pairs={{0,96},{16,112},{32,64},{48,80},{64,32},{80,48},{96,0},{112,16},{1... | collective-permute-start | bytes 221192 | tf_op jit(solution)/shard_map/ppermute | solution.py:30
  139.7 1.5 fusion.2
  141.1 0.1 copy.59
  141.2 1.2 collective-permute-done.9
  142.4 5.5 %collective-permute-start.10 = (f32[16,1152]{1,0:T(8,128)S(1)}, f32[16,1152]{1,0:T(8,128)S(1)}, u32[]{:S(2)}, u32[]{:S(2)}) collective-permute-start(f32[16,1152]{1,0:T(8,128)S(1)} %add.71), channel_id=1, source_target_pairs={{0,16},{16,0},{32,48},{48,32},{64,80},{80,64},{96,112},{112,96},{1... | collective-permute-start | bytes 221192 | tf_op jit(solution)/shard_map/ppermute | solution.py:30
  148.0 0.9 copy.66
  148.9 0.1 reshape.640
  149.0 0.7 copy.67
  (45 shorter events, 0.4 us)
Async XLA Ops:
  0.6 27.7 %copy-start.5 = (bf16[1,8,128,256]{3,2,1,0:T(8,128)(2,1)S(1)}, bf16[1,8,128,256]{3,2,1,0:T(8,128)(2,1)}, u32[]{:S(2)}) copy-start(bf16[1,8,128,256]{3,2,1,0:T(8,128)(2,1)} %param.4) | copy-start | bytes 1572868
  25.5 14.4 %collective-permute-start.2 = (bf16[16,16,1152]{2,1,0:T(8,128)(2,1)S(1)}, bf16[16,16,1152]{2,1,0:T(8,128)(2,1)S(1)}, u32[]{:S(2)}, u32[]{:S(2)}) collective-permute-start(bf16[16,16,1152]{2,1,0:T(8,128)(2,1)S(1)} %all_to_all.10), channel_id=1, source_target_pairs={{0,16},{16,0},{32,48},{48,32},{64,80},{80,64},{96,112},{112,96},{1... | collective-permute-start | bytes 1769480 | tf_op jit(solution)/shard_map/ppermute | solution.py:30
  28.6 10.9 %copy-start = (bf16[1,8,128,256]{3,1,2,0:T(8,128)(2,1)}, bf16[1,8,128,256]{3,1,2,0:T(8,128)(2,1)S(1)}, u32[]{:S(2)}) copy-start(bf16[1,8,128,256]{3,1,2,0:T(8,128)(2,1)S(1)} %copy.45) | copy-start | bytes 1572868
  28.8 9.1 %collective-permute-start = (bf16[1,1,128,256]{3,1,2,0:T(2,128)(2,1)S(1)}, bf16[1,1,128,256]{3,1,2,0:T(2,128)(2,1)S(1)}, u32[]{:S(2)}, u32[]{:S(2)}) collective-permute-start(bf16[1,1,128,256]{3,1,2,0:T(2,128)(2,1)S(1)} %get-tuple-element.19), channel_id=1, source_target_pairs={{0,1},{1,2},{2,3},{3,4},{4,5},{5,6},{6,7},{7,8},{8,9},{9,10},{10,1... | collective-permute-start | bytes 196616 | tf_op jit(solution)/shard_map/ppermute | solution.py:20
  31.0 7.8 %collective-permute-start.1 = (bf16[1,1,128,256]{3,1,2,0:T(2,128)(2,1)S(1)}, bf16[1,1,128,256]{3,1,2,0:T(2,128)(2,1)S(1)}, u32[]{:S(2)}, u32[]{:S(2)}) collective-permute-start(bf16[1,1,128,256]{3,1,2,0:T(2,128)(2,1)S(1)} %get-tuple-element.20), channel_id=1, source_target_pairs={{1,0},{2,1},{3,2},{4,3},{5,4},{6,5},{7,6},{8,7},{9,8},{10,9},{11,1... | collective-permute-start | bytes 196616 | tf_op jit(solution)/shard_map/ppermute | solution.py:21
  37.9 1.7 %copy-start.10 = (bf16[1,1,128,256]{3,1,2,0:T(2,128)(2,1)}, bf16[1,1,128,256]{3,1,2,0:T(2,128)(2,1)S(1)}, u32[]{:S(2)}) copy-start(bf16[1,1,128,256]{3,1,2,0:T(2,128)(2,1)S(1)} %collective-permute-done) | copy-start | bytes 196612
  39.9 0.9 copy-start.8
  39.9 1.0 copy-start.2
  42.5 1.4 copy-start.13
  47.2 1.0 copy-start.9
  47.2 1.0 copy-start.12
  51.5 1.0 copy-start.1
  51.5 1.1 copy-start.11
  53.0 1.0 copy-start.6
  59.6 5.5 %collective-permute-start.5 = (f32[256,1152]{1,0:T(8,128)S(1)}, f32[256,1152]{1,0:T(8,128)S(1)}, u32[]{:S(2)}, u32[]{:S(2)}) collective-permute-start(f32[256,1152]{1,0:T(8,128)S(1)} %broadcast_select_fusion), channel_id=1, source_target_pairs={{0,16},{16,0},{32,48},{48,32},{64,80},{80,64},{96,112},{112,96},{1... | collective-permute-start | bytes 3538952 | tf_op jit(solution)/shard_map/ppermute | solution.py:30
  101.2 14.9 %copy-start.3 = (bf16[16,16,1152]{2,1,0:T(8,128)(2,1)S(1)}, bf16[16,16,1152]{2,1,0:T(8,128)(2,1)}, u32[]{:S(2)}) copy-start(bf16[16,16,1152]{2,1,0:T(8,128)(2,1)} %copy-done.2) | copy-start | bytes 1769476
  101.2 11.0 %collective-permute-start.6 = (f32[16,1152]{1,0:T(8,128)S(1)}, f32[16,1152]{1,0:T(8,128)S(1)}, u32[]{:S(2)}, u32[]{:S(2)}) collective-permute-start(f32[16,1152]{1,0:T(8,128)S(1)} %reduce_sum.49), channel_id=1, source_target_pairs={{0,128},{16,144},{32,160},{48,176},{64,192},{80,208},{96,224},{112... | collective-permute-start | bytes 221192 | tf_op jit(solution)/shard_map/ppermute | solution.py:30
  104.7 23.3 %collective-permute-start.3 = (bf16[1,1,128,256]{3,1,2,0:T(2,128)(2,1)S(1)}, bf16[1,1,128,256]{3,1,2,0:T(2,128)(2,1)S(1)}, u32[]{:S(2)}, u32[]{:S(2)}) collective-permute-start(bf16[1,1,128,256]{3,1,2,0:T(2,128)(2,1)S(1)} %get-tuple-element.17), channel_id=1, source_target_pairs={{0,1},{1,2},{2,3},{3,4},{4,5},{5,6},{6,7},{7,8},{8,9},{9,10},{10,1... | collective-permute-start | bytes 196616 | tf_op jit(solution)/shard_map/ppermute | solution.py:20
  107.1 20.9 %collective-permute-start.4 = (bf16[1,1,128,256]{3,1,2,0:T(2,128)(2,1)S(1)}, bf16[1,1,128,256]{3,1,2,0:T(2,128)(2,1)S(1)}, u32[]{:S(2)}, u32[]{:S(2)}) collective-permute-start(bf16[1,1,128,256]{3,1,2,0:T(2,128)(2,1)S(1)} %get-tuple-element.18), channel_id=1, source_target_pairs={{1,0},{2,1},{3,2},{4,3},{5,4},{6,5},{7,6},{8,7},{9,8},{10,9},{11,1... | collective-permute-start | bytes 196616 | tf_op jit(solution)/shard_map/ppermute | solution.py:21
  112.3 6.9 %collective-permute-start.7 = (f32[16,1152]{1,0:T(8,128)S(1)}, f32[16,1152]{1,0:T(8,128)S(1)}, u32[]{:S(2)}, u32[]{:S(2)}) collective-permute-start(f32[16,1152]{1,0:T(8,128)S(1)} %add.68), channel_id=1, source_target_pairs={{0,384},{16,400},{32,416},{48,432},{64,448},{80,464},{96,480},{112... | collective-permute-start | bytes 221192 | tf_op jit(solution)/shard_map/ppermute | solution.py:30
  116.3 1.9 %copy-start.4 = (bf16[1,8,128,256]{3,1,2,0:T(8,128)(2,1)S(1)}, bf16[1,8,128,256]{3,1,2,0:T(8,128)(2,1)}, u32[]{:S(2)}) copy-start(bf16[1,8,128,256]{3,1,2,0:T(8,128)(2,1)} %get-tuple-element.14) | copy-start | bytes 1572868
  119.2 11.7 %collective-permute-start.8 = (f32[16,1152]{1,0:T(8,128)S(1)}, f32[16,1152]{1,0:T(8,128)S(1)}, u32[]{:S(2)}, u32[]{:S(2)}) collective-permute-start(f32[16,1152]{1,0:T(8,128)S(1)} %add.69), channel_id=1, source_target_pairs={{0,32},{16,48},{32,0},{48,16},{64,96},{80,112},{96,64},{112,80},{1... | collective-permute-start | bytes 221192 | tf_op jit(solution)/shard_map/ppermute | solution.py:30
  128.9 10.8 %copy-start.7 = (bf16[256,3,3,256]{3,2,1,0:T(4,128)(2,1)S(1)}, bf16[256,3,3,256]{3,2,1,0:T(4,128)(2,1)}, u32[]{:S(2)}) copy-start(bf16[256,3,3,256]{3,2,1,0:T(4,128)(2,1)} %select_n.51) | copy-start | bytes 3538948
  128.9 10.8 %copy-start.14 = (pred[8,17]{0,1:T(8,128)(4,1)S(1)}, pred[8,17]{0,1:T(8,128)(4,1)}, u32[]{:S(2)}) copy-start(pred[8,17]{0,1:T(8,128)(4,1)} %constant.46) | copy-start | bytes 412
  130.9 11.5 %collective-permute-start.9 = (f32[16,1152]{1,0:T(8,128)S(1)}, f32[16,1152]{1,0:T(8,128)S(1)}, u32[]{:S(2)}, u32[]{:S(2)}) collective-permute-start(f32[16,1152]{1,0:T(8,128)S(1)} %add.70), channel_id=1, source_target_pairs={{0,96},{16,112},{32,64},{48,80},{64,32},{80,48},{96,0},{112,16},{1... | collective-permute-start | bytes 221192 | tf_op jit(solution)/shard_map/ppermute | solution.py:30
  142.4 6.4 %collective-permute-start.10 = (f32[16,1152]{1,0:T(8,128)S(1)}, f32[16,1152]{1,0:T(8,128)S(1)}, u32[]{:S(2)}, u32[]{:S(2)}) collective-permute-start(f32[16,1152]{1,0:T(8,128)S(1)} %add.71), channel_id=1, source_target_pairs={{0,16},{16,0},{32,48},{48,32},{64,80},{80,64},{96,112},{112,96},{1... | collective-permute-start | bytes 221192 | tf_op jit(solution)/shard_map/ppermute | solution.py:30

commit v11 on v6

--- a/solution.py
+++ b/solution.py
@@ -101,19 +101,16 @@
     local_t = weight.reshape(taps, share).T
     core_bit = [0]
     half_t, _ = split_pair(local_t, (lax.axis_index("row") & 1) == 1, 1)
+    rimmed = padded_2(images, (("col", 1),), 1)
+    rimmed, half_t = lax.optimization_barrier((rimmed, half_t))
     kernel_t = double_join(gather_chunks(half_t, "col"), "row", core_bit, 2).reshape(-1, taps)
     out_chan = kernel_t.shape[0]
     whole_kernel = kernel_t.T.reshape(3, 3, in_chan, out_chan)
-    rimmed = padded_2(images, (("col", 1),), 1)
     padded = jnp.pad(rimmed, ((0, 0), (0, 0), (1, 1), (0, 0)))
-    conv_out = jnp.zeros((img_count * tile_rows * tile_cols, out_chan), jnp.float32)
-    for tap_row in range(3):
-        for tap_col in range(3):
-            conv_out = conv_out + jnp.dot(
-                window(padded, tap_row, tap_col, tile_rows, tile_cols),
-                whole_kernel[tap_row, tap_col],
-                preferred_element_type=jnp.float32,
-            )
+    conv_out = lax.conv_general_dilated(
+        padded, whole_kernel, (1, 1), "VALID", dimension_numbers=("NHWC", "HWIO", "NHWC"),
+        preferred_element_type=jnp.float32,
+    ).reshape(-1, out_chan)
     outputs, grad_pre = norm_act(conv_out, cotangent.reshape(-1, out_chan), norm_gain)
     grad_grid = grad_pre.reshape(img_count, tile_rows, tile_cols, out_chan)
     grad_rimmed = padded_2(grad_grid, (("col", 1),), 1)

time: 140 us -> 152 us (1.086)
  blocking collectives: 0 us -> 22.9 us
  waiting for transfers between devices: 38.3 us -> 30.4 us
  starting transfers between devices: 65.1 us -> 58 us
  other arithmetic: 6.32 us -> 8.92 us
  local copies, waits for them, and re-layouts: 14.5 us -> 16.7 us
    all_to_all x0 -> x1, blocking collectives: none -> 22.9 us  [gather_chunks(): return lax.all_to_all(copies, axis, 0, 0, tiled=False)]
    all_to_all x1 -> x0, waiting for transfers between devices: 8.48 us -> none  [gather_chunks(): return lax.all_to_all(copies, axis, 0, 0, tiled=False)]
    all_to_all x1 -> x0, starting transfers between devices: 7.64 us -> none  [gather_chunks(): return lax.all_to_all(copies, axis, 0, 0, tiled=False)]
    dot_general x9 -> x0, matrix products: 4.22 us -> none  [on_device(): jnp.dot(window(padded, tap_row, tap_col, tile_rows, tile_cols), whole_ker...]
    conv_general_dilated x0 -> x1, matrix products: none -> 2.96 us  [on_device(): lax.conv_general_dilated(padded, whole_kernel, (1, 1), 'VALID', dimension...]
    unnamed x34 -> x28, local copies, waits for them, and re-layouts: 8.78 us -> 10.2 us
  transfers between devices with their start and end apart: 13 -> 12, of which waited for: 7 -> 9; matrix products, arithmetic and copies ran while one was open for 7% -> 8% of each run, Pallas kernels for 0% -> 0%
where the time goes in v11:
time: 152 us; the launch traced here: 151 us
  starting transfers between devices  58 us (38%)
  waiting for transfers between devices  30.4 us (20%)
  blocking collectives  22.9 us (15%)
  local copies, waits for them, and re-layouts  16.7 us (11%)
  matrix products  12.6 us (8%)
  other arithmetic  8.92 us (6%)
    ppermute x7, starting transfers between devices, exchange(): return lax.ppermute(value, axis, pairs)  37.7 us
    all_to_all x1, blocking collectives, gather_chunks(): return lax.all_to_all(copies, axis, 0, 0, tiled=False)  22.9 us
    ppermute x2, waiting for transfers between devices, padded_2(): before = lax.ppermute(last, axis, up)  22.7 us
    unnamed x28, local copies, waits for them, and re-layouts  10.2 us
    ppermute x2, starting transfers between devices, padded_2(): after = lax.ppermute(initial, axis, down)  8.66 us
    ppermute x7, waiting for transfers between devices, exchange(): return lax.ppermute(value, axis, pairs)  6.71 us
    ppermute x2, starting transfers between devices, padded_2(): before = lax.ppermute(last, axis, up)  6.3 us
    dot_general x9, matrix products, on_device(): lax.dot_general(window(grad_pad, 2 - tap_row, 2 - tap_col, tile_rows, til...  6.2 us
  transfers between devices with their start and end apart: 12, of which 9 were waited for; matrix products, arithmetic and copies ran while one was open for 8% of the time, Pallas kernels for 0%

profile of v11, /device:TPU:65, one launch (start us, length us, event | category | flops | bytes accessed | tf_op | source)
XLA Modules:
  0.0 150.7 jit_solution(5949295153130060796)
XLA Ops:
  0.6 1.4 copy.33
  2.2 3.2 %collective-permute-start = (bf16[1,1,128,256]{3,1,2,0:T(2,128)(2,1)S(1)}, bf16[1,1,128,256]{3,1,2,0:T(2,128)(2,1)S(1)}, u32[]{:S(2)}, u32[]{:S(2)}) collective-permute-start(bf16[1,1,128,256]{3,1,2,0:T(2,128)(2,1)S(1)} %get-tuple-element.29), channel_id=1, source_target_pairs={{0,1},{1,2},{2,3},{3,4},{4,5},{5,6},{6,7},{7,8},{8,9},{9,10},{10,1... | collective-permute-start | bytes 196616 | tf_op jit(solution)/shard_map/ppermute | solution.py:20
  5.4 4.2 %collective-permute-start.1 = (bf16[1,1,128,256]{3,1,2,0:T(2,128)(2,1)S(1)}, bf16[1,1,128,256]{3,1,2,0:T(2,128)(2,1)S(1)}, u32[]{:S(2)}, u32[]{:S(2)}) collective-permute-start(bf16[1,1,128,256]{3,1,2,0:T(2,128)(2,1)S(1)} %get-tuple-element.30), channel_id=1, source_target_pairs={{1,0},{2,1},{3,2},{4,3},{5,4},{6,5},{7,6},{8,7},{9,8},{10,9},{11,1... | collective-permute-start | bytes 196616 | tf_op jit(solution)/shard_map/ppermute | solution.py:21
  9.8 0.8 collective-permute-done
  10.6 1.0 collective-permute-done.1
  11.5 0.7 pad_maximum_fusion
  12.3 22.9 %all_to_all.10 = bf16[16,16,1152]{2,1,0:T(8,128)(2,1)S(1)} all-to-all(bf16[16,16,1152]{2,1,0:T(8,128)(2,1)S(1)} %broadcast_in_dim.2), channel_id=1, replica_groups=mesh['row'=32,'col'=16] {'col'}, dimensions={0} | all-to-all | bytes 1179648 | tf_op jit(solution)/shard_map/all_to_all | solution.py:36
  35.2 3.8 %collective-permute-start.2 = (bf16[16,16,1152]{2,1,0:T(8,128)(2,1)S(1)}, bf16[16,16,1152]{2,1,0:T(8,128)(2,1)S(1)}, u32[]{:S(2)}, u32[]{:S(2)}) collective-permute-start(bf16[16,16,1152]{2,1,0:T(8,128)(2,1)S(1)} %all_to_all.10), channel_id=1, source_target_pairs={{0,16},{16,0},{32,48},{48,32},{64,80},{80,64},{96,112},{112,96},{1... | collective-permute-start | bytes 1769480 | tf_op jit(solution)/shard_map/ppermute | solution.py:30
  39.1 0.2 copy.39
  39.4 1.2 collective-permute-done.2
  40.6 0.3 fusion.6
  40.9 0.6 copy.40
  41.6 3.0 %convolution_select_fusion = f32[8,8,17,256]{3,1,2,0:T(8,128)S(1)} fusion(bf16[3,3,256,256]{3,2,1,0:T(8,128)(2,1)S(1)} %bitcast.185, bf16[10,1,7,2,256]{4,2,3,0,1:T(8,128)(2,1)S(1)} %slice.133, bf16[10,1,8,17,256]{4,2,3,0,1:T(8,128)(2,1)} %copy-done.6, pred[8,17]{0,1:T(8,128)(4,1)S(1)} %copy-done.10), kind=kOutput, calls=%fused_computation.14 | convolution fusion | flops 1286070272 | bytes 3061896 | tf_op jit(solution)/shard_map/conv_general_dilated | solution.py:110
  44.6 0.4 copy.41
  45.2 0.4 multiply_reduce_fusion.1
  45.6 0.4 copy-done.7
  46.0 1.8 %fusion.77 = (f32[8,128]{0,1:T(8,128)S(1)}, f32[8,128]{0,1:T(8,128)S(1)}, f32[1,8,128,256]{3,1,2,0:T(8,128)S(1)}, bf16[1,8,128,256]{3,1,2,0:T(8,128)(2,1)S(1)}) fusion(f32[8,128]{0,1:T(8,128)S(1)} %add_rsqrt_fusion, f32[8,128]{0,1:T(8,128)S(1)} %broadcast_multiply_fusion.2, f32[8,1,136,256]{3,0,2,1:T(8,128)S(1)} %bitcast.182, f32[256]{0:T(256)S(1)} %copy-done.9, ...), kind=kLoop, calls=%fused_computation.126 | loop fusion | flops 4978688 | bytes 3163136 | tf_op jit(solution)/shard_map/reduce_sum | solution.py:86
  47.8 0.7 multiply_convert_fusion
  48.5 0.4 fusion.15
  48.9 0.3 fusion.14
  49.3 0.4 fusion.13
  49.6 0.4 fusion.12
  50.0 0.4 fusion.11
  50.4 0.4 fusion.10
  50.8 0.4 fusion.9
  51.2 0.4 fusion.8
  51.6 0.4 fusion.7
  52.0 1.6 %fusion.79 = (f32[256,1152]{0,1:T(8,128)}, f32[256,1152]{0,1:T(8,128)}) fusion(f32[256,2304]{0,1:T(8,128)S(1)} %bitcast.196), kind=kLoop, calls=%fused_computation.127 | loop fusion | bytes 4718592 | tf_op jit(solution)/shard_map/split | solution.py:46
  53.6 1.6 %copy.59 = f32[256,1152]{1,0:T(8,128)S(1)} copy(f32[256,1152]{0,1:T(8,128)} %get-tuple-element.16) | data formatting | bytes 2359296
  55.3 2.7 %copy.60 = f32[256,1152]{1,0:T(8,128)} copy(f32[256,1152]{0,1:T(8,128)} %get-tuple-element.17) | data formatting | bytes 2359296
  57.9 1.5 broadcast_select_fusion
  59.4 1.9 %collective-permute-start.5 = (f32[256,1152]{1,0:T(8,128)S(1)}, f32[256,1152]{1,0:T(8,128)S(1)}, u32[]{:S(2)}, u32[]{:S(2)}) collective-permute-start(f32[256,1152]{1,0:T(8,128)S(1)} %broadcast_select_fusion), channel_id=1, source_target_pairs={{0,16},{16,0},{32,48},{48,32},{64,80},{80,64},{96,112},{112,96},{1... | collective-permute-start | bytes 3538952 | tf_op jit(solution)/shard_map/ppermute | solution.py:30
  61.3 2.8 %collective-permute-done.5 = f32[256,1152]{1,0:T(8,128)S(1)} collective-permute-done((f32[256,1152]{1,0:T(8,128)S(1)}, f32[256,1152]{1,0:T(8,128)S(1)}, u32[]{:S(2)}, u32[]{:S(2)}) %collective-permute-start.5) | collective-permute-done | bytes 1179680 | tf_op jit(solution)/shard_map/ppermute | solution.py:30
  64.2 1.2 select_add_fusion
  65.4 5.3 %all-to-all-start.1 = ((f32[16,16,1152]{2,1,0:T(8,128)}), f32[16,16,1152]{2,1,0:T(8,128)S(1)}, u32[]{:S(2)}, u32[]{:S(2)}) async-start(f32[16,16,1152]{2,1,0:T(8,128)} %bitcast.184), calls=%async_computation.1 | async-start | bytes 2359296 | tf_op jit(solution)/shard_map/all_to_all | solution.py:42
  70.8 3.1 %collective-permute-start.3 = (bf16[1,1,128,256]{3,1,2,0:T(2,128)(2,1)S(1)}, bf16[1,1,128,256]{3,1,2,0:T(2,128)(2,1)S(1)}, u32[]{:S(2)}, u32[]{:S(2)}) collective-permute-start(bf16[1,1,128,256]{3,1,2,0:T(2,128)(2,1)S(1)} %get-tuple-element.27), channel_id=1, source_target_pairs={{0,1},{1,2},{2,3},{3,4},{4,5},{5,6},{6,7},{7,8},{8,9},{9,10},{10,1... | collective-permute-start | bytes 196616 | tf_op jit(solution)/shard_map/ppermute | solution.py:20
  74.0 4.5 %collective-permute-start.4 = (bf16[1,1,128,256]{3,1,2,0:T(2,128)(2,1)S(1)}, bf16[1,1,128,256]{3,1,2,0:T(2,128)(2,1)S(1)}, u32[]{:S(2)}, u32[]{:S(2)}) collective-permute-start(bf16[1,1,128,256]{3,1,2,0:T(2,128)(2,1)S(1)} %get-tuple-element.28), channel_id=1, source_target_pairs={{1,0},{2,1},{3,2},{4,3},{5,4},{6,5},{7,6},{8,7},{9,8},{10,9},{11,1... | collective-permute-start | bytes 196616 | tf_op jit(solution)/shard_map/ppermute | solution.py:21
  78.4 0.9 copy.47
  79.3 0.9 copy.54
  80.2 21.9 %collective-permute-done.3 = bf16[1,1,128,256]{3,1,2,0:T(2,128)(2,1)S(1)} collective-permute-done((bf16[1,1,128,256]{3,1,2,0:T(2,128)(2,1)S(1)}, bf16[1,1,128,256]{3,1,2,0:T(2,128)(2,1)S(1)}, u32[]{:S(2)}, u32[]{:S(2)}) %collective-permute-start.3) | collective-permute-done | bytes 65568 | tf_op jit(solution)/shard_map/ppermute | solution.py:20
  102.2 1.3 pad_maximum_fusion.1
  103.6 0.7 fusion.17
  104.3 1.3 fusion.80
  105.9 1.0 copy-done.2
  106.9 0.3 fusion.67
  107.2 0.3 convolution_add_fusion.7
  107.6 0.3 convolution_add_fusion.6
  107.9 1.3 convolution_add_fusion.5
  109.3 3.1 %collective-permute-start.6 = (f32[16,1152]{1,0:T(8,128)S(1)}, f32[16,1152]{1,0:T(8,128)S(1)}, u32[]{:S(2)}, u32[]{:S(2)}) collective-permute-start(f32[16,1152]{1,0:T(8,128)S(1)} %reduce_sum.49), channel_id=1, source_target_pairs={{0,128},{16,144},{32,160},{48,176},{64,192},{80,208},{96,224},{112... | collective-permute-start | bytes 221192 | tf_op jit(solution)/shard_map/ppermute | solution.py:30
  112.4 1.8 %convolution_add_fusion.4 = f32[1024,256]{1,0:T(8,128)S(1)} fusion(f32[1024,256]{1,0:T(8,128)} %convolution_add_fusion.5, bf16[1024,256]{1,0:T(8,128)(2,1)} %bitcast.200, bf16[3,3,256,256]{3,2,1,0:T(8,128)(2,1)S(1)} %bitcast.190), kind=kOutput, calls=%fused_computation.10 | convolution fusion | flops 134479872 | bytes 2752512 | tf_op jit(solution)/shard_map/dot_general | solution.py:122
  114.4 4.4 %collective-permute-start.7 = (f32[16,1152]{1,0:T(8,128)S(1)}, f32[16,1152]{1,0:T(8,128)S(1)}, u32[]{:S(2)}, u32[]{:S(2)}) collective-permute-start(f32[16,1152]{1,0:T(8,128)S(1)} %add.102), channel_id=1, source_target_pairs={{0,384},{16,400},{32,416},{48,432},{64,448},{80,464},{96,480},{112... | collective-permute-start | bytes 221192 | tf_op jit(solution)/shard_map/ppermute | solution.py:30
  118.8 0.3 convolution_add_fusion.3
  119.1 0.7 copy-done.4
  119.9 0.8 collective-permute-done.7
  120.7 8.8 %collective-permute-start.8 = (f32[16,1152]{1,0:T(8,128)S(1)}, f32[16,1152]{1,0:T(8,128)S(1)}, u32[]{:S(2)}, u32[]{:S(2)}) collective-permute-start(f32[16,1152]{1,0:T(8,128)S(1)} %add.103), channel_id=1, source_target_pairs={{0,32},{16,48},{32,0},{48,16},{64,96},{80,112},{96,64},{112,80},{1... | collective-permute-start | bytes 221192 | tf_op jit(solution)/shard_map/ppermute | solution.py:30
  129.6 0.3 convolution_add_fusion.2
  129.9 0.7 copy-done.3
  130.7 0.6 collective-permute-done.8
  131.3 8.2 %collective-permute-start.9 = (f32[16,1152]{1,0:T(8,128)S(1)}, f32[16,1152]{1,0:T(8,128)S(1)}, u32[]{:S(2)}, u32[]{:S(2)}) collective-permute-start(f32[16,1152]{1,0:T(8,128)S(1)} %add.104), channel_id=1, source_target_pairs={{0,96},{16,112},{32,64},{48,80},{64,32},{80,48},{96,0},{112,16},{1... | collective-permute-start | bytes 221192 | tf_op jit(solution)/shard_map/ppermute | solution.py:30
  139.5 0.3 convolution_add_fusion.1
  139.9 1.3 collective-permute-done.9
  141.2 7.5 %collective-permute-start.10 = (f32[16,1152]{1,0:T(8,128)S(1)}, f32[16,1152]{1,0:T(8,128)S(1)}, u32[]{:S(2)}, u32[]{:S(2)}) collective-permute-start(f32[16,1152]{1,0:T(8,128)S(1)} %add.105), channel_id=1, source_target_pairs={{0,16},{16,0},{32,48},{48,32},{64,80},{80,64},{96,112},{112,96},{1... | collective-permute-start | bytes 221192 | tf_op jit(solution)/shard_map/ppermute | solution.py:30
  148.7 1.1 fusion.2
  150.0 0.7 copy.55
  (49 shorter events, 2.1 us)
Async XLA Ops:
  0.6 9.0 %copy-start.8 = (bf16[3,3,256,16]{2,3,1,0:T(8,128)(2,1)S(1)}, bf16[3,3,256,16]{2,3,1,0:T(8,128)(2,1)}, u32[]{:S(2)}) copy-start(bf16[3,3,256,16]{2,3,1,0:T(8,128)(2,1)} %param.5) | copy-start | bytes 221188
  2.2 8.4 %collective-permute-start = (bf16[1,1,128,256]{3,1,2,0:T(2,128)(2,1)S(1)}, bf16[1,1,128,256]{3,1,2,0:T(2,128)(2,1)S(1)}, u32[]{:S(2)}, u32[]{:S(2)}) collective-permute-start(bf16[1,1,128,256]{3,1,2,0:T(2,128)(2,1)S(1)} %get-tuple-element.29), channel_id=1, source_target_pairs={{0,1},{1,2},{2,3},{3,4},{4,5},{5,6},{6,7},{7,8},{8,9},{9,10},{10,1... | collective-permute-start | bytes 196616 | tf_op jit(solution)/shard_map/ppermute | solution.py:20
  5.4 6.1 %collective-permute-start.1 = (bf16[1,1,128,256]{3,1,2,0:T(2,128)(2,1)S(1)}, bf16[1,1,128,256]{3,1,2,0:T(2,128)(2,1)S(1)}, u32[]{:S(2)}, u32[]{:S(2)}) collective-permute-start(bf16[1,1,128,256]{3,1,2,0:T(2,128)(2,1)S(1)} %get-tuple-element.30), channel_id=1, source_target_pairs={{1,0},{2,1},{3,2},{4,3},{5,4},{6,5},{7,6},{8,7},{9,8},{10,9},{11,1... | collective-permute-start | bytes 196616 | tf_op jit(solution)/shard_map/ppermute | solution.py:21
  35.2 5.4 %collective-permute-start.2 = (bf16[16,16,1152]{2,1,0:T(8,128)(2,1)S(1)}, bf16[16,16,1152]{2,1,0:T(8,128)(2,1)S(1)}, u32[]{:S(2)}, u32[]{:S(2)}) collective-permute-start(bf16[16,16,1152]{2,1,0:T(8,128)(2,1)S(1)} %all_to_all.10), channel_id=1, source_target_pairs={{0,16},{16,0},{32,48},{48,32},{64,80},{80,64},{96,112},{112,96},{1... | collective-permute-start | bytes 1769480 | tf_op jit(solution)/shard_map/ppermute | solution.py:30
  39.4 1.3 copy-start.6
  40.9 0.7 copy-start.10
  41.5 3.0 %copy-start.1 = (bf16[2304,256]{1,0:T(8,128)(2,1)}, bf16[2304,256]{1,0:T(8,128)(2,1)S(1)}, u32[]{:S(2)}) copy-start(bf16[2304,256]{1,0:T(8,128)(2,1)S(1)} %copy.40) | copy-start | bytes 3538948
  44.9 1.0 copy-start.7
  44.9 1.0 copy-start.9
  57.9 6.2 %copy-start = (f32[256,1152]{1,0:T(8,128)S(1)}, f32[256,1152]{1,0:T(8,128)}, u32[]{:S(2)}) copy-start(f32[256,1152]{1,0:T(8,128)} %copy.60) | copy-start | bytes 3538948
  59.4 4.7 %collective-permute-start.5 = (f32[256,1152]{1,0:T(8,128)S(1)}, f32[256,1152]{1,0:T(8,128)S(1)}, u32[]{:S(2)}, u32[]{:S(2)}) collective-permute-start(f32[256,1152]{1,0:T(8,128)S(1)} %broadcast_select_fusion), channel_id=1, source_target_pairs={{0,16},{16,0},{32,48},{48,32},{64,80},{80,64},{96,112},{112,96},{1... | collective-permute-start | bytes 3538952 | tf_op jit(solution)/shard_map/ppermute | solution.py:30
  65.4 43.9 %all-to-all-start.1 = ((f32[16,16,1152]{2,1,0:T(8,128)}), f32[16,16,1152]{2,1,0:T(8,128)S(1)}, u32[]{:S(2)}, u32[]{:S(2)}) async-start(f32[16,16,1152]{2,1,0:T(8,128)} %bitcast.184), calls=%async_computation.1 | async-start | bytes 2359296 | tf_op jit(solution)/shard_map/all_to_all | solution.py:42
  70.8 31.3 %collective-permute-start.3 = (bf16[1,1,128,256]{3,1,2,0:T(2,128)(2,1)S(1)}, bf16[1,1,128,256]{3,1,2,0:T(2,128)(2,1)S(1)}, u32[]{:S(2)}, u32[]{:S(2)}) collective-permute-start(bf16[1,1,128,256]{3,1,2,0:T(2,128)(2,1)S(1)} %get-tuple-element.27), channel_id=1, source_target_pairs={{0,1},{1,2},{2,3},{3,4},{4,5},{5,6},{6,7},{7,8},{8,9},{9,10},{10,1... | collective-permute-start | bytes 196616 | tf_op jit(solution)/shard_map/ppermute | solution.py:20
  74.0 28.2 %collective-permute-start.4 = (bf16[1,1,128,256]{3,1,2,0:T(2,128)(2,1)S(1)}, bf16[1,1,128,256]{3,1,2,0:T(2,128)(2,1)S(1)}, u32[]{:S(2)}, u32[]{:S(2)}) collective-permute-start(bf16[1,1,128,256]{3,1,2,0:T(2,128)(2,1)S(1)} %get-tuple-element.28), channel_id=1, source_target_pairs={{1,0},{2,1},{3,2},{4,3},{5,4},{6,5},{7,6},{8,7},{9,8},{10,9},{11,1... | collective-permute-start | bytes 196616 | tf_op jit(solution)/shard_map/ppermute | solution.py:21
  105.6 1.3 copy-start.2
  109.3 5.1 %collective-permute-start.6 = (f32[16,1152]{1,0:T(8,128)S(1)}, f32[16,1152]{1,0:T(8,128)S(1)}, u32[]{:S(2)}, u32[]{:S(2)}) collective-permute-start(f32[16,1152]{1,0:T(8,128)S(1)} %reduce_sum.49), channel_id=1, source_target_pairs={{0,128},{16,144},{32,160},{48,176},{64,192},{80,208},{96,224},{112... | collective-permute-start | bytes 221192 | tf_op jit(solution)/shard_map/ppermute | solution.py:30
  112.4 1.8 %copy-start.5 = (bf16[1,8,128,256]{3,1,2,0:T(8,128)(2,1)S(1)}, bf16[1,8,128,256]{3,1,2,0:T(8,128)(2,1)}, u32[]{:S(2)}) copy-start(bf16[1,8,128,256]{3,1,2,0:T(8,128)(2,1)} %get-tuple-element.21) | copy-start | bytes 1572868
  114.4 6.3 %collective-permute-start.7 = (f32[16,1152]{1,0:T(8,128)S(1)}, f32[16,1152]{1,0:T(8,128)S(1)}, u32[]{:S(2)}, u32[]{:S(2)}) collective-permute-start(f32[16,1152]{1,0:T(8,128)S(1)} %add.102), channel_id=1, source_target_pairs={{0,384},{16,400},{32,416},{48,432},{64,448},{80,464},{96,480},{112... | collective-permute-start | bytes 221192 | tf_op jit(solution)/shard_map/ppermute | solution.py:30
  118.8 1.0 copy-start.4
  120.7 10.6 %collective-permute-start.8 = (f32[16,1152]{1,0:T(8,128)S(1)}, f32[16,1152]{1,0:T(8,128)S(1)}, u32[]{:S(2)}, u32[]{:S(2)}) collective-permute-start(f32[16,1152]{1,0:T(8,128)S(1)} %add.103), channel_id=1, source_target_pairs={{0,32},{16,48},{32,0},{48,16},{64,96},{80,112},{96,64},{112,80},{1... | collective-permute-start | bytes 221192 | tf_op jit(solution)/shard_map/ppermute | solution.py:30
  129.6 1.0 copy-start.3
  131.3 9.9 %collective-permute-start.9 = (f32[16,1152]{1,0:T(8,128)S(1)}, f32[16,1152]{1,0:T(8,128)S(1)}, u32[]{:S(2)}, u32[]{:S(2)}) collective-permute-start(f32[16,1152]{1,0:T(8,128)S(1)} %add.104), channel_id=1, source_target_pairs={{0,96},{16,112},{32,64},{48,80},{64,32},{80,48},{96,0},{112,16},{1... | collective-permute-start | bytes 221192 | tf_op jit(solution)/shard_map/ppermute | solution.py:30
  141.2 8.6 %collective-permute-start.10 = (f32[16,1152]{1,0:T(8,128)S(1)}, f32[16,1152]{1,0:T(8,128)S(1)}, u32[]{:S(2)}, u32[]{:S(2)}) collective-permute-start(f32[16,1152]{1,0:T(8,128)S(1)} %add.105), channel_id=1, source_target_pairs={{0,16},{16,0},{32,48},{48,32},{64,80},{80,64},{96,112},{112,96},{1... | collective-permute-start | bytes 221192 | tf_op jit(solution)/shard_map/ppermute | solution.py:30

commit v12 on v6

--- a/solution.py
+++ b/solution.py
@@ -139,7 +139,7 @@
     partial_value = jnp.stack(pieces, axis=1).reshape(out_chan, taps)
     core_sum = halve_sum(partial_value, "row", core_bit, 1)
     col_sum = scatter_sum(core_sum, "col")
-    row_piece = double_sum(col_sum, "row", [1 << 3, 3 << 3, 1 << 1, 3 << 1])
+    row_piece = double_sum(col_sum, "row", [1 << 1, 3 << 1, 1 << 3, 3 << 3])
     own_share = double_join(row_piece, "row", core_bit, 1)
     pixels = img_count * lax.axis_size("row") * tile_rows * lax.axis_size("col") * tile_cols
     weight_grad = (own_share * (1.0 / math.sqrt(pixels))).T.reshape(3, 3, in_chan, share)

time: 140 us -> 139 us (level)
  the two profiles are of different devices: /device:TPU:65 before, /device:TPU:71 now
where the time goes in v12:
time: 139 us; the launch traced here: 138 us
  starting transfers between devices  61.8 us (44%)
  waiting for transfers between devices  41.2 us (30%)
  local copies, waits for them, and re-layouts  14.5 us (10%)
  matrix products  13.3 us (10%)
  other arithmetic  6.32 us (5%)
    ppermute x7, starting transfers between devices, exchange(): return lax.ppermute(value, axis, pairs)  34.6 us
    ppermute x2, waiting for transfers between devices, padded_2(): before = lax.ppermute(last, axis, up)  22.3 us
    ppermute x7, waiting for transfers between devices, exchange(): return lax.ppermute(value, axis, pairs)  10.4 us
    unnamed x34, local copies, waits for them, and re-layouts  8.78 us
    ppermute x2, starting transfers between devices, padded_2(): after = lax.ppermute(initial, axis, down)  8.6 us
    all_to_all x1, waiting for transfers between devices, gather_chunks(): return lax.all_to_all(copies, axis, 0, 0, tiled=False)  8.5 us
    all_to_all x1, starting transfers between devices, gather_chunks(): return lax.all_to_all(copies, axis, 0, 0, tiled=False)  7.64 us
    ppermute x2, starting transfers between devices, padded_2(): before = lax.ppermute(last, axis, up)  6.18 us
  transfers between devices with their start and end apart: 13, of which 7 were waited for; matrix products, arithmetic and copies ran while one was open for 7% of the time, Pallas kernels for 0%

profile of v12, /device:TPU:71, one launch (start us, length us, event | category | flops | bytes accessed | tf_op | source)
XLA Modules:
  0.0 138.3 jit_solution(5212752127655685927)
XLA Ops:
  0.6 1.0 copy.14
  1.8 0.9 broadcast_in_dim.2
  2.6 7.6 %all-to-all-start = ((bf16[16,16,1152]{2,1,0:T(8,128)(2,1)}), bf16[16,16,1152]{2,1,0:T(8,128)(2,1)S(1)}, u32[]{:S(2)}, u32[]{:S(2)}) async-start(bf16[16,16,1152]{2,1,0:T(8,128)(2,1)} %broadcast_in_dim.2), calls=%async_computation | async-start | bytes 1179648 | tf_op jit(solution)/shard_map/all_to_all | solution.py:36
  10.3 3.1 %collective-permute-start = (bf16[1,1,128,256]{3,2,1,0:T(8,128)(2,1)S(1)}, bf16[1,1,128,256]{3,2,1,0:T(8,128)(2,1)S(1)}, u32[]{:S(2)}, u32[]{:S(2)}) collective-permute-start(bf16[1,1,128,256]{3,2,1,0:T(8,128)(2,1)S(1)} %get-tuple-element.33), channel_id=1, source_target_pairs={{0,1},{1,2},{2,3},{3,4},{4,5},{5,6},{6,7},{7,8},{8,9},{9,10},{10,1... | collective-permute-start | bytes 196616 | tf_op jit(solution)/shard_map/ppermute | solution.py:20
  13.4 4.3 %collective-permute-start.1 = (bf16[1,1,128,256]{3,2,1,0:T(8,128)(2,1)S(1)}, bf16[1,1,128,256]{3,2,1,0:T(8,128)(2,1)S(1)}, u32[]{:S(2)}, u32[]{:S(2)}) collective-permute-start(bf16[1,1,128,256]{3,2,1,0:T(8,128)(2,1)S(1)} %get-tuple-element.34), channel_id=1, source_target_pairs={{1,0},{2,1},{3,2},{4,3},{5,4},{6,5},{7,6},{8,7},{9,8},{10,9},{11,1... | collective-permute-start | bytes 196616 | tf_op jit(solution)/shard_map/ppermute | solution.py:21
  17.7 8.5 %all-to-all-done = bf16[16,16,1152]{2,1,0:T(8,128)(2,1)S(1)} async-done(((bf16[16,16,1152]{2,1,0:T(8,128)(2,1)}), bf16[16,16,1152]{2,1,0:T(8,128)(2,1)S(1)}, u32[]{:S(2)}, u32[]{:S(2)}) %all-to-all-start) | async-done | bytes 589856 | tf_op jit(solution)/shard_map/all_to_all | solution.py:36
  26.2 3.3 %collective-permute-start.2 = (bf16[16,16,1152]{2,1,0:T(8,128)(2,1)S(1)}, bf16[16,16,1152]{2,1,0:T(8,128)(2,1)S(1)}, u32[]{:S(2)}, u32[]{:S(2)}) collective-permute-start(bf16[16,16,1152]{2,1,0:T(8,128)(2,1)S(1)} %all-to-all-done), channel_id=1, source_target_pairs={{0,16},{16,0},{32,48},{48,32},{64,80},{80,64},{96,112},{112,96},{1... | collective-permute-start | bytes 1769480 | tf_op jit(solution)/shard_map/ppermute | solution.py:30
  29.8 1.1 pad_maximum_fusion.2
  30.8 1.6 %fusion.36 = (bf16[1,8,128,256]{3,2,1,0:T(8,128)(2,1)}, bf16[1,8,128,256]{3,2,1,0:T(8,128)(2,1)}, bf16[1,8,128,256]{3,2,1,0:T(8,128)(2,1)}, bf16[1,8,128,256]{3,...) fusion(bf16[1,10,130,256]{3,2,1,0:T(8,128)(2,1)S(1)} %select_maximum_fusion.2), kind=kLoop, calls=%fused_computation.91 | loop fusion | bytes 6291456 | tf_op jit(solution)/shard_map/slice | solution.py:93
  32.7 0.6 copy.15
  33.3 1.8 %fusion.27 = f32[1024,256]{1,0:T(8,128)S(1)} fusion(bf16[1024,256]{1,0:T(8,128)(2,1)} %bitcast.186, bf16[3,3,256,256]{3,2,1,0:T(8,128)(2,1)S(1)} %bitcast.159), kind=kOutput, calls=%fused_computation.78 | convolution fusion | flops 134217728 | bytes 1703936 | tf_op jit(solution)/shard_map/dot_general | solution.py:112
  35.4 0.7 copy-done.3
  36.4 0.3 fusion.31
  36.7 0.7 copy-done.9
  37.5 0.3 convolution_add_fusion.10
  37.8 0.7 copy-done.7
  38.8 0.7 copy-done.6
  39.6 0.3 convolution_add_fusion.8
  39.9 0.3 fusion.3
  40.2 0.7 copy-done.8
  40.9 0.4 fusion.39
  41.3 0.4 multiply_reduce_fusion.1
  41.7 0.6 copy-done.13
  42.4 1.9 %fusion.32 = (f32[1024]{0:T(1024)S(1)}, f32[1024]{0:T(1024)S(1)}, f32[1024,256]{1,0:T(8,128)S(1)}, bf16[1024,256]{1,0:T(8,128)(2,1)}) fusion(f32[1024]{0:T(1024)S(1)} %add_rsqrt_fusion, f32[1024,256]{1,0:T(8,128)S(1)} %get-tuple-element.36, f32[1024]{0:T(1024)S(1)} %broadcast_multiply_fusion.2, f32[256]{0:T(256)S(1)} %copy-done.14, ...), kind=kLoop, calls=%fused_computation.88 | loop fusion | flops 4978688 | bytes 3163136 | tf_op jit(solution)/shard_map/reduce_sum | solution.py:86
  44.3 0.8 multiply_convert_fusion
  45.3 0.3 fusion.16
  45.7 0.3 fusion.15
  46.0 0.3 fusion.14
  46.4 0.3 fusion.13
  46.7 0.3 fusion.12
  47.1 0.3 fusion.11
  47.4 0.3 fusion.10
  47.8 0.3 fusion.9
  48.2 0.3 fusion.8
  48.5 1.2 fusion.34
  49.7 0.4 copy.21
  50.0 1.6 %copy.22 = f32[256,1152]{1,0:T(8,128)S(1)} copy(f32[256,1152]{0,1:T(8,128)} %get-tuple-element.13) | data formatting | bytes 2359296
  51.8 1.9 %collective-permute-start.5 = (f32[256,1152]{1,0:T(8,128)S(1)}, f32[256,1152]{1,0:T(8,128)S(1)}, u32[]{:S(2)}, u32[]{:S(2)}) collective-permute-start(f32[256,1152]{1,0:T(8,128)S(1)} %broadcast_select_fusion), channel_id=1, source_target_pairs={{0,16},{16,0},{32,48},{48,32},{64,80},{80,64},{96,112},{112,96},{1... | collective-permute-start | bytes 3538952 | tf_op jit(solution)/shard_map/ppermute | solution.py:30
  53.7 2.8 %collective-permute-done.5 = f32[256,1152]{1,0:T(8,128)S(1)} collective-permute-done((f32[256,1152]{1,0:T(8,128)S(1)}, f32[256,1152]{1,0:T(8,128)S(1)}, u32[]{:S(2)}, u32[]{:S(2)}) %collective-permute-start.5) | collective-permute-done | bytes 1179680 | tf_op jit(solution)/shard_map/ppermute | solution.py:30
  56.6 1.2 select_add_fusion
  57.7 4.7 %all-to-all-start.1 = ((f32[16,16,1152]{2,1,0:T(8,128)}), f32[16,16,1152]{2,1,0:T(8,128)S(1)}, u32[]{:S(2)}, u32[]{:S(2)}) async-start(f32[16,16,1152]{2,1,0:T(8,128)} %bitcast.179), calls=%async_computation.1 | async-start | bytes 2359296 | tf_op jit(solution)/shard_map/all_to_all | solution.py:42
  62.5 3.1 %collective-permute-start.3 = (bf16[1,1,128,256]{3,2,1,0:T(8,128)(2,1)S(1)}, bf16[1,1,128,256]{3,2,1,0:T(8,128)(2,1)S(1)}, u32[]{:S(2)}, u32[]{:S(2)}) collective-permute-start(bf16[1,1,128,256]{3,2,1,0:T(8,128)(2,1)S(1)} %get-tuple-element.29), channel_id=1, source_target_pairs={{0,1},{1,2},{2,3},{3,4},{4,5},{5,6},{6,7},{7,8},{8,9},{9,10},{10,1... | collective-permute-start | bytes 196616 | tf_op jit(solution)/shard_map/ppermute | solution.py:20
  65.6 4.3 %collective-permute-start.4 = (bf16[1,1,128,256]{3,2,1,0:T(8,128)(2,1)S(1)}, bf16[1,1,128,256]{3,2,1,0:T(8,128)(2,1)S(1)}, u32[]{:S(2)}, u32[]{:S(2)}) collective-permute-start(bf16[1,1,128,256]{3,2,1,0:T(8,128)(2,1)S(1)} %get-tuple-element.30), channel_id=1, source_target_pairs={{1,0},{2,1},{3,2},{4,3},{5,4},{6,5},{7,6},{8,7},{9,8},{10,9},{11,1... | collective-permute-start | bytes 196616 | tf_op jit(solution)/shard_map/ppermute | solution.py:21
  69.9 22.3 %collective-permute-done.3 = bf16[1,1,128,256]{3,2,1,0:T(8,128)(2,1)S(1)} collective-permute-done((bf16[1,1,128,256]{3,2,1,0:T(8,128)(2,1)S(1)}, bf16[1,1,128,256]{3,2,1,0:T(8,128)(2,1)S(1)}, u32[]{:S(2)}, u32[]{:S(2)}) %collective-permute-start.3) | collective-permute-done | bytes 65568 | tf_op jit(solution)/shard_map/ppermute | solution.py:20
  92.4 1.3 fusion.35
  93.7 0.6 copy-done.1
  94.2 0.3 fusion.26
  94.6 0.3 convolution_add_fusion.6
  94.9 0.3 convolution_add_fusion.5
  95.2 1.3 convolution_add_fusion.4
  96.7 8.9 %collective-permute-start.6 = (f32[16,1152]{1,0:T(8,128)S(1)}, f32[16,1152]{1,0:T(8,128)S(1)}, u32[]{:S(2)}, u32[]{:S(2)}) collective-permute-start(f32[16,1152]{1,0:T(8,128)S(1)} %reduce_sum.49), channel_id=1, source_target_pairs={{0,32},{16,48},{32,0},{48,16},{64,96},{80,112},{96,64},{112,80},{1... | collective-permute-start | bytes 221192 | tf_op jit(solution)/shard_map/ppermute | solution.py:30
  105.6 1.6 %convolution_add_fusion.3 = f32[1024,256]{1,0:T(8,128)S(1)} fusion(f32[1024,256]{1,0:T(8,128)} %convolution_add_fusion.4, bf16[1024,256]{1,0:T(8,128)(2,1)S(1)} %multiply_convert_fusion, bf16[3,3,256,256]{3,2,1,0:T(8,128)(2,1)S(1)} %bitcast.172), kind=kOutput, calls=%fused_computation.12 | convolution fusion | flops 134479872 | bytes 2752512 | tf_op jit(solution)/shard_map/dot_general | solution.py:125
  107.3 8.4 %collective-permute-start.7 = (f32[16,1152]{1,0:T(8,128)S(1)}, f32[16,1152]{1,0:T(8,128)S(1)}, u32[]{:S(2)}, u32[]{:S(2)}) collective-permute-start(f32[16,1152]{1,0:T(8,128)S(1)} %add.109), channel_id=1, source_target_pairs={{0,96},{16,112},{32,64},{48,80},{64,32},{80,48},{96,0},{112,16},{1... | collective-permute-start | bytes 221192 | tf_op jit(solution)/shard_map/ppermute | solution.py:30
  115.8 0.3 convolution_add_fusion.2
  116.1 1.4 collective-permute-done.7
  117.5 2.5 %collective-permute-start.8 = (f32[16,1152]{1,0:T(8,128)S(1)}, f32[16,1152]{1,0:T(8,128)S(1)}, u32[]{:S(2)}, u32[]{:S(2)}) collective-permute-start(f32[16,1152]{1,0:T(8,128)S(1)} %add.110), channel_id=1, source_target_pairs={{0,128},{16,144},{32,160},{48,176},{64,192},{80,208},{96,224},{112... | collective-permute-start | bytes 221192 | tf_op jit(solution)/shard_map/ppermute | solution.py:30
  120.0 0.3 convolution_add_fusion.1
  120.3 2.3 %collective-permute-done.8 = f32[16,1152]{1,0:T(8,128)S(1)} collective-permute-done((f32[16,1152]{1,0:T(8,128)S(1)}, f32[16,1152]{1,0:T(8,128)S(1)}, u32[]{:S(2)}, u32[]{:S(2)}) %collective-permute-start.8) | collective-permute-done | bytes 73760 | tf_op jit(solution)/shard_map/ppermute | solution.py:30
  122.6 2.1 %collective-permute-start.9 = (f32[16,1152]{1,0:T(8,128)S(1)}, f32[16,1152]{1,0:T(8,128)S(1)}, u32[]{:S(2)}, u32[]{:S(2)}) collective-permute-start(f32[16,1152]{1,0:T(8,128)S(1)} %add.111), channel_id=1, source_target_pairs={{0,384},{16,400},{32,416},{48,432},{64,448},{80,464},{96,480},{112... | collective-permute-start | bytes 221192 | tf_op jit(solution)/shard_map/ppermute | solution.py:30
  124.7 0.3 fusion.30
  125.1 3.8 %collective-permute-done.9 = f32[16,1152]{1,0:T(8,128)S(1)} collective-permute-done((f32[16,1152]{1,0:T(8,128)S(1)}, f32[16,1152]{1,0:T(8,128)S(1)}, u32[]{:S(2)}, u32[]{:S(2)}) %collective-permute-start.9) | collective-permute-done | bytes 73760 | tf_op jit(solution)/shard_map/ppermute | solution.py:30
  128.9 7.5 %collective-permute-start.10 = (f32[16,1152]{1,0:T(8,128)S(1)}, f32[16,1152]{1,0:T(8,128)S(1)}, u32[]{:S(2)}, u32[]{:S(2)}) collective-permute-start(f32[16,1152]{1,0:T(8,128)S(1)} %add.112), channel_id=1, source_target_pairs={{0,16},{16,0},{32,48},{48,32},{64,80},{80,64},{96,112},{112,96},{1... | collective-permute-start | bytes 221192 | tf_op jit(solution)/shard_map/ppermute | solution.py:30
  136.4 1.1 fusion.6
  137.6 0.7 copy.19
  (52 shorter events, 2.5 us)
Async XLA Ops:
  0.6 9.7 %copy-start.2 = (bf16[1,8,128,256]{3,2,1,0:T(8,128)(2,1)S(1)}, bf16[1,8,128,256]{3,2,1,0:T(8,128)(2,1)}, u32[]{:S(2)}) copy-start(bf16[1,8,128,256]{3,2,1,0:T(8,128)(2,1)} %param.4) | copy-start | bytes 1572868
  2.6 23.6 %all-to-all-start = ((bf16[16,16,1152]{2,1,0:T(8,128)(2,1)}), bf16[16,16,1152]{2,1,0:T(8,128)(2,1)S(1)}, u32[]{:S(2)}, u32[]{:S(2)}) async-start(bf16[16,16,1152]{2,1,0:T(8,128)(2,1)} %broadcast_in_dim.2), calls=%async_computation | async-start | bytes 1179648 | tf_op jit(solution)/shard_map/all_to_all | solution.py:36
  10.3 19.2 %collective-permute-start = (bf16[1,1,128,256]{3,2,1,0:T(8,128)(2,1)S(1)}, bf16[1,1,128,256]{3,2,1,0:T(8,128)(2,1)S(1)}, u32[]{:S(2)}, u32[]{:S(2)}) collective-permute-start(bf16[1,1,128,256]{3,2,1,0:T(8,128)(2,1)S(1)} %get-tuple-element.33), channel_id=1, source_target_pairs={{0,1},{1,2},{2,3},{3,4},{4,5},{5,6},{6,7},{7,8},{8,9},{9,10},{10,1... | collective-permute-start | bytes 196616 | tf_op jit(solution)/shard_map/ppermute | solution.py:20
  13.4 16.2 %collective-permute-start.1 = (bf16[1,1,128,256]{3,2,1,0:T(8,128)(2,1)S(1)}, bf16[1,1,128,256]{3,2,1,0:T(8,128)(2,1)S(1)}, u32[]{:S(2)}, u32[]{:S(2)}) collective-permute-start(bf16[1,1,128,256]{3,2,1,0:T(8,128)(2,1)S(1)} %get-tuple-element.34), channel_id=1, source_target_pairs={{1,0},{2,1},{3,2},{4,3},{5,4},{6,5},{7,6},{8,7},{9,8},{10,9},{11,1... | collective-permute-start | bytes 196616 | tf_op jit(solution)/shard_map/ppermute | solution.py:21
  26.2 6.2 %collective-permute-start.2 = (bf16[16,16,1152]{2,1,0:T(8,128)(2,1)S(1)}, bf16[16,16,1152]{2,1,0:T(8,128)(2,1)S(1)}, u32[]{:S(2)}, u32[]{:S(2)}) collective-permute-start(bf16[16,16,1152]{2,1,0:T(8,128)(2,1)S(1)} %all-to-all-done), channel_id=1, source_target_pairs={{0,16},{16,0},{32,48},{48,32},{64,80},{80,64},{96,112},{112,96},{1... | collective-permute-start | bytes 1769480 | tf_op jit(solution)/shard_map/ppermute | solution.py:30
  33.3 6.9 %copy-start = (bf16[2304,256]{1,0:T(8,128)(2,1)}, bf16[2304,256]{1,0:T(8,128)(2,1)S(1)}, u32[]{:S(2)}) copy-start(bf16[2304,256]{1,0:T(8,128)(2,1)S(1)} %copy.15) | copy-start | bytes 3538948
  33.3 1.8 %copy-start.4 = (bf16[1,8,128,256]{3,2,1,0:T(8,128)(2,1)S(1)}, bf16[1,8,128,256]{3,2,1,0:T(8,128)(2,1)}, u32[]{:S(2)}) copy-start(bf16[1,8,128,256]{3,2,1,0:T(8,128)(2,1)} %get-tuple-element.23) | copy-start | bytes 1572868
  35.1 1.0 copy-start.3
  36.4 1.0 copy-start.9
  37.5 1.0 copy-start.7
  38.5 1.0 copy-start.6
  39.9 1.0 copy-start.8
  40.9 0.8 copy-start.14
  41.3 1.0 copy-start.13
  44.3 1.0 copy-start.5
  51.8 4.7 %collective-permute-start.5 = (f32[256,1152]{1,0:T(8,128)S(1)}, f32[256,1152]{1,0:T(8,128)S(1)}, u32[]{:S(2)}, u32[]{:S(2)}) collective-permute-start(f32[256,1152]{1,0:T(8,128)S(1)} %broadcast_select_fusion), channel_id=1, source_target_pairs={{0,16},{16,0},{32,48},{48,32},{64,80},{80,64},{96,112},{112,96},{1... | collective-permute-start | bytes 3538952 | tf_op jit(solution)/shard_map/ppermute | solution.py:30
  57.7 38.8 %all-to-all-start.1 = ((f32[16,16,1152]{2,1,0:T(8,128)}), f32[16,16,1152]{2,1,0:T(8,128)S(1)}, u32[]{:S(2)}, u32[]{:S(2)}) async-start(f32[16,16,1152]{2,1,0:T(8,128)} %bitcast.179), calls=%async_computation.1 | async-start | bytes 2359296 | tf_op jit(solution)/shard_map/all_to_all | solution.py:42
  62.5 29.7 %collective-permute-start.3 = (bf16[1,1,128,256]{3,2,1,0:T(8,128)(2,1)S(1)}, bf16[1,1,128,256]{3,2,1,0:T(8,128)(2,1)S(1)}, u32[]{:S(2)}, u32[]{:S(2)}) collective-permute-start(bf16[1,1,128,256]{3,2,1,0:T(8,128)(2,1)S(1)} %get-tuple-element.29), channel_id=1, source_target_pairs={{0,1},{1,2},{2,3},{3,4},{4,5},{5,6},{6,7},{7,8},{8,9},{9,10},{10,1... | collective-permute-start | bytes 196616 | tf_op jit(solution)/shard_map/ppermute | solution.py:20
  65.6 26.6 %collective-permute-start.4 = (bf16[1,1,128,256]{3,2,1,0:T(8,128)(2,1)S(1)}, bf16[1,1,128,256]{3,2,1,0:T(8,128)(2,1)S(1)}, u32[]{:S(2)}, u32[]{:S(2)}) collective-permute-start(bf16[1,1,128,256]{3,2,1,0:T(8,128)(2,1)S(1)} %get-tuple-element.30), channel_id=1, source_target_pairs={{1,0},{2,1},{3,2},{4,3},{5,4},{6,5},{7,6},{8,7},{9,8},{10,9},{11,1... | collective-permute-start | bytes 196616 | tf_op jit(solution)/shard_map/ppermute | solution.py:21
  92.4 1.8 %copy-start.1 = (bf16[2304,256]{1,0:T(8,128)(2,1)S(1)}, bf16[2304,256]{1,0:T(8,128)(2,1)}, u32[]{:S(2)}) copy-start(bf16[2304,256]{1,0:T(8,128)(2,1)} %copy-done) | copy-start | bytes 3538948
  96.6 19.1 %copy-start.12 = (bf16[1,8,128,256]{3,2,1,0:T(8,128)(2,1)S(1)}, bf16[1,8,128,256]{3,2,1,0:T(8,128)(2,1)}, u32[]{:S(2)}) copy-start(bf16[1,8,128,256]{3,2,1,0:T(8,128)(2,1)} %get-tuple-element.16) | copy-start | bytes 1572868
  96.7 10.7 %collective-permute-start.6 = (f32[16,1152]{1,0:T(8,128)S(1)}, f32[16,1152]{1,0:T(8,128)S(1)}, u32[]{:S(2)}, u32[]{:S(2)}) collective-permute-start(f32[16,1152]{1,0:T(8,128)S(1)} %reduce_sum.49), channel_id=1, source_target_pairs={{0,32},{16,48},{32,0},{48,16},{64,96},{80,112},{96,64},{112,80},{1... | collective-permute-start | bytes 221192 | tf_op jit(solution)/shard_map/ppermute | solution.py:30
  107.3 10.1 %collective-permute-start.7 = (f32[16,1152]{1,0:T(8,128)S(1)}, f32[16,1152]{1,0:T(8,128)S(1)}, u32[]{:S(2)}, u32[]{:S(2)}) collective-permute-start(f32[16,1152]{1,0:T(8,128)S(1)} %add.109), channel_id=1, source_target_pairs={{0,96},{16,112},{32,64},{48,80},{64,32},{80,48},{96,0},{112,16},{1... | collective-permute-start | bytes 221192 | tf_op jit(solution)/shard_map/ppermute | solution.py:30
  115.7 4.2 %copy-start.11 = (bf16[1,8,128,256]{3,2,1,0:T(8,128)(2,1)S(1)}, bf16[1,8,128,256]{3,2,1,0:T(8,128)(2,1)}, u32[]{:S(2)}) copy-start(bf16[1,8,128,256]{3,2,1,0:T(8,128)(2,1)} %get-tuple-element.15) | copy-start | bytes 1572868
  117.5 5.1 %collective-permute-start.8 = (f32[16,1152]{1,0:T(8,128)S(1)}, f32[16,1152]{1,0:T(8,128)S(1)}, u32[]{:S(2)}, u32[]{:S(2)}) collective-permute-start(f32[16,1152]{1,0:T(8,128)S(1)} %add.110), channel_id=1, source_target_pairs={{0,128},{16,144},{32,160},{48,176},{64,192},{80,208},{96,224},{112... | collective-permute-start | bytes 221192 | tf_op jit(solution)/shard_map/ppermute | solution.py:30
  120.0 4.8 %copy-start.10 = (bf16[1,8,128,256]{3,2,1,0:T(8,128)(2,1)S(1)}, bf16[1,8,128,256]{3,2,1,0:T(8,128)(2,1)}, u32[]{:S(2)}) copy-start(bf16[1,8,128,256]{3,2,1,0:T(8,128)(2,1)} %get-tuple-element.20) | copy-start | bytes 1572868
  122.6 6.3 %collective-permute-start.9 = (f32[16,1152]{1,0:T(8,128)S(1)}, f32[16,1152]{1,0:T(8,128)S(1)}, u32[]{:S(2)}, u32[]{:S(2)}) collective-permute-start(f32[16,1152]{1,0:T(8,128)S(1)} %add.111), channel_id=1, source_target_pairs={{0,384},{16,400},{32,416},{48,432},{64,448},{80,464},{96,480},{112... | collective-permute-start | bytes 221192 | tf_op jit(solution)/shard_map/ppermute | solution.py:30
  128.9 8.6 %collective-permute-start.10 = (f32[16,1152]{1,0:T(8,128)S(1)}, f32[16,1152]{1,0:T(8,128)S(1)}, u32[]{:S(2)}, u32[]{:S(2)}) collective-permute-start(f32[16,1152]{1,0:T(8,128)S(1)} %add.112), channel_id=1, source_target_pairs={{0,16},{16,0},{32,48},{48,32},{64,80},{80,64},{96,112},{112,96},{1... | collective-permute-start | bytes 221192 | tf_op jit(solution)/shard_map/ppermute | solution.py:30

commit v13 on v12

--- a/solution.py
+++ b/solution.py
@@ -137,6 +137,7 @@
                 )
             )
     partial_value = jnp.stack(pieces, axis=1).reshape(out_chan, taps)
+    grad_pad, partial_value = lax.optimization_barrier((grad_pad, partial_value))
     core_sum = halve_sum(partial_value, "row", core_bit, 1)
     col_sum = scatter_sum(core_sum, "col")
     row_piece = double_sum(col_sum, "row", [1 << 1, 3 << 1, 1 << 3, 3 << 3])

time: 139 us -> 152 us (1.094)
  the two profiles are of different devices: /device:TPU:71 before, /device:TPU:103 now
where the time goes in v13:
time: 152 us; the launch traced here: 151 us
  starting transfers between devices  71.8 us (47%)
  waiting for transfers between devices  36.7 us (24%)
  matrix products  19.8 us (13%)
  local copies, waits for them, and re-layouts  14.4 us (9%)
  other arithmetic  7.24 us (5%)
    ppermute x7, starting transfers between devices, exchange(): return lax.ppermute(value, axis, pairs)  41.7 us
    all_to_all x1, waiting for transfers between devices, scatter_sum(): return lax.all_to_all(blocks, axis, 0, 0, tiled=False).sum(0)  19.6 us
    ppermute x7, waiting for transfers between devices, exchange(): return lax.ppermute(value, axis, pairs)  10.2 us
    ppermute x2, starting transfers between devices, padded_2(): after = lax.ppermute(initial, axis, down)  9.77 us
    dot_general x9, matrix products, on_device(): lax.dot_general(grad_pre, window(padded, tap_row, tap_col, tile_rows, til...  9.53 us
    all_to_all x1, starting transfers between devices, scatter_sum(): return lax.all_to_all(blocks, axis, 0, 0, tiled=False).sum(0)  8.18 us
    unnamed x34, local copies, waits for them, and re-layouts  7.8 us
    all_to_all x1, starting transfers between devices, gather_chunks(): return lax.all_to_all(copies, axis, 0, 0, tiled=False)  7.19 us
  transfers between devices with their start and end apart: 13, of which 8 were waited for; matrix products, arithmetic and copies ran while one was open for 7% of the time, Pallas kernels for 0%

profile of v13, /device:TPU:103, one launch (start us, length us, event | category | flops | bytes accessed | tf_op | source)
XLA Modules:
  0.0 151.0 jit_solution(3550442126524905765)
XLA Ops:
  0.6 1.0 copy.14
  1.8 0.9 broadcast_in_dim.2
  2.6 7.2 %all-to-all-start = ((bf16[16,16,1152]{2,1,0:T(8,128)(2,1)}), bf16[16,16,1152]{2,1,0:T(8,128)(2,1)S(1)}, u32[]{:S(2)}, u32[]{:S(2)}) async-start(bf16[16,16,1152]{2,1,0:T(8,128)(2,1)} %broadcast_in_dim.2), calls=%async_computation | async-start | bytes 1179648 | tf_op jit(solution)/shard_map/all_to_all | solution.py:36
  9.9 3.1 %collective-permute-start = (bf16[1,1,128,256]{3,2,1,0:T(8,128)(2,1)S(1)}, bf16[1,1,128,256]{3,2,1,0:T(8,128)(2,1)S(1)}, u32[]{:S(2)}, u32[]{:S(2)}) collective-permute-start(bf16[1,1,128,256]{3,2,1,0:T(8,128)(2,1)S(1)} %get-tuple-element.33), channel_id=1, source_target_pairs={{0,1},{1,2},{2,3},{3,4},{4,5},{5,6},{6,7},{7,8},{8,9},{9,10},{10,1... | collective-permute-start | bytes 196616 | tf_op jit(solution)/shard_map/ppermute | solution.py:20
  13.0 4.3 %collective-permute-start.1 = (bf16[1,1,128,256]{3,2,1,0:T(8,128)(2,1)S(1)}, bf16[1,1,128,256]{3,2,1,0:T(8,128)(2,1)S(1)}, u32[]{:S(2)}, u32[]{:S(2)}) collective-permute-start(bf16[1,1,128,256]{3,2,1,0:T(8,128)(2,1)S(1)} %get-tuple-element.34), channel_id=1, source_target_pairs={{1,0},{2,1},{3,2},{4,3},{5,4},{6,5},{7,6},{8,7},{9,8},{10,9},{11,1... | collective-permute-start | bytes 196616 | tf_op jit(solution)/shard_map/ppermute | solution.py:21
  17.3 6.6 %all-to-all-done = bf16[16,16,1152]{2,1,0:T(8,128)(2,1)S(1)} async-done(((bf16[16,16,1152]{2,1,0:T(8,128)(2,1)}), bf16[16,16,1152]{2,1,0:T(8,128)(2,1)S(1)}, u32[]{:S(2)}, u32[]{:S(2)}) %all-to-all-start) | async-done | bytes 589856 | tf_op jit(solution)/shard_map/all_to_all | solution.py:36
  23.9 3.7 %collective-permute-start.2 = (bf16[16,16,1152]{2,1,0:T(8,128)(2,1)S(1)}, bf16[16,16,1152]{2,1,0:T(8,128)(2,1)S(1)}, u32[]{:S(2)}, u32[]{:S(2)}) collective-permute-start(bf16[16,16,1152]{2,1,0:T(8,128)(2,1)S(1)} %all-to-all-done), channel_id=1, source_target_pairs={{0,16},{16,0},{32,48},{48,32},{64,80},{80,64},{96,112},{112,96},{1... | collective-permute-start | bytes 1769480 | tf_op jit(solution)/shard_map/ppermute | solution.py:30
  27.8 1.1 pad_maximum_fusion.2
  28.8 1.6 %fusion.35 = (bf16[1,8,128,256]{3,2,1,0:T(8,128)(2,1)}, bf16[1,8,128,256]{3,2,1,0:T(8,128)(2,1)}, bf16[1,8,128,256]{3,2,1,0:T(8,128)(2,1)}, bf16[1,8,128,256]{3,...) fusion(bf16[1,10,130,256]{3,2,1,0:T(8,128)(2,1)S(1)} %select_maximum_fusion.2), kind=kLoop, calls=%fused_computation.90 | loop fusion | bytes 6291456 | tf_op jit(solution)/shard_map/slice | solution.py:93
  30.7 0.6 copy.15
  31.3 1.8 %fusion.27 = f32[1024,256]{1,0:T(8,128)S(1)} fusion(bf16[1024,256]{1,0:T(8,128)(2,1)} %bitcast.186, bf16[3,3,256,256]{3,2,1,0:T(8,128)(2,1)S(1)} %bitcast.159), kind=kOutput, calls=%fused_computation.78 | convolution fusion | flops 134217728 | bytes 1703936 | tf_op jit(solution)/shard_map/dot_general | solution.py:112
  33.4 0.7 copy-done.4
  34.5 0.3 fusion.31
  34.8 0.7 copy-done.10
  35.5 0.3 convolution_add_fusion.10
  35.8 0.7 copy-done.8
  36.8 0.7 copy-done.7
  37.6 0.3 convolution_add_fusion.8
  37.9 0.3 fusion.3
  38.2 0.7 copy-done.9
  38.9 0.4 fusion.38
  39.4 0.4 multiply_reduce_fusion.1
  39.7 0.6 copy-done.14
  40.4 1.9 %fusion.32 = (f32[1024]{0:T(1024)S(1)}, f32[1024]{0:T(1024)S(1)}, f32[1024,256]{1,0:T(8,128)S(1)}, bf16[1024,256]{1,0:T(8,128)(2,1)}) fusion(f32[1024]{0:T(1024)S(1)} %add_rsqrt_fusion, f32[1024,256]{1,0:T(8,128)S(1)} %get-tuple-element.36, f32[1024]{0:T(1024)S(1)} %broadcast_multiply_fusion.2, f32[256]{0:T(256)S(1)} %copy-done.15, ...), kind=kLoop, calls=%fused_computation.88 | loop fusion | flops 4978688 | bytes 3163136 | tf_op jit(solution)/shard_map/reduce_sum | solution.py:86
  42.3 0.8 multiply_convert_fusion
  43.3 1.1 fusion.16
  44.4 1.1 fusion.15
  45.4 1.1 fusion.14
  46.5 1.1 fusion.13
  47.6 1.1 fusion.12
  48.6 1.1 fusion.11
  49.7 1.1 fusion.10
  50.8 1.1 fusion.9
  51.8 1.9 %collective-permute-start.3 = (bf16[1,1,128,256]{3,2,1,0:T(8,128)(2,1)S(1)}, bf16[1,1,128,256]{3,2,1,0:T(8,128)(2,1)S(1)}, u32[]{:S(2)}, u32[]{:S(2)}) collective-permute-start(bf16[1,1,128,256]{3,2,1,0:T(8,128)(2,1)S(1)} %get-tuple-element.29), channel_id=1, source_target_pairs={{0,1},{1,2},{2,3},{3,4},{4,5},{5,6},{6,7},{7,8},{8,9},{9,10},{10,1... | collective-permute-start | bytes 196616 | tf_op jit(solution)/shard_map/ppermute | solution.py:20
  53.8 5.5 %collective-permute-start.4 = (bf16[1,1,128,256]{3,2,1,0:T(8,128)(2,1)S(1)}, bf16[1,1,128,256]{3,2,1,0:T(8,128)(2,1)S(1)}, u32[]{:S(2)}, u32[]{:S(2)}) collective-permute-start(bf16[1,1,128,256]{3,2,1,0:T(8,128)(2,1)S(1)} %get-tuple-element.30), channel_id=1, source_target_pairs={{1,0},{2,1},{3,2},{4,3},{5,4},{6,5},{7,6},{8,7},{9,8},{10,9},{11,1... | collective-permute-start | bytes 196616 | tf_op jit(solution)/shard_map/ppermute | solution.py:21
  59.3 1.0 fusion.8
  60.6 1.0 select_maximum_fusion
  61.6 2.0 %copy.17 = f32[256,2304]{1,0:T(8,128)S(1)} copy(f32[256,2304]{0,1:T(8,128)} %bitcast.45) | data formatting | bytes 4718592 | tf_op jit(solution)/shard_map/optimization_barrier | solution.py:140
  63.7 3.1 %collective-permute-start.5 = (f32[256,1152]{1,0:T(8,128)S(1)}, f32[256,1152]{1,0:T(8,128)S(1)}, u32[]{:S(2)}, u32[]{:S(2)}) collective-permute-start(f32[256,1152]{1,0:T(8,128)S(1)} %slice_select_fusion), channel_id=1, source_target_pairs={{0,16},{16,0},{32,48},{48,32},{64,80},{80,64},{96,112},{112,96},{1... | collective-permute-start | bytes 3538952 | tf_op jit(solution)/shard_map/ppermute | solution.py:30
  66.8 2.5 %collective-permute-done.5 = f32[256,1152]{1,0:T(8,128)S(1)} collective-permute-done((f32[256,1152]{1,0:T(8,128)S(1)}, f32[256,1152]{1,0:T(8,128)S(1)}, u32[]{:S(2)}, u32[]{:S(2)}) %collective-permute-start.5) | collective-permute-done | bytes 1179680 | tf_op jit(solution)/shard_map/ppermute | solution.py:30
  69.3 1.3 select_add_fusion
  70.5 8.2 %all-to-all-start.1 = ((f32[16,16,1152]{2,1,0:T(8,128)}), f32[16,16,1152]{2,1,0:T(8,128)S(1)}, u32[]{:S(2)}, u32[]{:S(2)}) async-start(f32[16,16,1152]{2,1,0:T(8,128)} %bitcast.179), calls=%async_computation.1 | async-start | bytes 2359296 | tf_op jit(solution)/shard_map/all_to_all | solution.py:42
  78.8 1.0 copy-done
  79.8 1.3 fusion.34
  81.1 0.6 copy-done.2
  81.6 0.3 fusion.26
  82.0 0.3 convolution_add_fusion.6
  82.3 0.3 convolution_add_fusion.5
  82.7 1.3 convolution_add_fusion.4
  84.0 19.6 %all-to-all-done.1 = f32[16,16,1152]{2,1,0:T(8,128)S(1)} async-done(((f32[16,16,1152]{2,1,0:T(8,128)}), f32[16,16,1152]{2,1,0:T(8,128)S(1)}, u32[]{:S(2)}, u32[]{:S(2)}) %all-to-all-start.1) | async-done | bytes 1179680 | tf_op jit(solution)/shard_map/all_to_all | solution.py:42
  103.7 9.0 %collective-permute-start.6 = (f32[16,1152]{1,0:T(8,128)S(1)}, f32[16,1152]{1,0:T(8,128)S(1)}, u32[]{:S(2)}, u32[]{:S(2)}) collective-permute-start(f32[16,1152]{1,0:T(8,128)S(1)} %reduce_sum.49), channel_id=1, source_target_pairs={{0,32},{16,48},{32,0},{48,16},{64,96},{80,112},{96,64},{112,80},{1... | collective-permute-start | bytes 221192 | tf_op jit(solution)/shard_map/ppermute | solution.py:30
  112.7 1.6 %convolution_add_fusion.3 = f32[1024,256]{1,0:T(8,128)S(1)} fusion(f32[1024,256]{1,0:T(8,128)} %convolution_add_fusion.4, bf16[1024,256]{1,0:T(8,128)(2,1)S(1)} %multiply_convert_fusion, bf16[3,3,256,256]{3,2,1,0:T(8,128)(2,1)S(1)} %bitcast.172), kind=kOutput, calls=%fused_computation.12 | convolution fusion | flops 134479872 | bytes 2752512 | tf_op jit(solution)/shard_map/dot_general | solution.py:125
  114.5 8.5 %collective-permute-start.7 = (f32[16,1152]{1,0:T(8,128)S(1)}, f32[16,1152]{1,0:T(8,128)S(1)}, u32[]{:S(2)}, u32[]{:S(2)}) collective-permute-start(f32[16,1152]{1,0:T(8,128)S(1)} %add.109), channel_id=1, source_target_pairs={{0,96},{16,112},{32,64},{48,80},{64,32},{80,48},{96,0},{112,16},{1... | collective-permute-start | bytes 221192 | tf_op jit(solution)/shard_map/ppermute | solution.py:30
  123.1 0.3 convolution_add_fusion.2
  123.5 1.4 collective-permute-done.7
  124.8 2.5 %collective-permute-start.8 = (f32[16,1152]{1,0:T(8,128)S(1)}, f32[16,1152]{1,0:T(8,128)S(1)}, u32[]{:S(2)}, u32[]{:S(2)}) collective-permute-start(f32[16,1152]{1,0:T(8,128)S(1)} %add.110), channel_id=1, source_target_pairs={{0,128},{16,144},{32,160},{48,176},{64,192},{80,208},{96,224},{112... | collective-permute-start | bytes 221192 | tf_op jit(solution)/shard_map/ppermute | solution.py:30
  127.3 0.3 convolution_add_fusion.1
  127.7 2.3 %collective-permute-done.8 = f32[16,1152]{1,0:T(8,128)S(1)} collective-permute-done((f32[16,1152]{1,0:T(8,128)S(1)}, f32[16,1152]{1,0:T(8,128)S(1)}, u32[]{:S(2)}, u32[]{:S(2)}) %collective-permute-start.8) | collective-permute-done | bytes 73760 | tf_op jit(solution)/shard_map/ppermute | solution.py:30
  129.9 2.1 %collective-permute-start.9 = (f32[16,1152]{1,0:T(8,128)S(1)}, f32[16,1152]{1,0:T(8,128)S(1)}, u32[]{:S(2)}, u32[]{:S(2)}) collective-permute-start(f32[16,1152]{1,0:T(8,128)S(1)} %add.111), channel_id=1, source_target_pairs={{0,384},{16,400},{32,416},{48,432},{64,448},{80,464},{96,480},{112... | collective-permute-start | bytes 221192 | tf_op jit(solution)/shard_map/ppermute | solution.py:30
  132.1 0.3 fusion.30
  132.4 3.8 %collective-permute-done.9 = f32[16,1152]{1,0:T(8,128)S(1)} collective-permute-done((f32[16,1152]{1,0:T(8,128)S(1)}, f32[16,1152]{1,0:T(8,128)S(1)}, u32[]{:S(2)}, u32[]{:S(2)}) %collective-permute-start.9) | collective-permute-done | bytes 73760 | tf_op jit(solution)/shard_map/ppermute | solution.py:30
  136.3 12.8 %collective-permute-start.10 = (f32[16,1152]{1,0:T(8,128)S(1)}, f32[16,1152]{1,0:T(8,128)S(1)}, u32[]{:S(2)}, u32[]{:S(2)}) collective-permute-start(f32[16,1152]{1,0:T(8,128)S(1)} %add.112), channel_id=1, source_target_pairs={{0,16},{16,0},{32,48},{48,32},{64,80},{80,64},{96,112},{112,96},{1... | collective-permute-start | bytes 221192 | tf_op jit(solution)/shard_map/ppermute | solution.py:30
  149.1 1.1 fusion.6
  150.3 0.7 copy.19
  (52 shorter events, 2.6 us)
Async XLA Ops:
  0.6 9.2 %copy-start.3 = (bf16[1,8,128,256]{3,2,1,0:T(8,128)(2,1)S(1)}, bf16[1,8,128,256]{3,2,1,0:T(8,128)(2,1)}, u32[]{:S(2)}) copy-start(bf16[1,8,128,256]{3,2,1,0:T(8,128)(2,1)} %param.4) | copy-start | bytes 1572868
  2.6 21.2 %all-to-all-start = ((bf16[16,16,1152]{2,1,0:T(8,128)(2,1)}), bf16[16,16,1152]{2,1,0:T(8,128)(2,1)S(1)}, u32[]{:S(2)}, u32[]{:S(2)}) async-start(bf16[16,16,1152]{2,1,0:T(8,128)(2,1)} %broadcast_in_dim.2), calls=%async_computation | async-start | bytes 1179648 | tf_op jit(solution)/shard_map/all_to_all | solution.py:36
  9.9 17.7 %collective-permute-start = (bf16[1,1,128,256]{3,2,1,0:T(8,128)(2,1)S(1)}, bf16[1,1,128,256]{3,2,1,0:T(8,128)(2,1)S(1)}, u32[]{:S(2)}, u32[]{:S(2)}) collective-permute-start(bf16[1,1,128,256]{3,2,1,0:T(8,128)(2,1)S(1)} %get-tuple-element.33), channel_id=1, source_target_pairs={{0,1},{1,2},{2,3},{3,4},{4,5},{5,6},{6,7},{7,8},{8,9},{9,10},{10,1... | collective-permute-start | bytes 196616 | tf_op jit(solution)/shard_map/ppermute | solution.py:20
  13.0 14.6 %collective-permute-start.1 = (bf16[1,1,128,256]{3,2,1,0:T(8,128)(2,1)S(1)}, bf16[1,1,128,256]{3,2,1,0:T(8,128)(2,1)S(1)}, u32[]{:S(2)}, u32[]{:S(2)}) collective-permute-start(bf16[1,1,128,256]{3,2,1,0:T(8,128)(2,1)S(1)} %get-tuple-element.34), channel_id=1, source_target_pairs={{1,0},{2,1},{3,2},{4,3},{5,4},{6,5},{7,6},{8,7},{9,8},{10,9},{11,1... | collective-permute-start | bytes 196616 | tf_op jit(solution)/shard_map/ppermute | solution.py:21
  23.9 6.5 %collective-permute-start.2 = (bf16[16,16,1152]{2,1,0:T(8,128)(2,1)S(1)}, bf16[16,16,1152]{2,1,0:T(8,128)(2,1)S(1)}, u32[]{:S(2)}, u32[]{:S(2)}) collective-permute-start(bf16[16,16,1152]{2,1,0:T(8,128)(2,1)S(1)} %all-to-all-done), channel_id=1, source_target_pairs={{0,16},{16,0},{32,48},{48,32},{64,80},{80,64},{96,112},{112,96},{1... | collective-permute-start | bytes 1769480 | tf_op jit(solution)/shard_map/ppermute | solution.py:30
  31.3 6.9 %copy-start.1 = (bf16[2304,256]{1,0:T(8,128)(2,1)}, bf16[2304,256]{1,0:T(8,128)(2,1)S(1)}, u32[]{:S(2)}) copy-start(bf16[2304,256]{1,0:T(8,128)(2,1)S(1)} %copy.15) | copy-start | bytes 3538948
  31.3 1.8 %copy-start.5 = (bf16[1,8,128,256]{3,2,1,0:T(8,128)(2,1)S(1)}, bf16[1,8,128,256]{3,2,1,0:T(8,128)(2,1)}, u32[]{:S(2)}) copy-start(bf16[1,8,128,256]{3,2,1,0:T(8,128)(2,1)} %get-tuple-element.23) | copy-start | bytes 1572868
  33.1 1.0 copy-start.4
  34.5 1.0 copy-start.10
  35.5 1.0 copy-start.8
  36.5 1.0 copy-start.7
  37.9 1.0 copy-start.9
  38.9 0.8 copy-start.15
  39.3 1.0 copy-start.14
  42.3 1.0 copy-start.6
  51.8 8.5 %collective-permute-start.3 = (bf16[1,1,128,256]{3,2,1,0:T(8,128)(2,1)S(1)}, bf16[1,1,128,256]{3,2,1,0:T(8,128)(2,1)S(1)}, u32[]{:S(2)}, u32[]{:S(2)}) collective-permute-start(bf16[1,1,128,256]{3,2,1,0:T(8,128)(2,1)S(1)} %get-tuple-element.29), channel_id=1, source_target_pairs={{0,1},{1,2},{2,3},{3,4},{4,5},{5,6},{6,7},{7,8},{8,9},{9,10},{10,1... | collective-permute-start | bytes 196616 | tf_op jit(solution)/shard_map/ppermute | solution.py:20
  53.8 6.8 %collective-permute-start.4 = (bf16[1,1,128,256]{3,2,1,0:T(8,128)(2,1)S(1)}, bf16[1,1,128,256]{3,2,1,0:T(8,128)(2,1)S(1)}, u32[]{:S(2)}, u32[]{:S(2)}) collective-permute-start(bf16[1,1,128,256]{3,2,1,0:T(8,128)(2,1)S(1)} %get-tuple-element.30), channel_id=1, source_target_pairs={{1,0},{2,1},{3,2},{4,3},{5,4},{6,5},{7,6},{8,7},{9,8},{10,9},{11,1... | collective-permute-start | bytes 196616 | tf_op jit(solution)/shard_map/ppermute | solution.py:21
  63.7 5.5 %collective-permute-start.5 = (f32[256,1152]{1,0:T(8,128)S(1)}, f32[256,1152]{1,0:T(8,128)S(1)}, u32[]{:S(2)}, u32[]{:S(2)}) collective-permute-start(f32[256,1152]{1,0:T(8,128)S(1)} %slice_select_fusion), channel_id=1, source_target_pairs={{0,16},{16,0},{32,48},{48,32},{64,80},{80,64},{96,112},{112,96},{1... | collective-permute-start | bytes 3538952 | tf_op jit(solution)/shard_map/ppermute | solution.py:30
  70.5 33.1 %all-to-all-start.1 = ((f32[16,16,1152]{2,1,0:T(8,128)}), f32[16,16,1152]{2,1,0:T(8,128)S(1)}, u32[]{:S(2)}, u32[]{:S(2)}) async-start(f32[16,16,1152]{2,1,0:T(8,128)} %bitcast.179), calls=%async_computation.1 | async-start | bytes 2359296 | tf_op jit(solution)/shard_map/all_to_all | solution.py:42
  78.7 1.1 copy-start
  79.8 1.8 %copy-start.2 = (bf16[2304,256]{1,0:T(8,128)(2,1)S(1)}, bf16[2304,256]{1,0:T(8,128)(2,1)}, u32[]{:S(2)}) copy-start(bf16[2304,256]{1,0:T(8,128)(2,1)} %copy-done.1) | copy-start | bytes 3538948
  103.7 19.4 %copy-start.13 = (bf16[1,8,128,256]{3,2,1,0:T(8,128)(2,1)S(1)}, bf16[1,8,128,256]{3,2,1,0:T(8,128)(2,1)}, u32[]{:S(2)}) copy-start(bf16[1,8,128,256]{3,2,1,0:T(8,128)(2,1)} %get-tuple-element.17) | copy-start | bytes 1572868
  103.7 10.8 %collective-permute-start.6 = (f32[16,1152]{1,0:T(8,128)S(1)}, f32[16,1152]{1,0:T(8,128)S(1)}, u32[]{:S(2)}, u32[]{:S(2)}) collective-permute-start(f32[16,1152]{1,0:T(8,128)S(1)} %reduce_sum.49), channel_id=1, source_target_pairs={{0,32},{16,48},{32,0},{48,16},{64,96},{80,112},{96,64},{112,80},{1... | collective-permute-start | bytes 221192 | tf_op jit(solution)/shard_map/ppermute | solution.py:30
  114.5 10.3 %collective-permute-start.7 = (f32[16,1152]{1,0:T(8,128)S(1)}, f32[16,1152]{1,0:T(8,128)S(1)}, u32[]{:S(2)}, u32[]{:S(2)}) collective-permute-start(f32[16,1152]{1,0:T(8,128)S(1)} %add.109), channel_id=1, source_target_pairs={{0,96},{16,112},{32,64},{48,80},{64,32},{80,48},{96,0},{112,16},{1... | collective-permute-start | bytes 221192 | tf_op jit(solution)/shard_map/ppermute | solution.py:30
  123.1 4.2 %copy-start.12 = (bf16[1,8,128,256]{3,2,1,0:T(8,128)(2,1)S(1)}, bf16[1,8,128,256]{3,2,1,0:T(8,128)(2,1)}, u32[]{:S(2)}) copy-start(bf16[1,8,128,256]{3,2,1,0:T(8,128)(2,1)} %get-tuple-element.15) | copy-start | bytes 1572868
  124.8 5.1 %collective-permute-start.8 = (f32[16,1152]{1,0:T(8,128)S(1)}, f32[16,1152]{1,0:T(8,128)S(1)}, u32[]{:S(2)}, u32[]{:S(2)}) collective-permute-start(f32[16,1152]{1,0:T(8,128)S(1)} %add.110), channel_id=1, source_target_pairs={{0,128},{16,144},{32,160},{48,176},{64,192},{80,208},{96,224},{112... | collective-permute-start | bytes 221192 | tf_op jit(solution)/shard_map/ppermute | solution.py:30
  127.3 4.7 %copy-start.11 = (bf16[1,8,128,256]{3,2,1,0:T(8,128)(2,1)S(1)}, bf16[1,8,128,256]{3,2,1,0:T(8,128)(2,1)}, u32[]{:S(2)}) copy-start(bf16[1,8,128,256]{3,2,1,0:T(8,128)(2,1)} %get-tuple-element.16) | copy-start | bytes 1572868
  129.9 6.3 %collective-permute-start.9 = (f32[16,1152]{1,0:T(8,128)S(1)}, f32[16,1152]{1,0:T(8,128)S(1)}, u32[]{:S(2)}, u32[]{:S(2)}) collective-permute-start(f32[16,1152]{1,0:T(8,128)S(1)} %add.111), channel_id=1, source_target_pairs={{0,384},{16,400},{32,416},{48,432},{64,448},{80,464},{96,480},{112... | collective-permute-start | bytes 221192 | tf_op jit(solution)/shard_map/ppermute | solution.py:30
  136.3 14.0 %collective-permute-start.10 = (f32[16,1152]{1,0:T(8,128)S(1)}, f32[16,1152]{1,0:T(8,128)S(1)}, u32[]{:S(2)}, u32[]{:S(2)}) collective-permute-start(f32[16,1152]{1,0:T(8,128)S(1)} %add.112), channel_id=1, source_target_pairs={{0,16},{16,0},{32,48},{48,32},{64,80},{80,64},{96,112},{112,96},{1... | collective-permute-start | bytes 221192 | tf_op jit(solution)/shard_map/ppermute | solution.py:30

commit v14 on v12

--- a/solution.py
+++ b/solution.py
@@ -99,21 +99,30 @@
     img_count, tile_rows, tile_cols, in_chan = images.shape
     taps, share = 9 * in_chan, weight.shape[3]
     local_t = weight.reshape(taps, share).T
-    core_bit = [0]
-    half_t, _ = split_pair(local_t, (lax.axis_index("row") & 1) == 1, 1)
-    kernel_t = double_join(gather_chunks(half_t, "col"), "row", core_bit, 2).reshape(-1, taps)
+    lower = (lax.axis_index("row") & 1) == 0
+    own_t = gather_chunks(jnp.where(lower, local_t[: share // 2], local_t[share // 2 :]), "col")
+    mate_t = exchange(own_t, "row", 0)
+    kernel_t = jnp.where(lower, jnp.concatenate([own_t, mate_t], 1), jnp.concatenate([mate_t, own_t], 1))
+    kernel_t = kernel_t.reshape(-1, taps)
     out_chan = kernel_t.shape[0]
     whole_kernel = kernel_t.T.reshape(3, 3, in_chan, out_chan)
     rimmed = padded_2(images, (("col", 1),), 1)
     padded = jnp.pad(rimmed, ((0, 0), (0, 0), (1, 1), (0, 0)))
-    conv_out = jnp.zeros((img_count * tile_rows * tile_cols, out_chan), jnp.float32)
-    for tap_row in range(3):
-        for tap_col in range(3):
-            conv_out = conv_out + jnp.dot(
-                window(padded, tap_row, tap_col, tile_rows, tile_cols),
-                whole_kernel[tap_row, tap_col],
-                preferred_element_type=jnp.float32,
-            )
+    def conv_part(part_t):
+        part = part_t.reshape(-1, taps).T.reshape(3, 3, in_chan, -1)
+        total = jnp.zeros((img_count * tile_rows * tile_cols, part.shape[3]), jnp.float32)
+        for tap_row in range(3):
+            for tap_col in range(3):
+                total = total + jnp.dot(
+                    window(padded, tap_row, tap_col, tile_rows, tile_cols),
+                    part[tap_row, tap_col],
+                    preferred_element_type=jnp.float32,
+                )
+        return total.reshape(total.shape[0], own_t.shape[0], 1, own_t.shape[1])
+
+    conv_own, conv_mate = conv_part(own_t), conv_part(mate_t)
+    conv_out = jnp.where(lower, jnp.concatenate([conv_own, conv_mate], 2), jnp.concatenate([conv_mate, conv_own], 2))
+    conv_out = conv_out.reshape(-1, out_chan)
     outputs, grad_pre = norm_act(conv_out, cotangent.reshape(-1, out_chan), norm_gain)
     grad_grid = grad_pre.reshape(img_count, tile_rows, tile_cols, out_chan)
     grad_rimmed = padded_2(grad_grid, (("col", 1),), 1)
@@ -137,10 +146,10 @@
                 )
             )
     partial_value = jnp.stack(pieces, axis=1).reshape(out_chan, taps)
-    core_sum = halve_sum(partial_value, "row", core_bit, 1)
+    core_sum = halve_sum(partial_value, "row", [0], 1)
     col_sum = scatter_sum(core_sum, "col")
     row_piece = double_sum(col_sum, "row", [1 << 1, 3 << 1, 1 << 3, 3 << 3])
-    own_share = double_join(row_piece, "row", core_bit, 1)
+    own_share = double_join(row_piece, "row", [0], 1)
     pixels = img_count * lax.axis_size("row") * tile_rows * lax.axis_size("col") * tile_cols
     weight_grad = (own_share * (1.0 / math.sqrt(pixels))).T.reshape(3, 3, in_chan, share)
     features = outputs.reshape(img_count, tile_rows, tile_cols, out_chan)

time: 139 us -> 169 us (1.22)
  local copies, waits for them, and re-layouts: 14.5 us -> 34.8 us
  other arithmetic: 6.32 us -> 13.9 us
  matrix products: 13.3 us -> 19.5 us
  waiting for transfers between devices: 41.2 us -> 37.6 us
    slice x2 -> x10, local copies, waits for them, and re-layouts: 2.85 us -> 14.7 us  [window(): padded[:, tap_row:tap_row + tile_rows, tap_col:tap_col + tile_cols, :]]
    all_to_all x1, waiting for transfers between devices: 8.5 us -> 0.01 us  [gather_chunks(): return lax.all_to_all(copies, axis, 0, 0, tiled=False)]
    concatenate x4, other arithmetic: 1.49 us -> 8.42 us  [padded_2(): value = jnp.concatenate([before, value, after], axis=dim)]
    dot_general x9 -> x18, matrix products: 4.23 us -> 10.4 us  [conv_part(): jnp.dot(window(padded, tap_row, tap_col, tile_rows, tile_cols), part[tap_...]
    ppermute x2, waiting for transfers between devices: 22.3 us -> 27.2 us  [padded_2(): before = lax.ppermute(last, axis, up)]
    unnamed x34 -> x64, local copies, waits for them, and re-layouts: 8.78 us -> 12 us
    transpose x0 -> x2, local copies, waits for them, and re-layouts: none -> 3.21 us  [conv_part(): part = part_t.reshape(-1, taps).T.reshape(3, 3, in_chan, -1)]
  transfers between devices with their start and end apart: 13 -> 13, of which waited for: 7 -> 7; matrix products, arithmetic and copies ran while one was open for 7% -> 22% of each run, Pallas kernels for 0% -> 0%
where the time goes in v14:
time: 169 us; the launch traced here: 168 us
  starting transfers between devices  60.6 us (36%)
  waiting for transfers between devices  37.6 us (22%)
  local copies, waits for them, and re-layouts  34.8 us (21%)
  matrix products  19.5 us (12%)
  other arithmetic  13.9 us (8%)
    ppermute x7, starting transfers between devices, exchange(): return lax.ppermute(value, axis, pairs)  34.2 us
    ppermute x2, waiting for transfers between devices, padded_2(): before = lax.ppermute(last, axis, up)  27.2 us
    slice x10, local copies, waits for them, and re-layouts, window(): padded[:, tap_row:tap_row + tile_rows, tap_col:tap_col + tile_cols, :]  14.7 us
    unnamed x64, local copies, waits for them, and re-layouts  12 us
    dot_general x18, matrix products, conv_part(): jnp.dot(window(padded, tap_row, tap_col, tile_rows, tile_cols), part[tap_...  10.4 us
    ppermute x7, waiting for transfers between devices, exchange(): return lax.ppermute(value, axis, pairs)  10.3 us
    ppermute x2, starting transfers between devices, padded_2(): after = lax.ppermute(initial, axis, down)  8.82 us
    concatenate x4, other arithmetic, padded_2(): value = jnp.concatenate([before, value, after], axis=dim)  8.42 us
  transfers between devices with their start and end apart: 13, of which 7 were waited for; matrix products, arithmetic and copies ran while one was open for 22% of the time, Pallas kernels for 0%

profile of v14, /device:TPU:71, one launch (start us, length us, event | category | flops | bytes accessed | tf_op | source)
XLA Modules:
  0.0 167.8 jit_solution(13475978060235360408)
XLA Ops:
  0.6 1.0 copy.52
  1.8 0.9 broadcast_in_dim.2
  2.6 7.8 %all-to-all-start = ((bf16[16,8,2304]{2,1,0:T(8,128)(2,1)}), bf16[16,8,2304]{2,1,0:T(8,128)(2,1)S(1)}, u32[]{:S(2)}, u32[]{:S(2)}) async-start(bf16[16,8,2304]{2,1,0:T(8,128)(2,1)} %broadcast_in_dim.2), calls=%async_computation | async-start | bytes 1179648 | tf_op jit(solution)/shard_map/all_to_all | solution.py:36
  10.7 3.1 %collective-permute-start = (bf16[1,1,128,256]{2,3,1,0:T(8,128)(2,1)S(1)}, bf16[1,1,128,256]{2,3,1,0:T(8,128)(2,1)S(1)}, u32[]{:S(2)}, u32[]{:S(2)}) collective-permute-start(bf16[1,1,128,256]{2,3,1,0:T(8,128)(2,1)S(1)} %get-tuple-element.35), channel_id=1, source_target_pairs={{0,1},{1,2},{2,3},{3,4},{4,5},{5,6},{6,7},{7,8},{8,9},{9,10},{10,1... | collective-permute-start | bytes 196616 | tf_op jit(solution)/shard_map/ppermute | solution.py:20
  13.8 4.3 %collective-permute-start.1 = (bf16[1,1,128,256]{2,3,1,0:T(8,128)(2,1)S(1)}, bf16[1,1,128,256]{2,3,1,0:T(8,128)(2,1)}, u32[]{:S(2)}, u32[]{:S(2)}) collective-permute-start(bf16[1,1,128,256]{2,3,1,0:T(8,128)(2,1)S(1)} %get-tuple-element.36), channel_id=1, source_target_pairs={{1,0},{2,1},{3,2},{4,3},{5,4},{6,5},{7,6},{8,7},{9,8},{10,9},{11,1... | collective-permute-start | bytes 196616 | tf_op jit(solution)/shard_map/ppermute | solution.py:21
  18.1 1.1 copy.68
  19.2 8.5 %collective-permute-done = bf16[1,1,128,256]{2,3,1,0:T(8,128)(2,1)S(1)} collective-permute-done((bf16[1,1,128,256]{2,3,1,0:T(8,128)(2,1)S(1)}, bf16[1,1,128,256]{2,3,1,0:T(8,128)(2,1)S(1)}, u32[]{:S(2)}, u32[]{:S(2)}) %collective-permute-start) | collective-permute-done | bytes 65568 | tf_op jit(solution)/shard_map/ppermute | solution.py:20
  27.7 1.5 fusion.11
  29.2 2.0 %fusion.79 = (bf16[1,8,128,256]{2,3,1,0:T(8,128)(2,1)}, bf16[1,8,128,256]{2,3,1,0:T(8,128)(2,1)}, bf16[1,8,128,256]{2,3,1,0:T(8,128)(2,1)}, bf16[1,8,128,256]{2,...) fusion(bf16[1,10,130,256]{2,3,1,0:T(8,128)(2,1)S(1)} %fusion.11), kind=kLoop, calls=%fused_computation.161 | loop fusion | bytes 6291456 | tf_op jit(solution)/shard_map/slice | solution.py:93
  31.2 1.0 copy.51
  32.3 1.7 %pad_maximum_fusion.2 = (bf16[1,8,128,256]{2,3,1,0:T(8,128)(2,1)}, bf16[1,8,128,256]{2,3,1,0:T(8,128)(2,1)S(1)}) fusion(bf16[1,1,128,256]{2,3,1,0:T(8,128)(2,1)} %collective-permute-done.1, bf16[1,8,128,256]{2,3,1,0:T(8,128)(2,1)S(1)} %copy.48, bf16[1,1,128,256]{2,3,1,0:T(8,128)(2,1)S(1)} %collective-permute-done), kind=kLoop, calls=%fused_computation.100 | loop fusion | flops 524288 | bytes 1703936 | tf_op jit(solution)/shard_map/concatenate | solution.py:22
  34.0 1.0 copy.55
  35.0 2.1 %copy.56 = bf16[1,8,128,256]{3,2,1,0:T(8,128)(2,1)} copy(bf16[1,8,128,256]{2,3,1,0:T(8,128)(2,1)} %get-tuple-element.26) | data formatting | bytes 1048576 | tf_op jit(solution)/shard_map/slice | solution.py:93
  37.1 1.0 copy.57
  38.1 2.1 %copy.58 = bf16[1,8,128,256]{3,2,1,0:T(8,128)(2,1)} copy(bf16[1,8,128,256]{2,3,1,0:T(8,128)(2,1)} %get-tuple-element.24) | data formatting | bytes 1048576 | tf_op jit(solution)/shard_map/slice | solution.py:93
  40.2 1.2 copy.59
  41.4 1.0 copy.61
  42.5 1.2 copy.62
  43.7 1.1 copy.53
  44.8 1.5 fusion.66
  46.3 1.1 fusion.65
  47.8 0.7 copy-done.5
  49.1 0.4 copy-done.3
  49.8 3.1 %collective-permute-start.2 = (bf16[16,8,2304]{2,1,0:T(8,128)(2,1)S(1)}, bf16[16,8,2304]{2,1,0:T(8,128)(2,1)S(1)}, u32[]{:S(2)}, u32[]{:S(2)}) collective-permute-start(bf16[16,8,2304]{2,1,0:T(8,128)(2,1)S(1)} %all-to-all-done), channel_id=1, source_target_pairs={{0,16},{16,0},{32,48},{48,32},{64,80},{80,64},{96,112},{112,96},{1... | collective-permute-start | bytes 1769480 | tf_op jit(solution)/shard_map/ppermute | solution.py:30
  53.6 1.1 fusion.16
  54.7 0.8 copy-done.16
  55.5 2.2 %copy.63 = bf16[2304,128]{1,0:T(8,128)(2,1)} copy(bf16[2304,128]{0,1:T(8,128)(2,1)} %bitcast.355) | data formatting | bytes 1179648 | tf_op jit(solution)/shard_map/transpose | solution.py:112
  57.7 1.5 fusion.64
  59.2 1.1 fusion.63
  60.7 0.7 copy-done.6
  62.0 0.4 copy-done.4
  63.1 0.4 copy-done.2
  64.1 0.4 copy-done.19
  65.1 0.7 copy-done.24
  65.8 1.9 %fusion.74 = (f32[8,128]{1,0:T(8,128)S(1)}, f32[8,128]{1,0:T(8,128)S(1)}, f32[1,8,128,256]{2,1,3,0:T(8,128)S(1)}, bf16[1,8,128,256]{2,1,3,0:T(8,128)(2,1)}) fusion(f32[8,128]{1,0:T(8,128)S(1)} %rsqrt_bitcast_fusion, f32[8,128]{1,0:T(8,128)S(1)} %get-tuple-element.37, f32[32,8,8,128]{3,2,1,0:T(8,128)S(1)} %copy.87, f32[256]{0:T(256)S(1)} %copy-done.27, ...), kind=kLoop, calls=%fused_computation.157 | loop fusion | flops 4978688 | bytes 3163136 | tf_op jit(solution)/shard_map/reduce_sum | solution.py:86
  68.6 0.7 copy-done.10
  72.4 1.2 fusion.77
  73.9 1.6 copy.86
  75.7 2.0 %collective-permute-start.5 = (f32[256,1152]{1,0:T(8,128)S(1)}, f32[256,1152]{1,0:T(8,128)S(1)}, u32[]{:S(2)}, u32[]{:S(2)}) collective-permute-start(f32[256,1152]{1,0:T(8,128)S(1)} %broadcast_select_fusion), channel_id=1, source_target_pairs={{0,16},{16,0},{32,48},{48,32},{64,80},{80,64},{96,112},{112,96},{1... | collective-permute-start | bytes 3538952 | tf_op jit(solution)/shard_map/ppermute | solution.py:30
  77.7 2.8 %collective-permute-done.5 = f32[256,1152]{1,0:T(8,128)S(1)} collective-permute-done((f32[256,1152]{1,0:T(8,128)S(1)}, f32[256,1152]{1,0:T(8,128)S(1)}, u32[]{:S(2)}, u32[]{:S(2)}) %collective-permute-start.5) | collective-permute-done | bytes 1179680 | tf_op jit(solution)/shard_map/ppermute | solution.py:30
  80.4 1.2 select_add_fusion
  81.7 3.7 %all-to-all-start.1 = ((f32[16,16,1152]{2,1,0:T(8,128)}), f32[16,16,1152]{2,1,0:T(8,128)S(1)}, u32[]{:S(2)}, u32[]{:S(2)}) async-start(f32[16,16,1152]{2,1,0:T(8,128)} %bitcast.338), calls=%async_computation.1 | async-start | bytes 2359296 | tf_op jit(solution)/shard_map/all_to_all | solution.py:42
  85.4 0.9 fusion.80
  86.2 3.1 %collective-permute-start.3 = (bf16[1,1,128,256]{2,1,3,0:T(2,128)(2,1)}, bf16[1,1,128,256]{2,1,3,0:T(2,128)(2,1)}, u32[]{:S(2)}, u32[]{:S(2)}) collective-permute-start(bf16[1,1,128,256]{2,1,3,0:T(2,128)(2,1)} %get-tuple-element.31), channel_id=1, source_target_pairs={{0,1},{1,2},{2,3},{3,4},{4,5},{5,6},{6,7},{7,8},{8,9},{9,10},{10,1... | collective-permute-start | bytes 196616 | tf_op jit(solution)/shard_map/ppermute | solution.py:20
  89.3 4.5 %collective-permute-start.4 = (bf16[1,1,128,256]{2,1,3,0:T(2,128)(2,1)}, bf16[1,1,128,256]{2,1,3,0:T(2,128)(2,1)}, u32[]{:S(2)}, u32[]{:S(2)}) collective-permute-start(bf16[1,1,128,256]{2,1,3,0:T(2,128)(2,1)} %get-tuple-element.32), channel_id=1, source_target_pairs={{1,0},{2,1},{3,2},{4,3},{5,4},{6,5},{7,6},{8,7},{9,8},{10,9},{11,1... | collective-permute-start | bytes 196616 | tf_op jit(solution)/shard_map/ppermute | solution.py:21
  93.8 1.5 maximum_select_fusion
  95.4 1.4 copy.69
  96.8 1.1 copy.82
  97.9 18.7 %collective-permute-done.3 = bf16[1,1,128,256]{2,1,3,0:T(2,128)(2,1)} collective-permute-done((bf16[1,1,128,256]{2,1,3,0:T(2,128)(2,1)}, bf16[1,1,128,256]{2,1,3,0:T(2,128)(2,1)}, u32[]{:S(2)}, u32[]{:S(2)}) %collective-permute-start.3) | collective-permute-done | bytes 65568 | tf_op jit(solution)/shard_map/ppermute | solution.py:20
  116.6 2.3 %pad_maximum_fusion = (bf16[1,8,128,256]{2,1,3,0:T(8,128)(2,1)}, bf16[1,8,128,256]{2,1,3,0:T(8,128)(2,1)S(1)}) fusion(bf16[1,8,128,256]{2,1,3,0:T(8,128)(2,1)S(1)} %multiply_convert_fusion, bf16[1,1,128,256]{2,1,3,0:T(2,128)(2,1)} %collective-permute-done.3, bf16[1,1,128,256]{2,1,3,0:T(2,128)(2,1)} %collective-permute-done.4), kind=kLoop, calls=%fused_computation.98 | loop fusion | flops 2097152 | bytes 1703936 | tf_op jit(solution)/shard_map/concatenate | solution.py:22
  118.9 2.9 %fusion.6 = bf16[1,10,130,256]{2,1,3,0:T(8,128)(2,1)S(1)} fusion(bf16[1,1,128,256]{2,1,3,0:T(2,128)(2,1)} %collective-permute-done.4, bf16[1,8,128,256]{2,1,3,0:T(8,128)(2,1)S(1)} %multiply_convert_fusion, bf16[1,1,128,256]{2,1,3,0:T(2,128)(2,1)} %collective-permute-done.3), kind=kLoop, calls=%fused_computation.10 | loop fusion | flops 3993600 | bytes 1320960 | tf_op jit(solution)/shard_map/concatenate | solution.py:22
  121.9 2.0 %fusion.78 = (bf16[1,8,128,256]{2,1,3,0:T(8,128)(2,1)S(1)}, bf16[1,8,128,256]{2,1,3,0:T(8,128)(2,1)}, bf16[1,8,128,256]{2,1,3,0:T(8,128)(2,1)}, bf16[1,8,128,256...) fusion(bf16[1,10,130,256]{2,1,3,0:T(8,128)(2,1)S(1)} %fusion.6), kind=kLoop, calls=%fused_computation.160 | loop fusion | bytes 6291456 | tf_op jit(solution)/shard_map/slice | solution.py:93
  124.9 1.3 convolution_add_fusion.5
  126.3 8.8 %collective-permute-start.6 = (f32[16,1152]{1,0:T(8,128)S(1)}, f32[16,1152]{1,0:T(8,128)S(1)}, u32[]{:S(2)}, u32[]{:S(2)}) collective-permute-start(f32[16,1152]{1,0:T(8,128)S(1)} %reduce_sum.49), channel_id=1, source_target_pairs={{0,32},{16,48},{32,0},{48,16},{64,96},{80,112},{96,64},{112,80},{1... | collective-permute-start | bytes 221192 | tf_op jit(solution)/shard_map/ppermute | solution.py:30
  135.2 1.6 convolution_add_fusion.4
  136.9 8.3 %collective-permute-start.7 = (f32[16,1152]{1,0:T(8,128)S(1)}, f32[16,1152]{1,0:T(8,128)S(1)}, u32[]{:S(2)}, u32[]{:S(2)}) collective-permute-start(f32[16,1152]{1,0:T(8,128)S(1)} %add.182), channel_id=1, source_target_pairs={{0,96},{16,112},{32,64},{48,80},{64,32},{80,48},{96,0},{112,16},{1... | collective-permute-start | bytes 221192 | tf_op jit(solution)/shard_map/ppermute | solution.py:30
  145.5 1.4 collective-permute-done.7
  146.9 2.5 %collective-permute-start.8 = (f32[16,1152]{1,0:T(8,128)S(1)}, f32[16,1152]{1,0:T(8,128)S(1)}, u32[]{:S(2)}, u32[]{:S(2)}) collective-permute-start(f32[16,1152]{1,0:T(8,128)S(1)} %add.183), channel_id=1, source_target_pairs={{0,128},{16,144},{32,160},{48,176},{64,192},{80,208},{96,224},{112... | collective-permute-start | bytes 221192 | tf_op jit(solution)/shard_map/ppermute | solution.py:30
  149.7 2.3 %collective-permute-done.8 = f32[16,1152]{1,0:T(8,128)S(1)} collective-permute-done((f32[16,1152]{1,0:T(8,128)S(1)}, f32[16,1152]{1,0:T(8,128)S(1)}, u32[]{:S(2)}, u32[]{:S(2)}) %collective-permute-start.8) | collective-permute-done | bytes 73760 | tf_op jit(solution)/shard_map/ppermute | solution.py:30
  152.0 2.1 %collective-permute-start.9 = (f32[16,1152]{1,0:T(8,128)S(1)}, f32[16,1152]{1,0:T(8,128)S(1)}, u32[]{:S(2)}, u32[]{:S(2)}) collective-permute-start(f32[16,1152]{1,0:T(8,128)S(1)} %add.184), channel_id=1, source_target_pairs={{0,384},{16,400},{32,416},{48,432},{64,448},{80,464},{96,480},{112... | collective-permute-start | bytes 221192 | tf_op jit(solution)/shard_map/ppermute | solution.py:30
  154.5 3.8 %collective-permute-done.9 = f32[16,1152]{1,0:T(8,128)S(1)} collective-permute-done((f32[16,1152]{1,0:T(8,128)S(1)}, f32[16,1152]{1,0:T(8,128)S(1)}, u32[]{:S(2)}, u32[]{:S(2)}) %collective-permute-start.9) | collective-permute-done | bytes 73760 | tf_op jit(solution)/shard_map/ppermute | solution.py:30
  158.3 7.5 %collective-permute-start.10 = (f32[16,1152]{1,0:T(8,128)S(1)}, f32[16,1152]{1,0:T(8,128)S(1)}, u32[]{:S(2)}, u32[]{:S(2)}) collective-permute-start(f32[16,1152]{1,0:T(8,128)S(1)} %add.185), channel_id=1, source_target_pairs={{0,16},{16,0},{32,48},{48,32},{64,80},{80,64},{96,112},{112,96},{1... | collective-permute-start | bytes 221192 | tf_op jit(solution)/shard_map/ppermute | solution.py:30
  165.8 1.1 fusion.12
  167.1 0.7 copy.83
  (103 shorter events, 11.8 us)
Async XLA Ops:
  0.6 9.8 %copy-start = (bf16[1,8,128,256]{3,2,1,0:T(8,128)(2,1)S(1)}, bf16[1,8,128,256]{3,2,1,0:T(8,128)(2,1)}, u32[]{:S(2)}) copy-start(bf16[1,8,128,256]{3,2,1,0:T(8,128)(2,1)} %param.4) | copy-start | bytes 1572868
  2.6 15.5 %copy-start.26 = (bf16[1,8,128,256]{3,2,1,0:T(8,128)(2,1)S(1)}, bf16[1,8,128,256]{3,2,1,0:T(8,128)(2,1)}, u32[]{:S(2)}) copy-start(bf16[1,8,128,256]{3,2,1,0:T(8,128)(2,1)} %param.7) | copy-start | bytes 1572868
  2.6 41.1 %all-to-all-start = ((bf16[16,8,2304]{2,1,0:T(8,128)(2,1)}), bf16[16,8,2304]{2,1,0:T(8,128)(2,1)S(1)}, u32[]{:S(2)}, u32[]{:S(2)}) async-start(bf16[16,8,2304]{2,1,0:T(8,128)(2,1)} %broadcast_in_dim.2), calls=%async_computation | async-start | bytes 1179648 | tf_op jit(solution)/shard_map/all_to_all | solution.py:36
  10.7 17.0 %collective-permute-start = (bf16[1,1,128,256]{2,3,1,0:T(8,128)(2,1)S(1)}, bf16[1,1,128,256]{2,3,1,0:T(8,128)(2,1)S(1)}, u32[]{:S(2)}, u32[]{:S(2)}) collective-permute-start(bf16[1,1,128,256]{2,3,1,0:T(8,128)(2,1)S(1)} %get-tuple-element.35), channel_id=1, source_target_pairs={{0,1},{1,2},{2,3},{3,4},{4,5},{5,6},{6,7},{7,8},{8,9},{9,10},{10,1... | collective-permute-start | bytes 196616 | tf_op jit(solution)/shard_map/ppermute | solution.py:20
  13.8 13.9 %collective-permute-start.1 = (bf16[1,1,128,256]{2,3,1,0:T(8,128)(2,1)S(1)}, bf16[1,1,128,256]{2,3,1,0:T(8,128)(2,1)}, u32[]{:S(2)}, u32[]{:S(2)}) collective-permute-start(bf16[1,1,128,256]{2,3,1,0:T(8,128)(2,1)S(1)} %get-tuple-element.36), channel_id=1, source_target_pairs={{1,0},{2,1},{3,2},{4,3},{5,4},{6,5},{7,6},{8,7},{9,8},{10,9},{11,1... | collective-permute-start | bytes 196616 | tf_op jit(solution)/shard_map/ppermute | solution.py:21
  34.0 4.1 %copy-start.9 = (bf16[1,8,128,256]{2,3,1,0:T(8,128)(2,1)}, bf16[1,8,128,256]{2,3,1,0:T(8,128)(2,1)S(1)}, u32[]{:S(2)}) copy-start(bf16[1,8,128,256]{2,3,1,0:T(8,128)(2,1)S(1)} %get-tuple-element.34) | copy-start | bytes 1572868
  34.0 3.1 %copy-start.20 = (bf16[1,8,128,256]{2,3,1,0:T(8,128)(2,1)S(1)}, bf16[1,8,128,256]{2,3,1,0:T(8,128)(2,1)}, u32[]{:S(2)}) copy-start(bf16[1,8,128,256]{2,3,1,0:T(8,128)(2,1)} %get-tuple-element.25) | copy-start | bytes 1572868
  38.1 3.4 %copy-start.7 = (bf16[1,8,128,256]{2,3,1,0:T(8,128)(2,1)S(1)}, bf16[1,8,128,256]{2,3,1,0:T(8,128)(2,1)}, u32[]{:S(2)}) copy-start(bf16[1,8,128,256]{2,3,1,0:T(8,128)(2,1)} %get-tuple-element.33) | copy-start | bytes 1572868
  44.8 1.5 copy-start.11
  44.8 2.7 %copy-start.13 = (bf16[1,8,128,256]{3,2,1,0:T(8,128)(2,1)S(1)}, bf16[1,8,128,256]{3,2,1,0:T(8,128)(2,1)}, u32[]{:S(2)}) copy-start(bf16[1,8,128,256]{3,2,1,0:T(8,128)(2,1)} %copy.56) | copy-start | bytes 1572868
  44.8 2.7 %copy-start.18 = (bf16[2304,128]{1,0:T(8,128)(2,1)S(1)}, bf16[2304,128]{1,0:T(8,128)(2,1)}, u32[]{:S(2)}) copy-start(bf16[2304,128]{1,0:T(8,128)(2,1)} %copy.53) | copy-start | bytes 1769476
  47.4 1.0 copy-start.5
  48.5 1.0 copy-start.3
  49.5 3.8 %copy-start.1 = (bf16[1,8,128,256]{3,2,1,0:T(8,128)(2,1)S(1)}, bf16[1,8,128,256]{3,2,1,0:T(8,128)(2,1)}, u32[]{:S(2)}) copy-start(bf16[1,8,128,256]{3,2,1,0:T(8,128)(2,1)} %copy.61) | copy-start | bytes 1572868
  49.8 4.9 %collective-permute-start.2 = (bf16[16,8,2304]{2,1,0:T(8,128)(2,1)S(1)}, bf16[16,8,2304]{2,1,0:T(8,128)(2,1)S(1)}, u32[]{:S(2)}, u32[]{:S(2)}) collective-permute-start(bf16[16,8,2304]{2,1,0:T(8,128)(2,1)S(1)} %all-to-all-done), channel_id=1, source_target_pairs={{0,16},{16,0},{32,48},{48,32},{64,80},{80,64},{96,112},{112,96},{1... | collective-permute-start | bytes 1769480 | tf_op jit(solution)/shard_map/ppermute | solution.py:30
  54.7 0.8 copy-start.16
  57.7 1.5 copy-start.12
  57.7 2.6 %copy-start.14 = (bf16[1,8,128,256]{3,2,1,0:T(8,128)(2,1)S(1)}, bf16[1,8,128,256]{3,2,1,0:T(8,128)(2,1)}, u32[]{:S(2)}) copy-start(bf16[1,8,128,256]{3,2,1,0:T(8,128)(2,1)} %copy.56) | copy-start | bytes 1572868
  57.7 2.7 %copy-start.17 = (bf16[2304,128]{1,0:T(8,128)(2,1)S(1)}, bf16[2304,128]{1,0:T(8,128)(2,1)}, u32[]{:S(2)}) copy-start(bf16[2304,128]{1,0:T(8,128)(2,1)} %copy.63) | copy-start | bytes 1769476
  60.3 1.0 copy-start.6
  61.4 1.0 copy-start.4
  62.4 1.0 copy-start.2
  63.5 1.0 copy-start.19
  64.7 1.0 copy-start.24
  64.7 1.0 copy-start.27
  68.3 1.0 copy-start.10
  70.6 1.0 copy-start.8
  75.7 4.7 %collective-permute-start.5 = (f32[256,1152]{1,0:T(8,128)S(1)}, f32[256,1152]{1,0:T(8,128)S(1)}, u32[]{:S(2)}, u32[]{:S(2)}) collective-permute-start(f32[256,1152]{1,0:T(8,128)S(1)} %broadcast_select_fusion), channel_id=1, source_target_pairs={{0,16},{16,0},{32,48},{48,32},{64,80},{80,64},{96,112},{112,96},{1... | collective-permute-start | bytes 3538952 | tf_op jit(solution)/shard_map/ppermute | solution.py:30
  81.7 44.6 %all-to-all-start.1 = ((f32[16,16,1152]{2,1,0:T(8,128)}), f32[16,16,1152]{2,1,0:T(8,128)S(1)}, u32[]{:S(2)}, u32[]{:S(2)}) async-start(f32[16,16,1152]{2,1,0:T(8,128)} %bitcast.338), calls=%async_computation.1 | async-start | bytes 2359296 | tf_op jit(solution)/shard_map/all_to_all | solution.py:42
  86.2 30.4 %collective-permute-start.3 = (bf16[1,1,128,256]{2,1,3,0:T(2,128)(2,1)}, bf16[1,1,128,256]{2,1,3,0:T(2,128)(2,1)}, u32[]{:S(2)}, u32[]{:S(2)}) collective-permute-start(bf16[1,1,128,256]{2,1,3,0:T(2,128)(2,1)} %get-tuple-element.31), channel_id=1, source_target_pairs={{0,1},{1,2},{2,3},{3,4},{4,5},{5,6},{6,7},{7,8},{8,9},{9,10},{10,1... | collective-permute-start | bytes 196616 | tf_op jit(solution)/shard_map/ppermute | solution.py:20
  89.3 27.3 %collective-permute-start.4 = (bf16[1,1,128,256]{2,1,3,0:T(2,128)(2,1)}, bf16[1,1,128,256]{2,1,3,0:T(2,128)(2,1)}, u32[]{:S(2)}, u32[]{:S(2)}) collective-permute-start(bf16[1,1,128,256]{2,1,3,0:T(2,128)(2,1)} %get-tuple-element.32), channel_id=1, source_target_pairs={{1,0},{2,1},{3,2},{4,3},{5,4},{6,5},{7,6},{8,7},{9,8},{10,9},{11,1... | collective-permute-start | bytes 196616 | tf_op jit(solution)/shard_map/ppermute | solution.py:21
  95.4 1.4 copy-start.25
  121.9 2.0 %copy-start.15 = (bf16[2304,256]{1,0:T(8,128)(2,1)S(1)}, bf16[2304,256]{1,0:T(8,128)(2,1)}, u32[]{:S(2)}) copy-start(bf16[2304,256]{1,0:T(8,128)(2,1)} %copy.69) | copy-start | bytes 3538948
  126.3 10.6 %collective-permute-start.6 = (f32[16,1152]{1,0:T(8,128)S(1)}, f32[16,1152]{1,0:T(8,128)S(1)}, u32[]{:S(2)}, u32[]{:S(2)}) collective-permute-start(f32[16,1152]{1,0:T(8,128)S(1)} %reduce_sum.49), channel_id=1, source_target_pairs={{0,32},{16,48},{32,0},{48,16},{64,96},{80,112},{96,64},{112,80},{1... | collective-permute-start | bytes 221192 | tf_op jit(solution)/shard_map/ppermute | solution.py:30
  135.1 10.0 %copy-start.23 = (bf16[1,8,128,256]{2,1,3,0:T(8,128)(2,1)S(1)}, bf16[1,8,128,256]{2,1,3,0:T(8,128)(2,1)}, u32[]{:S(2)}) copy-start(bf16[1,8,128,256]{2,1,3,0:T(8,128)(2,1)} %get-tuple-element.18) | copy-start | bytes 1572868
  136.9 10.0 %collective-permute-start.7 = (f32[16,1152]{1,0:T(8,128)S(1)}, f32[16,1152]{1,0:T(8,128)S(1)}, u32[]{:S(2)}, u32[]{:S(2)}) collective-permute-start(f32[16,1152]{1,0:T(8,128)S(1)} %add.182), channel_id=1, source_target_pairs={{0,96},{16,112},{32,64},{48,80},{64,32},{80,48},{96,0},{112,16},{1... | collective-permute-start | bytes 221192 | tf_op jit(solution)/shard_map/ppermute | solution.py:30
  145.2 4.2 %copy-start.22 = (bf16[1,8,128,256]{2,1,3,0:T(8,128)(2,1)S(1)}, bf16[1,8,128,256]{2,1,3,0:T(8,128)(2,1)}, u32[]{:S(2)}) copy-start(bf16[1,8,128,256]{2,1,3,0:T(8,128)(2,1)} %get-tuple-element.17) | copy-start | bytes 1572868
  146.9 5.1 %collective-permute-start.8 = (f32[16,1152]{1,0:T(8,128)S(1)}, f32[16,1152]{1,0:T(8,128)S(1)}, u32[]{:S(2)}, u32[]{:S(2)}) collective-permute-start(f32[16,1152]{1,0:T(8,128)S(1)} %add.183), channel_id=1, source_target_pairs={{0,128},{16,144},{32,160},{48,176},{64,192},{80,208},{96,224},{112... | collective-permute-start | bytes 221192 | tf_op jit(solution)/shard_map/ppermute | solution.py:30
  149.4 4.8 %copy-start.21 = (bf16[1,8,128,256]{2,1,3,0:T(8,128)(2,1)S(1)}, bf16[1,8,128,256]{2,1,3,0:T(8,128)(2,1)}, u32[]{:S(2)}) copy-start(bf16[1,8,128,256]{2,1,3,0:T(8,128)(2,1)} %get-tuple-element.29) | copy-start | bytes 1572868
  152.0 6.3 %collective-permute-start.9 = (f32[16,1152]{1,0:T(8,128)S(1)}, f32[16,1152]{1,0:T(8,128)S(1)}, u32[]{:S(2)}, u32[]{:S(2)}) collective-permute-start(f32[16,1152]{1,0:T(8,128)S(1)} %add.184), channel_id=1, source_target_pairs={{0,384},{16,400},{32,416},{48,432},{64,448},{80,464},{96,480},{112... | collective-permute-start | bytes 221192 | tf_op jit(solution)/shard_map/ppermute | solution.py:30
  158.3 8.6 %collective-permute-start.10 = (f32[16,1152]{1,0:T(8,128)S(1)}, f32[16,1152]{1,0:T(8,128)S(1)}, u32[]{:S(2)}, u32[]{:S(2)}) collective-permute-start(f32[16,1152]{1,0:T(8,128)S(1)} %add.185), channel_id=1, source_target_pairs={{0,16},{16,0},{32,48},{48,32},{64,80},{80,64},{96,112},{112,96},{1... | collective-permute-start | bytes 221192 | tf_op jit(solution)/shard_map/ppermute | solution.py:30

commit v15 on v12

--- a/solution.py
+++ b/solution.py
@@ -136,13 +136,13 @@
                     preferred_element_type=jnp.float32,
                 )
             )
-    partial_value = jnp.stack(pieces, axis=1).reshape(out_chan, taps)
+    pixels = img_count * lax.axis_size("row") * tile_rows * lax.axis_size("col") * tile_cols
+    partial_value = jnp.stack(pieces, axis=1).reshape(out_chan, taps) * (1.0 / math.sqrt(pixels))
     core_sum = halve_sum(partial_value, "row", core_bit, 1)
     col_sum = scatter_sum(core_sum, "col")
     row_piece = double_sum(col_sum, "row", [1 << 1, 3 << 1, 1 << 3, 3 << 3])
     own_share = double_join(row_piece, "row", core_bit, 1)
-    pixels = img_count * lax.axis_size("row") * tile_rows * lax.axis_size("col") * tile_cols
-    weight_grad = (own_share * (1.0 / math.sqrt(pixels))).T.reshape(3, 3, in_chan, share)
+    weight_grad = own_share.T.reshape(3, 3, in_chan, share)
     features = outputs.reshape(img_count, tile_rows, tile_cols, out_chan)
     input_grad = grad_input.astype(jnp.bfloat16).reshape(img_count, tile_rows, tile_cols, in_chan)
     return (features, input_grad, weight_grad)

time: 139 us -> 140 us (level)
  the two profiles are of different devices: /device:TPU:71 before, /device:TPU:65 now
where the time goes in v15:
time: 140 us; the launch traced here: 139 us
  starting transfers between devices  64.7 us (46%)
  waiting for transfers between devices  38.3 us (27%)
  local copies, waits for them, and re-layouts  14.5 us (10%)
  matrix products  13.3 us (10%)
  other arithmetic  6.52 us (5%)
    ppermute x7, starting transfers between devices, exchange(): return lax.ppermute(value, axis, pairs)  37.5 us
    ppermute x2, waiting for transfers between devices, padded_2(): before = lax.ppermute(last, axis, up)  22.3 us
    unnamed x34, local copies, waits for them, and re-layouts  8.78 us
    ppermute x2, starting transfers between devices, padded_2(): after = lax.ppermute(initial, axis, down)  8.6 us
    all_to_all x1, waiting for transfers between devices, gather_chunks(): return lax.all_to_all(copies, axis, 0, 0, tiled=False)  8.48 us
    all_to_all x1, starting transfers between devices, gather_chunks(): return lax.all_to_all(copies, axis, 0, 0, tiled=False)  7.64 us
    ppermute x7, waiting for transfers between devices, exchange(): return lax.ppermute(value, axis, pairs)  7.57 us
    ppermute x2, starting transfers between devices, padded_2(): before = lax.ppermute(last, axis, up)  6.18 us
  transfers between devices with their start and end apart: 13, of which 7 were waited for; matrix products, arithmetic and copies ran while one was open for 7% of the time, Pallas kernels for 0%

profile of v15, /device:TPU:65, one launch (start us, length us, event | category | flops | bytes accessed | tf_op | source)
XLA Modules:
  0.0 138.5 jit_solution(2728611311975962046)
XLA Ops:
  0.6 1.0 copy.14
  1.8 0.9 broadcast_in_dim.2
  2.6 7.6 %all-to-all-start = ((bf16[16,16,1152]{2,1,0:T(8,128)(2,1)}), bf16[16,16,1152]{2,1,0:T(8,128)(2,1)S(1)}, u32[]{:S(2)}, u32[]{:S(2)}) async-start(bf16[16,16,1152]{2,1,0:T(8,128)(2,1)} %broadcast_in_dim.2), calls=%async_computation | async-start | bytes 1179648 | tf_op jit(solution)/shard_map/all_to_all | solution.py:36
  10.3 3.1 %collective-permute-start = (bf16[1,1,128,256]{3,2,1,0:T(8,128)(2,1)S(1)}, bf16[1,1,128,256]{3,2,1,0:T(8,128)(2,1)S(1)}, u32[]{:S(2)}, u32[]{:S(2)}) collective-permute-start(bf16[1,1,128,256]{3,2,1,0:T(8,128)(2,1)S(1)} %get-tuple-element.33), channel_id=1, source_target_pairs={{0,1},{1,2},{2,3},{3,4},{4,5},{5,6},{6,7},{7,8},{8,9},{9,10},{10,1... | collective-permute-start | bytes 196616 | tf_op jit(solution)/shard_map/ppermute | solution.py:20
  13.4 4.3 %collective-permute-start.1 = (bf16[1,1,128,256]{3,2,1,0:T(8,128)(2,1)S(1)}, bf16[1,1,128,256]{3,2,1,0:T(8,128)(2,1)S(1)}, u32[]{:S(2)}, u32[]{:S(2)}) collective-permute-start(bf16[1,1,128,256]{3,2,1,0:T(8,128)(2,1)S(1)} %get-tuple-element.34), channel_id=1, source_target_pairs={{1,0},{2,1},{3,2},{4,3},{5,4},{6,5},{7,6},{8,7},{9,8},{10,9},{11,1... | collective-permute-start | bytes 196616 | tf_op jit(solution)/shard_map/ppermute | solution.py:21
  17.7 8.5 %all-to-all-done = bf16[16,16,1152]{2,1,0:T(8,128)(2,1)S(1)} async-done(((bf16[16,16,1152]{2,1,0:T(8,128)(2,1)}), bf16[16,16,1152]{2,1,0:T(8,128)(2,1)S(1)}, u32[]{:S(2)}, u32[]{:S(2)}) %all-to-all-start) | async-done | bytes 589856 | tf_op jit(solution)/shard_map/all_to_all | solution.py:36
  26.2 3.3 %collective-permute-start.2 = (bf16[16,16,1152]{2,1,0:T(8,128)(2,1)S(1)}, bf16[16,16,1152]{2,1,0:T(8,128)(2,1)S(1)}, u32[]{:S(2)}, u32[]{:S(2)}) collective-permute-start(bf16[16,16,1152]{2,1,0:T(8,128)(2,1)S(1)} %all-to-all-done), channel_id=1, source_target_pairs={{0,16},{16,0},{32,48},{48,32},{64,80},{80,64},{96,112},{112,96},{1... | collective-permute-start | bytes 1769480 | tf_op jit(solution)/shard_map/ppermute | solution.py:30
  29.8 1.1 pad_maximum_fusion.2
  30.8 1.6 %fusion.35 = (bf16[1,8,128,256]{3,2,1,0:T(8,128)(2,1)}, bf16[1,8,128,256]{3,2,1,0:T(8,128)(2,1)}, bf16[1,8,128,256]{3,2,1,0:T(8,128)(2,1)}, bf16[1,8,128,256]{3,...) fusion(bf16[1,10,130,256]{3,2,1,0:T(8,128)(2,1)S(1)} %select_maximum_fusion.2), kind=kLoop, calls=%fused_computation.91 | loop fusion | bytes 6291456 | tf_op jit(solution)/shard_map/slice | solution.py:93
  32.7 0.6 copy.15
  33.3 1.8 %fusion.26 = f32[1024,256]{1,0:T(8,128)S(1)} fusion(bf16[1024,256]{1,0:T(8,128)(2,1)} %bitcast.187, bf16[3,3,256,256]{3,2,1,0:T(8,128)(2,1)S(1)} %bitcast.159), kind=kOutput, calls=%fused_computation.78 | convolution fusion | flops 134217728 | bytes 1703936 | tf_op jit(solution)/shard_map/dot_general | solution.py:112
  35.1 0.3 fusion.27
  35.4 0.7 copy-done.3
  36.7 0.7 copy-done.9
  37.5 0.3 convolution_add_fusion.10
  37.8 0.7 copy-done.7
  38.5 0.3 convolution_add_fusion.9
  38.8 0.7 copy-done.6
  39.9 0.3 fusion.3
  40.2 0.7 copy-done.8
  40.9 0.4 fusion.38
  41.3 0.4 multiply_reduce_fusion.1
  41.7 0.6 copy-done.13
  42.3 1.9 %fusion.31 = (f32[1024]{0:T(1024)S(1)}, f32[1024]{0:T(1024)S(1)}, f32[1024,256]{1,0:T(8,128)S(1)}, bf16[1024,256]{1,0:T(8,128)(2,1)}) fusion(f32[1024]{0:T(1024)S(1)} %add_rsqrt_fusion, f32[1024,256]{1,0:T(8,128)S(1)} %get-tuple-element.36, f32[1024]{0:T(1024)S(1)} %broadcast_multiply_fusion.3, f32[256]{0:T(256)S(1)} %copy-done.14, ...), kind=kLoop, calls=%fused_computation.88 | loop fusion | flops 4978688 | bytes 3163136 | tf_op jit(solution)/shard_map/reduce_sum | solution.py:86
  44.3 0.8 multiply_convert_fusion
  45.3 0.3 fusion.16
  45.7 0.3 fusion.15
  46.0 0.3 fusion.14
  46.4 0.3 fusion.13
  46.7 0.3 fusion.12
  47.1 0.3 fusion.11
  47.4 0.3 fusion.10
  47.8 0.3 fusion.9
  48.1 0.3 fusion.8
  48.7 1.2 fusion.33
  49.9 0.4 copy.21
  50.2 1.6 %copy.22 = f32[256,1152]{1,0:T(8,128)S(1)} copy(f32[256,1152]{0,1:T(8,128)} %get-tuple-element.13) | data formatting | bytes 2359296
  52.0 1.9 %collective-permute-start.5 = (f32[256,1152]{1,0:T(8,128)S(1)}, f32[256,1152]{1,0:T(8,128)S(1)}, u32[]{:S(2)}, u32[]{:S(2)}) collective-permute-start(f32[256,1152]{1,0:T(8,128)S(1)} %broadcast_select_fusion), channel_id=1, source_target_pairs={{0,16},{16,0},{32,48},{48,32},{64,80},{80,64},{96,112},{112,96},{1... | collective-permute-start | bytes 3538952 | tf_op jit(solution)/shard_map/ppermute | solution.py:30
  53.9 2.8 %collective-permute-done.5 = f32[256,1152]{1,0:T(8,128)S(1)} collective-permute-done((f32[256,1152]{1,0:T(8,128)S(1)}, f32[256,1152]{1,0:T(8,128)S(1)}, u32[]{:S(2)}, u32[]{:S(2)}) %collective-permute-start.5) | collective-permute-done | bytes 1179680 | tf_op jit(solution)/shard_map/ppermute | solution.py:30
  56.8 1.2 select_add_fusion
  57.9 4.8 %all-to-all-start.1 = ((f32[16,16,1152]{2,1,0:T(8,128)}), f32[16,16,1152]{2,1,0:T(8,128)S(1)}, u32[]{:S(2)}, u32[]{:S(2)}) async-start(f32[16,16,1152]{2,1,0:T(8,128)} %bitcast.180), calls=%async_computation.1 | async-start | bytes 2359296 | tf_op jit(solution)/shard_map/all_to_all | solution.py:42
  62.7 3.1 %collective-permute-start.3 = (bf16[1,1,128,256]{3,2,1,0:T(8,128)(2,1)S(1)}, bf16[1,1,128,256]{3,2,1,0:T(8,128)(2,1)S(1)}, u32[]{:S(2)}, u32[]{:S(2)}) collective-permute-start(bf16[1,1,128,256]{3,2,1,0:T(8,128)(2,1)S(1)} %get-tuple-element.29), channel_id=1, source_target_pairs={{0,1},{1,2},{2,3},{3,4},{4,5},{5,6},{6,7},{7,8},{8,9},{9,10},{10,1... | collective-permute-start | bytes 196616 | tf_op jit(solution)/shard_map/ppermute | solution.py:20
  65.8 4.3 %collective-permute-start.4 = (bf16[1,1,128,256]{3,2,1,0:T(8,128)(2,1)S(1)}, bf16[1,1,128,256]{3,2,1,0:T(8,128)(2,1)S(1)}, u32[]{:S(2)}, u32[]{:S(2)}) collective-permute-start(bf16[1,1,128,256]{3,2,1,0:T(8,128)(2,1)S(1)} %get-tuple-element.30), channel_id=1, source_target_pairs={{1,0},{2,1},{3,2},{4,3},{5,4},{6,5},{7,6},{8,7},{9,8},{10,9},{11,1... | collective-permute-start | bytes 196616 | tf_op jit(solution)/shard_map/ppermute | solution.py:21
  70.1 22.3 %collective-permute-done.3 = bf16[1,1,128,256]{3,2,1,0:T(8,128)(2,1)S(1)} collective-permute-done((bf16[1,1,128,256]{3,2,1,0:T(8,128)(2,1)S(1)}, bf16[1,1,128,256]{3,2,1,0:T(8,128)(2,1)S(1)}, u32[]{:S(2)}, u32[]{:S(2)}) %collective-permute-start.3) | collective-permute-done | bytes 65568 | tf_op jit(solution)/shard_map/ppermute | solution.py:20
  92.6 1.3 fusion.34
  93.9 0.6 copy-done.1
  94.5 0.3 fusion.25
  94.8 0.3 convolution_add_fusion.6
  95.1 0.3 convolution_add_fusion.5
  95.5 1.3 convolution_add_fusion.4
  96.9 8.9 %collective-permute-start.6 = (f32[16,1152]{1,0:T(8,128)S(1)}, f32[16,1152]{1,0:T(8,128)S(1)}, u32[]{:S(2)}, u32[]{:S(2)}) collective-permute-start(f32[16,1152]{1,0:T(8,128)S(1)} %reduce_sum.49), channel_id=1, source_target_pairs={{0,32},{16,48},{32,0},{48,16},{64,96},{80,112},{96,64},{112,80},{1... | collective-permute-start | bytes 221192 | tf_op jit(solution)/shard_map/ppermute | solution.py:30
  105.8 1.6 %convolution_add_fusion.3 = f32[1024,256]{1,0:T(8,128)S(1)} fusion(f32[1024,256]{1,0:T(8,128)} %convolution_add_fusion.4, bf16[1024,256]{1,0:T(8,128)(2,1)S(1)} %multiply_convert_fusion, bf16[3,3,256,256]{3,2,1,0:T(8,128)(2,1)S(1)} %bitcast.172), kind=kOutput, calls=%fused_computation.12 | convolution fusion | flops 134479872 | bytes 2752512 | tf_op jit(solution)/shard_map/dot_general | solution.py:125
  107.6 8.4 %collective-permute-start.7 = (f32[16,1152]{1,0:T(8,128)S(1)}, f32[16,1152]{1,0:T(8,128)S(1)}, u32[]{:S(2)}, u32[]{:S(2)}) collective-permute-start(f32[16,1152]{1,0:T(8,128)S(1)} %add.109), channel_id=1, source_target_pairs={{0,96},{16,112},{32,64},{48,80},{64,32},{80,48},{96,0},{112,16},{1... | collective-permute-start | bytes 221192 | tf_op jit(solution)/shard_map/ppermute | solution.py:30
  116.0 0.3 convolution_add_fusion.2
  116.3 1.4 collective-permute-done.7
  117.7 3.1 %collective-permute-start.8 = (f32[16,1152]{1,0:T(8,128)S(1)}, f32[16,1152]{1,0:T(8,128)S(1)}, u32[]{:S(2)}, u32[]{:S(2)}) collective-permute-start(f32[16,1152]{1,0:T(8,128)S(1)} %add.110), channel_id=1, source_target_pairs={{0,128},{16,144},{32,160},{48,176},{64,192},{80,208},{96,224},{112... | collective-permute-start | bytes 221192 | tf_op jit(solution)/shard_map/ppermute | solution.py:30
  120.8 0.3 convolution_add_fusion.1
  121.2 1.6 %collective-permute-done.8 = f32[16,1152]{1,0:T(8,128)S(1)} collective-permute-done((f32[16,1152]{1,0:T(8,128)S(1)}, f32[16,1152]{1,0:T(8,128)S(1)}, u32[]{:S(2)}, u32[]{:S(2)}) %collective-permute-start.8) | collective-permute-done | bytes 73760 | tf_op jit(solution)/shard_map/ppermute | solution.py:30
  122.8 4.4 %collective-permute-start.9 = (f32[16,1152]{1,0:T(8,128)S(1)}, f32[16,1152]{1,0:T(8,128)S(1)}, u32[]{:S(2)}, u32[]{:S(2)}) collective-permute-start(f32[16,1152]{1,0:T(8,128)S(1)} %add.111), channel_id=1, source_target_pairs={{0,384},{16,400},{32,416},{48,432},{64,448},{80,464},{96,480},{112... | collective-permute-start | bytes 221192 | tf_op jit(solution)/shard_map/ppermute | solution.py:30
  127.2 0.3 fusion.29
  127.5 1.6 %collective-permute-done.9 = f32[16,1152]{1,0:T(8,128)S(1)} collective-permute-done((f32[16,1152]{1,0:T(8,128)S(1)}, f32[16,1152]{1,0:T(8,128)S(1)}, u32[]{:S(2)}, u32[]{:S(2)}) %collective-permute-start.9) | collective-permute-done | bytes 73760 | tf_op jit(solution)/shard_map/ppermute | solution.py:30
  129.1 7.4 %collective-permute-start.10 = (f32[16,1152]{1,0:T(8,128)S(1)}, f32[16,1152]{1,0:T(8,128)S(1)}, u32[]{:S(2)}, u32[]{:S(2)}) collective-permute-start(f32[16,1152]{1,0:T(8,128)S(1)} %add.112), channel_id=1, source_target_pairs={{0,16},{16,0},{32,48},{48,32},{64,80},{80,64},{96,112},{112,96},{1... | collective-permute-start | bytes 221192 | tf_op jit(solution)/shard_map/ppermute | solution.py:30
  136.6 1.1 fusion.6
  137.8 0.7 copy.19
  (53 shorter events, 2.7 us)
Async XLA Ops:
  0.6 9.7 %copy-start.2 = (bf16[1,8,128,256]{3,2,1,0:T(8,128)(2,1)S(1)}, bf16[1,8,128,256]{3,2,1,0:T(8,128)(2,1)}, u32[]{:S(2)}) copy-start(bf16[1,8,128,256]{3,2,1,0:T(8,128)(2,1)} %param.4) | copy-start | bytes 1572868
  2.6 23.6 %all-to-all-start = ((bf16[16,16,1152]{2,1,0:T(8,128)(2,1)}), bf16[16,16,1152]{2,1,0:T(8,128)(2,1)S(1)}, u32[]{:S(2)}, u32[]{:S(2)}) async-start(bf16[16,16,1152]{2,1,0:T(8,128)(2,1)} %broadcast_in_dim.2), calls=%async_computation | async-start | bytes 1179648 | tf_op jit(solution)/shard_map/all_to_all | solution.py:36
  10.3 19.2 %collective-permute-start = (bf16[1,1,128,256]{3,2,1,0:T(8,128)(2,1)S(1)}, bf16[1,1,128,256]{3,2,1,0:T(8,128)(2,1)S(1)}, u32[]{:S(2)}, u32[]{:S(2)}) collective-permute-start(bf16[1,1,128,256]{3,2,1,0:T(8,128)(2,1)S(1)} %get-tuple-element.33), channel_id=1, source_target_pairs={{0,1},{1,2},{2,3},{3,4},{4,5},{5,6},{6,7},{7,8},{8,9},{9,10},{10,1... | collective-permute-start | bytes 196616 | tf_op jit(solution)/shard_map/ppermute | solution.py:20
  13.4 16.2 %collective-permute-start.1 = (bf16[1,1,128,256]{3,2,1,0:T(8,128)(2,1)S(1)}, bf16[1,1,128,256]{3,2,1,0:T(8,128)(2,1)S(1)}, u32[]{:S(2)}, u32[]{:S(2)}) collective-permute-start(bf16[1,1,128,256]{3,2,1,0:T(8,128)(2,1)S(1)} %get-tuple-element.34), channel_id=1, source_target_pairs={{1,0},{2,1},{3,2},{4,3},{5,4},{6,5},{7,6},{8,7},{9,8},{10,9},{11,1... | collective-permute-start | bytes 196616 | tf_op jit(solution)/shard_map/ppermute | solution.py:21
  26.2 6.2 %collective-permute-start.2 = (bf16[16,16,1152]{2,1,0:T(8,128)(2,1)S(1)}, bf16[16,16,1152]{2,1,0:T(8,128)(2,1)S(1)}, u32[]{:S(2)}, u32[]{:S(2)}) collective-permute-start(bf16[16,16,1152]{2,1,0:T(8,128)(2,1)S(1)} %all-to-all-done), channel_id=1, source_target_pairs={{0,16},{16,0},{32,48},{48,32},{64,80},{80,64},{96,112},{112,96},{1... | collective-permute-start | bytes 1769480 | tf_op jit(solution)/shard_map/ppermute | solution.py:30
  33.3 6.9 %copy-start = (bf16[2304,256]{1,0:T(8,128)(2,1)}, bf16[2304,256]{1,0:T(8,128)(2,1)S(1)}, u32[]{:S(2)}) copy-start(bf16[2304,256]{1,0:T(8,128)(2,1)S(1)} %copy.15) | copy-start | bytes 3538948
  33.3 1.8 %copy-start.4 = (bf16[1,8,128,256]{3,2,1,0:T(8,128)(2,1)S(1)}, bf16[1,8,128,256]{3,2,1,0:T(8,128)(2,1)}, u32[]{:S(2)}) copy-start(bf16[1,8,128,256]{3,2,1,0:T(8,128)(2,1)} %get-tuple-element.23) | copy-start | bytes 1572868
  35.1 1.0 copy-start.3
  36.4 1.0 copy-start.9
  37.5 1.0 copy-start.7
  38.5 1.0 copy-start.6
  39.9 1.0 copy-start.8
  40.9 0.8 copy-start.14
  41.3 1.0 copy-start.13
  44.3 1.0 copy-start.5
  52.0 4.7 %collective-permute-start.5 = (f32[256,1152]{1,0:T(8,128)S(1)}, f32[256,1152]{1,0:T(8,128)S(1)}, u32[]{:S(2)}, u32[]{:S(2)}) collective-permute-start(f32[256,1152]{1,0:T(8,128)S(1)} %broadcast_select_fusion), channel_id=1, source_target_pairs={{0,16},{16,0},{32,48},{48,32},{64,80},{80,64},{96,112},{112,96},{1... | collective-permute-start | bytes 3538952 | tf_op jit(solution)/shard_map/ppermute | solution.py:30
  57.9 38.9 %all-to-all-start.1 = ((f32[16,16,1152]{2,1,0:T(8,128)}), f32[16,16,1152]{2,1,0:T(8,128)S(1)}, u32[]{:S(2)}, u32[]{:S(2)}) async-start(f32[16,16,1152]{2,1,0:T(8,128)} %bitcast.180), calls=%async_computation.1 | async-start | bytes 2359296 | tf_op jit(solution)/shard_map/all_to_all | solution.py:42
  62.7 29.7 %collective-permute-start.3 = (bf16[1,1,128,256]{3,2,1,0:T(8,128)(2,1)S(1)}, bf16[1,1,128,256]{3,2,1,0:T(8,128)(2,1)S(1)}, u32[]{:S(2)}, u32[]{:S(2)}) collective-permute-start(bf16[1,1,128,256]{3,2,1,0:T(8,128)(2,1)S(1)} %get-tuple-element.29), channel_id=1, source_target_pairs={{0,1},{1,2},{2,3},{3,4},{4,5},{5,6},{6,7},{7,8},{8,9},{9,10},{10,1... | collective-permute-start | bytes 196616 | tf_op jit(solution)/shard_map/ppermute | solution.py:20
  65.8 26.6 %collective-permute-start.4 = (bf16[1,1,128,256]{3,2,1,0:T(8,128)(2,1)S(1)}, bf16[1,1,128,256]{3,2,1,0:T(8,128)(2,1)S(1)}, u32[]{:S(2)}, u32[]{:S(2)}) collective-permute-start(bf16[1,1,128,256]{3,2,1,0:T(8,128)(2,1)S(1)} %get-tuple-element.30), channel_id=1, source_target_pairs={{1,0},{2,1},{3,2},{4,3},{5,4},{6,5},{7,6},{8,7},{9,8},{10,9},{11,1... | collective-permute-start | bytes 196616 | tf_op jit(solution)/shard_map/ppermute | solution.py:21
  92.6 1.8 %copy-start.1 = (bf16[2304,256]{1,0:T(8,128)(2,1)S(1)}, bf16[2304,256]{1,0:T(8,128)(2,1)}, u32[]{:S(2)}) copy-start(bf16[2304,256]{1,0:T(8,128)(2,1)} %copy-done) | copy-start | bytes 3538948
  96.9 19.1 %copy-start.12 = (bf16[1,8,128,256]{3,2,1,0:T(8,128)(2,1)S(1)}, bf16[1,8,128,256]{3,2,1,0:T(8,128)(2,1)}, u32[]{:S(2)}) copy-start(bf16[1,8,128,256]{3,2,1,0:T(8,128)(2,1)} %get-tuple-element.16) | copy-start | bytes 1572868
  96.9 10.7 %collective-permute-start.6 = (f32[16,1152]{1,0:T(8,128)S(1)}, f32[16,1152]{1,0:T(8,128)S(1)}, u32[]{:S(2)}, u32[]{:S(2)}) collective-permute-start(f32[16,1152]{1,0:T(8,128)S(1)} %reduce_sum.49), channel_id=1, source_target_pairs={{0,32},{16,48},{32,0},{48,16},{64,96},{80,112},{96,64},{112,80},{1... | collective-permute-start | bytes 221192 | tf_op jit(solution)/shard_map/ppermute | solution.py:30
  107.6 10.1 %collective-permute-start.7 = (f32[16,1152]{1,0:T(8,128)S(1)}, f32[16,1152]{1,0:T(8,128)S(1)}, u32[]{:S(2)}, u32[]{:S(2)}) collective-permute-start(f32[16,1152]{1,0:T(8,128)S(1)} %add.109), channel_id=1, source_target_pairs={{0,96},{16,112},{32,64},{48,80},{64,32},{80,48},{96,0},{112,16},{1... | collective-permute-start | bytes 221192 | tf_op jit(solution)/shard_map/ppermute | solution.py:30
  116.0 4.8 %copy-start.11 = (bf16[1,8,128,256]{3,2,1,0:T(8,128)(2,1)S(1)}, bf16[1,8,128,256]{3,2,1,0:T(8,128)(2,1)}, u32[]{:S(2)}) copy-start(bf16[1,8,128,256]{3,2,1,0:T(8,128)(2,1)} %get-tuple-element.15) | copy-start | bytes 1572868
  117.7 5.1 %collective-permute-start.8 = (f32[16,1152]{1,0:T(8,128)S(1)}, f32[16,1152]{1,0:T(8,128)S(1)}, u32[]{:S(2)}, u32[]{:S(2)}) collective-permute-start(f32[16,1152]{1,0:T(8,128)S(1)} %add.110), channel_id=1, source_target_pairs={{0,128},{16,144},{32,160},{48,176},{64,192},{80,208},{96,224},{112... | collective-permute-start | bytes 221192 | tf_op jit(solution)/shard_map/ppermute | solution.py:30
  120.8 6.4 %copy-start.10 = (bf16[1,8,128,256]{3,2,1,0:T(8,128)(2,1)S(1)}, bf16[1,8,128,256]{3,2,1,0:T(8,128)(2,1)}, u32[]{:S(2)}) copy-start(bf16[1,8,128,256]{3,2,1,0:T(8,128)(2,1)} %get-tuple-element.20) | copy-start | bytes 1572868
  122.8 6.3 %collective-permute-start.9 = (f32[16,1152]{1,0:T(8,128)S(1)}, f32[16,1152]{1,0:T(8,128)S(1)}, u32[]{:S(2)}, u32[]{:S(2)}) collective-permute-start(f32[16,1152]{1,0:T(8,128)S(1)} %add.111), channel_id=1, source_target_pairs={{0,384},{16,400},{32,416},{48,432},{64,448},{80,464},{96,480},{112... | collective-permute-start | bytes 221192 | tf_op jit(solution)/shard_map/ppermute | solution.py:30
  129.1 8.6 %collective-permute-start.10 = (f32[16,1152]{1,0:T(8,128)S(1)}, f32[16,1152]{1,0:T(8,128)S(1)}, u32[]{:S(2)}, u32[]{:S(2)}) collective-permute-start(f32[16,1152]{1,0:T(8,128)S(1)} %add.112), channel_id=1, source_target_pairs={{0,16},{16,0},{32,48},{48,32},{64,80},{80,64},{96,112},{112,96},{1... | collective-permute-start | bytes 221192 | tf_op jit(solution)/shard_map/ppermute | solution.py:30

commit v16 on v12

--- a/solution.py
+++ b/solution.py
@@ -104,20 +104,29 @@
     kernel_t = double_join(gather_chunks(half_t, "col"), "row", core_bit, 2).reshape(-1, taps)
     out_chan = kernel_t.shape[0]
     whole_kernel = kernel_t.T.reshape(3, 3, in_chan, out_chan)
-    rimmed = padded_2(images, (("col", 1),), 1)
-    padded = jnp.pad(rimmed, ((0, 0), (0, 0), (1, 1), (0, 0)))
-    conv_out = jnp.zeros((img_count * tile_rows * tile_cols, out_chan), jnp.float32)
+    both = jnp.concatenate([images, cotangent], axis=-1)
+    rimmed = padded_2(both, (("col", 1),), 2)
+    padded_all = jnp.pad(rimmed[..., :in_chan], ((0, 0), (0, 0), (1, 1), (0, 0)))
+    rows = tile_rows + 2
+    conv_out = jnp.zeros((img_count * rows * tile_cols, out_chan), jnp.float32)
     for tap_row in range(3):
         for tap_col in range(3):
             conv_out = conv_out + jnp.dot(
-                window(padded, tap_row, tap_col, tile_rows, tile_cols),
+                window(padded_all, tap_row, tap_col, rows, tile_cols),
                 whole_kernel[tap_row, tap_col],
                 preferred_element_type=jnp.float32,
             )
-    outputs, grad_pre = norm_act(conv_out, cotangent.reshape(-1, out_chan), norm_gain)
-    grad_grid = grad_pre.reshape(img_count, tile_rows, tile_cols, out_chan)
-    grad_rimmed = padded_2(grad_grid, (("col", 1),), 1)
-    grad_pad = jnp.pad(grad_rimmed, ((0, 0), (0, 0), (1, 1), (0, 0)))
+    upper_cot = rimmed[:, 1 : rows + 1, :, in_chan:].reshape(-1, out_chan)
+    outputs, grad_all = norm_act(conv_out, upper_cot, norm_gain)
+    outputs = outputs.reshape(img_count, rows, tile_cols, out_chan)[:, 1 : tile_rows + 1]
+    grad_all = grad_all.reshape(img_count, rows, tile_cols, out_chan)
+    me, peers = lax.axis_index("col"), lax.axis_size("col")
+    grid_row = jnp.arange(rows).reshape(1, rows, 1, 1)
+    inside = ((grid_row > 0) | (me > 0)) & ((grid_row < rows - 1) | (me < peers - 1))
+    grad_all = jnp.where(inside, grad_all, jnp.zeros_like(grad_all))
+    grad_pad = jnp.pad(grad_all, ((0, 0), (0, 0), (1, 1), (0, 0)))
+    grad_pre = grad_all[:, 1 : tile_rows + 1].reshape(-1, out_chan)
+    padded = padded_all[:, 1 : rows + 1]
     grad_input = jnp.zeros((img_count * tile_rows * tile_cols, in_chan), jnp.float32)
     pieces = []
     for tap_row in range(3):
@@ -143,7 +152,7 @@
     own_share = double_join(row_piece, "row", core_bit, 1)
     pixels = img_count * lax.axis_size("row") * tile_rows * lax.axis_size("col") * tile_cols
     weight_grad = (own_share * (1.0 / math.sqrt(pixels))).T.reshape(3, 3, in_chan, share)
-    features = outputs.reshape(img_count, tile_rows, tile_cols, out_chan)
+    features = outputs
     input_grad = grad_input.astype(jnp.bfloat16).reshape(img_count, tile_rows, tile_cols, in_chan)
     return (features, input_grad, weight_grad)
 

time: 139 us -> 173 us (1.24)
  the two profiles are of different devices: /device:TPU:71 before, /device:TPU:103 now
where the time goes in v16:
time: 173 us; the launch traced here: 171 us
  starting transfers between devices  60.8 us (35%)
  local copies, waits for them, and re-layouts  42.6 us (25%)
  waiting for transfers between devices  42 us (24%)
  matrix products  13.7 us (8%)
  other arithmetic  11 us (6%)
    ppermute x7, starting transfers between devices, exchange(): return lax.ppermute(value, axis, pairs)  39.3 us
    slice x13, local copies, waits for them, and re-layouts, window(): padded[:, tap_row:tap_row + tile_rows, tap_col:tap_col + tile_cols, :]  22.5 us
    all_to_all x1, waiting for transfers between devices, scatter_sum(): return lax.all_to_all(blocks, axis, 0, 0, tiled=False).sum(0)  21.5 us
    unnamed x56, local copies, waits for them, and re-layouts  12.6 us
    ppermute x7, waiting for transfers between devices, exchange(): return lax.ppermute(value, axis, pairs)  10.6 us
    ppermute x1, waiting for transfers between devices, padded_2(): before = lax.ppermute(last, axis, up)  9.96 us
    all_to_all x1, starting transfers between devices, gather_chunks(): return lax.all_to_all(copies, axis, 0, 0, tiled=False)  7.19 us
    all_to_all x1, starting transfers between devices, scatter_sum(): return lax.all_to_all(blocks, axis, 0, 0, tiled=False).sum(0)  6.9 us
  transfers between devices with their start and end apart: 11, of which 7 were waited for; matrix products, arithmetic and copies ran while one was open for 21% of the time, Pallas kernels for 0%

profile of v16, /device:TPU:103, one launch (start us, length us, event | category | flops | bytes accessed | tf_op | source)
XLA Modules:
  0.0 171.3 jit_solution(1008982638771210658)
XLA Ops:
  0.6 1.0 copy.32
  1.8 0.9 broadcast_in_dim.9
  2.6 7.2 %all-to-all-start = ((bf16[16,16,1152]{2,1,0:T(8,128)(2,1)}), bf16[16,16,1152]{2,1,0:T(8,128)(2,1)}, u32[]{:S(2)}, u32[]{:S(2)}) async-start(bf16[16,16,1152]{2,1,0:T(8,128)(2,1)} %broadcast_in_dim.9), calls=%async_computation | async-start | bytes 1179648 | tf_op jit(solution)/shard_map/all_to_all | solution.py:36
  10.4 3.1 %collective-permute-start = (bf16[1,2,128,512]{2,3,1,0:T(8,128)(2,1)S(1)}, bf16[1,2,128,512]{2,3,1,0:T(8,128)(2,1)S(1)}, u32[]{:S(2)}, u32[]{:S(2)}) collective-permute-start(bf16[1,2,128,512]{2,3,1,0:T(8,128)(2,1)S(1)} %get-tuple-element.19), channel_id=1, source_target_pairs={{0,1},{1,2},{2,3},{3,4},{4,5},{5,6},{6,7},{7,8},{8,9},{9,10},{10,1... | collective-permute-start | bytes 786440 | tf_op jit(solution)/shard_map/ppermute | solution.py:20
  13.5 4.3 %collective-permute-start.1 = (bf16[1,2,128,512]{2,3,1,0:T(8,128)(2,1)S(1)}, bf16[1,2,128,512]{2,3,1,0:T(8,128)(2,1)S(1)}, u32[]{:S(2)}, u32[]{:S(2)}) collective-permute-start(bf16[1,2,128,512]{2,3,1,0:T(8,128)(2,1)S(1)} %get-tuple-element.20), channel_id=1, source_target_pairs={{1,0},{2,1},{3,2},{4,3},{5,4},{6,5},{7,6},{8,7},{9,8},{10,9},{11,1... | collective-permute-start | bytes 786440 | tf_op jit(solution)/shard_map/ppermute | solution.py:21
  17.9 10.0 %collective-permute-done = bf16[1,2,128,512]{2,3,1,0:T(8,128)(2,1)S(1)} collective-permute-done((bf16[1,2,128,512]{2,3,1,0:T(8,128)(2,1)S(1)}, bf16[1,2,128,512]{2,3,1,0:T(8,128)(2,1)S(1)}, u32[]{:S(2)}, u32[]{:S(2)}) %collective-permute-start) | collective-permute-done | bytes 262176 | tf_op jit(solution)/shard_map/ppermute | solution.py:20
  27.8 0.7 copy-done.19
  28.5 0.7 copy-done.17
  29.4 3.2 %collective-permute-start.2 = (bf16[16,16,1152]{2,1,0:T(8,128)(2,1)}, bf16[16,16,1152]{2,1,0:T(8,128)(2,1)}, u32[]{:S(2)}, u32[]{:S(2)}) collective-permute-start(bf16[16,16,1152]{2,1,0:T(8,128)(2,1)} %all-to-all-done), channel_id=1, source_target_pairs={{0,16},{16,0},{32,48},{48,32},{64,80},{80,64},{96,112},{112,96},{1... | collective-permute-start | bytes 1769480 | tf_op jit(solution)/shard_map/ppermute | solution.py:30
  32.7 1.4 slice_convert_fusion
  34.1 2.9 %copy.42 = f32[1,10,128,256]{3,2,1,0:T(8,128)} copy(f32[1,10,128,256]{2,3,1,0:T(8,128)} %get-tuple-element.14) | data formatting | bytes 2621440 | tf_op jit(solution)/shard_map/convert_element_type | solution.py:85
  37.0 1.1 copy.37
  38.0 1.5 pad_maximum_fusion.1
  39.5 0.9 slice.211
  40.4 2.2 %copy.40 = bf16[1,10,128,256]{3,2,1,0:T(8,128)(2,1)} copy(bf16[1,10,128,256]{2,3,1,0:T(8,128)(2,1)} %slice.211) | data formatting | bytes 1310720 | tf_op jit(solution)/shard_map/slice | solution.py:93
  42.6 0.9 slice.203
  43.5 2.2 %copy.34 = bf16[1,10,128,256]{3,2,1,0:T(8,128)(2,1)} copy(bf16[1,10,128,256]{2,3,1,0:T(8,128)(2,1)} %slice.203) | data formatting | bytes 1310720 | tf_op jit(solution)/shard_map/slice | solution.py:93
  45.7 2.7 %pad_slice_fusion.6 = (bf16[1,10,128,256]{2,3,1,0:T(8,128)(2,1)}, bf16[1,10,128,256]{2,3,1,0:T(8,128)(2,1)}, bf16[1,10,128,256]{2,3,1,0:T(8,128)(2,1)}, bf16[1,1...) fusion(bf16[1,12,128,256]{2,3,1,0:T(8,128)(2,1)S(1)} %slice.201), kind=kLoop, calls=%fused_computation.6 | loop fusion | bytes 4718592 | tf_op jit(solution)/shard_map/slice | solution.py:93
  48.3 2.2 %copy.41 = bf16[1,10,128,256]{3,2,1,0:T(8,128)(2,1)} copy(bf16[1,10,128,256]{2,3,1,0:T(8,128)(2,1)} %get-tuple-element.21) | data formatting | bytes 1310720 | tf_op jit(solution)/shard_map/slice | solution.py:93
  50.5 2.2 %copy.35 = bf16[1,10,128,256]{3,2,1,0:T(8,128)(2,1)} copy(bf16[1,10,128,256]{2,3,1,0:T(8,128)(2,1)} %get-tuple-element.22) | data formatting | bytes 1310720 | tf_op jit(solution)/shard_map/slice | solution.py:93
  52.7 2.2 %copy.36 = bf16[1,10,128,256]{3,2,1,0:T(8,128)(2,1)} copy(bf16[1,10,128,256]{2,3,1,0:T(8,128)(2,1)} %get-tuple-element.23) | data formatting | bytes 1310720 | tf_op jit(solution)/shard_map/slice | solution.py:93
  54.9 2.2 %copy.38 = bf16[1,10,128,256]{3,2,1,0:T(8,128)(2,1)} copy(bf16[1,10,128,256]{2,3,1,0:T(8,128)(2,1)} %get-tuple-element.24) | data formatting | bytes 1310720 | tf_op jit(solution)/shard_map/slice | solution.py:93
  57.0 1.1 copy.39
  58.1 1.1 copy.31
  59.3 3.0 %fusion.7 = bf16[2304,256]{0,1:T(8,128)(2,1)} fusion(bf16[256,1152]{1,0:T(8,128)(2,1)} %bitcast.3, bf16[256,1152]{1,0:T(8,128)(2,1)} %bitcast.2, pred[]{:T(512)S(6)} %eq.8), kind=kLoop, calls=%fused_computation.46 | loop fusion | flops 5308416 | bytes 2359297 | tf_op jit(solution)/shard_map/transpose | solution.py:106
  62.2 1.6 copy.33
  63.8 1.9 %fusion.50 = f32[1280,256]{1,0:T(8,128)S(1)} fusion(bf16[1280,256]{1,0:T(8,128)(2,1)} %bitcast.205, bf16[3,3,256,256]{3,2,1,0:T(8,128)(2,1)S(1)} %bitcast.185), kind=kOutput, calls=%fused_computation.116 | convolution fusion | flops 167772160 | bytes 2097152 | tf_op jit(solution)/shard_map/dot_general | solution.py:114
  66.0 0.7 copy-done.10
  67.1 0.7 copy-done.9
  68.2 0.7 copy-done.4
  69.3 0.7 copy-done.8
  70.4 0.8 copy-done.7
  71.5 0.8 copy-done.3
  72.6 0.7 copy-done.5
  73.3 0.4 fusion.71
  73.8 0.4 multiply_reduce_fusion.1
  74.2 0.8 copy-done.2
  75.1 2.0 %fusion.68 = (f32[1280]{0:T(1024)S(1)}, f32[1280]{0:T(1024)S(1)}, f32[1280,256]{1,0:T(8,128)S(1)}, bf16[1280,256]{1,0:T(8,128)(2,1)}) fusion(f32[1280]{0:T(1024)S(1)} %add_rsqrt_fusion, f32[1280,256]{1,0:T(8,128)S(1)} %get-tuple-element.37, f32[1280]{0:T(1024)S(1)} %broadcast_multiply_fusion.2, f32[256]{0:T(256)S(1)} %copy-done.24, ...), kind=kLoop, calls=%fused_computation.140 | loop fusion | flops 5895680 | bytes 4609024 | tf_op jit(solution)/shard_map/reduce_sum | solution.py:86
  77.1 1.0 multiply_convert_fusion
  78.6 0.5 copy-done.20
  79.4 0.4 fusion.13
  81.8 0.4 fusion.8
  82.2 1.2 fusion.70
  83.3 0.4 copy.48
  83.7 1.6 copy.49
  85.5 1.9 %collective-permute-start.3 = (f32[256,1152]{1,0:T(8,128)S(1)}, f32[256,1152]{1,0:T(8,128)S(1)}, u32[]{:S(2)}, u32[]{:S(2)}) collective-permute-start(f32[256,1152]{1,0:T(8,128)S(1)} %broadcast_select_fusion.1), channel_id=1, source_target_pairs={{0,16},{16,0},{32,48},{48,32},{64,80},{80,64},{96,112},{112,96},{1... | collective-permute-start | bytes 3538952 | tf_op jit(solution)/shard_map/ppermute | solution.py:30
  87.4 2.8 %collective-permute-done.3 = f32[256,1152]{1,0:T(8,128)S(1)} collective-permute-done((f32[256,1152]{1,0:T(8,128)S(1)}, f32[256,1152]{1,0:T(8,128)S(1)}, u32[]{:S(2)}, u32[]{:S(2)}) %collective-permute-start.3) | collective-permute-done | bytes 1179680 | tf_op jit(solution)/shard_map/ppermute | solution.py:30
  90.2 1.2 select_add_fusion
  91.4 6.9 %all-to-all-start.1 = ((f32[16,16,1152]{2,1,0:T(8,128)}), f32[16,16,1152]{2,1,0:T(8,128)S(1)}, u32[]{:S(2)}, u32[]{:S(2)}) async-start(f32[16,16,1152]{2,1,0:T(8,128)} %bitcast.203), calls=%async_computation.1 | async-start | bytes 2359296 | tf_op jit(solution)/shard_map/all_to_all | solution.py:42
  98.3 1.7 pad_slice_fusion.12
  101.0 1.3 convolution_add_fusion.13
  102.3 21.5 %all-to-all-done.1 = f32[16,16,1152]{2,1,0:T(8,128)S(1)} async-done(((f32[16,16,1152]{2,1,0:T(8,128)}), f32[16,16,1152]{2,1,0:T(8,128)S(1)}, u32[]{:S(2)}, u32[]{:S(2)}) %all-to-all-start.1) | async-done | bytes 1179680 | tf_op jit(solution)/shard_map/all_to_all | solution.py:42
  123.8 8.8 %collective-permute-start.4 = (f32[16,1152]{1,0:T(8,128)S(1)}, f32[16,1152]{1,0:T(8,128)S(1)}, u32[]{:S(2)}, u32[]{:S(2)}) collective-permute-start(f32[16,1152]{1,0:T(8,128)S(1)} %reduce_sum.49), channel_id=1, source_target_pairs={{0,32},{16,48},{32,0},{48,16},{64,96},{80,112},{96,64},{112,80},{1... | collective-permute-start | bytes 221192 | tf_op jit(solution)/shard_map/ppermute | solution.py:30
  132.7 1.6 convolution_add_fusion.12
  134.6 8.1 %collective-permute-start.5 = (f32[16,1152]{1,0:T(8,128)S(1)}, f32[16,1152]{1,0:T(8,128)S(1)}, u32[]{:S(2)}, u32[]{:S(2)}) collective-permute-start(f32[16,1152]{1,0:T(8,128)S(1)} %add.109), channel_id=1, source_target_pairs={{0,96},{16,112},{32,64},{48,80},{64,32},{80,48},{96,0},{112,16},{1... | collective-permute-start | bytes 221192 | tf_op jit(solution)/shard_map/ppermute | solution.py:30
  143.1 1.4 collective-permute-done.5
  144.4 2.5 %collective-permute-start.6 = (f32[16,1152]{1,0:T(8,128)S(1)}, f32[16,1152]{1,0:T(8,128)S(1)}, u32[]{:S(2)}, u32[]{:S(2)}) collective-permute-start(f32[16,1152]{1,0:T(8,128)S(1)} %add.110), channel_id=1, source_target_pairs={{0,128},{16,144},{32,160},{48,176},{64,192},{80,208},{96,224},{112... | collective-permute-start | bytes 221192 | tf_op jit(solution)/shard_map/ppermute | solution.py:30
  147.2 2.3 %collective-permute-done.6 = f32[16,1152]{1,0:T(8,128)S(1)} collective-permute-done((f32[16,1152]{1,0:T(8,128)S(1)}, f32[16,1152]{1,0:T(8,128)S(1)}, u32[]{:S(2)}, u32[]{:S(2)}) %collective-permute-start.6) | collective-permute-done | bytes 73760 | tf_op jit(solution)/shard_map/ppermute | solution.py:30
  149.5 2.1 %collective-permute-start.7 = (f32[16,1152]{1,0:T(8,128)S(1)}, f32[16,1152]{1,0:T(8,128)S(1)}, u32[]{:S(2)}, u32[]{:S(2)}) collective-permute-start(f32[16,1152]{1,0:T(8,128)S(1)} %add.111), channel_id=1, source_target_pairs={{0,384},{16,400},{32,416},{48,432},{64,448},{80,464},{96,480},{112... | collective-permute-start | bytes 221192 | tf_op jit(solution)/shard_map/ppermute | solution.py:30
  152.0 3.8 %collective-permute-done.7 = f32[16,1152]{1,0:T(8,128)S(1)} collective-permute-done((f32[16,1152]{1,0:T(8,128)S(1)}, f32[16,1152]{1,0:T(8,128)S(1)}, u32[]{:S(2)}, u32[]{:S(2)}) %collective-permute-start.7) | collective-permute-done | bytes 73760 | tf_op jit(solution)/shard_map/ppermute | solution.py:30
  155.9 12.7 %collective-permute-start.8 = (f32[16,1152]{1,0:T(8,128)S(1)}, f32[16,1152]{1,0:T(8,128)S(1)}, u32[]{:S(2)}, u32[]{:S(2)}) collective-permute-start(f32[16,1152]{1,0:T(8,128)S(1)} %add.112), channel_id=1, source_target_pairs={{0,16},{16,0},{32,48},{48,32},{64,80},{80,64},{96,112},{112,96},{1... | collective-permute-start | bytes 221192 | tf_op jit(solution)/shard_map/ppermute | solution.py:30
  168.6 1.1 fusion.6
  169.7 0.8 slice.214
  170.6 0.7 copy.46
  (84 shorter events, 8.6 us)
Async XLA Ops:
  0.6 9.2 %copy-start.21 = (bf16[1,8,128,256]{3,2,1,0:T(8,128)(2,1)S(1)}, bf16[1,8,128,256]{3,2,1,0:T(8,128)(2,1)}, u32[]{:S(2)}) copy-start(bf16[1,8,128,256]{3,2,1,0:T(8,128)(2,1)} %param.7) | copy-start | bytes 1572868
  1.8 8.4 %copy-start.22 = (bf16[1,8,128,256]{3,2,1,0:T(8,128)(2,1)S(1)}, bf16[1,8,128,256]{3,2,1,0:T(8,128)(2,1)}, u32[]{:S(2)}) copy-start(bf16[1,8,128,256]{3,2,1,0:T(8,128)(2,1)} %param.4) | copy-start | bytes 1572868
  2.6 26.8 %all-to-all-start = ((bf16[16,16,1152]{2,1,0:T(8,128)(2,1)}), bf16[16,16,1152]{2,1,0:T(8,128)(2,1)}, u32[]{:S(2)}, u32[]{:S(2)}) async-start(bf16[16,16,1152]{2,1,0:T(8,128)(2,1)} %broadcast_in_dim.9), calls=%async_computation | async-start | bytes 1179648 | tf_op jit(solution)/shard_map/all_to_all | solution.py:36
  10.4 17.4 %collective-permute-start = (bf16[1,2,128,512]{2,3,1,0:T(8,128)(2,1)S(1)}, bf16[1,2,128,512]{2,3,1,0:T(8,128)(2,1)S(1)}, u32[]{:S(2)}, u32[]{:S(2)}) collective-permute-start(bf16[1,2,128,512]{2,3,1,0:T(8,128)(2,1)S(1)} %get-tuple-element.19), channel_id=1, source_target_pairs={{0,1},{1,2},{2,3},{3,4},{4,5},{5,6},{6,7},{7,8},{8,9},{9,10},{10,1... | collective-permute-start | bytes 786440 | tf_op jit(solution)/shard_map/ppermute | solution.py:20
  13.5 14.3 %collective-permute-start.1 = (bf16[1,2,128,512]{2,3,1,0:T(8,128)(2,1)S(1)}, bf16[1,2,128,512]{2,3,1,0:T(8,128)(2,1)S(1)}, u32[]{:S(2)}, u32[]{:S(2)}) collective-permute-start(bf16[1,2,128,512]{2,3,1,0:T(8,128)(2,1)S(1)} %get-tuple-element.20), channel_id=1, source_target_pairs={{1,0},{2,1},{3,2},{4,3},{5,4},{6,5},{7,6},{8,7},{9,8},{10,9},{11,1... | collective-permute-start | bytes 786440 | tf_op jit(solution)/shard_map/ppermute | solution.py:21
  27.8 0.7 copy-start.19
  28.5 0.7 copy-start.17
  29.4 29.8 %collective-permute-start.2 = (bf16[16,16,1152]{2,1,0:T(8,128)(2,1)}, bf16[16,16,1152]{2,1,0:T(8,128)(2,1)}, u32[]{:S(2)}, u32[]{:S(2)}) collective-permute-start(bf16[16,16,1152]{2,1,0:T(8,128)(2,1)} %all-to-all-done), channel_id=1, source_target_pairs={{0,16},{16,0},{32,48},{48,32},{64,80},{80,64},{96,112},{112,96},{1... | collective-permute-start | bytes 1769480 | tf_op jit(solution)/shard_map/ppermute | solution.py:30
  34.1 2.9 %copy-start.11 = (bf16[1,10,128,256]{2,3,1,0:T(8,128)(2,1)S(1)}, bf16[1,10,128,256]{2,3,1,0:T(8,128)(2,1)}, u32[]{:S(2)}) copy-start(bf16[1,10,128,256]{2,3,1,0:T(8,128)(2,1)} %get-tuple-element.15) | copy-start | bytes 1966084
  37.0 1.1 copy-start.18
  63.8 8.8 %copy-start = (bf16[2304,256]{1,0:T(8,128)(2,1)}, bf16[2304,256]{1,0:T(8,128)(2,1)S(1)}, u32[]{:S(2)}) copy-start(bf16[2304,256]{1,0:T(8,128)(2,1)S(1)} %copy.33) | copy-start | bytes 3538948
  63.8 1.9 %copy-start.6 = (bf16[1,10,128,256]{3,2,1,0:T(8,128)(2,1)S(1)}, bf16[1,10,128,256]{3,2,1,0:T(8,128)(2,1)}, u32[]{:S(2)}) copy-start(bf16[1,10,128,256]{3,2,1,0:T(8,128)(2,1)} %copy.34) | copy-start | bytes 1966084
  65.7 1.1 copy-start.10
  66.8 1.1 copy-start.9
  67.9 1.1 copy-start.4
  68.9 1.1 copy-start.8
  70.0 1.1 copy-start.7
  71.1 1.1 copy-start.3
  72.2 1.1 copy-start.5
  73.7 1.3 copy-start.2
  73.7 1.3 copy-start.24
  78.1 1.0 copy-start.20
  79.4 1.0 copy-start.23
  85.5 4.7 %collective-permute-start.3 = (f32[256,1152]{1,0:T(8,128)S(1)}, f32[256,1152]{1,0:T(8,128)S(1)}, u32[]{:S(2)}, u32[]{:S(2)}) collective-permute-start(f32[256,1152]{1,0:T(8,128)S(1)} %broadcast_select_fusion.1), channel_id=1, source_target_pairs={{0,16},{16,0},{32,48},{48,32},{64,80},{80,64},{96,112},{112,96},{1... | collective-permute-start | bytes 3538952 | tf_op jit(solution)/shard_map/ppermute | solution.py:30
  91.4 32.4 %all-to-all-start.1 = ((f32[16,16,1152]{2,1,0:T(8,128)}), f32[16,16,1152]{2,1,0:T(8,128)S(1)}, u32[]{:S(2)}, u32[]{:S(2)}) async-start(f32[16,16,1152]{2,1,0:T(8,128)} %bitcast.203), calls=%async_computation.1 | async-start | bytes 2359296 | tf_op jit(solution)/shard_map/all_to_all | solution.py:42
  98.3 1.7 copy-start.1
  102.3 30.4 %copy-start.16 = (bf16[1,8,128,256]{3,2,1,0:T(8,128)(2,1)S(1)}, bf16[1,8,128,256]{3,2,1,0:T(8,128)(2,1)}, u32[]{:S(2)}) copy-start(bf16[1,8,128,256]{3,2,1,0:T(8,128)(2,1)} %get-tuple-element.33) | copy-start | bytes 1572868
  123.8 10.7 %collective-permute-start.4 = (f32[16,1152]{1,0:T(8,128)S(1)}, f32[16,1152]{1,0:T(8,128)S(1)}, u32[]{:S(2)}, u32[]{:S(2)}) collective-permute-start(f32[16,1152]{1,0:T(8,128)S(1)} %reduce_sum.49), channel_id=1, source_target_pairs={{0,32},{16,48},{32,0},{48,16},{64,96},{80,112},{96,64},{112,80},{1... | collective-permute-start | bytes 221192 | tf_op jit(solution)/shard_map/ppermute | solution.py:30
  132.7 10.0 %copy-start.15 = (bf16[1,8,128,256]{3,2,1,0:T(8,128)(2,1)S(1)}, bf16[1,8,128,256]{3,2,1,0:T(8,128)(2,1)}, u32[]{:S(2)}) copy-start(bf16[1,8,128,256]{3,2,1,0:T(8,128)(2,1)} %get-tuple-element.30) | copy-start | bytes 1572868
  134.6 9.8 %collective-permute-start.5 = (f32[16,1152]{1,0:T(8,128)S(1)}, f32[16,1152]{1,0:T(8,128)S(1)}, u32[]{:S(2)}, u32[]{:S(2)}) collective-permute-start(f32[16,1152]{1,0:T(8,128)S(1)} %add.109), channel_id=1, source_target_pairs={{0,96},{16,112},{32,64},{48,80},{64,32},{80,48},{96,0},{112,16},{1... | collective-permute-start | bytes 221192 | tf_op jit(solution)/shard_map/ppermute | solution.py:30
  142.7 4.2 %copy-start.14 = (bf16[1,8,128,256]{3,2,1,0:T(8,128)(2,1)S(1)}, bf16[1,8,128,256]{3,2,1,0:T(8,128)(2,1)}, u32[]{:S(2)}) copy-start(bf16[1,8,128,256]{3,2,1,0:T(8,128)(2,1)} %get-tuple-element.31) | copy-start | bytes 1572868
  144.4 5.1 %collective-permute-start.6 = (f32[16,1152]{1,0:T(8,128)S(1)}, f32[16,1152]{1,0:T(8,128)S(1)}, u32[]{:S(2)}, u32[]{:S(2)}) collective-permute-start(f32[16,1152]{1,0:T(8,128)S(1)} %add.110), channel_id=1, source_target_pairs={{0,128},{16,144},{32,160},{48,176},{64,192},{80,208},{96,224},{112... | collective-permute-start | bytes 221192 | tf_op jit(solution)/shard_map/ppermute | solution.py:30
  146.9 4.8 %copy-start.13 = (bf16[1,8,128,256]{3,2,1,0:T(8,128)(2,1)S(1)}, bf16[1,8,128,256]{3,2,1,0:T(8,128)(2,1)}, u32[]{:S(2)}) copy-start(bf16[1,8,128,256]{3,2,1,0:T(8,128)(2,1)} %get-tuple-element.32) | copy-start | bytes 1572868
  149.5 6.3 %collective-permute-start.7 = (f32[16,1152]{1,0:T(8,128)S(1)}, f32[16,1152]{1,0:T(8,128)S(1)}, u32[]{:S(2)}, u32[]{:S(2)}) collective-permute-start(f32[16,1152]{1,0:T(8,128)S(1)} %add.111), channel_id=1, source_target_pairs={{0,384},{16,400},{32,416},{48,432},{64,448},{80,464},{96,480},{112... | collective-permute-start | bytes 221192 | tf_op jit(solution)/shard_map/ppermute | solution.py:30
  152.0 17.7 %copy-start.12 = (bf16[1280,256]{1,0:T(8,128)(2,1)S(1)}, bf16[1280,256]{1,0:T(8,128)(2,1)}, u32[]{:S(2)}) copy-start(bf16[1280,256]{1,0:T(8,128)(2,1)} %get-tuple-element.16) | copy-start | bytes 1966084
  155.9 14.7 %collective-permute-start.8 = (f32[16,1152]{1,0:T(8,128)S(1)}, f32[16,1152]{1,0:T(8,128)S(1)}, u32[]{:S(2)}, u32[]{:S(2)}) collective-permute-start(f32[16,1152]{1,0:T(8,128)S(1)} %add.112), channel_id=1, source_target_pairs={{0,16},{16,0},{32,48},{48,32},{64,80},{80,64},{96,112},{112,96},{1... | collective-permute-start | bytes 221192 | tf_op jit(solution)/shard_map/ppermute | solution.py:30

commit v17 on v12

--- a/solution.py
+++ b/solution.py
@@ -43,8 +43,9 @@
 
 
 def split_pair(value, upper, dim):
-    low, high = jnp.split(value, 2, axis=dim)
-    return jnp.where(upper, high, low), jnp.where(upper, low, high)
+    half = value.shape[dim] // 2
+    at = upper.astype(jnp.int32) * half
+    return lax.dynamic_slice_in_dim(value, at, half, dim), lax.dynamic_slice_in_dim(value, half - at, half, dim)
 
 
 def join_pair(value, other, upper, dim):

time: 139 us -> 143 us (1.029)
  the two profiles are of different devices: /device:TPU:71 before, /device:TPU:65 now
where the time goes in v17:
time: 143 us; the launch traced here: 142 us
  starting transfers between devices  64.7 us (45%)
  waiting for transfers between devices  37.3 us (26%)
  local copies, waits for them, and re-layouts  16.8 us (12%)
  matrix products  13 us (9%)
  other arithmetic  9.43 us (7%)
    ppermute x7, starting transfers between devices, exchange(): return lax.ppermute(value, axis, pairs)  37.6 us
    ppermute x2, waiting for transfers between devices, padded_2(): before = lax.ppermute(last, axis, up)  22.3 us
    unnamed x34, local copies, waits for them, and re-layouts  11.1 us
    ppermute x2, starting transfers between devices, padded_2(): after = lax.ppermute(initial, axis, down)  8.6 us
    all_to_all x1, waiting for transfers between devices, gather_chunks(): return lax.all_to_all(copies, axis, 0, 0, tiled=False)  8.48 us
    all_to_all x1, starting transfers between devices, gather_chunks(): return lax.all_to_all(copies, axis, 0, 0, tiled=False)  7.64 us
    ppermute x7, waiting for transfers between devices, exchange(): return lax.ppermute(value, axis, pairs)  6.53 us
    ppermute x2, starting transfers between devices, padded_2(): before = lax.ppermute(last, axis, up)  6.18 us
  transfers between devices with their start and end apart: 13, of which 7 were waited for; matrix products, arithmetic and copies ran while one was open for 8% of the time, Pallas kernels for 0%

profile of v17, /device:TPU:65, one launch (start us, length us, event | category | flops | bytes accessed | tf_op | source)
XLA Modules:
  0.0 142.4 jit_solution(7464491384613649945)
XLA Ops:
  0.6 1.0 copy.14
  1.8 0.9 broadcast_in_dim.2
  2.6 7.6 %all-to-all-start = ((bf16[16,16,1152]{2,1,0:T(8,128)(2,1)}), bf16[16,16,1152]{2,1,0:T(8,128)(2,1)S(1)}, u32[]{:S(2)}, u32[]{:S(2)}) async-start(bf16[16,16,1152]{2,1,0:T(8,128)(2,1)} %broadcast_in_dim.2), calls=%async_computation | async-start | bytes 1179648 | tf_op jit(solution)/shard_map/all_to_all | solution.py:36
  10.3 3.1 %collective-permute-start = (bf16[1,1,128,256]{3,2,1,0:T(8,128)(2,1)S(1)}, bf16[1,1,128,256]{3,2,1,0:T(8,128)(2,1)S(1)}, u32[]{:S(2)}, u32[]{:S(2)}) collective-permute-start(bf16[1,1,128,256]{3,2,1,0:T(8,128)(2,1)S(1)} %get-tuple-element.33), channel_id=1, source_target_pairs={{0,1},{1,2},{2,3},{3,4},{4,5},{5,6},{6,7},{7,8},{8,9},{9,10},{10,1... | collective-permute-start | bytes 196616 | tf_op jit(solution)/shard_map/ppermute | solution.py:20
  13.4 4.3 %collective-permute-start.1 = (bf16[1,1,128,256]{3,2,1,0:T(8,128)(2,1)S(1)}, bf16[1,1,128,256]{3,2,1,0:T(8,128)(2,1)S(1)}, u32[]{:S(2)}, u32[]{:S(2)}) collective-permute-start(bf16[1,1,128,256]{3,2,1,0:T(8,128)(2,1)S(1)} %get-tuple-element.34), channel_id=1, source_target_pairs={{1,0},{2,1},{3,2},{4,3},{5,4},{6,5},{7,6},{8,7},{9,8},{10,9},{11,1... | collective-permute-start | bytes 196616 | tf_op jit(solution)/shard_map/ppermute | solution.py:21
  17.7 8.5 %all-to-all-done = bf16[16,16,1152]{2,1,0:T(8,128)(2,1)S(1)} async-done(((bf16[16,16,1152]{2,1,0:T(8,128)(2,1)}), bf16[16,16,1152]{2,1,0:T(8,128)(2,1)S(1)}, u32[]{:S(2)}, u32[]{:S(2)}) %all-to-all-start) | async-done | bytes 589856 | tf_op jit(solution)/shard_map/all_to_all | solution.py:36
  26.2 3.3 %collective-permute-start.2 = (bf16[16,16,1152]{2,1,0:T(8,128)(2,1)S(1)}, bf16[16,16,1152]{2,1,0:T(8,128)(2,1)S(1)}, u32[]{:S(2)}, u32[]{:S(2)}) collective-permute-start(bf16[16,16,1152]{2,1,0:T(8,128)(2,1)S(1)} %all-to-all-done), channel_id=1, source_target_pairs={{0,16},{16,0},{32,48},{48,32},{64,80},{80,64},{96,112},{112,96},{1... | collective-permute-start | bytes 1769480 | tf_op jit(solution)/shard_map/ppermute | solution.py:30
  29.8 1.1 pad_maximum_fusion.2
  30.8 1.6 %fusion.35 = (bf16[1,8,128,256]{3,2,1,0:T(8,128)(2,1)}, bf16[1,8,128,256]{3,2,1,0:T(8,128)(2,1)}, bf16[1,8,128,256]{3,2,1,0:T(8,128)(2,1)}, bf16[1,8,128,256]{3,...) fusion(bf16[1,10,130,256]{3,2,1,0:T(8,128)(2,1)S(1)} %select_maximum_fusion.2), kind=kLoop, calls=%fused_computation.90 | loop fusion | bytes 6291456 | tf_op jit(solution)/shard_map/slice | solution.py:94
  32.4 0.8 copy-done.12
  33.2 1.9 %fusion.7 = bf16[2304,256]{0,1:T(8,128)(2,1)S(1)} fusion(bf16[256,1152]{1,0:T(8,128)(2,1)} %bitcast.197, bf16[256,1152]{1,0:T(8,128)(2,1)} %bitcast.206, pred[]{:T(512)S(6)} %eq.8), kind=kLoop, calls=%fused_computation.23 | loop fusion | flops 5308416 | bytes 2359297 | tf_op jit(solution)/shard_map/transpose | solution.py:107
  35.2 0.6 copy.15
  35.8 1.4 fusion.27
  37.2 0.3 fusion.28
  37.5 0.7 copy-done.1
  38.8 0.7 copy-done.7
  39.9 0.7 copy-done.5
  40.6 0.3 convolution_add_fusion.9
  40.9 0.7 copy-done.4
  42.0 0.3 fusion.3
  42.3 0.7 copy-done.6
  43.0 0.4 fusion.38
  43.4 0.4 multiply_reduce_fusion.1
  43.8 0.6 copy-done.13
  44.4 1.9 %fusion.32 = (f32[1024]{0:T(1024)S(1)}, f32[1024]{0:T(1024)S(1)}, f32[1024,256]{1,0:T(8,128)S(1)}, bf16[1024,256]{1,0:T(8,128)(2,1)}) fusion(f32[1024]{0:T(1024)S(1)} %add_rsqrt_fusion, f32[1024,256]{1,0:T(8,128)S(1)} %get-tuple-element.36, f32[1024]{0:T(1024)S(1)} %broadcast_multiply_fusion.2, f32[256]{0:T(256)S(1)} %copy-done.14, ...), kind=kLoop, calls=%fused_computation.88 | loop fusion | flops 4978688 | bytes 3163136 | tf_op jit(solution)/shard_map/reduce_sum | solution.py:87
  46.4 0.8 multiply_convert_fusion
  47.4 0.3 fusion.16
  47.8 0.3 fusion.15
  48.1 0.3 fusion.14
  48.5 0.3 fusion.13
  48.8 0.3 fusion.12
  49.2 0.3 fusion.11
  49.5 0.3 fusion.10
  49.9 0.3 fusion.9
  50.2 0.3 fusion.8
  50.6 1.2 constant_dynamic-slice_fusion
  51.8 2.6 %copy.22 = f32[256,1152]{1,0:T(8,128)} copy(f32[256,1152]{0,1:T(8,128)} %get-tuple-element.12) | data formatting | bytes 2359296
  54.4 1.9 %collective-permute-start.5 = (f32[256,1152]{1,0:T(8,128)}, f32[256,1152]{1,0:T(8,128)}, u32[]{:S(2)}, u32[]{:S(2)}) collective-permute-start(f32[256,1152]{1,0:T(8,128)} %copy.22), channel_id=1, source_target_pairs={{0,16},{16,0},{32,48},{48,32},{64,80},{80,64},{96,112},{112,96},{1... | collective-permute-start | bytes 3538952 | tf_op jit(solution)/shard_map/ppermute | solution.py:30
  56.4 1.4 copy.21
  57.8 1.7 %collective-permute-done.5 = f32[256,1152]{1,0:T(8,128)} collective-permute-done((f32[256,1152]{1,0:T(8,128)}, f32[256,1152]{1,0:T(8,128)}, u32[]{:S(2)}, u32[]{:S(2)}) %collective-permute-start.5) | collective-permute-done | bytes 1179680 | tf_op jit(solution)/shard_map/ppermute | solution.py:30
  59.5 2.8 %add.115 = f32[256,1152]{1,0:T(8,128)} add(f32[256,1152]{1,0:T(8,128)} %copy.21, f32[256,1152]{1,0:T(8,128)} %collective-permute-done.5) | non-fusion elementwise | flops 294912 | bytes 3538944 | tf_op jit(solution)/shard_map/add | solution.py:59
  62.3 4.8 %all-to-all-start.1 = ((f32[16,16,1152]{2,1,0:T(8,128)}), f32[16,16,1152]{2,1,0:T(8,128)S(1)}, u32[]{:S(2)}, u32[]{:S(2)}) async-start(f32[16,16,1152]{2,1,0:T(8,128)} %bitcast.46), calls=%async_computation.1 | async-start | bytes 2359296 | tf_op jit(solution)/shard_map/all_to_all | solution.py:42
  67.1 3.1 %collective-permute-start.3 = (bf16[1,1,128,256]{3,2,1,0:T(8,128)(2,1)S(1)}, bf16[1,1,128,256]{3,2,1,0:T(8,128)(2,1)S(1)}, u32[]{:S(2)}, u32[]{:S(2)}) collective-permute-start(bf16[1,1,128,256]{3,2,1,0:T(8,128)(2,1)S(1)} %get-tuple-element.29), channel_id=1, source_target_pairs={{0,1},{1,2},{2,3},{3,4},{4,5},{5,6},{6,7},{7,8},{8,9},{9,10},{10,1... | collective-permute-start | bytes 196616 | tf_op jit(solution)/shard_map/ppermute | solution.py:20
  70.2 4.3 %collective-permute-start.4 = (bf16[1,1,128,256]{3,2,1,0:T(8,128)(2,1)S(1)}, bf16[1,1,128,256]{3,2,1,0:T(8,128)(2,1)S(1)}, u32[]{:S(2)}, u32[]{:S(2)}) collective-permute-start(bf16[1,1,128,256]{3,2,1,0:T(8,128)(2,1)S(1)} %get-tuple-element.30), channel_id=1, source_target_pairs={{1,0},{2,1},{3,2},{4,3},{5,4},{6,5},{7,6},{8,7},{9,8},{10,9},{11,1... | collective-permute-start | bytes 196616 | tf_op jit(solution)/shard_map/ppermute | solution.py:21
  74.5 22.3 %collective-permute-done.3 = bf16[1,1,128,256]{3,2,1,0:T(8,128)(2,1)S(1)} collective-permute-done((bf16[1,1,128,256]{3,2,1,0:T(8,128)(2,1)S(1)}, bf16[1,1,128,256]{3,2,1,0:T(8,128)(2,1)S(1)}, u32[]{:S(2)}, u32[]{:S(2)}) %collective-permute-start.3) | collective-permute-done | bytes 65568 | tf_op jit(solution)/shard_map/ppermute | solution.py:20
  97.0 1.3 fusion.34
  98.3 0.3 fusion.26
  98.6 0.3 convolution_add_fusion.6
  98.9 0.3 convolution_add_fusion.5
  99.3 1.3 convolution_add_fusion.4
  100.7 8.9 %collective-permute-start.6 = (f32[16,1152]{1,0:T(8,128)S(1)}, f32[16,1152]{1,0:T(8,128)S(1)}, u32[]{:S(2)}, u32[]{:S(2)}) collective-permute-start(f32[16,1152]{1,0:T(8,128)S(1)} %reduce_sum.49), channel_id=1, source_target_pairs={{0,32},{16,48},{32,0},{48,16},{64,96},{80,112},{96,64},{112,80},{1... | collective-permute-start | bytes 221192 | tf_op jit(solution)/shard_map/ppermute | solution.py:30
  109.6 1.6 %convolution_add_fusion.3 = f32[1024,256]{1,0:T(8,128)S(1)} fusion(f32[1024,256]{1,0:T(8,128)} %convolution_add_fusion.4, bf16[1024,256]{1,0:T(8,128)(2,1)S(1)} %multiply_convert_fusion, bf16[3,3,256,256]{3,2,1,0:T(8,128)(2,1)S(1)} %bitcast.173), kind=kOutput, calls=%fused_computation.12 | convolution fusion | flops 134479872 | bytes 2752512 | tf_op jit(solution)/shard_map/dot_general | solution.py:126
  111.3 8.3 %collective-permute-start.7 = (f32[16,1152]{1,0:T(8,128)S(1)}, f32[16,1152]{1,0:T(8,128)S(1)}, u32[]{:S(2)}, u32[]{:S(2)}) collective-permute-start(f32[16,1152]{1,0:T(8,128)S(1)} %add.116), channel_id=1, source_target_pairs={{0,96},{16,112},{32,64},{48,80},{64,32},{80,48},{96,0},{112,16},{1... | collective-permute-start | bytes 221192 | tf_op jit(solution)/shard_map/ppermute | solution.py:30
  119.7 0.3 convolution_add_fusion.2
  120.1 1.4 collective-permute-done.7
  121.4 3.1 %collective-permute-start.8 = (f32[16,1152]{1,0:T(8,128)S(1)}, f32[16,1152]{1,0:T(8,128)S(1)}, u32[]{:S(2)}, u32[]{:S(2)}) collective-permute-start(f32[16,1152]{1,0:T(8,128)S(1)} %add.117), channel_id=1, source_target_pairs={{0,128},{16,144},{32,160},{48,176},{64,192},{80,208},{96,224},{112... | collective-permute-start | bytes 221192 | tf_op jit(solution)/shard_map/ppermute | solution.py:30
  124.5 0.3 convolution_add_fusion.1
  124.9 1.7 %collective-permute-done.8 = f32[16,1152]{1,0:T(8,128)S(1)} collective-permute-done((f32[16,1152]{1,0:T(8,128)S(1)}, f32[16,1152]{1,0:T(8,128)S(1)}, u32[]{:S(2)}, u32[]{:S(2)}) %collective-permute-start.8) | collective-permute-done | bytes 73760 | tf_op jit(solution)/shard_map/ppermute | solution.py:30
  126.5 4.4 %collective-permute-start.9 = (f32[16,1152]{1,0:T(8,128)S(1)}, f32[16,1152]{1,0:T(8,128)S(1)}, u32[]{:S(2)}, u32[]{:S(2)}) collective-permute-start(f32[16,1152]{1,0:T(8,128)S(1)} %add.118), channel_id=1, source_target_pairs={{0,384},{16,400},{32,416},{48,432},{64,448},{80,464},{96,480},{112... | collective-permute-start | bytes 221192 | tf_op jit(solution)/shard_map/ppermute | solution.py:30
  130.9 0.3 fusion.30
  131.3 1.6 %collective-permute-done.9 = f32[16,1152]{1,0:T(8,128)S(1)} collective-permute-done((f32[16,1152]{1,0:T(8,128)S(1)}, f32[16,1152]{1,0:T(8,128)S(1)}, u32[]{:S(2)}, u32[]{:S(2)}) %collective-permute-start.9) | collective-permute-done | bytes 73760 | tf_op jit(solution)/shard_map/ppermute | solution.py:30
  132.9 7.6 %collective-permute-start.10 = (f32[16,1152]{1,0:T(8,128)S(1)}, f32[16,1152]{1,0:T(8,128)S(1)}, u32[]{:S(2)}, u32[]{:S(2)}) collective-permute-start(f32[16,1152]{1,0:T(8,128)S(1)} %add.119), channel_id=1, source_target_pairs={{0,16},{16,0},{32,48},{48,32},{64,80},{80,64},{96,112},{112,96},{1... | collective-permute-start | bytes 221192 | tf_op jit(solution)/shard_map/ppermute | solution.py:30
  140.5 1.1 fusion.6
  141.7 0.7 copy.19
  (51 shorter events, 2.4 us)
Async XLA Ops:
  0.6 9.7 %copy-start = (bf16[1,8,128,256]{3,2,1,0:T(8,128)(2,1)S(1)}, bf16[1,8,128,256]{3,2,1,0:T(8,128)(2,1)}, u32[]{:S(2)}) copy-start(bf16[1,8,128,256]{3,2,1,0:T(8,128)(2,1)} %param.4) | copy-start | bytes 1572868
  2.6 23.6 %all-to-all-start = ((bf16[16,16,1152]{2,1,0:T(8,128)(2,1)}), bf16[16,16,1152]{2,1,0:T(8,128)(2,1)S(1)}, u32[]{:S(2)}, u32[]{:S(2)}) async-start(bf16[16,16,1152]{2,1,0:T(8,128)(2,1)} %broadcast_in_dim.2), calls=%async_computation | async-start | bytes 1179648 | tf_op jit(solution)/shard_map/all_to_all | solution.py:36
  10.3 19.3 %collective-permute-start = (bf16[1,1,128,256]{3,2,1,0:T(8,128)(2,1)S(1)}, bf16[1,1,128,256]{3,2,1,0:T(8,128)(2,1)S(1)}, u32[]{:S(2)}, u32[]{:S(2)}) collective-permute-start(bf16[1,1,128,256]{3,2,1,0:T(8,128)(2,1)S(1)} %get-tuple-element.33), channel_id=1, source_target_pairs={{0,1},{1,2},{2,3},{3,4},{4,5},{5,6},{6,7},{7,8},{8,9},{9,10},{10,1... | collective-permute-start | bytes 196616 | tf_op jit(solution)/shard_map/ppermute | solution.py:20
  13.4 16.2 %collective-permute-start.1 = (bf16[1,1,128,256]{3,2,1,0:T(8,128)(2,1)S(1)}, bf16[1,1,128,256]{3,2,1,0:T(8,128)(2,1)S(1)}, u32[]{:S(2)}, u32[]{:S(2)}) collective-permute-start(bf16[1,1,128,256]{3,2,1,0:T(8,128)(2,1)S(1)} %get-tuple-element.34), channel_id=1, source_target_pairs={{1,0},{2,1},{3,2},{4,3},{5,4},{6,5},{7,6},{8,7},{9,8},{10,9},{11,1... | collective-permute-start | bytes 196616 | tf_op jit(solution)/shard_map/ppermute | solution.py:21
  26.2 4.6 %copy-start.8 = (bf16[16,16,1152]{2,1,0:T(8,128)(2,1)}, bf16[16,16,1152]{2,1,0:T(8,128)(2,1)S(1)}, u32[]{:S(2)}) copy-start(bf16[16,16,1152]{2,1,0:T(8,128)(2,1)S(1)} %all-to-all-done) | copy-start | bytes 1769476
  26.2 6.2 %collective-permute-start.2 = (bf16[16,16,1152]{2,1,0:T(8,128)(2,1)S(1)}, bf16[16,16,1152]{2,1,0:T(8,128)(2,1)S(1)}, u32[]{:S(2)}, u32[]{:S(2)}) collective-permute-start(bf16[16,16,1152]{2,1,0:T(8,128)(2,1)S(1)} %all-to-all-done), channel_id=1, source_target_pairs={{0,16},{16,0},{32,48},{48,32},{64,80},{80,64},{96,112},{112,96},{1... | collective-permute-start | bytes 1769480 | tf_op jit(solution)/shard_map/ppermute | solution.py:30
  32.4 0.8 copy-start.12
  35.8 1.4 copy-start.2
  37.2 1.0 copy-start.1
  38.5 1.0 copy-start.7
  39.6 1.0 copy-start.5
  40.6 1.0 copy-start.4
  41.9 1.0 copy-start.6
  43.0 0.8 copy-start.14
  43.4 1.0 copy-start.13
  46.4 1.0 copy-start.3
  54.4 5.1 %collective-permute-start.5 = (f32[256,1152]{1,0:T(8,128)}, f32[256,1152]{1,0:T(8,128)}, u32[]{:S(2)}, u32[]{:S(2)}) collective-permute-start(f32[256,1152]{1,0:T(8,128)} %copy.22), channel_id=1, source_target_pairs={{0,16},{16,0},{32,48},{48,32},{64,80},{80,64},{96,112},{112,96},{1... | collective-permute-start | bytes 3538952 | tf_op jit(solution)/shard_map/ppermute | solution.py:30
  62.3 38.3 %all-to-all-start.1 = ((f32[16,16,1152]{2,1,0:T(8,128)}), f32[16,16,1152]{2,1,0:T(8,128)S(1)}, u32[]{:S(2)}, u32[]{:S(2)}) async-start(f32[16,16,1152]{2,1,0:T(8,128)} %bitcast.46), calls=%async_computation.1 | async-start | bytes 2359296 | tf_op jit(solution)/shard_map/all_to_all | solution.py:42
  67.1 29.7 %collective-permute-start.3 = (bf16[1,1,128,256]{3,2,1,0:T(8,128)(2,1)S(1)}, bf16[1,1,128,256]{3,2,1,0:T(8,128)(2,1)S(1)}, u32[]{:S(2)}, u32[]{:S(2)}) collective-permute-start(bf16[1,1,128,256]{3,2,1,0:T(8,128)(2,1)S(1)} %get-tuple-element.29), channel_id=1, source_target_pairs={{0,1},{1,2},{2,3},{3,4},{4,5},{5,6},{6,7},{7,8},{8,9},{9,10},{10,1... | collective-permute-start | bytes 196616 | tf_op jit(solution)/shard_map/ppermute | solution.py:20
  70.2 26.6 %collective-permute-start.4 = (bf16[1,1,128,256]{3,2,1,0:T(8,128)(2,1)S(1)}, bf16[1,1,128,256]{3,2,1,0:T(8,128)(2,1)S(1)}, u32[]{:S(2)}, u32[]{:S(2)}) collective-permute-start(bf16[1,1,128,256]{3,2,1,0:T(8,128)(2,1)S(1)} %get-tuple-element.30), channel_id=1, source_target_pairs={{1,0},{2,1},{3,2},{4,3},{5,4},{6,5},{7,6},{8,7},{9,8},{10,9},{11,1... | collective-permute-start | bytes 196616 | tf_op jit(solution)/shard_map/ppermute | solution.py:21
  100.7 19.0 %copy-start.11 = (bf16[1,8,128,256]{3,2,1,0:T(8,128)(2,1)S(1)}, bf16[1,8,128,256]{3,2,1,0:T(8,128)(2,1)}, u32[]{:S(2)}) copy-start(bf16[1,8,128,256]{3,2,1,0:T(8,128)(2,1)} %get-tuple-element.16) | copy-start | bytes 1572868
  100.7 10.6 %collective-permute-start.6 = (f32[16,1152]{1,0:T(8,128)S(1)}, f32[16,1152]{1,0:T(8,128)S(1)}, u32[]{:S(2)}, u32[]{:S(2)}) collective-permute-start(f32[16,1152]{1,0:T(8,128)S(1)} %reduce_sum.49), channel_id=1, source_target_pairs={{0,32},{16,48},{32,0},{48,16},{64,96},{80,112},{96,64},{112,80},{1... | collective-permute-start | bytes 221192 | tf_op jit(solution)/shard_map/ppermute | solution.py:30
  111.3 10.1 %collective-permute-start.7 = (f32[16,1152]{1,0:T(8,128)S(1)}, f32[16,1152]{1,0:T(8,128)S(1)}, u32[]{:S(2)}, u32[]{:S(2)}) collective-permute-start(f32[16,1152]{1,0:T(8,128)S(1)} %add.116), channel_id=1, source_target_pairs={{0,96},{16,112},{32,64},{48,80},{64,32},{80,48},{96,0},{112,16},{1... | collective-permute-start | bytes 221192 | tf_op jit(solution)/shard_map/ppermute | solution.py:30
  119.7 4.8 %copy-start.10 = (bf16[1,8,128,256]{3,2,1,0:T(8,128)(2,1)S(1)}, bf16[1,8,128,256]{3,2,1,0:T(8,128)(2,1)}, u32[]{:S(2)}) copy-start(bf16[1,8,128,256]{3,2,1,0:T(8,128)(2,1)} %get-tuple-element.15) | copy-start | bytes 1572868
  121.4 5.1 %collective-permute-start.8 = (f32[16,1152]{1,0:T(8,128)S(1)}, f32[16,1152]{1,0:T(8,128)S(1)}, u32[]{:S(2)}, u32[]{:S(2)}) collective-permute-start(f32[16,1152]{1,0:T(8,128)S(1)} %add.117), channel_id=1, source_target_pairs={{0,128},{16,144},{32,160},{48,176},{64,192},{80,208},{96,224},{112... | collective-permute-start | bytes 221192 | tf_op jit(solution)/shard_map/ppermute | solution.py:30
  124.5 6.4 %copy-start.9 = (bf16[1,8,128,256]{3,2,1,0:T(8,128)(2,1)S(1)}, bf16[1,8,128,256]{3,2,1,0:T(8,128)(2,1)}, u32[]{:S(2)}) copy-start(bf16[1,8,128,256]{3,2,1,0:T(8,128)(2,1)} %get-tuple-element.20) | copy-start | bytes 1572868
  126.5 6.3 %collective-permute-start.9 = (f32[16,1152]{1,0:T(8,128)S(1)}, f32[16,1152]{1,0:T(8,128)S(1)}, u32[]{:S(2)}, u32[]{:S(2)}) collective-permute-start(f32[16,1152]{1,0:T(8,128)S(1)} %add.118), channel_id=1, source_target_pairs={{0,384},{16,400},{32,416},{48,432},{64,448},{80,464},{96,480},{112... | collective-permute-start | bytes 221192 | tf_op jit(solution)/shard_map/ppermute | solution.py:30
  132.9 8.7 %collective-permute-start.10 = (f32[16,1152]{1,0:T(8,128)S(1)}, f32[16,1152]{1,0:T(8,128)S(1)}, u32[]{:S(2)}, u32[]{:S(2)}) collective-permute-start(f32[16,1152]{1,0:T(8,128)S(1)} %add.119), channel_id=1, source_target_pairs={{0,16},{16,0},{32,48},{48,32},{64,80},{80,64},{96,112},{112,96},{1... | collective-permute-start | bytes 221192 | tf_op jit(solution)/shard_map/ppermute | solution.py:30

commit v18 on v12

--- a/solution.py
+++ b/solution.py
@@ -54,7 +54,10 @@
 def halve_sum(value, axis, bits, dim):
     me = lax.axis_index(axis)
     for bit in bits:
-        keep, send = split_pair(value, ((me >> bit) & 1) == 1, dim)
+        half = value.shape[dim] // 2
+        at = ((me >> bit) & 1) * half
+        keep = lax.dynamic_slice_in_dim(value, at, half, dim)
+        send = lax.dynamic_slice_in_dim(value, half - at, half, dim)
         value = keep + exchange(send, axis, bit)
     return value
 

time: 139 us -> 141 us (1.014)
  the two profiles are of different devices: /device:TPU:71 before, /device:TPU:65 now
where the time goes in v18:
time: 141 us; the launch traced here: 140 us
  starting transfers between devices  64.7 us (46%)
  waiting for transfers between devices  37.2 us (26%)
  local copies, waits for them, and re-layouts  16 us (11%)
  matrix products  13 us (9%)
  other arithmetic  7.8 us (6%)
    ppermute x7, starting transfers between devices, exchange(): return lax.ppermute(value, axis, pairs)  37.6 us
    ppermute x2, waiting for transfers between devices, padded_2(): before = lax.ppermute(last, axis, up)  22.3 us
    unnamed x30, local copies, waits for them, and re-layouts  10.3 us
    ppermute x2, starting transfers between devices, padded_2(): after = lax.ppermute(initial, axis, down)  8.6 us
    all_to_all x1, waiting for transfers between devices, gather_chunks(): return lax.all_to_all(copies, axis, 0, 0, tiled=False)  8.48 us
    all_to_all x1, starting transfers between devices, gather_chunks(): return lax.all_to_all(copies, axis, 0, 0, tiled=False)  7.64 us
    ppermute x7, waiting for transfers between devices, exchange(): return lax.ppermute(value, axis, pairs)  6.5 us
    ppermute x2, starting transfers between devices, padded_2(): before = lax.ppermute(last, axis, up)  6.18 us
  transfers between devices with their start and end apart: 13, of which 7 were waited for; matrix products, arithmetic and copies ran while one was open for 8% of the time, Pallas kernels for 0%

profile of v18, /device:TPU:65, one launch (start us, length us, event | category | flops | bytes accessed | tf_op | source)
XLA Modules:
  0.0 139.9 jit_solution(2115690232805758504)
XLA Ops:
  0.6 1.0 copy.14
  1.8 0.9 broadcast_in_dim.2
  2.6 7.6 %all-to-all-start = ((bf16[16,16,1152]{2,1,0:T(8,128)(2,1)}), bf16[16,16,1152]{2,1,0:T(8,128)(2,1)S(1)}, u32[]{:S(2)}, u32[]{:S(2)}) async-start(bf16[16,16,1152]{2,1,0:T(8,128)(2,1)} %broadcast_in_dim.2), calls=%async_computation | async-start | bytes 1179648 | tf_op jit(solution)/shard_map/all_to_all | solution.py:36
  10.3 3.1 %collective-permute-start = (bf16[1,1,128,256]{3,2,1,0:T(8,128)(2,1)S(1)}, bf16[1,1,128,256]{3,2,1,0:T(8,128)(2,1)S(1)}, u32[]{:S(2)}, u32[]{:S(2)}) collective-permute-start(bf16[1,1,128,256]{3,2,1,0:T(8,128)(2,1)S(1)} %get-tuple-element.33), channel_id=1, source_target_pairs={{0,1},{1,2},{2,3},{3,4},{4,5},{5,6},{6,7},{7,8},{8,9},{9,10},{10,1... | collective-permute-start | bytes 196616 | tf_op jit(solution)/shard_map/ppermute | solution.py:20
  13.4 4.3 %collective-permute-start.1 = (bf16[1,1,128,256]{3,2,1,0:T(8,128)(2,1)S(1)}, bf16[1,1,128,256]{3,2,1,0:T(8,128)(2,1)S(1)}, u32[]{:S(2)}, u32[]{:S(2)}) collective-permute-start(bf16[1,1,128,256]{3,2,1,0:T(8,128)(2,1)S(1)} %get-tuple-element.34), channel_id=1, source_target_pairs={{1,0},{2,1},{3,2},{4,3},{5,4},{6,5},{7,6},{8,7},{9,8},{10,9},{11,1... | collective-permute-start | bytes 196616 | tf_op jit(solution)/shard_map/ppermute | solution.py:21
  17.7 8.5 %all-to-all-done = bf16[16,16,1152]{2,1,0:T(8,128)(2,1)S(1)} async-done(((bf16[16,16,1152]{2,1,0:T(8,128)(2,1)}), bf16[16,16,1152]{2,1,0:T(8,128)(2,1)S(1)}, u32[]{:S(2)}, u32[]{:S(2)}) %all-to-all-start) | async-done | bytes 589856 | tf_op jit(solution)/shard_map/all_to_all | solution.py:36
  26.2 3.3 %collective-permute-start.2 = (bf16[16,16,1152]{2,1,0:T(8,128)(2,1)S(1)}, bf16[16,16,1152]{2,1,0:T(8,128)(2,1)S(1)}, u32[]{:S(2)}, u32[]{:S(2)}) collective-permute-start(bf16[16,16,1152]{2,1,0:T(8,128)(2,1)S(1)} %all-to-all-done), channel_id=1, source_target_pairs={{0,16},{16,0},{32,48},{48,32},{64,80},{80,64},{96,112},{112,96},{1... | collective-permute-start | bytes 1769480 | tf_op jit(solution)/shard_map/ppermute | solution.py:30
  29.8 1.1 pad_maximum_fusion.2
  30.8 1.6 %fusion.35 = (bf16[1,8,128,256]{3,2,1,0:T(8,128)(2,1)}, bf16[1,8,128,256]{3,2,1,0:T(8,128)(2,1)}, bf16[1,8,128,256]{3,2,1,0:T(8,128)(2,1)}, bf16[1,8,128,256]{3,...) fusion(bf16[1,10,130,256]{3,2,1,0:T(8,128)(2,1)S(1)} %select_maximum_fusion.2), kind=kLoop, calls=%fused_computation.90 | loop fusion | bytes 6291456 | tf_op jit(solution)/shard_map/slice | solution.py:96
  32.7 0.6 copy.15
  33.3 1.4 fusion.27
  35.0 0.7 copy-done.1
  35.7 0.3 fusion.29
  36.0 0.3 fusion.31
  36.3 0.7 copy-done.7
  37.1 0.3 convolution_add_fusion.10
  37.4 0.7 copy-done.5
  38.4 0.7 copy-done.4
  39.2 0.3 convolution_add_fusion.8
  39.5 0.3 fusion.3
  39.8 0.7 copy-done.6
  40.5 0.4 fusion.38
  40.9 0.4 multiply_reduce_fusion.1
  41.3 0.6 copy-done.11
  42.0 1.9 %fusion.32 = (f32[1024]{0:T(1024)S(1)}, f32[1024]{0:T(1024)S(1)}, f32[1024,256]{1,0:T(8,128)S(1)}, bf16[1024,256]{1,0:T(8,128)(2,1)}) fusion(f32[1024]{0:T(1024)S(1)} %add_rsqrt_fusion, f32[1024,256]{1,0:T(8,128)S(1)} %get-tuple-element.36, f32[1024]{0:T(1024)S(1)} %broadcast_multiply_fusion.2, f32[256]{0:T(256)S(1)} %copy-done.12, ...), kind=kLoop, calls=%fused_computation.88 | loop fusion | flops 4978688 | bytes 3163136 | tf_op jit(solution)/shard_map/reduce_sum | solution.py:89
  43.9 0.8 multiply_convert_fusion
  44.9 0.3 fusion.16
  45.3 0.3 fusion.15
  45.6 0.3 fusion.14
  46.0 0.3 fusion.13
  46.3 0.3 fusion.12
  46.7 0.3 fusion.11
  47.0 0.3 fusion.10
  47.4 0.3 fusion.9
  47.8 0.3 fusion.8
  48.1 1.2 constant_dynamic-slice_fusion
  49.3 2.7 %copy.22 = f32[256,1152]{1,0:T(8,128)} copy(f32[256,1152]{0,1:T(8,128)} %get-tuple-element.12) | data formatting | bytes 2359296
  52.0 1.9 %collective-permute-start.5 = (f32[256,1152]{1,0:T(8,128)}, f32[256,1152]{1,0:T(8,128)}, u32[]{:S(2)}, u32[]{:S(2)}) collective-permute-start(f32[256,1152]{1,0:T(8,128)} %copy.22), channel_id=1, source_target_pairs={{0,16},{16,0},{32,48},{48,32},{64,80},{80,64},{96,112},{112,96},{1... | collective-permute-start | bytes 3538952 | tf_op jit(solution)/shard_map/ppermute | solution.py:30
  53.9 1.4 %copy.21 = f32[256,1152]{1,0:T(8,128)} copy(f32[256,1152]{0,1:T(8,128)S(1)} %get-tuple-element.13) | data formatting | bytes 2359296
  55.3 1.7 %collective-permute-done.5 = f32[256,1152]{1,0:T(8,128)} collective-permute-done((f32[256,1152]{1,0:T(8,128)}, f32[256,1152]{1,0:T(8,128)}, u32[]{:S(2)}, u32[]{:S(2)}) %collective-permute-start.5) | collective-permute-done | bytes 1179680 | tf_op jit(solution)/shard_map/ppermute | solution.py:30
  57.0 2.8 %add.117 = f32[256,1152]{1,0:T(8,128)} add(f32[256,1152]{1,0:T(8,128)} %copy.21, f32[256,1152]{1,0:T(8,128)} %collective-permute-done.5) | non-fusion elementwise | flops 294912 | bytes 3538944 | tf_op jit(solution)/shard_map/add | solution.py:61
  59.8 4.7 %all-to-all-start.1 = ((f32[16,16,1152]{2,1,0:T(8,128)}), f32[16,16,1152]{2,1,0:T(8,128)S(1)}, u32[]{:S(2)}, u32[]{:S(2)}) async-start(f32[16,16,1152]{2,1,0:T(8,128)} %bitcast.46), calls=%async_computation.1 | async-start | bytes 2359296 | tf_op jit(solution)/shard_map/all_to_all | solution.py:42
  64.5 3.1 %collective-permute-start.3 = (bf16[1,1,128,256]{3,2,1,0:T(8,128)(2,1)S(1)}, bf16[1,1,128,256]{3,2,1,0:T(8,128)(2,1)S(1)}, u32[]{:S(2)}, u32[]{:S(2)}) collective-permute-start(bf16[1,1,128,256]{3,2,1,0:T(8,128)(2,1)S(1)} %get-tuple-element.29), channel_id=1, source_target_pairs={{0,1},{1,2},{2,3},{3,4},{4,5},{5,6},{6,7},{7,8},{8,9},{9,10},{10,1... | collective-permute-start | bytes 196616 | tf_op jit(solution)/shard_map/ppermute | solution.py:20
  67.6 4.3 %collective-permute-start.4 = (bf16[1,1,128,256]{3,2,1,0:T(8,128)(2,1)S(1)}, bf16[1,1,128,256]{3,2,1,0:T(8,128)(2,1)S(1)}, u32[]{:S(2)}, u32[]{:S(2)}) collective-permute-start(bf16[1,1,128,256]{3,2,1,0:T(8,128)(2,1)S(1)} %get-tuple-element.30), channel_id=1, source_target_pairs={{1,0},{2,1},{3,2},{4,3},{5,4},{6,5},{7,6},{8,7},{9,8},{10,9},{11,1... | collective-permute-start | bytes 196616 | tf_op jit(solution)/shard_map/ppermute | solution.py:21
  72.0 22.3 %collective-permute-done.3 = bf16[1,1,128,256]{3,2,1,0:T(8,128)(2,1)S(1)} collective-permute-done((bf16[1,1,128,256]{3,2,1,0:T(8,128)(2,1)S(1)}, bf16[1,1,128,256]{3,2,1,0:T(8,128)(2,1)S(1)}, u32[]{:S(2)}, u32[]{:S(2)}) %collective-permute-start.3) | collective-permute-done | bytes 65568 | tf_op jit(solution)/shard_map/ppermute | solution.py:20
  94.5 1.3 fusion.34
  95.8 0.3 fusion.26
  96.1 0.3 convolution_add_fusion.6
  96.4 0.3 convolution_add_fusion.5
  96.8 1.3 convolution_add_fusion.4
  98.2 8.9 %collective-permute-start.6 = (f32[16,1152]{1,0:T(8,128)S(1)}, f32[16,1152]{1,0:T(8,128)S(1)}, u32[]{:S(2)}, u32[]{:S(2)}) collective-permute-start(f32[16,1152]{1,0:T(8,128)S(1)} %reduce_sum.49), channel_id=1, source_target_pairs={{0,32},{16,48},{32,0},{48,16},{64,96},{80,112},{96,64},{112,80},{1... | collective-permute-start | bytes 221192 | tf_op jit(solution)/shard_map/ppermute | solution.py:30
  107.1 1.6 %convolution_add_fusion.3 = f32[1024,256]{1,0:T(8,128)S(1)} fusion(f32[1024,256]{1,0:T(8,128)} %convolution_add_fusion.4, bf16[1024,256]{1,0:T(8,128)(2,1)S(1)} %multiply_convert_fusion, bf16[3,3,256,256]{3,2,1,0:T(8,128)(2,1)S(1)} %bitcast.172), kind=kOutput, calls=%fused_computation.12 | convolution fusion | flops 134479872 | bytes 2752512 | tf_op jit(solution)/shard_map/dot_general | solution.py:128
  108.8 8.3 %collective-permute-start.7 = (f32[16,1152]{1,0:T(8,128)S(1)}, f32[16,1152]{1,0:T(8,128)S(1)}, u32[]{:S(2)}, u32[]{:S(2)}) collective-permute-start(f32[16,1152]{1,0:T(8,128)S(1)} %add.118), channel_id=1, source_target_pairs={{0,96},{16,112},{32,64},{48,80},{64,32},{80,48},{96,0},{112,16},{1... | collective-permute-start | bytes 221192 | tf_op jit(solution)/shard_map/ppermute | solution.py:30
  117.2 0.3 convolution_add_fusion.2
  117.5 1.4 collective-permute-done.7
  118.9 3.1 %collective-permute-start.8 = (f32[16,1152]{1,0:T(8,128)S(1)}, f32[16,1152]{1,0:T(8,128)S(1)}, u32[]{:S(2)}, u32[]{:S(2)}) collective-permute-start(f32[16,1152]{1,0:T(8,128)S(1)} %add.119), channel_id=1, source_target_pairs={{0,128},{16,144},{32,160},{48,176},{64,192},{80,208},{96,224},{112... | collective-permute-start | bytes 221192 | tf_op jit(solution)/shard_map/ppermute | solution.py:30
  122.0 0.3 convolution_add_fusion.1
  122.4 1.6 %collective-permute-done.8 = f32[16,1152]{1,0:T(8,128)S(1)} collective-permute-done((f32[16,1152]{1,0:T(8,128)S(1)}, f32[16,1152]{1,0:T(8,128)S(1)}, u32[]{:S(2)}, u32[]{:S(2)}) %collective-permute-start.8) | collective-permute-done | bytes 73760 | tf_op jit(solution)/shard_map/ppermute | solution.py:30
  124.0 4.4 %collective-permute-start.9 = (f32[16,1152]{1,0:T(8,128)S(1)}, f32[16,1152]{1,0:T(8,128)S(1)}, u32[]{:S(2)}, u32[]{:S(2)}) collective-permute-start(f32[16,1152]{1,0:T(8,128)S(1)} %add.120), channel_id=1, source_target_pairs={{0,384},{16,400},{32,416},{48,432},{64,448},{80,464},{96,480},{112... | collective-permute-start | bytes 221192 | tf_op jit(solution)/shard_map/ppermute | solution.py:30
  128.4 0.3 fusion.30
  128.7 1.6 %collective-permute-done.9 = f32[16,1152]{1,0:T(8,128)S(1)} collective-permute-done((f32[16,1152]{1,0:T(8,128)S(1)}, f32[16,1152]{1,0:T(8,128)S(1)}, u32[]{:S(2)}, u32[]{:S(2)}) %collective-permute-start.9) | collective-permute-done | bytes 73760 | tf_op jit(solution)/shard_map/ppermute | solution.py:30
  130.3 7.6 %collective-permute-start.10 = (f32[16,1152]{1,0:T(8,128)S(1)}, f32[16,1152]{1,0:T(8,128)S(1)}, u32[]{:S(2)}, u32[]{:S(2)}) collective-permute-start(f32[16,1152]{1,0:T(8,128)S(1)} %add.121), channel_id=1, source_target_pairs={{0,16},{16,0},{32,48},{48,32},{64,80},{80,64},{96,112},{112,96},{1... | collective-permute-start | bytes 221192 | tf_op jit(solution)/shard_map/ppermute | solution.py:30
  138.0 1.1 fusion.6
  139.2 0.7 copy.19
  (47 shorter events, 2.0 us)
Async XLA Ops:
  0.6 9.6 %copy-start = (bf16[1,8,128,256]{3,2,1,0:T(8,128)(2,1)S(1)}, bf16[1,8,128,256]{3,2,1,0:T(8,128)(2,1)}, u32[]{:S(2)}) copy-start(bf16[1,8,128,256]{3,2,1,0:T(8,128)(2,1)} %param.4) | copy-start | bytes 1572868
  2.6 23.6 %all-to-all-start = ((bf16[16,16,1152]{2,1,0:T(8,128)(2,1)}), bf16[16,16,1152]{2,1,0:T(8,128)(2,1)S(1)}, u32[]{:S(2)}, u32[]{:S(2)}) async-start(bf16[16,16,1152]{2,1,0:T(8,128)(2,1)} %broadcast_in_dim.2), calls=%async_computation | async-start | bytes 1179648 | tf_op jit(solution)/shard_map/all_to_all | solution.py:36
  10.3 19.3 %collective-permute-start = (bf16[1,1,128,256]{3,2,1,0:T(8,128)(2,1)S(1)}, bf16[1,1,128,256]{3,2,1,0:T(8,128)(2,1)S(1)}, u32[]{:S(2)}, u32[]{:S(2)}) collective-permute-start(bf16[1,1,128,256]{3,2,1,0:T(8,128)(2,1)S(1)} %get-tuple-element.33), channel_id=1, source_target_pairs={{0,1},{1,2},{2,3},{3,4},{4,5},{5,6},{6,7},{7,8},{8,9},{9,10},{10,1... | collective-permute-start | bytes 196616 | tf_op jit(solution)/shard_map/ppermute | solution.py:20
  13.4 16.2 %collective-permute-start.1 = (bf16[1,1,128,256]{3,2,1,0:T(8,128)(2,1)S(1)}, bf16[1,1,128,256]{3,2,1,0:T(8,128)(2,1)S(1)}, u32[]{:S(2)}, u32[]{:S(2)}) collective-permute-start(bf16[1,1,128,256]{3,2,1,0:T(8,128)(2,1)S(1)} %get-tuple-element.34), channel_id=1, source_target_pairs={{1,0},{2,1},{3,2},{4,3},{5,4},{6,5},{7,6},{8,7},{9,8},{10,9},{11,1... | collective-permute-start | bytes 196616 | tf_op jit(solution)/shard_map/ppermute | solution.py:21
  26.2 6.2 %collective-permute-start.2 = (bf16[16,16,1152]{2,1,0:T(8,128)(2,1)S(1)}, bf16[16,16,1152]{2,1,0:T(8,128)(2,1)S(1)}, u32[]{:S(2)}, u32[]{:S(2)}) collective-permute-start(bf16[16,16,1152]{2,1,0:T(8,128)(2,1)S(1)} %all-to-all-done), channel_id=1, source_target_pairs={{0,16},{16,0},{32,48},{48,32},{64,80},{80,64},{96,112},{112,96},{1... | collective-permute-start | bytes 1769480 | tf_op jit(solution)/shard_map/ppermute | solution.py:30
  33.3 1.4 %copy-start.2 = (bf16[1,8,128,256]{3,2,1,0:T(8,128)(2,1)S(1)}, bf16[1,8,128,256]{3,2,1,0:T(8,128)(2,1)}, u32[]{:S(2)}) copy-start(bf16[1,8,128,256]{3,2,1,0:T(8,128)(2,1)} %get-tuple-element.23) | copy-start | bytes 1572868
  34.7 1.0 copy-start.1
  36.0 1.0 copy-start.7
  37.1 1.0 copy-start.5
  38.1 1.0 copy-start.4
  39.5 1.0 copy-start.6
  40.5 0.8 copy-start.12
  40.9 1.0 copy-start.11
  43.9 1.0 copy-start.3
  52.0 5.1 %collective-permute-start.5 = (f32[256,1152]{1,0:T(8,128)}, f32[256,1152]{1,0:T(8,128)}, u32[]{:S(2)}, u32[]{:S(2)}) collective-permute-start(f32[256,1152]{1,0:T(8,128)} %copy.22), channel_id=1, source_target_pairs={{0,16},{16,0},{32,48},{48,32},{64,80},{80,64},{96,112},{112,96},{1... | collective-permute-start | bytes 3538952 | tf_op jit(solution)/shard_map/ppermute | solution.py:30
  59.8 38.3 %all-to-all-start.1 = ((f32[16,16,1152]{2,1,0:T(8,128)}), f32[16,16,1152]{2,1,0:T(8,128)S(1)}, u32[]{:S(2)}, u32[]{:S(2)}) async-start(f32[16,16,1152]{2,1,0:T(8,128)} %bitcast.46), calls=%async_computation.1 | async-start | bytes 2359296 | tf_op jit(solution)/shard_map/all_to_all | solution.py:42
  64.5 29.7 %collective-permute-start.3 = (bf16[1,1,128,256]{3,2,1,0:T(8,128)(2,1)S(1)}, bf16[1,1,128,256]{3,2,1,0:T(8,128)(2,1)S(1)}, u32[]{:S(2)}, u32[]{:S(2)}) collective-permute-start(bf16[1,1,128,256]{3,2,1,0:T(8,128)(2,1)S(1)} %get-tuple-element.29), channel_id=1, source_target_pairs={{0,1},{1,2},{2,3},{3,4},{4,5},{5,6},{6,7},{7,8},{8,9},{9,10},{10,1... | collective-permute-start | bytes 196616 | tf_op jit(solution)/shard_map/ppermute | solution.py:20
  67.6 26.6 %collective-permute-start.4 = (bf16[1,1,128,256]{3,2,1,0:T(8,128)(2,1)S(1)}, bf16[1,1,128,256]{3,2,1,0:T(8,128)(2,1)S(1)}, u32[]{:S(2)}, u32[]{:S(2)}) collective-permute-start(bf16[1,1,128,256]{3,2,1,0:T(8,128)(2,1)S(1)} %get-tuple-element.30), channel_id=1, source_target_pairs={{1,0},{2,1},{3,2},{4,3},{5,4},{6,5},{7,6},{8,7},{9,8},{10,9},{11,1... | collective-permute-start | bytes 196616 | tf_op jit(solution)/shard_map/ppermute | solution.py:21
  98.2 19.0 %copy-start.10 = (bf16[1,8,128,256]{3,2,1,0:T(8,128)(2,1)S(1)}, bf16[1,8,128,256]{3,2,1,0:T(8,128)(2,1)}, u32[]{:S(2)}) copy-start(bf16[1,8,128,256]{3,2,1,0:T(8,128)(2,1)} %get-tuple-element.16) | copy-start | bytes 1572868
  98.2 10.6 %collective-permute-start.6 = (f32[16,1152]{1,0:T(8,128)S(1)}, f32[16,1152]{1,0:T(8,128)S(1)}, u32[]{:S(2)}, u32[]{:S(2)}) collective-permute-start(f32[16,1152]{1,0:T(8,128)S(1)} %reduce_sum.49), channel_id=1, source_target_pairs={{0,32},{16,48},{32,0},{48,16},{64,96},{80,112},{96,64},{112,80},{1... | collective-permute-start | bytes 221192 | tf_op jit(solution)/shard_map/ppermute | solution.py:30
  108.8 10.1 %collective-permute-start.7 = (f32[16,1152]{1,0:T(8,128)S(1)}, f32[16,1152]{1,0:T(8,128)S(1)}, u32[]{:S(2)}, u32[]{:S(2)}) collective-permute-start(f32[16,1152]{1,0:T(8,128)S(1)} %add.118), channel_id=1, source_target_pairs={{0,96},{16,112},{32,64},{48,80},{64,32},{80,48},{96,0},{112,16},{1... | collective-permute-start | bytes 221192 | tf_op jit(solution)/shard_map/ppermute | solution.py:30
  117.2 4.8 %copy-start.9 = (bf16[1,8,128,256]{3,2,1,0:T(8,128)(2,1)S(1)}, bf16[1,8,128,256]{3,2,1,0:T(8,128)(2,1)}, u32[]{:S(2)}) copy-start(bf16[1,8,128,256]{3,2,1,0:T(8,128)(2,1)} %get-tuple-element.15) | copy-start | bytes 1572868
  118.9 5.1 %collective-permute-start.8 = (f32[16,1152]{1,0:T(8,128)S(1)}, f32[16,1152]{1,0:T(8,128)S(1)}, u32[]{:S(2)}, u32[]{:S(2)}) collective-permute-start(f32[16,1152]{1,0:T(8,128)S(1)} %add.119), channel_id=1, source_target_pairs={{0,128},{16,144},{32,160},{48,176},{64,192},{80,208},{96,224},{112... | collective-permute-start | bytes 221192 | tf_op jit(solution)/shard_map/ppermute | solution.py:30
  122.0 6.4 %copy-start.8 = (bf16[1,8,128,256]{3,2,1,0:T(8,128)(2,1)S(1)}, bf16[1,8,128,256]{3,2,1,0:T(8,128)(2,1)}, u32[]{:S(2)}) copy-start(bf16[1,8,128,256]{3,2,1,0:T(8,128)(2,1)} %get-tuple-element.20) | copy-start | bytes 1572868
  124.0 6.3 %collective-permute-start.9 = (f32[16,1152]{1,0:T(8,128)S(1)}, f32[16,1152]{1,0:T(8,128)S(1)}, u32[]{:S(2)}, u32[]{:S(2)}) collective-permute-start(f32[16,1152]{1,0:T(8,128)S(1)} %add.120), channel_id=1, source_target_pairs={{0,384},{16,400},{32,416},{48,432},{64,448},{80,464},{96,480},{112... | collective-permute-start | bytes 221192 | tf_op jit(solution)/shard_map/ppermute | solution.py:30
  130.3 8.8 %collective-permute-start.10 = (f32[16,1152]{1,0:T(8,128)S(1)}, f32[16,1152]{1,0:T(8,128)S(1)}, u32[]{:S(2)}, u32[]{:S(2)}) collective-permute-start(f32[16,1152]{1,0:T(8,128)S(1)} %add.121), channel_id=1, source_target_pairs={{0,16},{16,0},{32,48},{48,32},{64,80},{80,64},{96,112},{112,96},{1... | collective-permute-start | bytes 221192 | tf_op jit(solution)/shard_map/ppermute | solution.py:30
